TPU v7x, 32 devices: a whole 2x2x4 slice. The times are simulated.
32 devices in a mesh: space: 8 (over z, x), chan: 4 (over y, core).
Axes of the slice: x: 2, y: 2, z: 4, core: 2. Of those that a mesh axis runs over, the one named last changes fastest.
Arguments:
- volume: bfloat16 [8, 4, 64, 512], P('space'), may hold values from -6 to 6
- weight_one: bfloat16 [3, 3, 3, 512, 512], P(None, None, None, 'chan'), may hold values from -0.0546875 to 0.0546875
- bias_one: float32 [512], P('chan'), may hold values from -3 to 3
- weight_two: bfloat16 [3, 3, 3, 512, 512], P(None, None, None, 'chan'), may hold values from -0.0546875 to 0.0546875
- bias_two: float32 [512], P('chan'), may hold values from -3 to 3
Outputs:
- features: bfloat16 [8, 512, 256], P('space', 'chan')
All inputs are finite; a program needn't handle non-finite values.
Results may differ from a plain program's by a relative error of at most 0.0044.
Values may be sent and summed in bfloat16 or wider, within the bound.
No kernel may reach another device: no remote copies, remote signals or barrier semaphores. Data moves between devices by JAX's collectives and lax.ppermute only.
A program may use at most 64 MiB of HBM per device.

v0:
```python
import jax
import jax.numpy as jnp
from jax import lax
from jax.sharding import PartitionSpec as P


def passed_along(shard, axis, by):
    length = lax.axis_size(axis)
    return lax.ppermute(shard, axis, [(i, (i + by) % length) for i in range(length)])


def plane_taps(slab, kernel_part, depth_tap):
    planes, rows_n, cols_n, count_in = slab.shape
    outs = kernel_part.shape[3]
    stacked = kernel_part[depth_tap].reshape(9 * outs, count_in)
    products = lax.dot_general(
        slab.reshape(-1, count_in),
        stacked,
        (((1,), (1,)), ((), ())),
        preferred_element_type=jnp.float32,
    )
    products = products.reshape(planes, rows_n, cols_n, 3, 3, outs)
    summed = jnp.zeros((planes, rows_n, cols_n, outs), jnp.float32)
    for row_tap in range(3):
        for col_tap in range(3):
            summed = summed + jnp.roll(
                products[:, :, :, row_tap, col_tap], (1 - row_tap, 1 - col_tap), axis=(1, 2)
            )
    return summed


def conv_layer(field, kernel, bias):
    planes, rows_n, cols_n, owned = field.shape
    outs = kernel.shape[3]
    empty = jnp.zeros((planes * rows_n * cols_n, outs), jnp.float32)
    gathered = lax.all_gather(field, "chan", axis=3, tiled=True)
    first_tap = plane_taps(gathered, kernel, 0)
    middle_tap = plane_taps(gathered, kernel, 1)
    last_tap = plane_taps(gathered, kernel, 2)
    below = passed_along(first_tap, "space", 1)
    above = passed_along(last_tap, "space", -1)
    from_below = jnp.concatenate([below, first_tap[:-1]], axis=0)
    from_above = jnp.concatenate([last_tap[1:], above], axis=0)
    total = (middle_tap + from_below + from_above).reshape(empty.shape)
    result = jnp.maximum(total + bias[None, :], 0.0).astype(jnp.bfloat16)
    return result.reshape(planes, rows_n, cols_n, outs)


def per_device(volume, weight_one, bias_one, weight_two, bias_two):
    width_in = weight_one.shape[4]
    share = width_in // lax.axis_size("chan")
    first = lax.axis_index("chan") * share
    local_in = lax.dynamic_slice_in_dim(volume, first, share, 3)
    hidden = conv_layer(local_in, weight_one, bias_one)
    output = conv_layer(hidden, weight_two, bias_two)
    planes, rows_n, cols_n, owned = output.shape
    return output.reshape(planes, rows_n * cols_n, owned).transpose(0, 2, 1)


def solution(mesh):
    return jax.shard_map(
        per_device,
        mesh=mesh,
        in_specs=(
            P("space", None, None, None),
            P(None, None, None, "chan", None),
            P("chan"),
            P(None, None, None, "chan", None),
            P("chan"),
        ),
        out_specs=P("space", "chan", None),
        check_vma=False,
    )
```

profile of v0, /device:TPU:0, one launch (start us, length us, event | category | flops | bytes accessed | tf_op | source)
XLA Modules:
  0.0 44.1 jit_solution(14822002702201880432)
XLA Ops:
  0.0 0.0 copy-start
  0.0 0.9 %copy-done = bf16[1,4,64,512]{3,2,1,0:T(8,128)(2,1)S(1)} copy-done((bf16[1,4,64,512]{3,2,1,0:T(8,128)(2,1)S(1)}, bf16[1,4,64,512]{3,2,1,0:T(8,128)(2,1)}, u32[]{:S(2)}) %copy-start) | copy-done | bytes 262168
  1.0 7.2 %all_gather.6 = bf16[1,4,64,512]{3,2,1,0:T(8,128)(2,1)S(1)} all-gather(bf16[1,4,64,128]{3,2,1,0:T(8,128)(2,1)S(1)} %constant_dynamic-slice_fusion), channel_id=1, replica_groups=mesh['space'=8,'chan'=4] {'chan'}, dimensions={3}, use_global_device_ids=true | all-gather | bytes 327680 | tf_op jit(solution)/shard_map/all_gather | solution.py:36
  8.2 1.8 %convolution_bitcast_fusion.3 = f32[1,4,64,3,3,128]{5,2,1,4,3,0:T(8,128)S(1)} fusion(bf16[3,3,3,128,512]{4,3,2,1,0:T(8,128)(2,1)} %param.6, bf16[1,4,64,512]{3,2,1,0:T(8,128)(2,1)S(1)} %all_gather.6), kind=kOutput, calls=%fused_computation.3 | convolution fusion | flops 301989888 | bytes 2621440 | tf_op jit(solution)/shard_map/dot_general | solution.py:16
  10.0 0.1 slice_bitcast_fusion.28
  10.1 0.0 copy-start.1
  10.4 0.1 fusion.57
  10.4 4.6 %collective-permute-start.1 = (f32[1,4,64,128]{3,2,1,0:T(8,128)S(1)}, f32[1,4,64,128]{3,2,1,0:T(8,128)S(1)}, u32[]{:S(2)}, u32[]{:S(2)}) collective-permute-start(f32[1,4,64,128]{3,2,1,0:T(8,128)S(1)} %fusion.57), channel_id=1, source_target_pairs={{0,28},{4,0},{8,4},{12,8},{16,12},{20,16},{24,20},{28,24},{1,29},{... | collective-permute-start | bytes 393224 | tf_op jit(solution)/shard_map/ppermute | solution.py:9
  15.1 0.0 copy-done.1
  15.1 0.5 %convolution_bitcast_fusion.4 = f32[1,4,64,3,3,128]{5,2,1,4,3,0:T(8,128)S(1)} fusion(bf16[3,3,3,128,512]{4,3,2,1,0:T(8,128)(2,1)S(1)} %copy-done.1, bf16[1,4,64,512]{3,2,1,0:T(8,128)(2,1)S(1)} %all_gather.6), kind=kOutput, calls=%fused_computation.4 | convolution fusion | flops 301989888 | bytes 2621440 | tf_op jit(solution)/shard_map/dot_general | solution.py:16
  15.6 0.1 slice_bitcast_fusion.37
  15.9 0.1 fusion.69
  16.0 0.1 collective-permute-start
  16.1 0.5 %convolution_bitcast_fusion.5 = f32[1,4,64,3,3,128]{5,2,4,3,1,0:T(8,128)S(1)} fusion(bf16[3,3,3,128,512]{4,3,2,1,0:T(8,128)(2,1)S(1)} %copy-done.1, bf16[1,4,64,512]{3,2,1,0:T(8,128)(2,1)S(1)} %all_gather.6), kind=kOutput, calls=%fused_computation.5 | convolution fusion | flops 301989888 | bytes 2621440 | tf_op jit(solution)/shard_map/dot_general | solution.py:16
  16.6 0.1 slice_bitcast_fusion.46
  16.7 0.0 copy-start.4
  16.8 0.0 copy-start.2
  17.0 1.3 %collective-permute-done.1 = f32[1,4,64,128]{3,2,1,0:T(8,128)S(1)} collective-permute-done((f32[1,4,64,128]{3,2,1,0:T(8,128)S(1)}, f32[1,4,64,128]{3,2,1,0:T(8,128)S(1)}, u32[]{:S(2)}, u32[]{:S(2)}) %collective-permute-start.1) | collective-permute-done | bytes 131104 | tf_op jit(solution)/shard_map/ppermute | solution.py:9
  18.3 5.9 %collective-permute-done = f32[1,4,64,128]{3,2,1,0:T(8,128)S(1)} collective-permute-done((f32[1,4,64,128]{3,2,1,0:T(8,128)S(1)}, f32[1,4,64,128]{3,2,1,0:T(8,128)S(1)}, u32[]{:S(2)}, u32[]{:S(2)}) %collective-permute-start) | collective-permute-done | bytes 131104 | tf_op jit(solution)/shard_map/ppermute | solution.py:9
  24.2 0.0 copy-done.4
  24.2 0.1 fusion.86
  24.3 5.8 %all_gather.7 = bf16[1,4,64,512]{3,2,1,0:T(8,128)(2,1)S(1)} all-gather(bf16[1,4,64,128]{3,2,1,0:T(8,128)(2,1)S(1)} %fusion.86), channel_id=1, replica_groups=mesh['space'=8,'chan'=4] {'chan'}, dimensions={3}, use_global_device_ids=true | all-gather | bytes 327680 | tf_op jit(solution)/shard_map/all_gather | solution.py:36
  30.2 0.0 copy-done.2
  30.2 0.5 %convolution_bitcast_fusion = f32[1,4,64,3,3,128]{5,2,1,4,3,0:T(8,128)S(1)} fusion(bf16[3,3,3,128,512]{4,3,2,1,0:T(8,128)(2,1)S(1)} %copy-done.2, bf16[1,4,64,512]{3,2,1,0:T(8,128)(2,1)S(1)} %all_gather.7), kind=kOutput, calls=%fused_computation | convolution fusion | flops 301989888 | bytes 2621440 | tf_op jit(solution)/shard_map/dot_general | solution.py:16
  30.7 0.1 slice_bitcast_fusion.1
  31.0 0.5 %convolution_bitcast_fusion.1 = f32[1,4,64,3,3,128]{5,2,1,4,3,0:T(8,128)S(1)} fusion(bf16[3,3,3,128,512]{4,3,2,1,0:T(8,128)(2,1)S(1)} %copy-done.2, bf16[1,4,64,512]{3,2,1,0:T(8,128)(2,1)S(1)} %all_gather.7), kind=kOutput, calls=%fused_computation.1 | convolution fusion | flops 301989888 | bytes 2621440 | tf_op jit(solution)/shard_map/dot_general | solution.py:16
  31.5 0.1 slice_bitcast_fusion.10
  31.9 0.5 %convolution_bitcast_fusion.2 = f32[1,4,64,3,3,128]{5,2,4,3,1,0:T(8,128)S(1)} fusion(bf16[3,3,3,128,512]{4,3,2,1,0:T(8,128)(2,1)S(1)} %copy-done.2, bf16[1,4,64,512]{3,2,1,0:T(8,128)(2,1)S(1)} %all_gather.7), kind=kOutput, calls=%fused_computation.2 | convolution fusion | flops 301989888 | bytes 2621440 | tf_op jit(solution)/shard_map/dot_general | solution.py:16
  32.4 0.1 slice_bitcast_fusion.19
  32.6 0.1 fusion.19
  32.6 2.1 %collective-permute-start.3 = (f32[1,4,64,128]{3,2,1,0:T(8,128)S(1)}, f32[1,4,64,128]{3,2,1,0:T(8,128)S(1)}, u32[]{:S(2)}, u32[]{:S(2)}) collective-permute-start(f32[1,4,64,128]{3,2,1,0:T(8,128)S(1)} %fusion.19), channel_id=1, source_target_pairs={{0,28},{4,0},{8,4},{12,8},{16,12},{20,16},{24,20},{28,24},{1,29},{... | collective-permute-start | bytes 393224 | tf_op jit(solution)/shard_map/ppermute | solution.py:9
  34.8 0.1 fusion.31
  34.9 0.1 collective-permute-start.2
  35.2 0.0 copy-start.3
  35.2 3.3 %collective-permute-done.3 = f32[1,4,64,128]{3,2,1,0:T(8,128)S(1)} collective-permute-done((f32[1,4,64,128]{3,2,1,0:T(8,128)S(1)}, f32[1,4,64,128]{3,2,1,0:T(8,128)S(1)}, u32[]{:S(2)}, u32[]{:S(2)}) %collective-permute-start.3) | collective-permute-done | bytes 131104 | tf_op jit(solution)/shard_map/ppermute | solution.py:9
  38.5 4.6 %collective-permute-done.2 = f32[1,4,64,128]{3,2,1,0:T(8,128)S(1)} collective-permute-done((f32[1,4,64,128]{3,2,1,0:T(8,128)S(1)}, f32[1,4,64,128]{3,2,1,0:T(8,128)S(1)}, u32[]{:S(2)}, u32[]{:S(2)}) %collective-permute-start.2) | collective-permute-done | bytes 131104 | tf_op jit(solution)/shard_map/ppermute | solution.py:9
  43.1 0.1 fusion.45
  43.2 0.1 copy.26
  43.3 0.0 copy-done.3
  43.3 0.7 %fusion.97 = bf16[1,128,256]{2,1,0:T(8,128)(2,1)} fusion(f32[1,256,128]{1,2,0:T(8,128)S(1)} %copy.26, f32[128]{0:T(128)S(1)} %copy-done.3), kind=kLoop, calls=%fused_computation.206 | loop fusion | flops 98304 | bytes 197120 | tf_op jit(solution)/shard_map/transpose | solution.py:57
  (100 shorter events, 0.7 us)
Async XLA Ops:
  0.0 1.0 %copy-start = (bf16[1,4,64,512]{3,2,1,0:T(8,128)(2,1)S(1)}, bf16[1,4,64,512]{3,2,1,0:T(8,128)(2,1)}, u32[]{:S(2)}) copy-start(bf16[1,4,64,512]{3,2,1,0:T(8,128)(2,1)} %param.5) | copy-start | bytes 786436
  10.1 4.9 %copy-start.1 = (bf16[3,3,3,128,512]{4,3,2,1,0:T(8,128)(2,1)S(1)}, bf16[3,3,3,128,512]{4,3,2,1,0:T(8,128)(2,1)}, u32[]{:S(2)}) copy-start(bf16[3,3,3,128,512]{4,3,2,1,0:T(8,128)(2,1)} %param.6) | copy-start | bytes 10616836
  10.4 7.9 %collective-permute-start.1 = (f32[1,4,64,128]{3,2,1,0:T(8,128)S(1)}, f32[1,4,64,128]{3,2,1,0:T(8,128)S(1)}, u32[]{:S(2)}, u32[]{:S(2)}) collective-permute-start(f32[1,4,64,128]{3,2,1,0:T(8,128)S(1)} %fusion.57), channel_id=1, source_target_pairs={{0,28},{4,0},{8,4},{12,8},{16,12},{20,16},{24,20},{28,24},{1,29},{... | collective-permute-start | bytes 393224 | tf_op jit(solution)/shard_map/ppermute | solution.py:9
  16.0 8.2 %collective-permute-start = (f32[1,4,64,128]{3,2,1,0:T(8,128)S(1)}, f32[1,4,64,128]{3,2,1,0:T(8,128)S(1)}, u32[]{:S(2)}, u32[]{:S(2)}) collective-permute-start(f32[1,4,64,128]{3,2,1,0:T(8,128)S(1)} %fusion.69), channel_id=1, source_target_pairs={{0,4},{4,8},{8,12},{12,16},{16,20},{20,24},{24,28},{28,0},{1,5},{5... | collective-permute-start | bytes 393224 | tf_op jit(solution)/shard_map/ppermute | solution.py:9
  16.7 7.5 %copy-start.4 = (f32[128]{0:T(128)S(1)}, f32[128]{0:T(128)}, u32[]{:S(2)}) copy-start(f32[128]{0:T(128)} %param.7) | copy-start | bytes 1540
  16.8 13.4 %copy-start.2 = (bf16[3,3,3,128,512]{4,3,2,1,0:T(8,128)(2,1)S(1)}, bf16[3,3,3,128,512]{4,3,2,1,0:T(8,128)(2,1)}, u32[]{:S(2)}) copy-start(bf16[3,3,3,128,512]{4,3,2,1,0:T(8,128)(2,1)} %param.8) | copy-start | bytes 10616836
  32.6 5.8 %collective-permute-start.3 = (f32[1,4,64,128]{3,2,1,0:T(8,128)S(1)}, f32[1,4,64,128]{3,2,1,0:T(8,128)S(1)}, u32[]{:S(2)}, u32[]{:S(2)}) collective-permute-start(f32[1,4,64,128]{3,2,1,0:T(8,128)S(1)} %fusion.19), channel_id=1, source_target_pairs={{0,28},{4,0},{8,4},{12,8},{16,12},{20,16},{24,20},{28,24},{1,29},{... | collective-permute-start | bytes 393224 | tf_op jit(solution)/shard_map/ppermute | solution.py:9
  34.9 8.2 %collective-permute-start.2 = (f32[1,4,64,128]{3,2,1,0:T(8,128)S(1)}, f32[1,4,64,128]{3,2,1,0:T(8,128)S(1)}, u32[]{:S(2)}, u32[]{:S(2)}) collective-permute-start(f32[1,4,64,128]{3,2,1,0:T(8,128)S(1)} %fusion.31), channel_id=1, source_target_pairs={{0,4},{4,8},{8,12},{12,16},{16,20},{20,24},{24,28},{28,0},{1,5},{5... | collective-permute-start | bytes 393224 | tf_op jit(solution)/shard_map/ppermute | solution.py:9
  35.2 8.1 %copy-start.3 = (f32[128]{0:T(128)S(1)}, f32[128]{0:T(128)}, u32[]{:S(2)}) copy-start(f32[128]{0:T(128)} %param.9) | copy-start | bytes 1540
where the time goes:
time: 44.2 us; the launch traced here: 44.1 us
  waiting for transfers between devices  15.2 us (34%)
  blocking collectives  13.1 us (30%)
  starting transfers between devices  6.84 us (15%)
  matrix products  4.45 us (10%)
  local copies, waits for them, and re-layouts  2.15 us (5%)
  other arithmetic  1.43 us (3%)
  between operations  0.96 us (2%)
    ppermute x4, waiting for transfers between devices, passed_along(): lax.ppermute(shard, axis, [(i, (i + by) % length) for i in range(length)])  15.2 us
    all_gather x2, blocking collectives, conv_layer(): gathered = lax.all_gather(field, 'chan', axis=3, tiled=True)  13.1 us
    ppermute x4, starting transfers between devices, passed_along(): lax.ppermute(shard, axis, [(i, (i + by) % length) for i in range(length)])  6.84 us
    dot_general x6, matrix products, plane_taps(): lax.dot_general(slab.reshape(-1, count_in), stacked, (((1,), (1,)), ((),...  4.45 us
    unnamed x10, local copies, waits for them, and re-layouts  0.98 us
  transfers between devices with their start and end apart: 4, of which 4 were waited for; matrix products, arithmetic and copies ran while one was open for 4% of the time, Pallas kernels for 0%

commit v1 on v0

v1 whole, which is shorter than its diff:
```python
import jax
import jax.numpy as jnp
from jax import lax
from jax.sharding import PartitionSpec as P


def shifted_from(block, by):
    length = lax.axis_size("space")
    return lax.ppermute(block, "space", [((i + by) % length, i) for i in range(length)])


def grid_from(block, by_space, by_chan):
    spaces = lax.axis_size("space")
    chans = lax.axis_size("chan")
    pairs = []
    for s in range(spaces):
        for c in range(chans):
            source = ((s + by_space) % spaces) * chans + (c + by_chan) % chans
            pairs.append((source, s * chans + c))
    return lax.ppermute(block, ("space", "chan"), pairs)


def spatial_sum(products, rows_n, cols_n, outs):
    products = products.reshape(rows_n, cols_n, 3, 3, outs)
    summed = None
    for row_tap in range(3):
        for col_tap in range(3):
            term = jnp.roll(products[:, :, row_tap, col_tap], (1 - row_tap, 1 - col_tap), axis=(0, 1))
            summed = term if summed is None else summed + term
    return summed


def tap_products(plane, kernel_tap):
    rows_n, cols_n, count_in = plane.shape
    outs = kernel_tap.shape[2]
    return lax.dot_general(
        plane.reshape(rows_n * cols_n, count_in),
        kernel_tap.reshape(9 * outs, count_in),
        (((1,), (1,)), ((), ())),
        preferred_element_type=jnp.float32,
    )


def conv_planes(planes, kernel, bias):
    rows_n, cols_n, _ = planes[1].shape
    outs = kernel.shape[3]
    products = None
    for depth_tap in (1, 0, 2):
        term = tap_products(planes[depth_tap], kernel[depth_tap])
        products = term if products is None else products + term
    total = spatial_sum(products, rows_n, cols_n, outs)
    return jnp.maximum(total + bias, 0.0)


def per_device(volume, weight_one, bias_one, weight_two, bias_two):
    plane = volume[0]
    rows_n, cols_n, _ = plane.shape
    planes = [shifted_from(plane, -1), plane, shifted_from(plane, 1)]
    hidden = conv_planes(planes, weight_one, bias_one).astype(jnp.bfloat16)

    chans = lax.axis_size("chan")
    me = lax.axis_index("chan")
    gathered = []
    for depth_tap in range(3):
        blocks = []
        for by_chan in range(chans):
            if depth_tap == 1 and by_chan == 0:
                blocks.append(hidden)
            else:
                blocks.append(grid_from(hidden, depth_tap - 1, by_chan))
        rotated = jnp.concatenate(blocks, axis=-1)
        owned = hidden.shape[-1]
        gathered.append(jnp.roll(rotated, me * owned, axis=-1))
    output = conv_planes(gathered, weight_two, bias_two).astype(jnp.bfloat16)
    outs = output.shape[-1]
    return output.reshape(1, rows_n * cols_n, outs).transpose(0, 2, 1)


def solution(mesh):
    return jax.shard_map(
        per_device,
        mesh=mesh,
        in_specs=(
            P("space", None, None, None),
            P(None, None, None, "chan", None),
            P("chan"),
            P(None, None, None, "chan", None),
            P("chan"),
        ),
        out_specs=P("space", "chan", None),
        check_vma=False,
    )
```

time: 44.2 us -> 46 us (1.041)
  starting transfers between devices: 6.84 us -> 20.7 us
  blocking collectives: 13.1 us -> 0 us
  local copies, waits for them, and re-layouts: 2.15 us -> 6.91 us
  waiting for transfers between devices: 15.2 us -> 11.7 us
  other arithmetic: 1.43 us -> 2.96 us
  matrix products: 4.45 us -> 3.21 us
  between operations: 0.96 us -> 0.32 us
    ppermute x4 -> x13, starting transfers between devices: 6.84 us -> 20.7 us  [the longest x11 14.7 us: grid_from(): return lax.ppermute(block, ('space', 'chan'), pairs)]
    all_gather x2 -> x0, blocking collectives: 13.1 us -> none  [conv_layer(): gathered = lax.all_gather(field, 'chan', axis=3, tiled=True)]
    slice x90 -> x14, local copies, waits for them, and re-layouts: 0.59 us -> 4.63 us  [the longest x2 2.64 us: conv_planes(): term = tap_products(planes[depth_tap], kernel[depth_tap])]
    ppermute x4 -> x13, waiting for transfers between devices: 15.2 us -> 11.7 us  [the longest x2 7.13 us: shifted_from(): lax.ppermute(block, 'space', [((i + by) % length, i) for i in range(lengt...]
    concatenate x9 -> x10, other arithmetic: 0.15 us -> 2.09 us  [the longest x3 1.98 us: per_device(): gathered.append(jnp.roll(rotated, me * owned, axis=-1))]
    dot_general x6, matrix products: 4.45 us -> 3.21 us  [tap_products(): lax.dot_general(plane.reshape(rows_n * cols_n, count_in), kernel_tap.resh...]
    reshape x1 -> x2, local copies, waits for them, and re-layouts: 0.09 us -> 1.04 us  [spatial_sum(): products = products.reshape(rows_n, cols_n, 3, 3, outs)]
    transpose x0 -> x1, local copies, waits for them, and re-layouts: none -> 0.74 us  [per_device(): return output.reshape(1, rows_n * cols_n, outs).transpose(0, 2, 1)]
  transfers between devices with their start and end apart: 4 -> 13, of which waited for: 4 -> 5; matrix products, arithmetic and copies ran while one was open for 4% -> 14% of each run, Pallas kernels for 0% -> 0%
where the time goes in v1:
time: 46 us; the launch traced here: 45.8 us
  starting transfers between devices  20.7 us (45%)
  waiting for transfers between devices  11.7 us (25%)
  local copies, waits for them, and re-layouts  6.91 us (15%)
  matrix products  3.21 us (7%)
  other arithmetic  2.96 us (6%)
    ppermute x11, starting transfers between devices, grid_from(): return lax.ppermute(block, ('space', 'chan'), pairs)  14.7 us
    ppermute x2, waiting for transfers between devices, shifted_from(): lax.ppermute(block, 'space', [((i + by) % length, i) for i in range(lengt...  7.13 us
    ppermute x2, starting transfers between devices, shifted_from(): lax.ppermute(block, 'space', [((i + by) % length, i) for i in range(lengt...  6.03 us
    ppermute x11, waiting for transfers between devices, grid_from(): return lax.ppermute(block, ('space', 'chan'), pairs)  4.56 us
    dot_general x6, matrix products, tap_products(): lax.dot_general(plane.reshape(rows_n * cols_n, count_in), kernel_tap.resh...  3.21 us
    slice x2, local copies, waits for them, and re-layouts, conv_planes(): term = tap_products(planes[depth_tap], kernel[depth_tap])  2.64 us
    concatenate x3, other arithmetic, per_device(): gathered.append(jnp.roll(rotated, me * owned, axis=-1))  1.98 us
    slice x10, local copies, waits for them, and re-layouts, spatial_sum(): jnp.roll(products[:, :, row_tap, col_tap], (1 - row_tap, 1 - col_tap), ax...  1.39 us
  transfers between devices with their start and end apart: 13, of which 5 were waited for; matrix products, arithmetic and copies ran while one was open for 14% of the time, Pallas kernels for 0%

profile of v1, /device:TPU:0, one launch (start us, length us, event | category | flops | bytes accessed | tf_op | source)
XLA Modules:
  0.0 45.8 jit_solution(15521549770026416716)
XLA Ops:
  0.0 2.9 %collective-permute-start = (bf16[4,64,512]{2,1,0:T(8,128)(2,1)}, bf16[4,64,512]{2,1,0:T(8,128)(2,1)S(1)}, u32[]{:S(2)}, u32[]{:S(2)}) collective-permute-start(bf16[4,64,512]{2,1,0:T(8,128)(2,1)} %bitcast.184), channel_id=1, source_target_pairs={{28,0},{0,4},{4,8},{8,12},{12,16},{16,20},{20,24},{24,28},{29,1},{... | collective-permute-start | bytes 786440 | tf_op jit(solution)/shard_map/ppermute | solution.py:9
  2.9 3.1 %collective-permute-start.1 = (bf16[4,64,512]{2,1,0:T(8,128)(2,1)}, bf16[4,64,512]{2,1,0:T(8,128)(2,1)S(1)}, u32[]{:S(2)}, u32[]{:S(2)}) collective-permute-start(bf16[4,64,512]{2,1,0:T(8,128)(2,1)} %bitcast.185), channel_id=1, source_target_pairs={{4,0},{8,4},{12,8},{16,12},{20,16},{24,20},{28,24},{0,28},{5,1},{9... | collective-permute-start | bytes 786440 | tf_op jit(solution)/shard_map/ppermute | solution.py:9
  6.0 2.3 %fusion.48 = (bf16[1,3,3,128,512]{4,3,2,1,0:T(8,128)(2,1)S(1)}, bf16[1,3,3,128,512]{4,3,2,1,0:T(8,128)(2,1)S(1)}, bf16[1,3,3,128,512]{4,3,2,1,0:T(8,128)(2,1)S(1)}) fusion(bf16[3,3,3,128,512]{4,3,2,1,0:T(8,128)(2,1)} %param.8), kind=kLoop, calls=%fused_computation.99 | loop fusion | bytes 7077888 | tf_op jit(solution)/shard_map/slice | solution.py:49
  8.3 0.5 %fusion.55 = f32[256,1152]{1,0:T(8,128)S(1)} fusion(bf16[256,512]{1,0:T(8,128)(2,1)S(1)} %bitcast.186, bf16[1152,512]{1,0:T(8,128)(2,1)S(1)} %bitcast.137), kind=kOutput, calls=%fused_computation.106 | convolution fusion | flops 301989888 | bytes 2621440 | tf_op jit(solution)/shard_map/dot_general | solution.py:36
  8.9 5.6 %collective-permute-done = bf16[4,64,512]{2,1,0:T(8,128)(2,1)S(1)} collective-permute-done((bf16[4,64,512]{2,1,0:T(8,128)(2,1)}, bf16[4,64,512]{2,1,0:T(8,128)(2,1)S(1)}, u32[]{:S(2)}, u32[]{:S(2)}) %collective-permute-start) | collective-permute-done | bytes 262176 | tf_op jit(solution)/shard_map/ppermute | solution.py:9
  14.4 0.5 %convolution_add_fusion.3 = f32[256,1152]{1,0:T(8,128)S(1)} fusion(f32[256,1152]{1,0:T(8,128)S(1)} %fusion.55, bf16[256,512]{1,0:T(8,128)(2,1)S(1)} %bitcast.188, bf16[1152,512]{1,0:T(8,128)(2,1)S(1)} %bitcast.141), kind=kOutput, calls=%fused_computation.3 | convolution fusion | flops 302284800 | bytes 3801088 | tf_op jit(solution)/shard_map/dot_general | solution.py:36
  15.0 1.6 %collective-permute-done.1 = bf16[4,64,512]{2,1,0:T(8,128)(2,1)S(1)} collective-permute-done((bf16[4,64,512]{2,1,0:T(8,128)(2,1)}, bf16[4,64,512]{2,1,0:T(8,128)(2,1)S(1)}, u32[]{:S(2)}, u32[]{:S(2)}) %collective-permute-start.1) | collective-permute-done | bytes 262176 | tf_op jit(solution)/shard_map/ppermute | solution.py:9
  16.5 0.5 %convolution_add_fusion.2 = f32[256,1152]{1,0:T(8,128)S(1)} fusion(f32[256,1152]{1,0:T(8,128)S(1)} %convolution_add_fusion.3, bf16[256,512]{1,0:T(8,128)(2,1)S(1)} %bitcast.187, bf16[1152,512]{1,0:T(8,128)(2,1)S(1)} %bitcast.140), kind=kOutput, calls=%fused_computation.2 | convolution fusion | flops 302284800 | bytes 3801088 | tf_op jit(solution)/shard_map/dot_general | solution.py:36
  17.1 0.5 %reshape.164 = f32[4,64,3,3,128]{4,3,2,1,0:T(4,128)S(1)} reshape(f32[256,1152]{1,0:T(8,128)S(1)} %convolution_add_fusion.2) | data formatting | bytes 2359296 | tf_op jit(solution)/shard_map/reshape | solution.py:24
  17.6 0.0 copy-start.2
  17.6 0.1 fusion.53
  17.8 0.0 copy-start
  17.8 0.5 %fusion.52 = (f32[3,64,1,1,128]{4,3,2,1,0:T(1,128)S(1)}, f32[3,64,1,1,128]{4,3,2,1,0:T(1,128)S(1)}, f32[3,64,1,1,128]{4,3,2,1,0:T(1,128)S(1)}, f32[3,64,1,1,128]...) fusion(f32[4,64,3,3,128]{4,3,2,1,0:T(4,128)S(1)} %reshape.164), kind=kLoop, calls=%fused_computation.103 | loop fusion | bytes 1179648 | tf_op jit(solution)/shard_map/jit(_roll_static)/slice | solution.py:28
  18.3 0.3 fusion.54
  18.7 0.8 %fusion.32 = bf16[4,64,128]{2,1,0:T(8,128)(2,1)} fusion(f32[1,64,128]{2,1,0:T(8,128)S(1)} %bitcast.179, f32[3,64,128]{2,1,0:T(8,128)S(1)} %bitcast.152, f32[1,64,128]{2,1,0:T(8,128)S(1)} %bitcast.192, f32[3,64,128]{2,1,0:T(8,128)S(1)} %bitcast.173, f32[4,64,128]{2,1,0:T(8,128)S(1)} %bitcast.167, f32[3,64,128]{2,1,0:T(8,128)S(1)} %bitcast.150, ...), kind=kLoop, calls=%fused_computation.69 | loop fusion | flops 819200 | bytes 1503744 | tf_op jit(solution)/shard_map/convert_element_type | solution.py:59
  19.5 1.5 %collective-permute-start.3 = (bf16[4,64,128]{2,1,0:T(8,128)(2,1)}, bf16[4,64,128]{2,1,0:T(8,128)(2,1)}, u32[]{:S(2)}, u32[]{:S(2)}) collective-permute-start(bf16[4,64,128]{2,1,0:T(8,128)(2,1)} %fusion.32), channel_id=1, source_target_pairs={{2,0},{3,1},{0,2},{1,3},{6,4},{7,5},{4,6},{5,7},{10,8},{11,9},{8,1... | collective-permute-start | bytes 196616 | tf_op jit(solution)/shard_map/ppermute | solution.py:20
  21.0 0.2 collective-permute-start.4
  21.2 0.4 fusion.47
  21.6 0.9 %collective-permute-start.5 = (bf16[4,64,128]{2,1,0:T(8,128)(2,1)}, bf16[4,64,128]{2,1,0:T(8,128)(2,1)S(1)}, u32[]{:S(2)}, u32[]{:S(2)}) collective-permute-start(bf16[4,64,128]{2,1,0:T(8,128)(2,1)} %fusion.32), channel_id=1, source_target_pairs={{28,0},{29,1},{30,2},{31,3},{0,4},{1,5},{2,6},{3,7},{4,8},{5,9},{6... | collective-permute-start | bytes 196616 | tf_op jit(solution)/shard_map/ppermute | solution.py:20
  22.5 2.7 %collective-permute-start.6 = (bf16[4,64,128]{2,1,0:T(8,128)(2,1)}, bf16[4,64,128]{2,1,0:T(8,128)(2,1)S(1)}, u32[]{:S(2)}, u32[]{:S(2)}) collective-permute-start(bf16[4,64,128]{2,1,0:T(8,128)(2,1)} %fusion.32), channel_id=1, source_target_pairs={{29,0},{30,1},{31,2},{28,3},{1,4},{2,5},{3,6},{0,7},{5,8},{6,9},{7... | collective-permute-start | bytes 196616 | tf_op jit(solution)/shard_map/ppermute | solution.py:20
  25.2 1.3 %collective-permute-start.7 = (bf16[4,64,128]{2,1,0:T(8,128)(2,1)}, bf16[4,64,128]{2,1,0:T(8,128)(2,1)S(1)}, u32[]{:S(2)}, u32[]{:S(2)}) collective-permute-start(bf16[4,64,128]{2,1,0:T(8,128)(2,1)} %fusion.32), channel_id=1, source_target_pairs={{30,0},{31,1},{28,2},{29,3},{2,4},{3,5},{0,6},{1,7},{6,8},{7,9},{4... | collective-permute-start | bytes 196616 | tf_op jit(solution)/shard_map/ppermute | solution.py:20
  26.5 0.0 collective-permute-done.3
  26.5 1.2 %collective-permute-start.8 = (bf16[4,64,128]{2,1,0:T(8,128)(2,1)}, bf16[4,64,128]{2,1,0:T(8,128)(2,1)S(1)}, u32[]{:S(2)}, u32[]{:S(2)}) collective-permute-start(bf16[4,64,128]{2,1,0:T(8,128)(2,1)} %fusion.32), channel_id=1, source_target_pairs={{31,0},{28,1},{29,2},{30,3},{3,4},{0,5},{1,6},{2,7},{7,8},{4,9},{5... | collective-permute-start | bytes 196616 | tf_op jit(solution)/shard_map/ppermute | solution.py:20
  27.7 0.0 collective-permute-done.4
  27.7 3.2 %collective-permute-start.9 = (bf16[4,64,128]{2,1,0:T(8,128)(2,1)}, bf16[4,64,128]{2,1,0:T(8,128)(2,1)S(1)}, u32[]{:S(2)}, u32[]{:S(2)}) collective-permute-start(bf16[4,64,128]{2,1,0:T(8,128)(2,1)} %fusion.32), channel_id=1, source_target_pairs={{4,0},{5,1},{6,2},{7,3},{8,4},{9,5},{10,6},{11,7},{12,8},{13,9},{1... | collective-permute-start | bytes 196616 | tf_op jit(solution)/shard_map/ppermute | solution.py:20
  30.9 1.3 %fusion.17 = bf16[4,64,512]{2,1,0:T(8,128)(2,1)S(1)} fusion(s32[]{:T(128)S(6)} %select_n.15, bf16[4,64,128]{2,1,0:T(8,128)(2,1)} %fusion.32, bf16[4,64,128]{2,1,0:T(8,128)(2,1)} %collective-permute-done.2, bf16[4,64,128]{2,1,0:T(8,128)(2,1)} %collective-permute-done.3, bf16[4,64,128]{2,1,0:T(8,128)(2,1)} %collective-permute-done.4), kind=kLoop, calls=%fused_computation.45 | loop fusion | flops 2097152 | bytes 524292 | tf_op jit(solution)/shard_map/jit(_roll_dynamic)/concatenate | solution.py:73
  32.3 0.5 %fusion.56 = f32[256,1152]{1,0:T(8,128)S(1)} fusion(bf16[256,512]{1,0:T(8,128)(2,1)S(1)} %bitcast.142, bf16[1152,512]{1,0:T(8,128)(2,1)S(1)} %bitcast.136), kind=kOutput, calls=%fused_computation.107 | convolution fusion | flops 301989888 | bytes 2621440 | tf_op jit(solution)/shard_map/dot_general | solution.py:36
  32.8 0.0 collective-permute-done.5
  32.8 2.4 %collective-permute-start.10 = (bf16[4,64,128]{2,1,0:T(8,128)(2,1)}, bf16[4,64,128]{2,1,0:T(8,128)(2,1)S(1)}, u32[]{:S(2)}, u32[]{:S(2)}) collective-permute-start(bf16[4,64,128]{2,1,0:T(8,128)(2,1)} %fusion.32), channel_id=1, source_target_pairs={{5,0},{6,1},{7,2},{4,3},{9,4},{10,5},{11,6},{8,7},{13,8},{14,9},{1... | collective-permute-start | bytes 196616 | tf_op jit(solution)/shard_map/ppermute | solution.py:20
  35.2 1.2 %collective-permute-start.11 = (bf16[4,64,128]{2,1,0:T(8,128)(2,1)}, bf16[4,64,128]{2,1,0:T(8,128)(2,1)S(1)}, u32[]{:S(2)}, u32[]{:S(2)}) collective-permute-start(bf16[4,64,128]{2,1,0:T(8,128)(2,1)} %fusion.32), channel_id=1, source_target_pairs={{6,0},{7,1},{4,2},{5,3},{10,4},{11,5},{8,6},{9,7},{14,8},{15,9},{1... | collective-permute-start | bytes 196616 | tf_op jit(solution)/shard_map/ppermute | solution.py:20
  36.4 0.0 collective-permute-start.12
  36.4 0.0 collective-permute-done.8
  36.4 0.3 fusion.10
  36.8 0.5 %convolution_add_fusion.1 = f32[256,1152]{1,0:T(8,128)S(1)} fusion(f32[256,1152]{1,0:T(8,128)S(1)} %fusion.56, bf16[256,512]{1,0:T(8,128)(2,1)S(1)} %bitcast.144, bf16[1152,512]{1,0:T(8,128)(2,1)S(1)} %bitcast.139), kind=kOutput, calls=%fused_computation.1 | convolution fusion | flops 302284800 | bytes 3801088 | tf_op jit(solution)/shard_map/dot_general | solution.py:36
  37.3 0.0 collective-permute-done.9
  37.3 0.2 collective-permute-done.10
  37.5 3.2 %collective-permute-done.11 = bf16[4,64,128]{2,1,0:T(8,128)(2,1)S(1)} collective-permute-done((bf16[4,64,128]{2,1,0:T(8,128)(2,1)}, bf16[4,64,128]{2,1,0:T(8,128)(2,1)S(1)}, u32[]{:S(2)}, u32[]{:S(2)}) %collective-permute-start.11) | collective-permute-done | bytes 65568 | tf_op jit(solution)/shard_map/ppermute | solution.py:20
  40.7 1.2 %collective-permute-done.12 = bf16[4,64,128]{2,1,0:T(8,128)(2,1)S(1)} collective-permute-done((bf16[4,64,128]{2,1,0:T(8,128)(2,1)}, bf16[4,64,128]{2,1,0:T(8,128)(2,1)S(1)}, u32[]{:S(2)}, u32[]{:S(2)}) %collective-permute-start.12) | collective-permute-done | bytes 65568 | tf_op jit(solution)/shard_map/ppermute | solution.py:20
  41.9 0.3 fusion.3
  42.2 0.5 %convolution_add_fusion = f32[256,1152]{1,0:T(8,128)S(1)} fusion(f32[256,1152]{1,0:T(8,128)S(1)} %convolution_add_fusion.1, bf16[256,512]{1,0:T(8,128)(2,1)S(1)} %bitcast.143, bf16[1152,512]{1,0:T(8,128)(2,1)S(1)} %bitcast.138), kind=kOutput, calls=%fused_computation | convolution fusion | flops 302284800 | bytes 3801088 | tf_op jit(solution)/shard_map/dot_general | solution.py:36
  42.7 0.5 %reshape.168 = f32[4,64,3,3,128]{4,3,2,1,0:T(4,128)S(1)} reshape(f32[256,1152]{1,0:T(8,128)S(1)} %convolution_add_fusion) | data formatting | bytes 2359296 | tf_op jit(solution)/shard_map/reshape | solution.py:24
  43.3 0.3 fusion.49
  43.6 0.1 fusion.50
  43.7 0.5 %fusion.51 = (f32[3,64,1,1,128]{4,3,2,1,0:T(1,128)S(1)}, f32[3,64,1,1,128]{4,3,2,1,0:T(1,128)S(1)}, f32[3,64,1,1,128]{4,3,2,1,0:T(1,128)S(1)}, f32[3,64,1,1,128]...) fusion(f32[4,64,3,3,128]{4,3,2,1,0:T(4,128)S(1)} %reshape.168), kind=kLoop, calls=%fused_computation.102 | loop fusion | bytes 1179648 | tf_op jit(solution)/shard_map/jit(_roll_static)/slice | solution.py:28
  44.3 0.0 copy-start.3
  44.5 0.5 %copy-done.3 = f32[128]{0:T(128)S(1)} copy-done((f32[128]{0:T(128)S(1)}, f32[128]{0:T(128)}, u32[]{:S(2)}) %copy-start.3) | copy-done | bytes 536
  45.0 0.1 fusion.46
  45.0 0.7 %copy.50 = bf16[1,128,256]{2,1,0:T(8,128)(2,1)} copy(bf16[1,128,256]{1,2,0:T(8,128)(2,1)S(1)} %fusion.46) | data formatting | bytes 131072 | tf_op jit(solution)/shard_map/transpose | solution.py:76
  (22 shorter events, 0.2 us)
Async XLA Ops:
  0.0 8.3 %copy-start.1 = (bf16[1,4,64,512]{3,2,1,0:T(8,128)(2,1)S(1)}, bf16[1,4,64,512]{3,2,1,0:T(8,128)(2,1)}, u32[]{:S(2)}) copy-start(bf16[1,4,64,512]{3,2,1,0:T(8,128)(2,1)} %param.7) | copy-start | bytes 786436
  0.0 14.4 %collective-permute-start = (bf16[4,64,512]{2,1,0:T(8,128)(2,1)}, bf16[4,64,512]{2,1,0:T(8,128)(2,1)S(1)}, u32[]{:S(2)}, u32[]{:S(2)}) collective-permute-start(bf16[4,64,512]{2,1,0:T(8,128)(2,1)} %bitcast.184), channel_id=1, source_target_pairs={{28,0},{0,4},{4,8},{8,12},{12,16},{16,20},{20,24},{24,28},{29,1},{... | collective-permute-start | bytes 786440 | tf_op jit(solution)/shard_map/ppermute | solution.py:9
  2.9 13.6 %collective-permute-start.1 = (bf16[4,64,512]{2,1,0:T(8,128)(2,1)}, bf16[4,64,512]{2,1,0:T(8,128)(2,1)S(1)}, u32[]{:S(2)}, u32[]{:S(2)}) collective-permute-start(bf16[4,64,512]{2,1,0:T(8,128)(2,1)} %bitcast.185), channel_id=1, source_target_pairs={{4,0},{8,4},{12,8},{16,12},{20,16},{24,20},{28,24},{0,28},{5,1},{9... | collective-permute-start | bytes 786440 | tf_op jit(solution)/shard_map/ppermute | solution.py:9
  17.6 1.1 %copy-start.2 = (f32[128]{0:T(128)S(1)}, f32[128]{0:T(128)}, u32[]{:S(2)}) copy-start(f32[128]{0:T(128)} %param.9) | copy-start | bytes 1540
  17.8 3.5 %copy-start = (bf16[3,3,3,128,512]{4,3,2,1,0:T(8,128)(2,1)S(1)}, bf16[3,3,3,128,512]{4,3,2,1,0:T(8,128)(2,1)}, u32[]{:S(2)}) copy-start(bf16[3,3,3,128,512]{4,3,2,1,0:T(8,128)(2,1)} %param.10) | copy-start | bytes 10616836
  19.5 5.7 %collective-permute-start.2 = (bf16[4,64,128]{2,1,0:T(8,128)(2,1)}, bf16[4,64,128]{2,1,0:T(8,128)(2,1)}, u32[]{:S(2)}, u32[]{:S(2)}) collective-permute-start(bf16[4,64,128]{2,1,0:T(8,128)(2,1)} %fusion.32), channel_id=1, source_target_pairs={{1,0},{2,1},{3,2},{0,3},{5,4},{6,5},{7,6},{4,7},{9,8},{10,9},{11,1... | collective-permute-start | bytes 196616 | tf_op jit(solution)/shard_map/ppermute | solution.py:20
  19.5 7.0 %collective-permute-start.3 = (bf16[4,64,128]{2,1,0:T(8,128)(2,1)}, bf16[4,64,128]{2,1,0:T(8,128)(2,1)}, u32[]{:S(2)}, u32[]{:S(2)}) collective-permute-start(bf16[4,64,128]{2,1,0:T(8,128)(2,1)} %fusion.32), channel_id=1, source_target_pairs={{2,0},{3,1},{0,2},{1,3},{6,4},{7,5},{4,6},{5,7},{10,8},{11,9},{8,1... | collective-permute-start | bytes 196616 | tf_op jit(solution)/shard_map/ppermute | solution.py:20
  21.0 6.7 %collective-permute-start.4 = (bf16[4,64,128]{2,1,0:T(8,128)(2,1)}, bf16[4,64,128]{2,1,0:T(8,128)(2,1)}, u32[]{:S(2)}, u32[]{:S(2)}) collective-permute-start(bf16[4,64,128]{2,1,0:T(8,128)(2,1)} %fusion.32), channel_id=1, source_target_pairs={{3,0},{0,1},{1,2},{2,3},{7,4},{4,5},{5,6},{6,7},{11,8},{8,9},{9,10... | collective-permute-start | bytes 196616 | tf_op jit(solution)/shard_map/ppermute | solution.py:20
  21.6 11.2 %collective-permute-start.5 = (bf16[4,64,128]{2,1,0:T(8,128)(2,1)}, bf16[4,64,128]{2,1,0:T(8,128)(2,1)S(1)}, u32[]{:S(2)}, u32[]{:S(2)}) collective-permute-start(bf16[4,64,128]{2,1,0:T(8,128)(2,1)} %fusion.32), channel_id=1, source_target_pairs={{28,0},{29,1},{30,2},{31,3},{0,4},{1,5},{2,6},{3,7},{4,8},{5,9},{6... | collective-permute-start | bytes 196616 | tf_op jit(solution)/shard_map/ppermute | solution.py:20
  22.5 12.7 %collective-permute-start.6 = (bf16[4,64,128]{2,1,0:T(8,128)(2,1)}, bf16[4,64,128]{2,1,0:T(8,128)(2,1)S(1)}, u32[]{:S(2)}, u32[]{:S(2)}) collective-permute-start(bf16[4,64,128]{2,1,0:T(8,128)(2,1)} %fusion.32), channel_id=1, source_target_pairs={{29,0},{30,1},{31,2},{28,3},{1,4},{2,5},{3,6},{0,7},{5,8},{6,9},{7... | collective-permute-start | bytes 196616 | tf_op jit(solution)/shard_map/ppermute | solution.py:20
  25.2 11.2 %collective-permute-start.7 = (bf16[4,64,128]{2,1,0:T(8,128)(2,1)}, bf16[4,64,128]{2,1,0:T(8,128)(2,1)S(1)}, u32[]{:S(2)}, u32[]{:S(2)}) collective-permute-start(bf16[4,64,128]{2,1,0:T(8,128)(2,1)} %fusion.32), channel_id=1, source_target_pairs={{30,0},{31,1},{28,2},{29,3},{2,4},{3,5},{0,6},{1,7},{6,8},{7,9},{4... | collective-permute-start | bytes 196616 | tf_op jit(solution)/shard_map/ppermute | solution.py:20
  26.5 9.9 %collective-permute-start.8 = (bf16[4,64,128]{2,1,0:T(8,128)(2,1)}, bf16[4,64,128]{2,1,0:T(8,128)(2,1)S(1)}, u32[]{:S(2)}, u32[]{:S(2)}) collective-permute-start(bf16[4,64,128]{2,1,0:T(8,128)(2,1)} %fusion.32), channel_id=1, source_target_pairs={{31,0},{28,1},{29,2},{30,3},{3,4},{0,5},{1,6},{2,7},{7,8},{4,9},{5... | collective-permute-start | bytes 196616 | tf_op jit(solution)/shard_map/ppermute | solution.py:20
  27.7 9.6 %collective-permute-start.9 = (bf16[4,64,128]{2,1,0:T(8,128)(2,1)}, bf16[4,64,128]{2,1,0:T(8,128)(2,1)S(1)}, u32[]{:S(2)}, u32[]{:S(2)}) collective-permute-start(bf16[4,64,128]{2,1,0:T(8,128)(2,1)} %fusion.32), channel_id=1, source_target_pairs={{4,0},{5,1},{6,2},{7,3},{8,4},{9,5},{10,6},{11,7},{12,8},{13,9},{1... | collective-permute-start | bytes 196616 | tf_op jit(solution)/shard_map/ppermute | solution.py:20
  32.8 4.7 %collective-permute-start.10 = (bf16[4,64,128]{2,1,0:T(8,128)(2,1)}, bf16[4,64,128]{2,1,0:T(8,128)(2,1)S(1)}, u32[]{:S(2)}, u32[]{:S(2)}) collective-permute-start(bf16[4,64,128]{2,1,0:T(8,128)(2,1)} %fusion.32), channel_id=1, source_target_pairs={{5,0},{6,1},{7,2},{4,3},{9,4},{10,5},{11,6},{8,7},{13,8},{14,9},{1... | collective-permute-start | bytes 196616 | tf_op jit(solution)/shard_map/ppermute | solution.py:20
  35.2 5.5 %collective-permute-start.11 = (bf16[4,64,128]{2,1,0:T(8,128)(2,1)}, bf16[4,64,128]{2,1,0:T(8,128)(2,1)S(1)}, u32[]{:S(2)}, u32[]{:S(2)}) collective-permute-start(bf16[4,64,128]{2,1,0:T(8,128)(2,1)} %fusion.32), channel_id=1, source_target_pairs={{6,0},{7,1},{4,2},{5,3},{10,4},{11,5},{8,6},{9,7},{14,8},{15,9},{1... | collective-permute-start | bytes 196616 | tf_op jit(solution)/shard_map/ppermute | solution.py:20
  36.4 5.4 %collective-permute-start.12 = (bf16[4,64,128]{2,1,0:T(8,128)(2,1)}, bf16[4,64,128]{2,1,0:T(8,128)(2,1)S(1)}, u32[]{:S(2)}, u32[]{:S(2)}) collective-permute-start(bf16[4,64,128]{2,1,0:T(8,128)(2,1)} %fusion.32), channel_id=1, source_target_pairs={{7,0},{4,1},{5,2},{6,3},{11,4},{8,5},{9,6},{10,7},{15,8},{12,9},{1... | collective-permute-start | bytes 196616 | tf_op jit(solution)/shard_map/ppermute | solution.py:20
  44.3 0.7 %copy-start.3 = (f32[128]{0:T(128)S(1)}, f32[128]{0:T(128)}, u32[]{:S(2)}) copy-start(f32[128]{0:T(128)} %param.11) | copy-start | bytes 1540

commit v2 on v1

v2 whole, which is shorter than its diff:
```python
import jax
import jax.numpy as jnp
from jax import lax
from jax.sharding import PartitionSpec as P


def gathered_from(block, source_of):
    spaces = lax.axis_size("space")
    chans = lax.axis_size("chan")
    pairs = []
    for s in range(spaces):
        for c in range(chans):
            source_s, source_c = source_of(s, c)
            pairs.append(((source_s % spaces) * chans + source_c % chans, s * chans + c))
    return lax.ppermute(block, ("space", "chan"), pairs)


def from_side(block, distance):
    return gathered_from(block, lambda s, c: (s - distance if c % 2 == 0 else s + distance, c))


def from_chan_partner(block, bit):
    return gathered_from(block, lambda s, c: (s, c ^ bit))


def spatial_sum(products, outs):
    planes, rows_n, cols_n, _ = products.shape
    products = products.reshape(planes, rows_n, cols_n, 3, 3, outs)
    summed = None
    for row_tap in range(3):
        for col_tap in range(3):
            term = jnp.roll(products[:, :, :, row_tap, col_tap], (1 - row_tap, 1 - col_tap), axis=(1, 2))
            summed = term if summed is None else summed + term
    return summed


def conv_stack(field, kernel, bias, planes_out):
    _, rows_n, cols_n, count_in = field.shape
    outs = kernel.shape[3]
    products = None
    for depth_tap in range(3):
        window = field[depth_tap:depth_tap + planes_out].reshape(planes_out * rows_n * cols_n, count_in)
        term = lax.dot_general(
            window,
            kernel[depth_tap].reshape(9 * outs, count_in),
            (((1,), (1,)), ((), ())),
            preferred_element_type=jnp.float32,
        )
        products = term if products is None else products + term
    products = products.reshape(planes_out, rows_n, cols_n, 9 * outs)
    return jnp.maximum(spatial_sum(products, outs) + bias, 0.0)


def xor_order(held, me):
    count = len(held)
    blocks = list(held)
    bit = 1
    while bit < count:
        flip = (me & bit) != 0
        swapped = [blocks[j ^ bit] for j in range(count)]
        blocks = [jnp.where(flip, swapped[j], blocks[j]) for j in range(count)]
        bit *= 2
    return blocks


def per_device(volume, weight_one, bias_one, weight_two, bias_two):
    plane = volume[0]
    rows_n, cols_n, _ = plane.shape
    me = lax.axis_index("chan")
    chans = lax.axis_size("chan")

    near = from_side(plane, 1)
    far = from_side(plane, 2)
    mine = jnp.stack([near, far])
    theirs = from_chan_partner(mine, 1)
    odd = (me % 2) == 1
    below = jnp.where(odd, theirs, mine)
    above = jnp.where(odd, mine, theirs)
    field = jnp.stack([below[1], below[0], plane, above[0], above[1]])
    hidden = conv_stack(field, weight_one, bias_one, 3).astype(jnp.bfloat16)

    held = {0: hidden}
    bit = 1
    while bit < chans:
        bit *= 2
    bit //= 2
    while bit >= 1:
        offsets = sorted(held)
        sent = jnp.stack([held[j] for j in offsets])
        got = from_chan_partner(sent, bit)
        for position, j in enumerate(offsets):
            held[j ^ bit] = got[position]
        bit //= 2
    blocks = xor_order([held[j] for j in range(chans)], me)
    gathered = jnp.concatenate(blocks, axis=-1)
    output = conv_stack(gathered, weight_two, bias_two, 1).astype(jnp.bfloat16)
    outs = output.shape[-1]
    return output.reshape(1, rows_n * cols_n, outs).transpose(0, 2, 1)


def solution(mesh):
    return jax.shard_map(
        per_device,
        mesh=mesh,
        in_specs=(
            P("space", None, None, None),
            P(None, None, None, "chan", None),
            P("chan"),
            P(None, None, None, "chan", None),
            P("chan"),
        ),
        out_specs=P("space", "chan", None),
        check_vma=False,
    )
```

time: 46 us -> 61.1 us (1.33)
  local copies, waits for them, and re-layouts: 6.91 us -> 24.5 us
  starting transfers between devices: 20.7 us -> 6.46 us
  other arithmetic: 2.96 us -> 8.58 us
  waiting for transfers between devices: 11.7 us -> 15.2 us
  matrix products: 3.21 us -> 5.25 us
    ppermute x13 -> x5, starting transfers between devices: 20.7 us -> 6.46 us  [gathered_from(): return lax.ppermute(block, ('space', 'chan'), pairs)]
    slice x14 -> x42, local copies, waits for them, and re-layouts: 4.63 us -> 17.2 us  [the longest x2 8.77 us: spatial_sum(): products[:, :, :, row_tap, col_tap]]
    another operation x0 -> x2, local copies, waits for them, and re-layouts: none -> 4.2 us  [spatial_sum(): products = products.reshape(planes, rows_n, cols_n, 3, 3, outs)]
    ppermute x13 -> x5, waiting for transfers between devices: 11.7 us -> 15.2 us  [gathered_from(): return lax.ppermute(block, ('space', 'chan'), pairs)]
    select_n x0 -> x3, other arithmetic: none -> 3.08 us  [the longest x2 3.01 us: xor_order(): blocks = [jnp.where(flip, swapped[j], blocks[j]) for j in range(count)]]
    dot_general x6, matrix products: 3.21 us -> 5.25 us  [conv_stack(): lax.dot_general(window, kernel[depth_tap].reshape(9 * outs, count_in), ((...]
    concatenate x10 -> x15, other arithmetic: 2.09 us -> 3.88 us  [the longest x14 3.77 us: spatial_sum(): jnp.roll(products[:, :, :, row_tap, col_tap], (1 - row_tap, 1 - col_tap),...]
    unnamed x8 -> x35, local copies, waits for them, and re-layouts: 0.5 us -> 2.12 us
  transfers between devices with their start and end apart: 13 -> 5, of which waited for: 5 -> 3; matrix products, arithmetic and copies ran while one was open for 14% -> 9% of each run, Pallas kernels for 0% -> 0%
where the time goes in v2:
time: 61.1 us; the launch traced here: 60.7 us
  local copies, waits for them, and re-layouts  24.5 us (40%)
  waiting for transfers between devices  15.2 us (25%)
  other arithmetic  8.58 us (14%)
  starting transfers between devices  6.46 us (11%)
  matrix products  5.25 us (9%)
  between operations  0.72 us (1%)
    ppermute x5, waiting for transfers between devices, gathered_from(): return lax.ppermute(block, ('space', 'chan'), pairs)  15.2 us
    slice x2, local copies, waits for them, and re-layouts, spatial_sum(): products[:, :, :, row_tap, col_tap]  8.77 us
    ppermute x5, starting transfers between devices, gathered_from(): return lax.ppermute(block, ('space', 'chan'), pairs)  6.46 us
    dot_general x6, matrix products, conv_stack(): lax.dot_general(window, kernel[depth_tap].reshape(9 * outs, count_in), ((...  5.25 us
    slice x36, local copies, waits for them, and re-layouts, spatial_sum(): jnp.roll(products[:, :, :, row_tap, col_tap], (1 - row_tap, 1 - col_tap),...  4.69 us
    another operation x2, local copies, waits for them, and re-layouts, spatial_sum(): products = products.reshape(planes, rows_n, cols_n, 3, 3, outs)  4.2 us
    concatenate x14, other arithmetic, spatial_sum(): jnp.roll(products[:, :, :, row_tap, col_tap], (1 - row_tap, 1 - col_tap),...  3.77 us
    slice x2, local copies, waits for them, and re-layouts, conv_stack(): kernel[depth_tap].reshape(9 * outs, count_in)  3.66 us
  transfers between devices with their start and end apart: 5, of which 3 were waited for; matrix products, arithmetic and copies ran while one was open for 9% of the time, Pallas kernels for 0%

profile of v2, /device:TPU:0, one launch (start us, length us, event | category | flops | bytes accessed | tf_op | source)
XLA Modules:
  0.0 60.7 jit_solution(5619241174490970146)
XLA Ops:
  0.0 2.9 %collective-permute-start = (bf16[4,64,512]{2,1,0:T(8,128)(2,1)}, bf16[4,64,512]{2,1,0:T(8,128)(2,1)S(1)}, u32[]{:S(2)}, u32[]{:S(2)}) collective-permute-start(bf16[4,64,512]{2,1,0:T(8,128)(2,1)} %bitcast.185), channel_id=1, source_target_pairs={{28,0},{5,1},{30,2},{7,3},{0,4},{9,5},{2,6},{11,7},{4,8},{13,9},{6... | collective-permute-start | bytes 786440 | tf_op jit(solution)/shard_map/ppermute | solution.py:15
  2.9 1.6 %collective-permute-start.1 = (bf16[4,64,512]{2,1,0:T(8,128)(2,1)}, bf16[4,64,512]{2,1,0:T(8,128)(2,1)S(1)}, u32[]{:S(2)}, u32[]{:S(2)}) collective-permute-start(bf16[4,64,512]{2,1,0:T(8,128)(2,1)} %bitcast.186), channel_id=1, source_target_pairs={{24,0},{9,1},{26,2},{11,3},{28,4},{13,5},{30,6},{15,7},{0,8},{17,9... | collective-permute-start | bytes 786440 | tf_op jit(solution)/shard_map/ppermute | solution.py:15
  4.5 8.4 %collective-permute-done = bf16[4,64,512]{2,1,0:T(8,128)(2,1)S(1)} collective-permute-done((bf16[4,64,512]{2,1,0:T(8,128)(2,1)}, bf16[4,64,512]{2,1,0:T(8,128)(2,1)S(1)}, u32[]{:S(2)}, u32[]{:S(2)}) %collective-permute-start) | collective-permute-done | bytes 262176 | tf_op jit(solution)/shard_map/ppermute | solution.py:15
  12.9 1.3 %collective-permute-done.1 = bf16[4,64,512]{2,1,0:T(8,128)(2,1)S(1)} collective-permute-done((bf16[4,64,512]{2,1,0:T(8,128)(2,1)}, bf16[4,64,512]{2,1,0:T(8,128)(2,1)S(1)}, u32[]{:S(2)}, u32[]{:S(2)}) %collective-permute-start.1) | collective-permute-done | bytes 262176 | tf_op jit(solution)/shard_map/ppermute | solution.py:15
  14.2 0.1 pad_maximum_fusion.5
  14.2 0.4 collective-permute-start.2
  14.6 2.3 %fusion.33 = (bf16[1,3,3,128,512]{4,3,2,1,0:T(8,128)(2,1)S(1)}, bf16[1,3,3,128,512]{4,3,2,1,0:T(8,128)(2,1)S(1)}, bf16[1,3,3,128,512]{4,3,2,1,0:T(8,128)(2,1)S(1)}) fusion(bf16[3,3,3,128,512]{4,3,2,1,0:T(8,128)(2,1)} %param.6), kind=kLoop, calls=%fused_computation.99 | loop fusion | bytes 7077888 | tf_op jit(solution)/shard_map/slice | solution.py:45
  16.9 0.0 copy-start.8
  16.9 0.1 broadcast_select_fusion
  17.1 0.8 %copy-done.8 = bf16[1,4,64,512]{3,2,1,0:T(8,128)(2,1)S(1)} copy-done((bf16[1,4,64,512]{3,2,1,0:T(8,128)(2,1)S(1)}, bf16[1,4,64,512]{3,2,1,0:T(8,128)(2,1)}, u32[]{:S(2)}) %copy-start.8) | copy-done | bytes 262168
  17.9 0.2 pad_maximum_fusion.3
  18.1 1.2 %fusion.43 = f32[768,1152]{1,0:T(8,128)S(1)} fusion(bf16[768,512]{1,0:T(8,128)(2,1)S(1)} %bitcast.156, bf16[1152,512]{1,0:T(8,128)(2,1)S(1)} %bitcast.153), kind=kOutput, calls=%fused_computation.109 | convolution fusion | flops 905969664 | bytes 5505024 | tf_op jit(solution)/shard_map/dot_general | solution.py:43
  19.3 1.2 %convolution_add_fusion.1 = f32[768,1152]{1,0:T(8,128)S(1)} fusion(f32[768,1152]{1,0:T(8,128)S(1)} %fusion.43, bf16[768,512]{1,0:T(8,128)(2,1)S(1)} %bitcast.155, bf16[1152,512]{1,0:T(8,128)(2,1)S(1)} %bitcast.149), kind=kOutput, calls=%fused_computation.1 | convolution fusion | flops 906854400 | bytes 9043968 | tf_op jit(solution)/shard_map/dot_general | solution.py:43
  20.5 1.2 %convolution_add_fusion = f32[768,1152]{1,0:T(8,128)S(1)} fusion(f32[768,1152]{1,0:T(8,128)S(1)} %convolution_add_fusion.1, bf16[768,512]{1,0:T(8,128)(2,1)S(1)} %bitcast.154, bf16[1152,512]{1,0:T(8,128)(2,1)S(1)} %bitcast.148), kind=kOutput, calls=%fused_computation | convolution fusion | flops 906854400 | bytes 9043968 | tf_op jit(solution)/shard_map/dot_general | solution.py:43
  21.8 3.7 %reshape_reshape.6 = f32[3,4,64,3,3,128]{5,4,3,2,1,0:T(4,128)} reshape(f32[768,1152]{1,0:T(8,128)S(1)} %convolution_add_fusion) | data formatting | bytes 7077888 | tf_op jit(solution)/shard_map/reshape;reshape | solution.py:28
  25.4 7.6 %fusion.31 = (f32[3,4,64,1,1,128]{5,4,3,2,1,0:T(1,128)S(1)}, f32[3,4,64,1,1,128]{5,4,3,2,1,0:T(1,128)S(1)}, f32[3,4,64,1,1,128]{5,4,3,2,1,0:T(1,128)S(1)}, f32[3...) fusion(f32[3,4,64,3,3,128]{5,4,3,2,1,0:T(4,128)} %reshape_reshape.6), kind=kLoop, calls=%fused_computation.97 | loop fusion | bytes 7077888 | tf_op jit(solution)/shard_map/slice | solution.py:32
  33.1 0.1 copy_bitcast_fusion.4
  33.2 0.1 copy_bitcast_fusion
  33.4 0.8 %pad_maximum_fusion.6 = (f32[3,4,63,128]{3,2,0,1:T(8,128)}, f32[1,3,4,63,128]{4,3,1,2,0:T(8,128)S(1)}) fusion(f32[3,1,64,128]{3,2,0,1:T(8,128)S(1)} %slice.398, f32[3,3,64,128]{3,2,0,1:T(8,128)S(1)} %slice.397), kind=kLoop, calls=%fused_computation.13 | loop fusion | flops 96768 | bytes 1167360 | tf_op jit(solution)/shard_map/jit(_roll_static)/concatenate | solution.py:32
  34.2 0.1 copy_bitcast_fusion.2
  34.3 0.8 %fusion.40 = (f32[3,4,63,128]{3,2,0,1:T(8,128)}, f32[1,3,4,63,128]{4,3,1,2,0:T(8,128)S(1)}) fusion(f32[3,4,64,128]{3,2,0,1:T(8,128)S(1)} %get-tuple-element.63), kind=kLoop, calls=%fused_computation.106 | loop fusion | bytes 1161216 | tf_op jit(solution)/shard_map/jit(_roll_static)/slice | solution.py:32
  35.1 0.8 %fusion.39 = (f32[3,4,63,128]{3,2,0,1:T(8,128)}, f32[1,3,4,63,128]{4,3,1,2,0:T(8,128)S(1)}) fusion(f32[3,4,64,128]{3,2,0,1:T(8,128)S(1)} %get-tuple-element.62), kind=kLoop, calls=%fused_computation.105 | loop fusion | bytes 1161216 | tf_op jit(solution)/shard_map/jit(_roll_static)/slice | solution.py:32
  36.0 0.8 %fusion.42 = (f32[3,3,64,128]{3,2,0,1:T(8,128)}, f32[1,3,3,64,128]{4,3,1,2,0:T(8,128)S(1)}) fusion(f32[3,4,64,128]{3,2,0,1:T(8,128)S(1)} %get-tuple-element.65), kind=kLoop, calls=%fused_computation.108 | loop fusion | bytes 884736 | tf_op jit(solution)/shard_map/jit(_roll_static)/slice | solution.py:32
  36.7 0.6 %fusion.41 = (f32[3,1,64,128]{3,2,0,1:T(8,128)}, f32[1,3,1,64,128]{4,3,1,2,0:T(8,128)S(1)}) fusion(f32[3,4,64,128]{3,2,0,1:T(8,128)S(1)} %get-tuple-element.65), kind=kLoop, calls=%fused_computation.107 | loop fusion | bytes 294912 | tf_op jit(solution)/shard_map/jit(_roll_static)/slice | solution.py:32
  37.5 0.8 %pad_maximum_fusion.7 = (f32[3,4,63,128]{3,2,0,1:T(8,128)}, f32[1,3,4,63,128]{4,3,1,2,0:T(8,128)S(1)}) fusion(f32[3,3,64,128]{3,2,0,1:T(8,128)S(1)} %slice.380, f32[3,1,64,128]{3,2,0,1:T(8,128)S(1)} %slice.379), kind=kLoop, calls=%fused_computation.15 | loop fusion | flops 96768 | bytes 1167360 | tf_op jit(solution)/shard_map/jit(_roll_static)/concatenate | solution.py:32
  38.4 0.8 %fusion.37 = (f32[3,3,64,128]{3,2,0,1:T(8,128)}, f32[1,3,3,64,128]{4,3,1,2,0:T(8,128)S(1)}) fusion(f32[3,4,64,128]{3,2,0,1:T(8,128)S(1)} %get-tuple-element.60), kind=kLoop, calls=%fused_computation.103 | loop fusion | bytes 884736 | tf_op jit(solution)/shard_map/jit(_roll_static)/slice | solution.py:32
  39.2 0.6 %fusion.38 = (f32[3,1,64,128]{3,2,0,1:T(8,128)}, f32[1,3,1,64,128]{4,3,2,1,0:T(8,128)S(1)}) fusion(f32[3,4,64,128]{3,2,0,1:T(8,128)S(1)} %get-tuple-element.60), kind=kLoop, calls=%fused_computation.104 | loop fusion | bytes 294912 | tf_op jit(solution)/shard_map/jit(_roll_static)/slice | solution.py:32
  40.0 0.0 copy-start.1
  40.0 0.4 fusion.8
  40.4 1.6 %collective-permute-start.3 = (bf16[1,3,4,64,128]{4,3,2,1,0:T(8,128)(2,1)S(1)}, bf16[1,3,4,64,128]{4,3,2,1,0:T(8,128)(2,1)S(1)}, u32[]{:S(2)}, u32[]{:S(2)}) collective-permute-start(bf16[1,3,4,64,128]{4,3,2,1,0:T(8,128)(2,1)S(1)} %fusion.8), channel_id=1, source_target_pairs={{2,0},{3,1},{0,2},{1,3},{6,4},{7,5},{4,6},{5,7},{10,8},{11,9},{8,1... | collective-permute-start | bytes 589832 | tf_op jit(solution)/shard_map/ppermute | solution.py:15
  42.0 5.5 %collective-permute-done.3 = bf16[1,3,4,64,128]{4,3,2,1,0:T(8,128)(2,1)S(1)} collective-permute-done((bf16[1,3,4,64,128]{4,3,2,1,0:T(8,128)(2,1)S(1)}, bf16[1,3,4,64,128]{4,3,2,1,0:T(8,128)(2,1)S(1)}, u32[]{:S(2)}, u32[]{:S(2)}) %collective-permute-start.3) | collective-permute-done | bytes 196640 | tf_op jit(solution)/shard_map/ppermute | solution.py:15
  47.5 0.8 %pad_maximum_fusion.8 = bf16[2,3,4,64,128]{4,3,2,1,0:T(8,128)(2,1)} fusion(bf16[1,3,4,64,128]{4,3,2,1,0:T(8,128)(2,1)S(1)} %collective-permute-done.3, bf16[1,3,4,64,128]{4,3,2,1,0:T(8,128)(2,1)S(1)} %fusion.8), kind=kLoop, calls=%fused_computation.27 | loop fusion | flops 196608 | bytes 786432 | tf_op jit(solution)/shard_map/stack | solution.py:89
  48.3 1.4 %fusion.32 = (bf16[1,3,3,128,512]{4,3,2,1,0:T(8,128)(2,1)S(1)}, bf16[1,3,3,128,512]{4,3,2,1,0:T(8,128)(2,1)S(1)}, bf16[1,3,3,128,512]{4,3,2,1,0:T(8,128)(2,1)}) fusion(bf16[3,3,3,128,512]{4,3,2,1,0:T(8,128)(2,1)S(1)} %copy-done.1), kind=kLoop, calls=%fused_computation.98 | loop fusion | bytes 7077888 | tf_op jit(solution)/shard_map/slice | solution.py:45
  49.7 1.0 %slice_maximum_fusion.1 = f32[3,4,63,128]{3,2,0,1:T(8,128)S(1)} fusion(f32[3,3,64,128]{3,2,0,1:T(8,128)S(1)} %slice.386, f32[3,1,64,128]{3,2,0,1:T(8,128)} %copy-done.6), kind=kLoop, calls=%fused_computation.14 | loop fusion | flops 96768 | bytes 780288 | tf_op jit(solution)/shard_map/jit(_roll_static)/concatenate | solution.py:32
  50.7 0.9 %slice_maximum_fusion = f32[3,4,63,128]{3,2,1,0:T(8,128)S(1)} fusion(f32[3,1,64,128]{3,2,1,0:T(8,128)} %copy-done.7, f32[3,3,64,128]{3,2,1,0:T(8,128)S(1)} %slice.403), kind=kLoop, calls=%fused_computation.12 | loop fusion | flops 96768 | bytes 780288 | tf_op jit(solution)/shard_map/jit(_roll_static)/concatenate | solution.py:32
  51.7 1.9 %bitcast_select_fusion.3 = (bf16[3,4,64,128]{3,2,1,0:T(8,128)(2,1)S(1)}, bf16[3,4,64,128]{3,2,1,0:T(8,128)(2,1)S(1)}) fusion(pred[]{:T(512)S(6)} %ne.12, bf16[1,3,4,64,128]{4,3,2,1,0:T(8,128)(2,1)S(1)} %collective-permute-done.3, bf16[2,3,4,64,128]{4,3,2,1,0:T(8,128)(2,1)} %collective-permute-done.4, pred[]{:T(512)S(6)} %ne.13, f32[128]{0:T(128)} %param.7, ...), kind=kLoop, calls=%fused_computation.50 | loop fusion | flops 2162688 | bytes 4524032 | tf_op jit(solution)/shard_map/jit(_where)/select_n | solution.py:61
  53.7 1.1 %bitcast_select_fusion.1 = (bf16[3,4,64,128]{3,2,1,0:T(8,128)(2,1)S(1)}, bf16[3,4,64,128]{3,2,1,0:T(8,128)(2,1)S(1)}, bf16[3,4,64,128]{3,2,1,0:T(8,128)(2,1)S(1)}) fusion(pred[]{:T(512)S(6)} %ne.12, bf16[1,3,4,64,128]{4,3,2,1,0:T(8,128)(2,1)S(1)} %collective-permute-done.3, bf16[2,3,4,64,128]{4,3,2,1,0:T(8,128)(2,1)} %collective-permute-done.4, pred[]{:T(512)S(6)} %ne.13, ...), kind=kLoop, calls=%fused_computation.48 | loop fusion | flops 688128 | bytes 1377792 | tf_op jit(solution)/shard_map/jit(_where)/select_n | solution.py:61
  54.8 0.1 pad_maximum_fusion.4
  54.9 0.1 fusion.35
  55.0 0.5 fusion.44
  55.5 0.7 %copy-done = bf16[1,3,3,128,512]{4,3,2,1,0:T(8,128)(2,1)S(1)} copy-done((bf16[1,3,3,128,512]{4,3,2,1,0:T(8,128)(2,1)S(1)}, bf16[1,3,3,128,512]{4,3,2,1,0:T(8,128)(2,1)}, u32[]{:S(2)}) %copy-start) | copy-done | bytes 1179672
  56.2 0.5 convolution_add_fusion.3
  56.8 0.5 convolution_add_fusion.2
  57.3 0.5 reshape_reshape.7
  57.8 1.1 %fusion.34 = (f32[1,4,64,1,1,128]{5,4,3,2,1,0:T(1,128)S(1)}, f32[1,4,64,1,1,128]{5,4,3,2,1,0:T(1,128)S(1)}, f32[1,4,64,1,1,128]{5,4,3,2,1,0:T(1,128)S(1)}, f32[1...) fusion(f32[1,4,64,3,3,128]{5,4,3,2,1,0:T(4,128)S(1)} %reshape_r, ...), kind=kLoop, calls=%fused_computation.100 | loop fusion | bytes 2359296 | tf_op jit(solution)/shard_map/slice | solution.py:32
  59.2 0.0 copy-start.16
  59.4 0.5 copy-done.16
  59.9 0.7 %copy.82 = bf16[1,128,256]{2,1,0:T(8,128)(2,1)} copy(bf16[1,128,256]{1,2,0:T(8,128)(2,1)S(1)} %bitcast.187) | data formatting | bytes 131072 | tf_op jit(solution)/shard_map/transpose | solution.py:98
  (82 shorter events, 0.7 us)
Async XLA Ops:
  0.0 12.9 %collective-permute-start = (bf16[4,64,512]{2,1,0:T(8,128)(2,1)}, bf16[4,64,512]{2,1,0:T(8,128)(2,1)S(1)}, u32[]{:S(2)}, u32[]{:S(2)}) collective-permute-start(bf16[4,64,512]{2,1,0:T(8,128)(2,1)} %bitcast.185), channel_id=1, source_target_pairs={{28,0},{5,1},{30,2},{7,3},{0,4},{9,5},{2,6},{11,7},{4,8},{13,9},{6... | collective-permute-start | bytes 786440 | tf_op jit(solution)/shard_map/ppermute | solution.py:15
  2.9 11.3 %collective-permute-start.1 = (bf16[4,64,512]{2,1,0:T(8,128)(2,1)}, bf16[4,64,512]{2,1,0:T(8,128)(2,1)S(1)}, u32[]{:S(2)}, u32[]{:S(2)}) collective-permute-start(bf16[4,64,512]{2,1,0:T(8,128)(2,1)} %bitcast.186), channel_id=1, source_target_pairs={{24,0},{9,1},{26,2},{11,3},{28,4},{13,5},{30,6},{15,7},{0,8},{17,9... | collective-permute-start | bytes 786440 | tf_op jit(solution)/shard_map/ppermute | solution.py:15
  14.2 2.7 %collective-permute-start.2 = (bf16[2,4,64,512]{3,2,1,0:T(8,128)(2,1)S(1)}, bf16[2,4,64,512]{3,2,1,0:T(8,128)(2,1)S(1)}, u32[]{:S(2)}, u32[]{:S(2)}) collective-permute-start(bf16[2,4,64,512]{3,2,1,0:T(8,128)(2,1)S(1)} %pad_maximum_fusion.5), channel_id=1, source_target_pairs={{1,0},{0,1},{3,2},{2,3},{5,4},{4,5},{7,6},{6,7},{9,8},{8,9},{11,10... | collective-permute-start | bytes 1572872 | tf_op jit(solution)/shard_map/ppermute | solution.py:15
  16.9 1.0 %copy-start.8 = (bf16[1,4,64,512]{3,2,1,0:T(8,128)(2,1)S(1)}, bf16[1,4,64,512]{3,2,1,0:T(8,128)(2,1)}, u32[]{:S(2)}) copy-start(bf16[1,4,64,512]{3,2,1,0:T(8,128)(2,1)} %param.5) | copy-start | bytes 786436
  33.2 2.8 %copy-start.6 = (f32[3,1,64,128]{3,2,0,1:T(8,128)}, f32[3,1,64,128]{3,2,0,1:T(8,128)S(1)}, u32[]{:S(2)}) copy-start(f32[3,1,64,128]{3,2,0,1:T(8,128)S(1)} %slice.385) | copy-start | bytes 294916
  33.2 5.1 %copy-start.7 = (f32[3,1,64,128]{3,2,1,0:T(8,128)}, f32[3,1,64,128]{3,2,1,0:T(8,128)S(1)}, u32[]{:S(2)}) copy-start(f32[3,1,64,128]{3,2,1,0:T(8,128)S(1)} %slice.404) | copy-start | bytes 294916
  33.4 6.4 %copy-start.11 = (f32[3,4,1,128]{3,2,0,1:T(1,128)}, f32[3,4,1,128]{3,2,0,1:T(1,128)S(1)}, u32[]{:S(2)}) copy-start(f32[3,4,1,128]{3,2,0,1:T(1,128)S(1)} %pad_maximum_fusion.18) | copy-start | bytes 18436
  35.9 3.9 %copy-start.9 = (f32[3,4,1,128]{3,2,0,1:T(1,128)}, f32[3,4,1,128]{3,2,0,1:T(1,128)S(1)}, u32[]{:S(2)}) copy-start(f32[3,4,1,128]{3,2,0,1:T(1,128)S(1)} %slice.395) | copy-start | bytes 18436
  36.0 3.9 %copy-start.13 = (f32[3,4,1,128]{3,2,0,1:T(1,128)}, f32[3,4,1,128]{3,2,0,1:T(1,128)S(1)}, u32[]{:S(2)}) copy-start(f32[3,4,1,128]{3,2,0,1:T(1,128)S(1)} %pad_maximum_fusion.19) | copy-start | bytes 18436
  37.5 2.4 %copy-start.14 = (f32[3,4,1,128]{3,2,0,1:T(1,128)}, f32[3,4,1,128]{3,2,0,1:T(1,128)S(1)}, u32[]{:S(2)}) copy-start(f32[3,4,1,128]{3,2,0,1:T(1,128)S(1)} %pad_maximum_fusion.20) | copy-start | bytes 18436
  38.3 1.6 %copy-start.15 = (f32[128]{0:T(128)S(1)}, f32[128]{0:T(128)}, u32[]{:S(2)}) copy-start(f32[128]{0:T(128)} %param.7) | copy-start | bytes 1540
  40.0 8.3 %copy-start.1 = (bf16[3,3,3,128,512]{4,3,2,1,0:T(8,128)(2,1)S(1)}, bf16[3,3,3,128,512]{4,3,2,1,0:T(8,128)(2,1)}, u32[]{:S(2)}) copy-start(bf16[3,3,3,128,512]{4,3,2,1,0:T(8,128)(2,1)} %param.8) | copy-start | bytes 10616836
  40.4 7.1 %collective-permute-start.3 = (bf16[1,3,4,64,128]{4,3,2,1,0:T(8,128)(2,1)S(1)}, bf16[1,3,4,64,128]{4,3,2,1,0:T(8,128)(2,1)S(1)}, u32[]{:S(2)}, u32[]{:S(2)}) collective-permute-start(bf16[1,3,4,64,128]{4,3,2,1,0:T(8,128)(2,1)S(1)} %fusion.8), channel_id=1, source_target_pairs={{2,0},{3,1},{0,2},{1,3},{6,4},{7,5},{4,6},{5,7},{10,8},{11,9},{8,1... | collective-permute-start | bytes 589832 | tf_op jit(solution)/shard_map/ppermute | solution.py:15
  48.3 3.4 %collective-permute-start.4 = (bf16[2,3,4,64,128]{4,3,2,1,0:T(8,128)(2,1)}, bf16[2,3,4,64,128]{4,3,2,1,0:T(8,128)(2,1)}, u32[]{:S(2)}, u32[]{:S(2)}) collective-permute-start(bf16[2,3,4,64,128]{4,3,2,1,0:T(8,128)(2,1)} %pad_maximum_fusion.8), channel_id=1, source_target_pairs={{1,0},{0,1},{3,2},{2,3},{5,4},{4,5},{7,6},{6,7},{9,8},{8,9},{11,10... | collective-permute-start | bytes 1179656 | tf_op jit(solution)/shard_map/ppermute | solution.py:15
  49.7 2.0 %copy-start.2 = (f32[3,4,63,128]{3,2,0,1:T(8,128)S(1)}, f32[3,4,63,128]{3,2,0,1:T(8,128)}, u32[]{:S(2)}) copy-start(f32[3,4,63,128]{3,2,0,1:T(8,128)} %get-tuple-element.48) | copy-start | bytes 1161220
  49.7 2.0 %copy-start.3 = (f32[3,4,63,128]{3,2,0,1:T(8,128)S(1)}, f32[3,4,63,128]{3,2,0,1:T(8,128)}, u32[]{:S(2)}) copy-start(f32[3,4,63,128]{3,2,0,1:T(8,128)} %get-tuple-element.52) | copy-start | bytes 1161220
  49.7 2.0 %copy-start.4 = (f32[3,4,63,128]{3,2,0,1:T(8,128)S(1)}, f32[3,4,63,128]{3,2,0,1:T(8,128)}, u32[]{:S(2)}) copy-start(f32[3,4,63,128]{3,2,0,1:T(8,128)} %get-tuple-element.50) | copy-start | bytes 1161220
  49.7 2.0 %copy-start.5 = (f32[3,4,63,128]{3,2,0,1:T(8,128)S(1)}, f32[3,4,63,128]{3,2,0,1:T(8,128)}, u32[]{:S(2)}) copy-start(f32[3,4,63,128]{3,2,0,1:T(8,128)} %get-tuple-element.58) | copy-start | bytes 1161220
  49.7 2.1 %copy-start.10 = (f32[3,4,1,128]{3,2,0,1:T(1,128)S(1)}, f32[3,4,1,128]{3,2,0,1:T(1,128)}, u32[]{:S(2)}) copy-start(f32[3,4,1,128]{3,2,0,1:T(1,128)} %copy-done.9) | copy-start | bytes 18436
  49.7 2.1 %copy-start.12 = (f32[3,4,1,128]{3,2,0,1:T(1,128)S(1)}, f32[3,4,1,128]{3,2,0,1:T(1,128)}, u32[]{:S(2)}) copy-start(f32[3,4,1,128]{3,2,0,1:T(1,128)} %copy-done.11) | copy-start | bytes 18436
  55.0 1.3 %copy-start = (bf16[1,3,3,128,512]{4,3,2,1,0:T(8,128)(2,1)S(1)}, bf16[1,3,3,128,512]{4,3,2,1,0:T(8,128)(2,1)}, u32[]{:S(2)}) copy-start(bf16[1,3,3,128,512]{4,3,2,1,0:T(8,128)(2,1)} %get-tuple-element.18) | copy-start | bytes 3538948
  59.2 0.7 %copy-start.16 = (f32[128]{0:T(128)S(1)}, f32[128]{0:T(128)}, u32[]{:S(2)}) copy-start(f32[128]{0:T(128)} %param.9) | copy-start | bytes 1540

commit v3 on v2

v3 whole, which is shorter than its diff:
```python
import functools

import jax
import jax.numpy as jnp
from jax import lax
from jax.experimental import pallas as pl
from jax.experimental.pallas import tpu as pltpu
from jax.sharding import PartitionSpec as P


def gathered_from(block, source_of):
    spaces = lax.axis_size("space")
    chans = lax.axis_size("chan")
    pairs = []
    for s in range(spaces):
        for c in range(chans):
            source_s, source_c = source_of(s, c)
            pairs.append(((source_s % spaces) * chans + source_c % chans, s * chans + c))
    return lax.ppermute(block, ("space", "chan"), pairs)


def from_side(block, distance):
    return gathered_from(block, lambda s, c: (s - distance if c % 2 == 0 else s + distance, c))


def from_chan_partner(block, bit):
    return gathered_from(block, lambda s, c: (s, c ^ bit))


def spatial_epilogue(acc_ref, plane, rows_n, cols_n, outs, bias):
    cells = rows_n * cols_n
    base = plane * cells
    column = lax.broadcasted_iota(jnp.int32, (cells, outs), 0) % cols_n
    total = None
    for col_tap in range(3):
        shifted = None
        for row_tap in range(3):
            tap = row_tap * 3 + col_tap
            part = acc_ref[pl.ds(base, cells), pl.ds(tap * outs, outs)]
            amount = ((1 - row_tap) * cols_n) % cells
            if amount:
                part = pltpu.roll(part, amount, 0)
            shifted = part if shifted is None else shifted + part
        if col_tap == 0:
            shifted = jnp.where(
                column == 0,
                pltpu.roll(shifted, (1 - cols_n) % cells, 0),
                pltpu.roll(shifted, 1, 0),
            )
        elif col_tap == 2:
            shifted = jnp.where(
                column == cols_n - 1,
                pltpu.roll(shifted, cols_n - 1, 0),
                pltpu.roll(shifted, cells - 1, 0),
            )
        total = shifted if total is None else total + shifted
    return jnp.maximum(total + bias, 0.0)


def conv_kernel(fill, planes_out, rows_n, cols_n, transpose_out, *refs):
    flag_ref = refs[0]
    w_ref, b_ref, o_ref, field_ref, acc_ref = refs[-5:]
    inputs = refs[1:-5]
    depth_tap = pl.program_id(0)
    cells = rows_n * cols_n
    outs = b_ref.shape[1]

    @pl.when(depth_tap == 0)
    def _():
        fill(flag_ref[0], inputs, field_ref)

    window = field_ref[pl.ds(depth_tap, planes_out)]
    window = window.reshape(planes_out * cells, window.shape[-1])
    products = lax.dot_general(
        window, w_ref[0], (((1,), (1,)), ((), ())), preferred_element_type=jnp.float32
    )

    @pl.when(depth_tap == 0)
    def _():
        acc_ref[...] = products

    @pl.when(depth_tap > 0)
    def _():
        acc_ref[...] += products

    @pl.when(depth_tap == 2)
    def _():
        bias = b_ref[...]
        for plane in range(planes_out):
            result = spatial_epilogue(acc_ref, plane, rows_n, cols_n, outs, bias)
            if transpose_out:
                o_ref[plane] = result.T.astype(o_ref.dtype)
            else:
                o_ref[plane] = result.astype(o_ref.dtype)


def conv_call(fill, flag, inputs, kernel, bias, field_shape, planes_out, rows_n, cols_n, transpose_out):
    outs = kernel.shape[3]
    count_in = kernel.shape[4]
    cells = rows_n * cols_n
    stacked = kernel.reshape(3, 9 * outs, count_in)
    in_specs = [pl.BlockSpec(x.shape, lambda a, f, n=x.ndim: (0,) * n) for x in inputs]
    in_specs.append(pl.BlockSpec((1, 9 * outs, count_in), lambda a, f: (a, 0, 0)))
    in_specs.append(pl.BlockSpec((1, outs), lambda a, f: (0, 0)))
    out_shape = (planes_out, outs, cells) if transpose_out else (planes_out, cells, outs)
    flops = 2 * 3 * planes_out * cells * count_in * 9 * outs
    moved = stacked.size * 2 + sum(x.size * 2 for x in inputs) + planes_out * cells * outs * 2
    return pl.pallas_call(
        functools.partial(conv_kernel, fill, planes_out, rows_n, cols_n, transpose_out),
        out_shape=jax.ShapeDtypeStruct(out_shape, jnp.bfloat16),
        grid_spec=pltpu.PrefetchScalarGridSpec(
            num_scalar_prefetch=1,
            grid=(3,),
            in_specs=in_specs,
            out_specs=pl.BlockSpec(out_shape, lambda a, f: (0, 0, 0)),
            scratch_shapes=[
                pltpu.VMEM(field_shape, jnp.bfloat16),
                pltpu.VMEM((planes_out * cells, 9 * outs), jnp.float32),
            ],
        ),
        compiler_params=pltpu.CompilerParams(
            dimension_semantics=("arbitrary",), vmem_limit_bytes=48 * 1024 * 1024
        ),
        cost_estimate=pl.CostEstimate(flops=flops, transcendentals=0, bytes_accessed=moved),
    )(flag, *inputs, stacked, bias.reshape(1, outs))


def fill_volume(odd, inputs, field_ref):
    own, mine, theirs = inputs
    is_odd = odd != 0
    below = jnp.where(is_odd, theirs[...], mine[...])
    above = jnp.where(is_odd, mine[...], theirs[...])
    field_ref[0] = below[1]
    field_ref[1] = below[0]
    field_ref[2] = own[...]
    field_ref[3] = above[0]
    field_ref[4] = above[1]


def fill_hidden(layout, me, inputs, field_ref):
    blocks = {}
    for ref, offsets in zip(inputs, layout):
        for position, j in enumerate(offsets):
            blocks[j] = ref[position]
    count = len(blocks)
    ordered = [blocks[j] for j in range(count)]
    bit = 1
    while bit < count:
        flip = (me & bit) != 0
        ordered = [jnp.where(flip, ordered[j ^ bit], ordered[j]) for j in range(count)]
        bit *= 2
    owned = ordered[0].shape[-1]
    for position in range(count):
        field_ref[:, :, pl.ds(position * owned, owned)] = ordered[position]


def per_device(volume, weight_one, bias_one, weight_two, bias_two):
    plane = volume[0]
    rows_n, cols_n, count_in = plane.shape
    cells = rows_n * cols_n
    me = lax.axis_index("chan")
    chans = lax.axis_size("chan")

    flat = plane.reshape(cells, count_in)
    mine = jnp.stack([from_side(flat, 1), from_side(flat, 2)])
    theirs = from_chan_partner(mine, 1)
    odd = (me % 2).astype(jnp.int32).reshape(1)
    hidden = conv_call(
        fill_volume, odd, [flat, mine, theirs], weight_one, bias_one,
        (5, cells, count_in), 3, rows_n, cols_n, False,
    )

    held = [(hidden[None], (0,))]
    offsets = [0]
    bit = 1
    while bit < chans:
        bit *= 2
    bit //= 2
    while bit >= 1:
        sent = jnp.stack([blk for arr, offs in held for blk in [arr[i] for i in range(len(offs))]])
        got = from_chan_partner(sent, bit)
        held.append((got, tuple(j ^ bit for j in offsets)))
        offsets = offsets + [j ^ bit for j in offsets]
        bit //= 2
    layout = tuple(offs for _, offs in held)
    inputs = [arr for arr, _ in held]
    me_flag = me.astype(jnp.int32).reshape(1)
    output = conv_call(
        functools.partial(fill_hidden, layout), me_flag, inputs, weight_two, bias_two,
        (3, cells, count_in), 1, rows_n, cols_n, True,
    )
    return output


def solution(mesh):
    return jax.shard_map(
        per_device,
        mesh=mesh,
        in_specs=(
            P("space", None, None, None),
            P(None, None, None, "chan", None),
            P("chan"),
            P(None, None, None, "chan", None),
            P("chan"),
        ),
        out_specs=P("space", "chan", None),
        check_vma=False,
    )
```

time: 61.1 us -> 37.9 us (0.62)
  local copies, waits for them, and re-layouts: 24.5 us -> 3.61 us
  other arithmetic: 8.58 us -> 0.09 us
  Pallas kernels: 0 us -> 7.74 us
  matrix products: 5.25 us -> 0 us
  waiting for transfers between devices: 15.2 us -> 20 us
  between operations: 0.72 us -> 0.05 us
    slice x42 -> x0, local copies, waits for them, and re-layouts: 17.2 us -> none  [the longest x2 8.77 us: spatial_sum(): products[:, :, :, row_tap, col_tap]]
    pallas_call x0 -> x2, Pallas kernels: none -> 7.74 us  [conv_call(): pl.pallas_call(functools.partial(conv_kernel, fill, planes_out, rows_n, c...]
    dot_general x6 -> x0, matrix products: 5.25 us -> none  [conv_stack(): lax.dot_general(window, kernel[depth_tap].reshape(9 * outs, count_in), ((...]
    ppermute x5, waiting for transfers between devices: 15.2 us -> 20 us  [gathered_from(): return lax.ppermute(block, ('space', 'chan'), pairs)]
    another operation x2 -> x0, local copies, waits for them, and re-layouts: 4.2 us -> none  [spatial_sum(): products = products.reshape(planes, rows_n, cols_n, 3, 3, outs)]
    concatenate x15 -> x0, other arithmetic: 3.88 us -> none  [the longest x14 3.77 us: spatial_sum(): jnp.roll(products[:, :, :, row_tap, col_tap], (1 - row_tap, 1 - col_tap),...]
    select_n x3 -> x0, other arithmetic: 3.08 us -> none  [the longest x2 3.01 us: xor_order(): blocks = [jnp.where(flip, swapped[j], blocks[j]) for j in range(count)]]
    unnamed x35 -> x10, local copies, waits for them, and re-layouts: 2.12 us -> 3.61 us
  transfers between devices with their start and end apart: 5 -> 5, of which waited for: 3 -> 5; matrix products, arithmetic and copies ran while one was open for 9% -> 0% of each run, Pallas kernels for 0% -> 0%
where the time goes in v3:
time: 37.9 us; the launch traced here: 37.7 us
  waiting for transfers between devices  20 us (53%)
  Pallas kernels  7.74 us (20%)
  starting transfers between devices  6.24 us (16%)
  local copies, waits for them, and re-layouts  3.61 us (10%)
    ppermute x5, waiting for transfers between devices, gathered_from(): return lax.ppermute(block, ('space', 'chan'), pairs)  20 us
    pallas_call x2, Pallas kernels, conv_call(): pl.pallas_call(functools.partial(conv_kernel, fill, planes_out, rows_n, c...  7.74 us
    ppermute x5, starting transfers between devices, gathered_from(): return lax.ppermute(block, ('space', 'chan'), pairs)  6.24 us
    unnamed x10, local copies, waits for them, and re-layouts  3.61 us
  transfers between devices with their start and end apart: 5, of which 5 were waited for; matrix products, arithmetic and copies ran while one was open for 0% of the time, Pallas kernels for 0%

profile of v3, /device:TPU:0, one launch (start us, length us, event | category | flops | bytes accessed | tf_op | source)
XLA Modules:
  0.0 37.7 jit_solution(16123188307066602341)
XLA Ops:
  0.0 3.0 %collective-permute-start.1 = (bf16[256,512]{1,0:T(8,128)(2,1)}, bf16[256,512]{1,0:T(8,128)(2,1)S(1)}, u32[]{:S(2)}, u32[]{:S(2)}) collective-permute-start(bf16[256,512]{1,0:T(8,128)(2,1)} %bitcast.16), channel_id=1, source_target_pairs={{24,0},{9,1},{26,2},{11,3},{28,4},{13,5},{30,6},{15,7},{0,8},{17,9... | collective-permute-start | bytes 786440 | tf_op jit(solution)/shard_map/ppermute | solution.py:19
  3.0 1.5 %collective-permute-start = (bf16[256,512]{1,0:T(8,128)(2,1)}, bf16[256,512]{1,0:T(8,128)(2,1)S(1)}, u32[]{:S(2)}, u32[]{:S(2)}) collective-permute-start(bf16[256,512]{1,0:T(8,128)(2,1)} %bitcast.17), channel_id=1, source_target_pairs={{28,0},{5,1},{30,2},{7,3},{0,4},{9,5},{2,6},{11,7},{4,8},{13,9},{6... | collective-permute-start | bytes 786440 | tf_op jit(solution)/shard_map/ppermute | solution.py:19
  4.5 7.9 %collective-permute-done.1 = bf16[256,512]{1,0:T(8,128)(2,1)S(1)} collective-permute-done((bf16[256,512]{1,0:T(8,128)(2,1)}, bf16[256,512]{1,0:T(8,128)(2,1)S(1)}, u32[]{:S(2)}, u32[]{:S(2)}) %collective-permute-start.1) | collective-permute-done | bytes 262176 | tf_op jit(solution)/shard_map/ppermute | solution.py:19
  12.4 3.1 %collective-permute-done = bf16[256,512]{1,0:T(8,128)(2,1)S(1)} collective-permute-done((bf16[256,512]{1,0:T(8,128)(2,1)}, bf16[256,512]{1,0:T(8,128)(2,1)S(1)}, u32[]{:S(2)}, u32[]{:S(2)}) %collective-permute-start) | collective-permute-done | bytes 262176 | tf_op jit(solution)/shard_map/ppermute | solution.py:19
  15.5 0.1 pad_maximum_fusion.refs_2_
  15.5 0.1 collective-permute-start.2
  15.6 1.9 %collective-permute-done.2.refs_3_ = bf16[2,256,512]{2,1,0:T(8,128)(2,1)S(1)} collective-permute-done((bf16[2,256,512]{2,1,0:T(8,128)(2,1)S(1)}, bf16[2,256,512]{2,1,0:T(8,128)(2,1)S(1)}, u32[]{:S(2)}, u32[]{:S(2)}) %collective-permute-start.2) | collective-permute-done | bytes 524320 | tf_op jit(solution)/shard_map/ppermute | solution.py:19
  17.5 0.0 copy-start.2
  17.5 2.0 %copy-done.2 = bf16[3,3,3,128,512]{4,3,2,1,0:T(8,128)(2,1)S(1)} copy-done((bf16[3,3,3,128,512]{4,3,2,1,0:T(8,128)(2,1)S(1)}, bf16[3,3,3,128,512]{4,3,2,1,0:T(8,128)(2,1)}, u32[]{:S(2)}) %copy-start.2) | copy-done | bytes 3538968
  19.5 0.0 copy-start.3
  19.5 0.9 %copy-done.3 = bf16[1,4,64,512]{3,2,1,0:T(8,128)(2,1)S(1)} copy-done((bf16[1,4,64,512]{3,2,1,0:T(8,128)(2,1)S(1)}, bf16[1,4,64,512]{3,2,1,0:T(8,128)(2,1)}, u32[]{:S(2)}) %copy-start.3) | copy-done | bytes 262168
  20.4 0.0 copy-start.4
  20.5 0.7 %copy-done.4 = f32[128]{0:T(128)S(1)} copy-done((f32[128]{0:T(128)S(1)}, f32[128]{0:T(128)}, u32[]{:S(2)}) %copy-start.4) | copy-done | bytes 536
  21.1 0.0 copy-start
  21.1 0.0 copy-start.1
  21.1 4.8 %shard_map.55 = bf16[3,256,128]{2,1,0:T(8,128)(2,1)S(1)} custom-call(s32[1]{0:T(128)} %bitcast.1.refs_0_, bf16[256,512]{1,0:T(8,128)(2,1)S(1)} %bitcast.18, bf16[2,256,512]{2,1,0:T(8,128)(2,1)S(1)} %pad_maximum_fusion.refs_2_, bf16[2,256,512]{2,1,0:T(8,128)(2,1)S(1)} %collective-permute-done.2.refs_3_, bf16[3,1152,512]{2,1,0:T(8,128)(2,1)S(1)} %bitcast.15, ...), custom_call_target="tpu_custom_call" | custom-call | flops 2717908992 | bytes 5046272 | tf_op jit(solution)/shard_map/pallas_call | solution.py:108
  25.9 1.6 %collective-permute-start.3 = (bf16[1,3,256,128]{3,2,1,0:T(8,128)(2,1)S(1)}, bf16[1,3,256,128]{3,2,1,0:T(8,128)(2,1)S(1)}, u32[]{:S(2)}, u32[]{:S(2)}) collective-permute-start(bf16[1,3,256,128]{3,2,1,0:T(8,128)(2,1)S(1)} %bitcast.11), channel_id=1, source_target_pairs={{2,0},{3,1},{0,2},{1,3},{6,4},{7,5},{4,6},{5,7},{10,8},{11,9},{8,1... | collective-permute-start | bytes 589832 | tf_op jit(solution)/shard_map/ppermute | solution.py:19
  27.5 5.4 %collective-permute-done.3.refs_2_ = bf16[1,3,256,128]{3,2,1,0:T(8,128)(2,1)S(1)} collective-permute-done((bf16[1,3,256,128]{3,2,1,0:T(8,128)(2,1)S(1)}, bf16[1,3,256,128]{3,2,1,0:T(8,128)(2,1)S(1)}, u32[]{:S(2)}, u32[]{:S(2)}) %collective-permute-start.3) | collective-permute-done | bytes 196640 | tf_op jit(solution)/shard_map/ppermute | solution.py:19
  32.9 0.1 collective-permute-start.4
  33.0 1.7 %collective-permute-done.4.refs_3_ = bf16[2,3,256,128]{3,2,1,0:T(8,128)(2,1)S(1)} collective-permute-done((bf16[2,3,256,128]{3,2,1,0:T(8,128)(2,1)S(1)}, bf16[2,3,256,128]{3,2,1,0:T(8,128)(2,1)S(1)}, u32[]{:S(2)}, u32[]{:S(2)}) %collective-permute-start.4) | collective-permute-done | bytes 393248 | tf_op jit(solution)/shard_map/ppermute | solution.py:19
  34.7 0.0 copy-done
  34.7 0.0 copy-done.1
  34.7 3.0 %shard_map.56 = bf16[1,128,256]{2,1,0:T(8,128)(2,1)} custom-call(s32[1]{0:T(128)} %bitcast.refs_0_, bf16[1,3,256,128]{3,2,1,0:T(8,128)(2,1)S(1)} %bitcast.13, bf16[1,3,256,128]{3,2,1,0:T(8,128)(2,1)S(1)} %collective-permute-done.3.refs_2_, bf16[2,3,256,128]{3,2,1,0:T(8,128)(2,1)S(1)} %collective-permute-done.4.refs_3_, bf16[3,1152,512]{2,1,0:T(8,128)(2,1)S(1)} %bitcast.10, ...), custom_call_target="tpu_custom_call" | custom-call | flops 905969664 | bytes 4390912 | tf_op jit(solution)/shard_map/pallas_call | solution.py:108
  (1 shorter events, 0.0 us)
Async XLA Ops:
  0.0 12.4 %collective-permute-start.1 = (bf16[256,512]{1,0:T(8,128)(2,1)}, bf16[256,512]{1,0:T(8,128)(2,1)S(1)}, u32[]{:S(2)}, u32[]{:S(2)}) collective-permute-start(bf16[256,512]{1,0:T(8,128)(2,1)} %bitcast.16), channel_id=1, source_target_pairs={{24,0},{9,1},{26,2},{11,3},{28,4},{13,5},{30,6},{15,7},{0,8},{17,9... | collective-permute-start | bytes 786440 | tf_op jit(solution)/shard_map/ppermute | solution.py:19
  3.0 12.4 %collective-permute-start = (bf16[256,512]{1,0:T(8,128)(2,1)}, bf16[256,512]{1,0:T(8,128)(2,1)S(1)}, u32[]{:S(2)}, u32[]{:S(2)}) collective-permute-start(bf16[256,512]{1,0:T(8,128)(2,1)} %bitcast.17), channel_id=1, source_target_pairs={{28,0},{5,1},{30,2},{7,3},{0,4},{9,5},{2,6},{11,7},{4,8},{13,9},{6... | collective-permute-start | bytes 786440 | tf_op jit(solution)/shard_map/ppermute | solution.py:19
  15.5 2.0 %collective-permute-start.2 = (bf16[2,256,512]{2,1,0:T(8,128)(2,1)S(1)}, bf16[2,256,512]{2,1,0:T(8,128)(2,1)S(1)}, u32[]{:S(2)}, u32[]{:S(2)}) collective-permute-start(bf16[2,256,512]{2,1,0:T(8,128)(2,1)S(1)} %pad_maximum_fusion.refs_2_), channel_id=1, source_target_pairs={{1,0},{0,1},{3,2},{2,3},{5,4},{4,5},{7,6},{6,7},{9,8},{8,9},{11,10... | collective-permute-start | bytes 1572872 | tf_op jit(solution)/shard_map/ppermute | solution.py:19
  17.5 2.0 %copy-start.2 = (bf16[3,3,3,128,512]{4,3,2,1,0:T(8,128)(2,1)S(1)}, bf16[3,3,3,128,512]{4,3,2,1,0:T(8,128)(2,1)}, u32[]{:S(2)}) copy-start(bf16[3,3,3,128,512]{4,3,2,1,0:T(8,128)(2,1)} %param.6) | copy-start | bytes 10616836
  19.5 0.9 %copy-start.3 = (bf16[1,4,64,512]{3,2,1,0:T(8,128)(2,1)S(1)}, bf16[1,4,64,512]{3,2,1,0:T(8,128)(2,1)}, u32[]{:S(2)}) copy-start(bf16[1,4,64,512]{3,2,1,0:T(8,128)(2,1)} %param.5) | copy-start | bytes 786436
  20.4 0.7 %copy-start.4 = (f32[128]{0:T(128)S(1)}, f32[128]{0:T(128)}, u32[]{:S(2)}) copy-start(f32[128]{0:T(128)} %param.7) | copy-start | bytes 1540
  21.1 13.6 %copy-start = (bf16[3,3,3,128,512]{4,3,2,1,0:T(8,128)(2,1)S(1)}, bf16[3,3,3,128,512]{4,3,2,1,0:T(8,128)(2,1)}, u32[]{:S(2)}) copy-start(bf16[3,3,3,128,512]{4,3,2,1,0:T(8,128)(2,1)} %param.8) | copy-start | bytes 10616836
  21.1 13.6 %copy-start.1 = (f32[128]{0:T(128)S(1)}, f32[128]{0:T(128)}, u32[]{:S(2)}) copy-start(f32[128]{0:T(128)} %param.9) | copy-start | bytes 1540
  25.9 7.0 %collective-permute-start.3 = (bf16[1,3,256,128]{3,2,1,0:T(8,128)(2,1)S(1)}, bf16[1,3,256,128]{3,2,1,0:T(8,128)(2,1)S(1)}, u32[]{:S(2)}, u32[]{:S(2)}) collective-permute-start(bf16[1,3,256,128]{3,2,1,0:T(8,128)(2,1)S(1)} %bitcast.11), channel_id=1, source_target_pairs={{2,0},{3,1},{0,2},{1,3},{6,4},{7,5},{4,6},{5,7},{10,8},{11,9},{8,1... | collective-permute-start | bytes 589832 | tf_op jit(solution)/shard_map/ppermute | solution.py:19
  32.9 1.8 %collective-permute-start.4 = (bf16[2,3,256,128]{3,2,1,0:T(8,128)(2,1)S(1)}, bf16[2,3,256,128]{3,2,1,0:T(8,128)(2,1)S(1)}, u32[]{:S(2)}, u32[]{:S(2)}) collective-permute-start(bf16[2,3,256,128]{3,2,1,0:T(8,128)(2,1)S(1)} %pad_maximum_fusion.1), channel_id=1, source_target_pairs={{1,0},{0,1},{3,2},{2,3},{5,4},{4,5},{7,6},{6,7},{9,8},{8,9},{11,10... | collective-permute-start | bytes 1179656 | tf_op jit(solution)/shard_map/ppermute | solution.py:19

commit v4 on v3

v4 whole, which is shorter than its diff:
```python
import functools

import jax
import jax.numpy as jnp
from jax import lax
from jax.experimental import pallas as pl
from jax.experimental.pallas import tpu as pltpu
from jax.sharding import PartitionSpec as P


def gathered_from(block, source_of):
    spaces = lax.axis_size("space")
    chans = lax.axis_size("chan")
    pairs = []
    for s in range(spaces):
        for c in range(chans):
            source_s, source_c = source_of(s, c)
            pairs.append(((source_s % spaces) * chans + source_c % chans, s * chans + c))
    return lax.ppermute(block, ("space", "chan"), pairs)


def from_side(block, distance):
    return gathered_from(block, lambda s, c: (s - distance if c % 2 == 0 else s + distance, c))


def from_chan_partner(block, bit):
    return gathered_from(block, lambda s, c: (s, c ^ bit))


def spatial_sum(acc_ref, plane, rows_n, cols_n, outs):
    cells = rows_n * cols_n
    column = lax.broadcasted_iota(jnp.int32, (cells, outs), 0) % cols_n
    total = None
    for col_tap in range(3):
        shifted = None
        for row_tap in range(3):
            tap = row_tap * 3 + col_tap
            part = acc_ref[plane, :, pl.ds(tap * outs, outs)]
            amount = ((1 - row_tap) * cols_n) % cells
            if amount:
                part = pltpu.roll(part, amount, 0)
            shifted = part if shifted is None else shifted + part
        if col_tap == 0:
            shifted = jnp.where(
                column == 0,
                pltpu.roll(shifted, (1 - cols_n) % cells, 0),
                pltpu.roll(shifted, 1, 0),
            )
        elif col_tap == 2:
            shifted = jnp.where(
                column == cols_n - 1,
                pltpu.roll(shifted, cols_n - 1, 0),
                pltpu.roll(shifted, cells - 1, 0),
            )
        total = shifted if total is None else total + shifted
    return total


def tap_product(plane, w_ref, depth_tap):
    return lax.dot_general(
        plane, w_ref[depth_tap], (((1,), (1,)), ((), ())), preferred_element_type=jnp.float32
    )


def own_plane_kernel(rows_n, cols_n, x_ref, w_ref, o_ref, acc_ref):
    outs = o_ref.shape[2]
    x = x_ref[...]
    for plane in range(3):
        acc_ref[plane] = tap_product(x, w_ref, 2 - plane)
    for plane in range(3):
        o_ref[plane] = spatial_sum(acc_ref, plane, rows_n, cols_n, outs)


def neighbour_kernel(rows_n, cols_n, odd_ref, mine_ref, theirs_ref, part_ref, w_ref, b_ref, o_ref, acc_ref):
    outs = o_ref.shape[2]
    is_odd = odd_ref[0] != 0

    def side(below, index):
        if below:
            return jnp.where(is_odd, theirs_ref[index], mine_ref[index])
        return jnp.where(is_odd, mine_ref[index], theirs_ref[index])

    minus_one, minus_two = side(True, 0), side(True, 1)
    plus_one, plus_two = side(False, 0), side(False, 1)
    acc_ref[0] = tap_product(minus_two, w_ref, 0) + tap_product(minus_one, w_ref, 1)
    acc_ref[1] = tap_product(minus_one, w_ref, 0) + tap_product(plus_one, w_ref, 2)
    acc_ref[2] = tap_product(plus_one, w_ref, 1) + tap_product(plus_two, w_ref, 2)
    bias = b_ref[...]
    for plane in range(3):
        total = spatial_sum(acc_ref, plane, rows_n, cols_n, outs) + part_ref[plane]
        o_ref[plane] = jnp.maximum(total + bias, 0.0).astype(o_ref.dtype)


def second_kernel(rows_n, cols_n, layout, me_ref, *refs):
    inputs = refs[:len(layout)]
    w_ref, b_ref, o_ref, field_ref, acc_ref = refs[len(layout):]
    outs = b_ref.shape[1]
    me = me_ref[0]
    blocks = {}
    for ref, offsets in zip(inputs, layout):
        for position, j in enumerate(offsets):
            blocks[j] = ref[position]
    count = len(blocks)
    ordered = [blocks[j] for j in range(count)]
    bit = 1
    while bit < count:
        flip = (me & bit) != 0
        ordered = [jnp.where(flip, ordered[j ^ bit], ordered[j]) for j in range(count)]
        bit *= 2
    for position in range(count):
        field_ref[:, :, pl.ds(position * outs, outs)] = ordered[position]
    products = None
    for depth_tap in range(3):
        term = tap_product(field_ref[depth_tap], w_ref, depth_tap)
        products = term if products is None else products + term
    acc_ref[0] = products
    total = spatial_sum(acc_ref, 0, rows_n, cols_n, outs)
    result = jnp.maximum(total + b_ref[...], 0.0)
    o_ref[0] = result.T.astype(o_ref.dtype)


def vmem_call(kernel, out_shape, operands, scratch, flops, smem_first=False):
    specs = [pl.BlockSpec(memory_space=pltpu.VMEM) for _ in operands]
    if smem_first:
        specs[0] = pl.BlockSpec(memory_space=pltpu.SMEM)
    moved = sum(x.size * x.dtype.itemsize for x in operands) + out_shape.size * out_shape.dtype.itemsize
    return pl.pallas_call(
        kernel,
        out_shape=out_shape,
        in_specs=specs,
        out_specs=pl.BlockSpec(memory_space=pltpu.VMEM),
        scratch_shapes=scratch,
        compiler_params=pltpu.CompilerParams(vmem_limit_bytes=48 * 1024 * 1024),
        cost_estimate=pl.CostEstimate(flops=flops, transcendentals=0, bytes_accessed=moved),
    )(*operands)


def per_device(volume, weight_one, bias_one, weight_two, bias_two):
    plane = volume[0]
    rows_n, cols_n, count_in = plane.shape
    cells = rows_n * cols_n
    outs = weight_one.shape[3]
    me = lax.axis_index("chan")
    chans = lax.axis_size("chan")
    one_stack = weight_one.reshape(3, 9 * outs, count_in)
    two_stack = weight_two.reshape(3, 9 * outs, count_in)
    tap_flops = 2 * cells * count_in * 9 * outs

    flat = plane.reshape(cells, count_in)
    near, far = from_side(flat, 1), from_side(flat, 2)
    own_terms = vmem_call(
        functools.partial(own_plane_kernel, rows_n, cols_n),
        jax.ShapeDtypeStruct((3, cells, outs), jnp.float32),
        [flat, one_stack],
        [pltpu.VMEM((3, cells, 9 * outs), jnp.float32)],
        3 * tap_flops,
    )
    near, far, own_terms = lax.optimization_barrier((near, far, own_terms))
    mine = jnp.stack([near, far])
    theirs = from_chan_partner(mine, 1)
    odd = (me % 2).astype(jnp.int32).reshape(1)
    hidden = vmem_call(
        functools.partial(neighbour_kernel, rows_n, cols_n),
        jax.ShapeDtypeStruct((3, cells, outs), jnp.bfloat16),
        [odd, mine, theirs, own_terms, one_stack, bias_one.reshape(1, outs)],
        [pltpu.VMEM((3, cells, 9 * outs), jnp.float32)],
        6 * tap_flops,
        smem_first=True,
    )

    held = [(hidden[None], (0,))]
    offsets = [0]
    bit = 1
    while bit < chans:
        bit *= 2
    bit //= 2
    while bit >= 1:
        sent = jnp.stack([arr[i] for arr, offs in held for i in range(len(offs))])
        got = from_chan_partner(sent, bit)
        held.append((got, tuple(j ^ bit for j in offsets)))
        offsets = offsets + [j ^ bit for j in offsets]
        bit //= 2
    layout = tuple(offs for _, offs in held)
    me_flag = me.astype(jnp.int32).reshape(1)
    output = vmem_call(
        functools.partial(second_kernel, rows_n, cols_n, layout),
        jax.ShapeDtypeStruct((1, outs, cells), jnp.bfloat16),
        [me_flag] + [arr for arr, _ in held] + [two_stack, bias_two.reshape(1, outs)],
        [pltpu.VMEM((3, cells, count_in), jnp.bfloat16), pltpu.VMEM((1, cells, 9 * outs), jnp.float32)],
        3 * tap_flops,
        smem_first=True,
    )
    return output


def solution(mesh):
    return jax.shard_map(
        per_device,
        mesh=mesh,
        in_specs=(
            P("space", None, None, None),
            P(None, None, None, "chan", None),
            P("chan"),
            P(None, None, None, "chan", None),
            P("chan"),
        ),
        out_specs=P("space", "chan", None),
        check_vma=False,
    )
```

time: 37.9 us -> 34.2 us (0.902)
  waiting for transfers between devices: 20 us -> 15.4 us
  local copies, waits for them, and re-layouts: 3.61 us -> 4.72 us
  Pallas kernels: 7.74 us -> 6.77 us
  other arithmetic: 0.09 us -> 0.89 us
    ppermute x5, waiting for transfers between devices: 20 us -> 15.4 us  [gathered_from(): return lax.ppermute(block, ('space', 'chan'), pairs)]
    unnamed x10 -> x16, local copies, waits for them, and re-layouts: 3.61 us -> 4.72 us
    pallas_call x2 -> x3, Pallas kernels: 7.74 us -> 6.77 us  [vmem_call(): pl.pallas_call(kernel, out_shape=out_shape, in_specs=specs, out_specs=pl....]
    another operation x2, other arithmetic: 0.09 us -> 0.89 us  [the longest x1 0.85 us: per_device(): mine = jnp.stack([near, far])]
  transfers between devices with their start and end apart: 5 -> 5, of which waited for: 5 -> 5; matrix products, arithmetic and copies ran while one was open for 0% -> 0% of each run, Pallas kernels for 0% -> 4%
where the time goes in v4:
time: 34.2 us; the launch traced here: 34 us
  waiting for transfers between devices  15.4 us (45%)
  Pallas kernels  6.77 us (20%)
  starting transfers between devices  6.17 us (18%)
  local copies, waits for them, and re-layouts  4.72 us (14%)
  other arithmetic  0.89 us (3%)
    ppermute x5, waiting for transfers between devices, gathered_from(): return lax.ppermute(block, ('space', 'chan'), pairs)  15.4 us
    pallas_call x3, Pallas kernels, vmem_call(): pl.pallas_call(kernel, out_shape=out_shape, in_specs=specs, out_specs=pl....  6.77 us
    ppermute x5, starting transfers between devices, gathered_from(): return lax.ppermute(block, ('space', 'chan'), pairs)  6.17 us
    unnamed x16, local copies, waits for them, and re-layouts  4.72 us
    another operation x1, other arithmetic, per_device(): mine = jnp.stack([near, far])  0.85 us
  transfers between devices with their start and end apart: 5, of which 5 were waited for; matrix products, arithmetic and copies ran while one was open for 0% of the time, Pallas kernels for 4%

profile of v4, /device:TPU:0, one launch (start us, length us, event | category | flops | bytes accessed | tf_op | source)
XLA Modules:
  0.0 34.0 jit_solution(10842018229490877273)
XLA Ops:
  0.0 0.0 copy-start.7
  0.0 3.0 %collective-permute-start.1 = (bf16[256,512]{1,0:T(8,128)(2,1)}, bf16[256,512]{1,0:T(8,128)(2,1)S(1)}, u32[]{:S(2)}, u32[]{:S(2)}) collective-permute-start(bf16[256,512]{1,0:T(8,128)(2,1)} %bitcast.16), channel_id=1, source_target_pairs={{24,0},{9,1},{26,2},{11,3},{28,4},{13,5},{30,6},{15,7},{0,8},{17,9... | collective-permute-start | bytes 786440 | tf_op jit(solution)/shard_map/ppermute | solution.py:19
  3.0 1.5 %collective-permute-start = (bf16[256,512]{1,0:T(8,128)(2,1)}, bf16[256,512]{1,0:T(8,128)(2,1)S(1)}, u32[]{:S(2)}, u32[]{:S(2)}) collective-permute-start(bf16[256,512]{1,0:T(8,128)(2,1)} %bitcast.17), channel_id=1, source_target_pairs={{28,0},{5,1},{30,2},{7,3},{0,4},{9,5},{2,6},{11,7},{4,8},{13,9},{6... | collective-permute-start | bytes 786440 | tf_op jit(solution)/shard_map/ppermute | solution.py:19
  4.5 0.0 copy-start.1
  4.5 2.0 %copy-done.1 = bf16[3,3,3,128,512]{4,3,2,1,0:T(8,128)(2,1)S(1)} copy-done((bf16[3,3,3,128,512]{4,3,2,1,0:T(8,128)(2,1)S(1)}, bf16[3,3,3,128,512]{4,3,2,1,0:T(8,128)(2,1)}, u32[]{:S(2)}) %copy-start.1) | copy-done | bytes 3538968
  6.5 0.0 copy-start.5
  6.5 0.9 %copy-done.5 = bf16[1,4,64,512]{3,2,1,0:T(8,128)(2,1)S(1)} copy-done((bf16[1,4,64,512]{3,2,1,0:T(8,128)(2,1)S(1)}, bf16[1,4,64,512]{3,2,1,0:T(8,128)(2,1)}, u32[]{:S(2)}) %copy-start.5) | copy-done | bytes 262168
  7.5 0.0 copy-start.2
  7.5 1.2 %shard_map.55.part_ref = f32[3,256,128]{2,1,0:T(8,128)S(1)} custom-call(bf16[256,512]{1,0:T(8,128)(2,1)S(1)} %bitcast.18, bf16[3,1152,512]{2,1,0:T(8,128)(2,1)S(1)} %bitcast.11), custom_call_target="tpu_custom_call" | custom-call | flops 905969664 | bytes 4194304 | tf_op jit(solution)/shard_map/pallas_call | solution.py:127
  8.7 0.0 copy-start.3
  8.7 0.8 %copy-done.3 = f32[3,256,128]{2,1,0:T(8,128)} copy-done((f32[3,256,128]{2,1,0:T(8,128)}, f32[3,256,128]{2,1,0:T(8,128)S(1)}, u32[]{:S(2)}) %copy-start.3) | copy-done | bytes 393240
  9.5 2.9 %collective-permute-done.1 = bf16[256,512]{1,0:T(8,128)(2,1)S(1)} collective-permute-done((bf16[256,512]{1,0:T(8,128)(2,1)}, bf16[256,512]{1,0:T(8,128)(2,1)S(1)}, u32[]{:S(2)}, u32[]{:S(2)}) %collective-permute-start.1) | collective-permute-done | bytes 262176 | tf_op jit(solution)/shard_map/ppermute | solution.py:19
  12.4 3.1 %collective-permute-done = bf16[256,512]{1,0:T(8,128)(2,1)S(1)} collective-permute-done((bf16[256,512]{1,0:T(8,128)(2,1)}, bf16[256,512]{1,0:T(8,128)(2,1)S(1)}, u32[]{:S(2)}, u32[]{:S(2)}) %collective-permute-start) | collective-permute-done | bytes 262176 | tf_op jit(solution)/shard_map/ppermute | solution.py:19
  15.5 0.9 %pad_maximum_fusion.mine_ref = bf16[2,256,512]{2,1,0:T(8,128)(2,1)} fusion(bf16[1,256,512]{2,1,0:T(8,128)(2,1)S(1)} %bitcast.21, bf16[1,256,512]{2,1,0:T(8,128)(2,1)S(1)} %bitcast.22), kind=kLoop, calls=%fused_computation | loop fusion | flops 262144 | bytes 1048576 | tf_op jit(solution)/shard_map/stack | solution.py:159
  16.3 0.0 collective-permute-start.2
  16.3 2.2 %collective-permute-done.2.theirs_ref = bf16[2,256,512]{2,1,0:T(8,128)(2,1)} collective-permute-done((bf16[2,256,512]{2,1,0:T(8,128)(2,1)}, bf16[2,256,512]{2,1,0:T(8,128)(2,1)}, u32[]{:S(2)}, u32[]{:S(2)}) %collective-permute-start.2) | collective-permute-done | bytes 524320 | tf_op jit(solution)/shard_map/ppermute | solution.py:19
  18.6 0.0 copy-done.7
  18.6 0.0 copy-done.2
  18.6 0.0 copy-start.4
  18.6 1.0 %copy-done.4 = f32[3,256,128]{2,1,0:T(8,128)S(1)} copy-done((f32[3,256,128]{2,1,0:T(8,128)S(1)}, f32[3,256,128]{2,1,0:T(8,128)}, u32[]{:S(2)}) %copy-start.4) | copy-done | bytes 393240
  19.6 0.0 copy-start
  19.6 0.0 copy-start.6
  19.6 3.6 %shard_map.56 = bf16[3,256,128]{2,1,0:T(8,128)(2,1)S(1)} custom-call(s32[1]{0:T(128)} %bitcast.1.odd_ref, bf16[2,256,512]{2,1,0:T(8,128)(2,1)} %pad_maximum_fusion.mine_ref, bf16[2,256,512]{2,1,0:T(8,128)(2,1)} %collective-permute-done.2.theirs_ref, f32[3,256,128]{2,1,0:T(8,128)S(1)} %copy-done.4, bf16[3,1152,512]{2,1,0:T(8,128)(2,1)S(1)} %bitcast.12, ...), custom_call_target="tpu_custom_call" | custom-call | flops 1811939328 | bytes 5177860 | tf_op jit(solution)/shard_map/pallas_call | solution.py:127
  23.2 1.6 %collective-permute-start.3 = (bf16[1,3,256,128]{3,2,1,0:T(8,128)(2,1)S(1)}, bf16[1,3,256,128]{3,2,1,0:T(8,128)(2,1)S(1)}, u32[]{:S(2)}, u32[]{:S(2)}) collective-permute-start(bf16[1,3,256,128]{3,2,1,0:T(8,128)(2,1)S(1)} %bitcast.13), channel_id=1, source_target_pairs={{2,0},{3,1},{0,2},{1,3},{6,4},{7,5},{4,6},{5,7},{10,8},{11,9},{8,1... | collective-permute-start | bytes 589832 | tf_op jit(solution)/shard_map/ppermute | solution.py:19
  24.8 5.4 %collective-permute-done.3.refs_1_ = bf16[1,3,256,128]{3,2,1,0:T(8,128)(2,1)S(1)} collective-permute-done((bf16[1,3,256,128]{3,2,1,0:T(8,128)(2,1)S(1)}, bf16[1,3,256,128]{3,2,1,0:T(8,128)(2,1)S(1)}, u32[]{:S(2)}, u32[]{:S(2)}) %collective-permute-start.3) | collective-permute-done | bytes 196640 | tf_op jit(solution)/shard_map/ppermute | solution.py:19
  30.2 0.1 collective-permute-start.4
  30.3 1.7 %collective-permute-done.4.refs_2_ = bf16[2,3,256,128]{3,2,1,0:T(8,128)(2,1)S(1)} collective-permute-done((bf16[2,3,256,128]{3,2,1,0:T(8,128)(2,1)S(1)}, bf16[2,3,256,128]{3,2,1,0:T(8,128)(2,1)S(1)}, u32[]{:S(2)}, u32[]{:S(2)}) %collective-permute-start.4) | collective-permute-done | bytes 393248 | tf_op jit(solution)/shard_map/ppermute | solution.py:19
  32.0 0.0 copy-done
  32.0 0.0 copy-done.6
  32.0 2.0 %shard_map.57 = bf16[1,128,256]{2,1,0:T(8,128)(2,1)} custom-call(s32[1]{0:T(128)} %bitcast.me_ref, bf16[1,3,256,128]{3,2,1,0:T(8,128)(2,1)S(1)} %bitcast.15, bf16[1,3,256,128]{3,2,1,0:T(8,128)(2,1)S(1)} %collective-permute-done.3.refs_1_, bf16[2,3,256,128]{3,2,1,0:T(8,128)(2,1)S(1)} %collective-permute-done.4.refs_2_, bf16[3,1152,512]{2,1,0:T(8,128)(2,1)S(1)} %bitcast.10, ...), custom_call_target="tpu_custom_call" | custom-call | flops 905969664 | bytes 4391428 | tf_op jit(solution)/shard_map/pallas_call | solution.py:127
  (1 shorter events, 0.0 us)
Async XLA Ops:
  0.0 18.6 %copy-start.7 = (f32[128]{0:T(128)S(1)}, f32[128]{0:T(128)}, u32[]{:S(2)}) copy-start(f32[128]{0:T(128)} %param.7) | copy-start | bytes 1540
  0.0 12.4 %collective-permute-start.1 = (bf16[256,512]{1,0:T(8,128)(2,1)}, bf16[256,512]{1,0:T(8,128)(2,1)S(1)}, u32[]{:S(2)}, u32[]{:S(2)}) collective-permute-start(bf16[256,512]{1,0:T(8,128)(2,1)} %bitcast.16), channel_id=1, source_target_pairs={{24,0},{9,1},{26,2},{11,3},{28,4},{13,5},{30,6},{15,7},{0,8},{17,9... | collective-permute-start | bytes 786440 | tf_op jit(solution)/shard_map/ppermute | solution.py:19
  3.0 12.4 %collective-permute-start = (bf16[256,512]{1,0:T(8,128)(2,1)}, bf16[256,512]{1,0:T(8,128)(2,1)S(1)}, u32[]{:S(2)}, u32[]{:S(2)}) collective-permute-start(bf16[256,512]{1,0:T(8,128)(2,1)} %bitcast.17), channel_id=1, source_target_pairs={{28,0},{5,1},{30,2},{7,3},{0,4},{9,5},{2,6},{11,7},{4,8},{13,9},{6... | collective-permute-start | bytes 786440 | tf_op jit(solution)/shard_map/ppermute | solution.py:19
  4.5 2.0 %copy-start.1 = (bf16[3,3,3,128,512]{4,3,2,1,0:T(8,128)(2,1)S(1)}, bf16[3,3,3,128,512]{4,3,2,1,0:T(8,128)(2,1)}, u32[]{:S(2)}) copy-start(bf16[3,3,3,128,512]{4,3,2,1,0:T(8,128)(2,1)} %param.6) | copy-start | bytes 10616836
  6.5 0.9 %copy-start.5 = (bf16[1,4,64,512]{3,2,1,0:T(8,128)(2,1)S(1)}, bf16[1,4,64,512]{3,2,1,0:T(8,128)(2,1)}, u32[]{:S(2)}) copy-start(bf16[1,4,64,512]{3,2,1,0:T(8,128)(2,1)} %param.5) | copy-start | bytes 786436
  7.5 11.1 %copy-start.2 = (bf16[3,3,3,128,512]{4,3,2,1,0:T(8,128)(2,1)S(1)}, bf16[3,3,3,128,512]{4,3,2,1,0:T(8,128)(2,1)}, u32[]{:S(2)}) copy-start(bf16[3,3,3,128,512]{4,3,2,1,0:T(8,128)(2,1)} %param.6) | copy-start | bytes 10616836
  8.7 0.8 %copy-start.3 = (f32[3,256,128]{2,1,0:T(8,128)}, f32[3,256,128]{2,1,0:T(8,128)S(1)}, u32[]{:S(2)}) copy-start(f32[3,256,128]{2,1,0:T(8,128)S(1)} %shard_map.55.part_ref) | copy-start | bytes 1179652
  16.3 2.3 %collective-permute-start.2 = (bf16[2,256,512]{2,1,0:T(8,128)(2,1)}, bf16[2,256,512]{2,1,0:T(8,128)(2,1)}, u32[]{:S(2)}, u32[]{:S(2)}) collective-permute-start(bf16[2,256,512]{2,1,0:T(8,128)(2,1)} %pad_maximum_fusion.mine_ref), channel_id=1, source_target_pairs={{1,0},{0,1},{3,2},{2,3},{5,4},{4,5},{7,6},{6,7},{9,8},{8,9},{11,10... | collective-permute-start | bytes 1572872 | tf_op jit(solution)/shard_map/ppermute | solution.py:19
  18.6 1.0 %copy-start.4 = (f32[3,256,128]{2,1,0:T(8,128)S(1)}, f32[3,256,128]{2,1,0:T(8,128)}, u32[]{:S(2)}) copy-start(f32[3,256,128]{2,1,0:T(8,128)} %copy-done.3) | copy-start | bytes 1179652
  19.6 12.4 %copy-start = (bf16[3,3,3,128,512]{4,3,2,1,0:T(8,128)(2,1)S(1)}, bf16[3,3,3,128,512]{4,3,2,1,0:T(8,128)(2,1)}, u32[]{:S(2)}) copy-start(bf16[3,3,3,128,512]{4,3,2,1,0:T(8,128)(2,1)} %param.8) | copy-start | bytes 10616836
  19.6 12.4 %copy-start.6 = (f32[128]{0:T(128)S(1)}, f32[128]{0:T(128)}, u32[]{:S(2)}) copy-start(f32[128]{0:T(128)} %param.9) | copy-start | bytes 1540
  23.2 7.0 %collective-permute-start.3 = (bf16[1,3,256,128]{3,2,1,0:T(8,128)(2,1)S(1)}, bf16[1,3,256,128]{3,2,1,0:T(8,128)(2,1)S(1)}, u32[]{:S(2)}, u32[]{:S(2)}) collective-permute-start(bf16[1,3,256,128]{3,2,1,0:T(8,128)(2,1)S(1)} %bitcast.13), channel_id=1, source_target_pairs={{2,0},{3,1},{0,2},{1,3},{6,4},{7,5},{4,6},{5,7},{10,8},{11,9},{8,1... | collective-permute-start | bytes 589832 | tf_op jit(solution)/shard_map/ppermute | solution.py:19
  30.2 1.8 %collective-permute-start.4 = (bf16[2,3,256,128]{3,2,1,0:T(8,128)(2,1)S(1)}, bf16[2,3,256,128]{3,2,1,0:T(8,128)(2,1)S(1)}, u32[]{:S(2)}, u32[]{:S(2)}) collective-permute-start(bf16[2,3,256,128]{3,2,1,0:T(8,128)(2,1)S(1)} %pad_maximum_fusion.1), channel_id=1, source_target_pairs={{1,0},{0,1},{3,2},{2,3},{5,4},{4,5},{7,6},{6,7},{9,8},{8,9},{11,10... | collective-permute-start | bytes 1179656 | tf_op jit(solution)/shard_map/ppermute | solution.py:19

commit v5 on v4

--- a/solution.py
+++ b/solution.py
@@ -71,17 +71,14 @@
         o_ref[plane] = spatial_sum(acc_ref, plane, rows_n, cols_n, outs)
 
 
-def neighbour_kernel(rows_n, cols_n, odd_ref, mine_ref, theirs_ref, part_ref, w_ref, b_ref, o_ref, acc_ref):
+def neighbour_kernel(rows_n, cols_n, odd_ref, near_ref, far_ref, their_near_ref, their_far_ref, part_ref,
+                     w_ref, b_ref, o_ref, acc_ref):
     outs = o_ref.shape[2]
     is_odd = odd_ref[0] != 0
-
-    def side(below, index):
-        if below:
-            return jnp.where(is_odd, theirs_ref[index], mine_ref[index])
-        return jnp.where(is_odd, mine_ref[index], theirs_ref[index])
-
-    minus_one, minus_two = side(True, 0), side(True, 1)
-    plus_one, plus_two = side(False, 0), side(False, 1)
+    minus_one = jnp.where(is_odd, their_near_ref[...], near_ref[...])
+    minus_two = jnp.where(is_odd, their_far_ref[...], far_ref[...])
+    plus_one = jnp.where(is_odd, near_ref[...], their_near_ref[...])
+    plus_two = jnp.where(is_odd, far_ref[...], their_far_ref[...])
     acc_ref[0] = tap_product(minus_two, w_ref, 0) + tap_product(minus_one, w_ref, 1)
     acc_ref[1] = tap_product(minus_one, w_ref, 0) + tap_product(plus_one, w_ref, 2)
     acc_ref[2] = tap_product(plus_one, w_ref, 1) + tap_product(plus_two, w_ref, 2)
@@ -156,13 +153,12 @@
         3 * tap_flops,
     )
     near, far, own_terms = lax.optimization_barrier((near, far, own_terms))
-    mine = jnp.stack([near, far])
-    theirs = from_chan_partner(mine, 1)
+    their_near, their_far = from_chan_partner(near, 1), from_chan_partner(far, 1)
     odd = (me % 2).astype(jnp.int32).reshape(1)
     hidden = vmem_call(
         functools.partial(neighbour_kernel, rows_n, cols_n),
         jax.ShapeDtypeStruct((3, cells, outs), jnp.bfloat16),
-        [odd, mine, theirs, own_terms, one_stack, bias_one.reshape(1, outs)],
+        [odd, near, far, their_near, their_far, own_terms, one_stack, bias_one.reshape(1, outs)],
         [pltpu.VMEM((3, cells, 9 * outs), jnp.float32)],
         6 * tap_flops,
         smem_first=True,

time: 34.2 us -> 33.4 us (0.977)
  other arithmetic: 0.89 us -> 0.04 us
  starting transfers between devices: 6.17 us -> 6.68 us
  waiting for transfers between devices: 15.4 us -> 15 us
    another operation x1 -> x0, other arithmetic: 0.85 us -> none  [per_device(): mine = jnp.stack([near, far])]
    ppermute x5 -> x6, starting transfers between devices: 6.17 us -> 6.68 us  [gathered_from(): return lax.ppermute(block, ('space', 'chan'), pairs)]
    ppermute x5 -> x6, waiting for transfers between devices: 15.4 us -> 15 us  [gathered_from(): return lax.ppermute(block, ('space', 'chan'), pairs)]
  transfers between devices with their start and end apart: 5 -> 6, of which waited for: 5 -> 6; matrix products, arithmetic and copies ran while one was open for 0% -> 0% of each run, Pallas kernels for 4% -> 4%
where the time goes in v5:
time: 33.4 us; the launch traced here: 33.2 us
  waiting for transfers between devices  15 us (45%)
  Pallas kernels  6.76 us (20%)
  starting transfers between devices  6.68 us (20%)
  local copies, waits for them, and re-layouts  4.7 us (14%)
    ppermute x6, waiting for transfers between devices, gathered_from(): return lax.ppermute(block, ('space', 'chan'), pairs)  15 us
    pallas_call x3, Pallas kernels, vmem_call(): pl.pallas_call(kernel, out_shape=out_shape, in_specs=specs, out_specs=pl....  6.76 us
    ppermute x6, starting transfers between devices, gathered_from(): return lax.ppermute(block, ('space', 'chan'), pairs)  6.68 us
    unnamed x16, local copies, waits for them, and re-layouts  4.7 us
  transfers between devices with their start and end apart: 6, of which 6 were waited for; matrix products, arithmetic and copies ran while one was open for 0% of the time, Pallas kernels for 4%

profile of v5, /device:TPU:0, one launch (start us, length us, event | category | flops | bytes accessed | tf_op | source)
XLA Modules:
  0.0 33.2 jit_solution(14419078785695713031)
XLA Ops:
  0.0 0.0 copy-start.7
  0.0 3.0 %collective-permute-start.1 = (bf16[256,512]{1,0:T(8,128)(2,1)}, bf16[256,512]{1,0:T(8,128)(2,1)}, u32[]{:S(2)}, u32[]{:S(2)}) collective-permute-start(bf16[256,512]{1,0:T(8,128)(2,1)} %bitcast.14), channel_id=1, source_target_pairs={{24,0},{9,1},{26,2},{11,3},{28,4},{13,5},{30,6},{15,7},{0,8},{17,9... | collective-permute-start | bytes 786440 | tf_op jit(solution)/shard_map/ppermute | solution.py:19
  3.0 1.5 %collective-permute-start = (bf16[256,512]{1,0:T(8,128)(2,1)}, bf16[256,512]{1,0:T(8,128)(2,1)}, u32[]{:S(2)}, u32[]{:S(2)}) collective-permute-start(bf16[256,512]{1,0:T(8,128)(2,1)} %bitcast.15), channel_id=1, source_target_pairs={{28,0},{5,1},{30,2},{7,3},{0,4},{9,5},{2,6},{11,7},{4,8},{13,9},{6... | collective-permute-start | bytes 786440 | tf_op jit(solution)/shard_map/ppermute | solution.py:19
  4.5 0.0 copy-start.1
  4.5 2.0 %copy-done.1 = bf16[3,3,3,128,512]{4,3,2,1,0:T(8,128)(2,1)S(1)} copy-done((bf16[3,3,3,128,512]{4,3,2,1,0:T(8,128)(2,1)S(1)}, bf16[3,3,3,128,512]{4,3,2,1,0:T(8,128)(2,1)}, u32[]{:S(2)}) %copy-start.1) | copy-done | bytes 3538968
  6.5 0.0 copy-start.5
  6.5 0.9 %copy-done.5 = bf16[1,4,64,512]{3,2,1,0:T(8,128)(2,1)S(1)} copy-done((bf16[1,4,64,512]{3,2,1,0:T(8,128)(2,1)S(1)}, bf16[1,4,64,512]{3,2,1,0:T(8,128)(2,1)}, u32[]{:S(2)}) %copy-start.5) | copy-done | bytes 262168
  7.5 0.0 copy-start.2
  7.5 1.2 %shard_map.55.part_ref = f32[3,256,128]{2,1,0:T(8,128)S(1)} custom-call(bf16[256,512]{1,0:T(8,128)(2,1)S(1)} %bitcast.16, bf16[3,1152,512]{2,1,0:T(8,128)(2,1)S(1)} %bitcast.9), custom_call_target="tpu_custom_call" | custom-call | flops 905969664 | bytes 4194304 | tf_op jit(solution)/shard_map/pallas_call | solution.py:124
  8.7 0.0 copy-start.3
  8.7 0.7 %copy-done.3 = f32[3,256,128]{2,1,0:T(8,128)} copy-done((f32[3,256,128]{2,1,0:T(8,128)}, f32[3,256,128]{2,1,0:T(8,128)S(1)}, u32[]{:S(2)}) %copy-start.3) | copy-done | bytes 393240
  9.4 3.0 %collective-permute-done.1.far_ref = bf16[256,512]{1,0:T(8,128)(2,1)} collective-permute-done((bf16[256,512]{1,0:T(8,128)(2,1)}, bf16[256,512]{1,0:T(8,128)(2,1)}, u32[]{:S(2)}, u32[]{:S(2)}) %collective-permute-start.1) | collective-permute-done | bytes 262176 | tf_op jit(solution)/shard_map/ppermute | solution.py:19
  12.5 3.1 %collective-permute-done.near_ref = bf16[256,512]{1,0:T(8,128)(2,1)} collective-permute-done((bf16[256,512]{1,0:T(8,128)(2,1)}, bf16[256,512]{1,0:T(8,128)(2,1)}, u32[]{:S(2)}, u32[]{:S(2)}) %collective-permute-start) | collective-permute-done | bytes 262176 | tf_op jit(solution)/shard_map/ppermute | solution.py:19
  15.6 0.0 collective-permute-start.2
  15.6 0.5 %collective-permute-start.3 = (bf16[256,512]{1,0:T(8,128)(2,1)}, bf16[256,512]{1,0:T(8,128)(2,1)}, u32[]{:S(2)}, u32[]{:S(2)}) collective-permute-start(bf16[256,512]{1,0:T(8,128)(2,1)} %collective-permute-done.1.far_ref), channel_id=1, source_target_pairs={{1,0},{0,1},{3,2},{2,3},{5,4},{4,5},{7,6},{6,7},{9,8},{8,9},{11,10... | collective-permute-start | bytes 786440 | tf_op jit(solution)/shard_map/ppermute | solution.py:19
  16.1 1.4 %collective-permute-done.2.their_near_ref = bf16[256,512]{1,0:T(8,128)(2,1)} collective-permute-done((bf16[256,512]{1,0:T(8,128)(2,1)}, bf16[256,512]{1,0:T(8,128)(2,1)}, u32[]{:S(2)}, u32[]{:S(2)}) %collective-permute-start.2) | collective-permute-done | bytes 262176 | tf_op jit(solution)/shard_map/ppermute | solution.py:19
  17.5 0.4 %collective-permute-done.3.their_far_ref = bf16[256,512]{1,0:T(8,128)(2,1)} collective-permute-done((bf16[256,512]{1,0:T(8,128)(2,1)}, bf16[256,512]{1,0:T(8,128)(2,1)}, u32[]{:S(2)}, u32[]{:S(2)}) %collective-permute-start.3) | collective-permute-done | bytes 262176 | tf_op jit(solution)/shard_map/ppermute | solution.py:19
  17.8 0.0 copy-done.7
  17.8 0.0 copy-done.2
  17.8 0.0 copy-start.4
  17.8 1.0 %copy-done.4 = f32[3,256,128]{2,1,0:T(8,128)S(1)} copy-done((f32[3,256,128]{2,1,0:T(8,128)S(1)}, f32[3,256,128]{2,1,0:T(8,128)}, u32[]{:S(2)}) %copy-start.4) | copy-done | bytes 393240
  18.8 0.0 copy-start
  18.8 0.0 copy-start.6
  18.8 3.6 %shard_map.56 = bf16[3,256,128]{2,1,0:T(8,128)(2,1)S(1)} custom-call(s32[1]{0:T(128)} %bitcast.1.odd_ref, bf16[256,512]{1,0:T(8,128)(2,1)} %collective-permute-done.near_ref, bf16[256,512]{1,0:T(8,128)(2,1)} %collective-permute-done.1.far_ref, bf16[256,512]{1,0:T(8,128)(2,1)} %collective-permute-done.2.their_near_ref, ...), custom_call_target="tpu_custom_call" | custom-call | flops 1811939328 | bytes 5177860 | tf_op jit(solution)/shard_map/pallas_call | solution.py:124
  22.4 1.6 %collective-permute-start.4 = (bf16[1,3,256,128]{3,2,1,0:T(8,128)(2,1)S(1)}, bf16[1,3,256,128]{3,2,1,0:T(8,128)(2,1)S(1)}, u32[]{:S(2)}, u32[]{:S(2)}) collective-permute-start(bf16[1,3,256,128]{3,2,1,0:T(8,128)(2,1)S(1)} %bitcast.11), channel_id=1, source_target_pairs={{2,0},{3,1},{0,2},{1,3},{6,4},{7,5},{4,6},{5,7},{10,8},{11,9},{8,1... | collective-permute-start | bytes 589832 | tf_op jit(solution)/shard_map/ppermute | solution.py:19
  24.0 5.4 %collective-permute-done.4.refs_1_ = bf16[1,3,256,128]{3,2,1,0:T(8,128)(2,1)S(1)} collective-permute-done((bf16[1,3,256,128]{3,2,1,0:T(8,128)(2,1)S(1)}, bf16[1,3,256,128]{3,2,1,0:T(8,128)(2,1)S(1)}, u32[]{:S(2)}, u32[]{:S(2)}) %collective-permute-start.4) | collective-permute-done | bytes 196640 | tf_op jit(solution)/shard_map/ppermute | solution.py:19
  29.5 0.1 collective-permute-start.5
  29.6 1.7 %collective-permute-done.5.refs_2_ = bf16[2,3,256,128]{3,2,1,0:T(8,128)(2,1)S(1)} collective-permute-done((bf16[2,3,256,128]{3,2,1,0:T(8,128)(2,1)S(1)}, bf16[2,3,256,128]{3,2,1,0:T(8,128)(2,1)S(1)}, u32[]{:S(2)}, u32[]{:S(2)}) %collective-permute-start.5) | collective-permute-done | bytes 393248 | tf_op jit(solution)/shard_map/ppermute | solution.py:19
  31.3 0.0 copy-done
  31.3 0.0 copy-done.6
  31.3 2.0 %shard_map.57 = bf16[1,128,256]{2,1,0:T(8,128)(2,1)} custom-call(s32[1]{0:T(128)} %bitcast.me_ref, bf16[1,3,256,128]{3,2,1,0:T(8,128)(2,1)S(1)} %bitcast.13, bf16[1,3,256,128]{3,2,1,0:T(8,128)(2,1)S(1)} %collective-permute-done.4.refs_1_, bf16[2,3,256,128]{3,2,1,0:T(8,128)(2,1)S(1)} %collective-permute-done.5.refs_2_, bf16[3,1152,512]{2,1,0:T(8,128)(2,1)S(1)} %bitcast.8, ...), custom_call_target="tpu_custom_call" | custom-call | flops 905969664 | bytes 4391428 | tf_op jit(solution)/shard_map/pallas_call | solution.py:124
  (1 shorter events, 0.0 us)
Async XLA Ops:
  0.0 17.8 %copy-start.7 = (f32[128]{0:T(128)S(1)}, f32[128]{0:T(128)}, u32[]{:S(2)}) copy-start(f32[128]{0:T(128)} %param.7) | copy-start | bytes 1540
  0.0 12.5 %collective-permute-start.1 = (bf16[256,512]{1,0:T(8,128)(2,1)}, bf16[256,512]{1,0:T(8,128)(2,1)}, u32[]{:S(2)}, u32[]{:S(2)}) collective-permute-start(bf16[256,512]{1,0:T(8,128)(2,1)} %bitcast.14), channel_id=1, source_target_pairs={{24,0},{9,1},{26,2},{11,3},{28,4},{13,5},{30,6},{15,7},{0,8},{17,9... | collective-permute-start | bytes 786440 | tf_op jit(solution)/shard_map/ppermute | solution.py:19
  3.0 12.5 %collective-permute-start = (bf16[256,512]{1,0:T(8,128)(2,1)}, bf16[256,512]{1,0:T(8,128)(2,1)}, u32[]{:S(2)}, u32[]{:S(2)}) collective-permute-start(bf16[256,512]{1,0:T(8,128)(2,1)} %bitcast.15), channel_id=1, source_target_pairs={{28,0},{5,1},{30,2},{7,3},{0,4},{9,5},{2,6},{11,7},{4,8},{13,9},{6... | collective-permute-start | bytes 786440 | tf_op jit(solution)/shard_map/ppermute | solution.py:19
  4.5 2.0 %copy-start.1 = (bf16[3,3,3,128,512]{4,3,2,1,0:T(8,128)(2,1)S(1)}, bf16[3,3,3,128,512]{4,3,2,1,0:T(8,128)(2,1)}, u32[]{:S(2)}) copy-start(bf16[3,3,3,128,512]{4,3,2,1,0:T(8,128)(2,1)} %param.6) | copy-start | bytes 10616836
  6.5 0.9 %copy-start.5 = (bf16[1,4,64,512]{3,2,1,0:T(8,128)(2,1)S(1)}, bf16[1,4,64,512]{3,2,1,0:T(8,128)(2,1)}, u32[]{:S(2)}) copy-start(bf16[1,4,64,512]{3,2,1,0:T(8,128)(2,1)} %param.5) | copy-start | bytes 786436
  7.5 10.4 %copy-start.2 = (bf16[3,3,3,128,512]{4,3,2,1,0:T(8,128)(2,1)S(1)}, bf16[3,3,3,128,512]{4,3,2,1,0:T(8,128)(2,1)}, u32[]{:S(2)}) copy-start(bf16[3,3,3,128,512]{4,3,2,1,0:T(8,128)(2,1)} %param.6) | copy-start | bytes 10616836
  8.7 0.7 %copy-start.3 = (f32[3,256,128]{2,1,0:T(8,128)}, f32[3,256,128]{2,1,0:T(8,128)S(1)}, u32[]{:S(2)}) copy-start(f32[3,256,128]{2,1,0:T(8,128)S(1)} %shard_map.55.part_ref) | copy-start | bytes 1179652
  15.6 1.9 %collective-permute-start.2 = (bf16[256,512]{1,0:T(8,128)(2,1)}, bf16[256,512]{1,0:T(8,128)(2,1)}, u32[]{:S(2)}, u32[]{:S(2)}) collective-permute-start(bf16[256,512]{1,0:T(8,128)(2,1)} %collective-permute-done.near_ref), channel_id=1, source_target_pairs={{1,0},{0,1},{3,2},{2,3},{5,4},{4,5},{7,6},{6,7},{9,8},{8,9},{11,10... | collective-permute-start | bytes 786440 | tf_op jit(solution)/shard_map/ppermute | solution.py:19
  15.6 2.2 %collective-permute-start.3 = (bf16[256,512]{1,0:T(8,128)(2,1)}, bf16[256,512]{1,0:T(8,128)(2,1)}, u32[]{:S(2)}, u32[]{:S(2)}) collective-permute-start(bf16[256,512]{1,0:T(8,128)(2,1)} %collective-permute-done.1.far_ref), channel_id=1, source_target_pairs={{1,0},{0,1},{3,2},{2,3},{5,4},{4,5},{7,6},{6,7},{9,8},{8,9},{11,10... | collective-permute-start | bytes 786440 | tf_op jit(solution)/shard_map/ppermute | solution.py:19
  17.8 1.0 %copy-start.4 = (f32[3,256,128]{2,1,0:T(8,128)S(1)}, f32[3,256,128]{2,1,0:T(8,128)}, u32[]{:S(2)}) copy-start(f32[3,256,128]{2,1,0:T(8,128)} %copy-done.3) | copy-start | bytes 1179652
  18.8 12.4 %copy-start = (bf16[3,3,3,128,512]{4,3,2,1,0:T(8,128)(2,1)S(1)}, bf16[3,3,3,128,512]{4,3,2,1,0:T(8,128)(2,1)}, u32[]{:S(2)}) copy-start(bf16[3,3,3,128,512]{4,3,2,1,0:T(8,128)(2,1)} %param.8) | copy-start | bytes 10616836
  18.8 12.4 %copy-start.6 = (f32[128]{0:T(128)S(1)}, f32[128]{0:T(128)}, u32[]{:S(2)}) copy-start(f32[128]{0:T(128)} %param.9) | copy-start | bytes 1540
  22.4 7.0 %collective-permute-start.4 = (bf16[1,3,256,128]{3,2,1,0:T(8,128)(2,1)S(1)}, bf16[1,3,256,128]{3,2,1,0:T(8,128)(2,1)S(1)}, u32[]{:S(2)}, u32[]{:S(2)}) collective-permute-start(bf16[1,3,256,128]{3,2,1,0:T(8,128)(2,1)S(1)} %bitcast.11), channel_id=1, source_target_pairs={{2,0},{3,1},{0,2},{1,3},{6,4},{7,5},{4,6},{5,7},{10,8},{11,9},{8,1... | collective-permute-start | bytes 589832 | tf_op jit(solution)/shard_map/ppermute | solution.py:19
  29.5 1.8 %collective-permute-start.5 = (bf16[2,3,256,128]{3,2,1,0:T(8,128)(2,1)S(1)}, bf16[2,3,256,128]{3,2,1,0:T(8,128)(2,1)S(1)}, u32[]{:S(2)}, u32[]{:S(2)}) collective-permute-start(bf16[2,3,256,128]{3,2,1,0:T(8,128)(2,1)S(1)} %pad_maximum_fusion), channel_id=1, source_target_pairs={{1,0},{0,1},{3,2},{2,3},{5,4},{4,5},{7,6},{6,7},{9,8},{8,9},{11,10... | collective-permute-start | bytes 1179656 | tf_op jit(solution)/shard_map/ppermute | solution.py:19

commit v6 on v5

--- a/solution.py
+++ b/solution.py
@@ -74,14 +74,20 @@
 def neighbour_kernel(rows_n, cols_n, odd_ref, near_ref, far_ref, their_near_ref, their_far_ref, part_ref,
                      w_ref, b_ref, o_ref, acc_ref):
     outs = o_ref.shape[2]
-    is_odd = odd_ref[0] != 0
-    minus_one = jnp.where(is_odd, their_near_ref[...], near_ref[...])
-    minus_two = jnp.where(is_odd, their_far_ref[...], far_ref[...])
-    plus_one = jnp.where(is_odd, near_ref[...], their_near_ref[...])
-    plus_two = jnp.where(is_odd, far_ref[...], their_far_ref[...])
-    acc_ref[0] = tap_product(minus_two, w_ref, 0) + tap_product(minus_one, w_ref, 1)
-    acc_ref[1] = tap_product(minus_one, w_ref, 0) + tap_product(plus_one, w_ref, 2)
-    acc_ref[2] = tap_product(plus_one, w_ref, 1) + tap_product(plus_two, w_ref, 2)
+
+    def accumulate(minus_one, minus_two, plus_one, plus_two):
+        acc_ref[0] = tap_product(minus_two[...], w_ref, 0) + tap_product(minus_one[...], w_ref, 1)
+        acc_ref[1] = tap_product(minus_one[...], w_ref, 0) + tap_product(plus_one[...], w_ref, 2)
+        acc_ref[2] = tap_product(plus_one[...], w_ref, 1) + tap_product(plus_two[...], w_ref, 2)
+
+    @pl.when(odd_ref[0] == 0)
+    def _():
+        accumulate(near_ref, far_ref, their_near_ref, their_far_ref)
+
+    @pl.when(odd_ref[0] != 0)
+    def _():
+        accumulate(their_near_ref, their_far_ref, near_ref, far_ref)
+
     bias = b_ref[...]
     for plane in range(3):
         total = spatial_sum(acc_ref, plane, rows_n, cols_n, outs) + part_ref[plane]
@@ -96,16 +102,15 @@
     blocks = {}
     for ref, offsets in zip(inputs, layout):
         for position, j in enumerate(offsets):
-            blocks[j] = ref[position]
+            blocks[j] = (ref, position)
     count = len(blocks)
-    ordered = [blocks[j] for j in range(count)]
-    bit = 1
-    while bit < count:
-        flip = (me & bit) != 0
-        ordered = [jnp.where(flip, ordered[j ^ bit], ordered[j]) for j in range(count)]
-        bit *= 2
-    for position in range(count):
-        field_ref[:, :, pl.ds(position * outs, outs)] = ordered[position]
+    for index in range(count):
+
+        @pl.when(me == index)
+        def _():
+            for j in range(count):
+                ref, position = blocks[j]
+                field_ref[:, :, pl.ds((index ^ j) * outs, outs)] = ref[position]
     products = None
     for depth_tap in range(3):
         term = tap_product(field_ref[depth_tap], w_ref, depth_tap)

time: 33.4 us -> 33.8 us (1.012)
  no operation moved by 1% of the time
where the time goes in v6:
time: 33.8 us; the launch traced here: 33.6 us
  waiting for transfers between devices  15 us (44%)
  Pallas kernels  7.09 us (21%)
  starting transfers between devices  6.68 us (20%)
  local copies, waits for them, and re-layouts  4.7 us (14%)
    ppermute x6, waiting for transfers between devices, gathered_from(): return lax.ppermute(block, ('space', 'chan'), pairs)  15 us
    pallas_call x3, Pallas kernels, vmem_call(): pl.pallas_call(kernel, out_shape=out_shape, in_specs=specs, out_specs=pl....  7.09 us
    ppermute x6, starting transfers between devices, gathered_from(): return lax.ppermute(block, ('space', 'chan'), pairs)  6.68 us
    unnamed x16, local copies, waits for them, and re-layouts  4.7 us
  transfers between devices with their start and end apart: 6, of which 6 were waited for; matrix products, arithmetic and copies ran while one was open for 0% of the time, Pallas kernels for 4%

profile of v6, /device:TPU:0, one launch (start us, length us, event | category | flops | bytes accessed | tf_op | source)
XLA Modules:
  0.0 33.6 jit_solution(17624728886078585405)
XLA Ops:
  0.0 0.0 copy-start.7
  0.0 3.0 %collective-permute-start.1 = (bf16[256,512]{1,0:T(8,128)(2,1)}, bf16[256,512]{1,0:T(8,128)(2,1)}, u32[]{:S(2)}, u32[]{:S(2)}) collective-permute-start(bf16[256,512]{1,0:T(8,128)(2,1)} %bitcast.14), channel_id=1, source_target_pairs={{24,0},{9,1},{26,2},{11,3},{28,4},{13,5},{30,6},{15,7},{0,8},{17,9... | collective-permute-start | bytes 786440 | tf_op jit(solution)/shard_map/ppermute | solution.py:19
  3.0 1.5 %collective-permute-start = (bf16[256,512]{1,0:T(8,128)(2,1)}, bf16[256,512]{1,0:T(8,128)(2,1)}, u32[]{:S(2)}, u32[]{:S(2)}) collective-permute-start(bf16[256,512]{1,0:T(8,128)(2,1)} %bitcast.15), channel_id=1, source_target_pairs={{28,0},{5,1},{30,2},{7,3},{0,4},{9,5},{2,6},{11,7},{4,8},{13,9},{6... | collective-permute-start | bytes 786440 | tf_op jit(solution)/shard_map/ppermute | solution.py:19
  4.5 0.0 copy-start.1
  4.5 2.0 %copy-done.1 = bf16[3,3,3,128,512]{4,3,2,1,0:T(8,128)(2,1)S(1)} copy-done((bf16[3,3,3,128,512]{4,3,2,1,0:T(8,128)(2,1)S(1)}, bf16[3,3,3,128,512]{4,3,2,1,0:T(8,128)(2,1)}, u32[]{:S(2)}) %copy-start.1) | copy-done | bytes 3538968
  6.5 0.0 copy-start.5
  6.5 0.9 %copy-done.5 = bf16[1,4,64,512]{3,2,1,0:T(8,128)(2,1)S(1)} copy-done((bf16[1,4,64,512]{3,2,1,0:T(8,128)(2,1)S(1)}, bf16[1,4,64,512]{3,2,1,0:T(8,128)(2,1)}, u32[]{:S(2)}) %copy-start.5) | copy-done | bytes 262168
  7.5 0.0 copy-start.2
  7.5 1.2 %shard_map.55.part_ref = f32[3,256,128]{2,1,0:T(8,128)S(1)} custom-call(bf16[256,512]{1,0:T(8,128)(2,1)S(1)} %bitcast.16, bf16[3,1152,512]{2,1,0:T(8,128)(2,1)S(1)} %bitcast.9), custom_call_target="tpu_custom_call" | custom-call | flops 905969664 | bytes 4194304 | tf_op jit(solution)/shard_map/pallas_call | solution.py:129
  8.7 0.0 copy-start.3
  8.7 0.7 %copy-done.3 = f32[3,256,128]{2,1,0:T(8,128)} copy-done((f32[3,256,128]{2,1,0:T(8,128)}, f32[3,256,128]{2,1,0:T(8,128)S(1)}, u32[]{:S(2)}) %copy-start.3) | copy-done | bytes 393240
  9.4 3.0 %collective-permute-done.1.far_ref = bf16[256,512]{1,0:T(8,128)(2,1)} collective-permute-done((bf16[256,512]{1,0:T(8,128)(2,1)}, bf16[256,512]{1,0:T(8,128)(2,1)}, u32[]{:S(2)}, u32[]{:S(2)}) %collective-permute-start.1) | collective-permute-done | bytes 262176 | tf_op jit(solution)/shard_map/ppermute | solution.py:19
  12.5 3.1 %collective-permute-done.near_ref = bf16[256,512]{1,0:T(8,128)(2,1)} collective-permute-done((bf16[256,512]{1,0:T(8,128)(2,1)}, bf16[256,512]{1,0:T(8,128)(2,1)}, u32[]{:S(2)}, u32[]{:S(2)}) %collective-permute-start) | collective-permute-done | bytes 262176 | tf_op jit(solution)/shard_map/ppermute | solution.py:19
  15.6 0.0 collective-permute-start.2
  15.6 0.5 %collective-permute-start.3 = (bf16[256,512]{1,0:T(8,128)(2,1)}, bf16[256,512]{1,0:T(8,128)(2,1)}, u32[]{:S(2)}, u32[]{:S(2)}) collective-permute-start(bf16[256,512]{1,0:T(8,128)(2,1)} %collective-permute-done.1.far_ref), channel_id=1, source_target_pairs={{1,0},{0,1},{3,2},{2,3},{5,4},{4,5},{7,6},{6,7},{9,8},{8,9},{11,10... | collective-permute-start | bytes 786440 | tf_op jit(solution)/shard_map/ppermute | solution.py:19
  16.1 1.4 %collective-permute-done.2.their_near_ref = bf16[256,512]{1,0:T(8,128)(2,1)} collective-permute-done((bf16[256,512]{1,0:T(8,128)(2,1)}, bf16[256,512]{1,0:T(8,128)(2,1)}, u32[]{:S(2)}, u32[]{:S(2)}) %collective-permute-start.2) | collective-permute-done | bytes 262176 | tf_op jit(solution)/shard_map/ppermute | solution.py:19
  17.5 0.4 %collective-permute-done.3.their_far_ref = bf16[256,512]{1,0:T(8,128)(2,1)} collective-permute-done((bf16[256,512]{1,0:T(8,128)(2,1)}, bf16[256,512]{1,0:T(8,128)(2,1)}, u32[]{:S(2)}, u32[]{:S(2)}) %collective-permute-start.3) | collective-permute-done | bytes 262176 | tf_op jit(solution)/shard_map/ppermute | solution.py:19
  17.8 0.0 copy-done.7
  17.8 0.0 copy-done.2
  17.8 0.0 copy-start.4
  17.8 1.0 %copy-done.4 = f32[3,256,128]{2,1,0:T(8,128)S(1)} copy-done((f32[3,256,128]{2,1,0:T(8,128)S(1)}, f32[3,256,128]{2,1,0:T(8,128)}, u32[]{:S(2)}) %copy-start.4) | copy-done | bytes 393240
  18.8 0.0 copy-start
  18.8 0.0 copy-start.6
  18.8 3.8 %shard_map.56 = bf16[3,256,128]{2,1,0:T(8,128)(2,1)S(1)} custom-call(s32[1]{0:T(128)} %bitcast.1.odd_ref, bf16[256,512]{1,0:T(8,128)(2,1)} %collective-permute-done.near_ref, bf16[256,512]{1,0:T(8,128)(2,1)} %collective-permute-done.1.far_ref, bf16[256,512]{1,0:T(8,128)(2,1)} %collective-permute-done.2.their_near_ref, ...), custom_call_target="tpu_custom_call" | custom-call | flops 1811939328 | bytes 5177860 | tf_op jit(solution)/shard_map/pallas_call | solution.py:129
  22.6 1.6 %collective-permute-start.4 = (bf16[1,3,256,128]{3,2,1,0:T(8,128)(2,1)S(1)}, bf16[1,3,256,128]{3,2,1,0:T(8,128)(2,1)S(1)}, u32[]{:S(2)}, u32[]{:S(2)}) collective-permute-start(bf16[1,3,256,128]{3,2,1,0:T(8,128)(2,1)S(1)} %bitcast.11), channel_id=1, source_target_pairs={{2,0},{3,1},{0,2},{1,3},{6,4},{7,5},{4,6},{5,7},{10,8},{11,9},{8,1... | collective-permute-start | bytes 589832 | tf_op jit(solution)/shard_map/ppermute | solution.py:19
  24.2 5.4 %collective-permute-done.4.refs_1_ = bf16[1,3,256,128]{3,2,1,0:T(8,128)(2,1)S(1)} collective-permute-done((bf16[1,3,256,128]{3,2,1,0:T(8,128)(2,1)S(1)}, bf16[1,3,256,128]{3,2,1,0:T(8,128)(2,1)S(1)}, u32[]{:S(2)}, u32[]{:S(2)}) %collective-permute-start.4) | collective-permute-done | bytes 196640 | tf_op jit(solution)/shard_map/ppermute | solution.py:19
  29.7 0.1 collective-permute-start.5
  29.7 1.7 %collective-permute-done.5.refs_2_ = bf16[2,3,256,128]{3,2,1,0:T(8,128)(2,1)S(1)} collective-permute-done((bf16[2,3,256,128]{3,2,1,0:T(8,128)(2,1)S(1)}, bf16[2,3,256,128]{3,2,1,0:T(8,128)(2,1)S(1)}, u32[]{:S(2)}, u32[]{:S(2)}) %collective-permute-start.5) | collective-permute-done | bytes 393248 | tf_op jit(solution)/shard_map/ppermute | solution.py:19
  31.5 0.0 copy-done
  31.5 0.0 copy-done.6
  31.5 2.1 %shard_map.57 = bf16[1,128,256]{2,1,0:T(8,128)(2,1)} custom-call(s32[1]{0:T(128)} %bitcast.me_ref, bf16[1,3,256,128]{3,2,1,0:T(8,128)(2,1)S(1)} %bitcast.13, bf16[1,3,256,128]{3,2,1,0:T(8,128)(2,1)S(1)} %collective-permute-done.4.refs_1_, bf16[2,3,256,128]{3,2,1,0:T(8,128)(2,1)S(1)} %collective-permute-done.5.refs_2_, bf16[3,1152,512]{2,1,0:T(8,128)(2,1)S(1)} %bitcast.8, ...), custom_call_target="tpu_custom_call" | custom-call | flops 905969664 | bytes 4391428 | tf_op jit(solution)/shard_map/pallas_call | solution.py:129
  (1 shorter events, 0.0 us)
Async XLA Ops:
  0.0 17.8 %copy-start.7 = (f32[128]{0:T(128)S(1)}, f32[128]{0:T(128)}, u32[]{:S(2)}) copy-start(f32[128]{0:T(128)} %param.7) | copy-start | bytes 1540
  0.0 12.5 %collective-permute-start.1 = (bf16[256,512]{1,0:T(8,128)(2,1)}, bf16[256,512]{1,0:T(8,128)(2,1)}, u32[]{:S(2)}, u32[]{:S(2)}) collective-permute-start(bf16[256,512]{1,0:T(8,128)(2,1)} %bitcast.14), channel_id=1, source_target_pairs={{24,0},{9,1},{26,2},{11,3},{28,4},{13,5},{30,6},{15,7},{0,8},{17,9... | collective-permute-start | bytes 786440 | tf_op jit(solution)/shard_map/ppermute | solution.py:19
  3.0 12.5 %collective-permute-start = (bf16[256,512]{1,0:T(8,128)(2,1)}, bf16[256,512]{1,0:T(8,128)(2,1)}, u32[]{:S(2)}, u32[]{:S(2)}) collective-permute-start(bf16[256,512]{1,0:T(8,128)(2,1)} %bitcast.15), channel_id=1, source_target_pairs={{28,0},{5,1},{30,2},{7,3},{0,4},{9,5},{2,6},{11,7},{4,8},{13,9},{6... | collective-permute-start | bytes 786440 | tf_op jit(solution)/shard_map/ppermute | solution.py:19
  4.5 2.0 %copy-start.1 = (bf16[3,3,3,128,512]{4,3,2,1,0:T(8,128)(2,1)S(1)}, bf16[3,3,3,128,512]{4,3,2,1,0:T(8,128)(2,1)}, u32[]{:S(2)}) copy-start(bf16[3,3,3,128,512]{4,3,2,1,0:T(8,128)(2,1)} %param.6) | copy-start | bytes 10616836
  6.5 0.9 %copy-start.5 = (bf16[1,4,64,512]{3,2,1,0:T(8,128)(2,1)S(1)}, bf16[1,4,64,512]{3,2,1,0:T(8,128)(2,1)}, u32[]{:S(2)}) copy-start(bf16[1,4,64,512]{3,2,1,0:T(8,128)(2,1)} %param.5) | copy-start | bytes 786436
  7.5 10.4 %copy-start.2 = (bf16[3,3,3,128,512]{4,3,2,1,0:T(8,128)(2,1)S(1)}, bf16[3,3,3,128,512]{4,3,2,1,0:T(8,128)(2,1)}, u32[]{:S(2)}) copy-start(bf16[3,3,3,128,512]{4,3,2,1,0:T(8,128)(2,1)} %param.6) | copy-start | bytes 10616836
  8.7 0.7 %copy-start.3 = (f32[3,256,128]{2,1,0:T(8,128)}, f32[3,256,128]{2,1,0:T(8,128)S(1)}, u32[]{:S(2)}) copy-start(f32[3,256,128]{2,1,0:T(8,128)S(1)} %shard_map.55.part_ref) | copy-start | bytes 1179652
  15.6 1.9 %collective-permute-start.2 = (bf16[256,512]{1,0:T(8,128)(2,1)}, bf16[256,512]{1,0:T(8,128)(2,1)}, u32[]{:S(2)}, u32[]{:S(2)}) collective-permute-start(bf16[256,512]{1,0:T(8,128)(2,1)} %collective-permute-done.near_ref), channel_id=1, source_target_pairs={{1,0},{0,1},{3,2},{2,3},{5,4},{4,5},{7,6},{6,7},{9,8},{8,9},{11,10... | collective-permute-start | bytes 786440 | tf_op jit(solution)/shard_map/ppermute | solution.py:19
  15.6 2.2 %collective-permute-start.3 = (bf16[256,512]{1,0:T(8,128)(2,1)}, bf16[256,512]{1,0:T(8,128)(2,1)}, u32[]{:S(2)}, u32[]{:S(2)}) collective-permute-start(bf16[256,512]{1,0:T(8,128)(2,1)} %collective-permute-done.1.far_ref), channel_id=1, source_target_pairs={{1,0},{0,1},{3,2},{2,3},{5,4},{4,5},{7,6},{6,7},{9,8},{8,9},{11,10... | collective-permute-start | bytes 786440 | tf_op jit(solution)/shard_map/ppermute | solution.py:19
  17.8 1.0 %copy-start.4 = (f32[3,256,128]{2,1,0:T(8,128)S(1)}, f32[3,256,128]{2,1,0:T(8,128)}, u32[]{:S(2)}) copy-start(f32[3,256,128]{2,1,0:T(8,128)} %copy-done.3) | copy-start | bytes 1179652
  18.8 12.6 %copy-start = (bf16[3,3,3,128,512]{4,3,2,1,0:T(8,128)(2,1)S(1)}, bf16[3,3,3,128,512]{4,3,2,1,0:T(8,128)(2,1)}, u32[]{:S(2)}) copy-start(bf16[3,3,3,128,512]{4,3,2,1,0:T(8,128)(2,1)} %param.8) | copy-start | bytes 10616836
  18.8 12.6 %copy-start.6 = (f32[128]{0:T(128)S(1)}, f32[128]{0:T(128)}, u32[]{:S(2)}) copy-start(f32[128]{0:T(128)} %param.9) | copy-start | bytes 1540
  22.6 7.0 %collective-permute-start.4 = (bf16[1,3,256,128]{3,2,1,0:T(8,128)(2,1)S(1)}, bf16[1,3,256,128]{3,2,1,0:T(8,128)(2,1)S(1)}, u32[]{:S(2)}, u32[]{:S(2)}) collective-permute-start(bf16[1,3,256,128]{3,2,1,0:T(8,128)(2,1)S(1)} %bitcast.11), channel_id=1, source_target_pairs={{2,0},{3,1},{0,2},{1,3},{6,4},{7,5},{4,6},{5,7},{10,8},{11,9},{8,1... | collective-permute-start | bytes 589832 | tf_op jit(solution)/shard_map/ppermute | solution.py:19
  29.7 1.8 %collective-permute-start.5 = (bf16[2,3,256,128]{3,2,1,0:T(8,128)(2,1)S(1)}, bf16[2,3,256,128]{3,2,1,0:T(8,128)(2,1)S(1)}, u32[]{:S(2)}, u32[]{:S(2)}) collective-permute-start(bf16[2,3,256,128]{3,2,1,0:T(8,128)(2,1)S(1)} %pad_maximum_fusion), channel_id=1, source_target_pairs={{1,0},{0,1},{3,2},{2,3},{5,4},{4,5},{7,6},{6,7},{9,8},{8,9},{11,10... | collective-permute-start | bytes 1179656 | tf_op jit(solution)/shard_map/ppermute | solution.py:19

commit v7 on v5

--- a/solution.py
+++ b/solution.py
@@ -152,8 +152,10 @@
         [pltpu.VMEM((3, cells, 9 * outs), jnp.float32)],
         3 * tap_flops,
     )
-    near, far, own_terms = lax.optimization_barrier((near, far, own_terms))
-    their_near, their_far = from_chan_partner(near, 1), from_chan_partner(far, 1)
+    far, own_terms = lax.optimization_barrier((far, own_terms))
+    their_far = from_chan_partner(far, 1)
+    near, own_terms, their_far = lax.optimization_barrier((near, own_terms, their_far))
+    their_near = from_chan_partner(near, 1)
     odd = (me % 2).astype(jnp.int32).reshape(1)
     hidden = vmem_call(
         functools.partial(neighbour_kernel, rows_n, cols_n),

time: 33.4 us -> 35.6 us (1.066)
  local copies, waits for them, and re-layouts: 4.7 us -> 8.01 us
  waiting for transfers between devices: 15 us -> 14.4 us
  starting transfers between devices: 6.68 us -> 6.18 us
    unnamed x16 -> x24, local copies, waits for them, and re-layouts: 4.7 us -> 8.01 us
    ppermute x6, waiting for transfers between devices: 15 us -> 14.4 us  [gathered_from(): return lax.ppermute(block, ('space', 'chan'), pairs)]
    ppermute x6, starting transfers between devices: 6.68 us -> 6.18 us  [gathered_from(): return lax.ppermute(block, ('space', 'chan'), pairs)]
  transfers between devices with their start and end apart: 6 -> 6, of which waited for: 6 -> 5; matrix products, arithmetic and copies ran while one was open for 0% -> 0% of each run, Pallas kernels for 4% -> 3%
where the time goes in v7:
time: 35.6 us; the launch traced here: 35.3 us
  waiting for transfers between devices  14.4 us (40%)
  local copies, waits for them, and re-layouts  8.01 us (22%)
  Pallas kernels  6.65 us (19%)
  starting transfers between devices  6.18 us (17%)
    ppermute x6, waiting for transfers between devices, gathered_from(): return lax.ppermute(block, ('space', 'chan'), pairs)  14.4 us
    unnamed x24, local copies, waits for them, and re-layouts  8.01 us
    pallas_call x3, Pallas kernels, vmem_call(): pl.pallas_call(kernel, out_shape=out_shape, in_specs=specs, out_specs=pl....  6.65 us
    ppermute x6, starting transfers between devices, gathered_from(): return lax.ppermute(block, ('space', 'chan'), pairs)  6.18 us
  transfers between devices with their start and end apart: 6, of which 5 were waited for; matrix products, arithmetic and copies ran while one was open for 0% of the time, Pallas kernels for 3%

profile of v7, /device:TPU:0, one launch (start us, length us, event | category | flops | bytes accessed | tf_op | source)
XLA Modules:
  0.0 35.3 jit_solution(15264754237894903549)
XLA Ops:
  0.0 0.0 copy-start.11
  0.0 3.0 %collective-permute-start.1 = (bf16[256,512]{1,0:T(8,128)(2,1)}, bf16[256,512]{1,0:T(8,128)(2,1)S(1)}, u32[]{:S(2)}, u32[]{:S(2)}) collective-permute-start(bf16[256,512]{1,0:T(8,128)(2,1)} %bitcast.14), channel_id=1, source_target_pairs={{24,0},{9,1},{26,2},{11,3},{28,4},{13,5},{30,6},{15,7},{0,8},{17,9... | collective-permute-start | bytes 786440 | tf_op jit(solution)/shard_map/ppermute | solution.py:19
  3.0 1.5 %collective-permute-start = (bf16[256,512]{1,0:T(8,128)(2,1)}, bf16[256,512]{1,0:T(8,128)(2,1)}, u32[]{:S(2)}, u32[]{:S(2)}) collective-permute-start(bf16[256,512]{1,0:T(8,128)(2,1)} %bitcast.15), channel_id=1, source_target_pairs={{28,0},{5,1},{30,2},{7,3},{0,4},{9,5},{2,6},{11,7},{4,8},{13,9},{6... | collective-permute-start | bytes 786440 | tf_op jit(solution)/shard_map/ppermute | solution.py:19
  4.5 0.0 copy-start.1
  4.5 2.0 %copy-done.1 = bf16[3,3,3,128,512]{4,3,2,1,0:T(8,128)(2,1)S(1)} copy-done((bf16[3,3,3,128,512]{4,3,2,1,0:T(8,128)(2,1)S(1)}, bf16[3,3,3,128,512]{4,3,2,1,0:T(8,128)(2,1)}, u32[]{:S(2)}) %copy-start.1) | copy-done | bytes 3538968
  6.5 0.0 copy-start.5
  6.5 0.9 %copy-done.5 = bf16[1,4,64,512]{3,2,1,0:T(8,128)(2,1)S(1)} copy-done((bf16[1,4,64,512]{3,2,1,0:T(8,128)(2,1)S(1)}, bf16[1,4,64,512]{3,2,1,0:T(8,128)(2,1)}, u32[]{:S(2)}) %copy-start.5) | copy-done | bytes 262168
  7.5 0.0 copy-start.2
  7.5 1.2 %shard_map.55.part_ref = f32[3,256,128]{2,1,0:T(8,128)S(1)} custom-call(bf16[256,512]{1,0:T(8,128)(2,1)S(1)} %bitcast.16, bf16[3,1152,512]{2,1,0:T(8,128)(2,1)S(1)} %bitcast.9), custom_call_target="tpu_custom_call" | custom-call | flops 905969664 | bytes 4194304 | tf_op jit(solution)/shard_map/pallas_call | solution.py:124
  8.7 0.0 copy-start.3
  8.7 0.7 %copy-done.3 = f32[3,256,128]{2,1,0:T(8,128)} copy-done((f32[3,256,128]{2,1,0:T(8,128)}, f32[3,256,128]{2,1,0:T(8,128)S(1)}, u32[]{:S(2)}) %copy-start.3) | copy-done | bytes 393240
  9.5 2.9 %collective-permute-done.1.far_ref = bf16[256,512]{1,0:T(8,128)(2,1)S(1)} collective-permute-done((bf16[256,512]{1,0:T(8,128)(2,1)}, bf16[256,512]{1,0:T(8,128)(2,1)S(1)}, u32[]{:S(2)}, u32[]{:S(2)}) %collective-permute-start.1) | collective-permute-done | bytes 262176 | tf_op jit(solution)/shard_map/ppermute | solution.py:19
  12.4 0.0 collective-permute-start.2
  12.4 0.0 copy-start.7
  12.4 0.7 %copy-done.7 = bf16[256,512]{1,0:T(8,128)(2,1)} copy-done((bf16[256,512]{1,0:T(8,128)(2,1)}, bf16[256,512]{1,0:T(8,128)(2,1)S(1)}, u32[]{:S(2)}) %copy-start.7) | copy-done | bytes 262168
  13.1 2.5 %collective-permute-done.near_ref = bf16[256,512]{1,0:T(8,128)(2,1)} collective-permute-done((bf16[256,512]{1,0:T(8,128)(2,1)}, bf16[256,512]{1,0:T(8,128)(2,1)}, u32[]{:S(2)}, u32[]{:S(2)}) %collective-permute-start) | collective-permute-done | bytes 262176 | tf_op jit(solution)/shard_map/ppermute | solution.py:19
  15.6 0.0 collective-permute-done.2.their_far_ref
  15.6 0.0 copy-start.9
  15.6 0.7 %copy-done.9 = bf16[256,512]{1,0:T(8,128)(2,1)} copy-done((bf16[256,512]{1,0:T(8,128)(2,1)}, bf16[256,512]{1,0:T(8,128)(2,1)S(1)}, u32[]{:S(2)}) %copy-start.9) | copy-done | bytes 262168
  16.3 0.0 collective-permute-start.3
  16.3 1.9 %collective-permute-done.3.their_near_ref = bf16[256,512]{1,0:T(8,128)(2,1)} collective-permute-done((bf16[256,512]{1,0:T(8,128)(2,1)}, bf16[256,512]{1,0:T(8,128)(2,1)}, u32[]{:S(2)}, u32[]{:S(2)}) %collective-permute-start.3) | collective-permute-done | bytes 262176 | tf_op jit(solution)/shard_map/ppermute | solution.py:19
  18.2 0.0 copy-done.11
  18.2 0.0 copy-done.2
  18.2 0.0 copy-start.4
  18.2 1.0 %copy-done.4 = f32[3,256,128]{2,1,0:T(8,128)S(1)} copy-done((f32[3,256,128]{2,1,0:T(8,128)S(1)}, f32[3,256,128]{2,1,0:T(8,128)}, u32[]{:S(2)}) %copy-start.4) | copy-done | bytes 393240
  19.2 0.0 copy-start.8
  19.2 0.9 %copy-done.8 = bf16[256,512]{1,0:T(8,128)(2,1)S(1)} copy-done((bf16[256,512]{1,0:T(8,128)(2,1)S(1)}, bf16[256,512]{1,0:T(8,128)(2,1)}, u32[]{:S(2)}) %copy-start.8) | copy-done | bytes 262168
  20.1 0.0 copy-start.10
  20.1 0.9 %copy-done.10 = bf16[256,512]{1,0:T(8,128)(2,1)S(1)} copy-done((bf16[256,512]{1,0:T(8,128)(2,1)S(1)}, bf16[256,512]{1,0:T(8,128)(2,1)}, u32[]{:S(2)}) %copy-start.10) | copy-done | bytes 262168
  21.1 0.0 copy-start
  21.1 0.0 copy-start.6
  21.1 3.5 %shard_map.56 = bf16[3,256,128]{2,1,0:T(8,128)(2,1)S(1)} custom-call(s32[1]{0:T(128)} %bitcast.1.odd_ref, bf16[256,512]{1,0:T(8,128)(2,1)} %collective-permute-done.near_ref, bf16[256,512]{1,0:T(8,128)(2,1)S(1)} %copy-done.8, bf16[256,512]{1,0:T(8,128)(2,1)} %collective-permute-done.3.their_near_ref, bf16[256,512]{1,0:T(8,128)(2,1)S(1)} %copy-done.10, ...), custom_call_target="tpu_custom_call" | custom-call | flops 1811939328 | bytes 5177860 | tf_op jit(solution)/shard_map/pallas_call | solution.py:124
  24.5 1.6 %collective-permute-start.4 = (bf16[1,3,256,128]{3,2,1,0:T(8,128)(2,1)S(1)}, bf16[1,3,256,128]{3,2,1,0:T(8,128)(2,1)S(1)}, u32[]{:S(2)}, u32[]{:S(2)}) collective-permute-start(bf16[1,3,256,128]{3,2,1,0:T(8,128)(2,1)S(1)} %bitcast.11), channel_id=1, source_target_pairs={{2,0},{3,1},{0,2},{1,3},{6,4},{7,5},{4,6},{5,7},{10,8},{11,9},{8,1... | collective-permute-start | bytes 589832 | tf_op jit(solution)/shard_map/ppermute | solution.py:19
  26.1 5.4 %collective-permute-done.4.refs_1_ = bf16[1,3,256,128]{3,2,1,0:T(8,128)(2,1)S(1)} collective-permute-done((bf16[1,3,256,128]{3,2,1,0:T(8,128)(2,1)S(1)}, bf16[1,3,256,128]{3,2,1,0:T(8,128)(2,1)S(1)}, u32[]{:S(2)}, u32[]{:S(2)}) %collective-permute-start.4) | collective-permute-done | bytes 196640 | tf_op jit(solution)/shard_map/ppermute | solution.py:19
  31.6 0.1 collective-permute-start.5
  31.7 1.7 %collective-permute-done.5.refs_2_ = bf16[2,3,256,128]{3,2,1,0:T(8,128)(2,1)S(1)} collective-permute-done((bf16[2,3,256,128]{3,2,1,0:T(8,128)(2,1)S(1)}, bf16[2,3,256,128]{3,2,1,0:T(8,128)(2,1)S(1)}, u32[]{:S(2)}, u32[]{:S(2)}) %collective-permute-start.5) | collective-permute-done | bytes 393248 | tf_op jit(solution)/shard_map/ppermute | solution.py:19
  33.4 0.0 copy-done
  33.4 0.0 copy-done.6
  33.4 2.0 %shard_map.57 = bf16[1,128,256]{2,1,0:T(8,128)(2,1)} custom-call(s32[1]{0:T(128)} %bitcast.me_ref, bf16[1,3,256,128]{3,2,1,0:T(8,128)(2,1)S(1)} %bitcast.13, bf16[1,3,256,128]{3,2,1,0:T(8,128)(2,1)S(1)} %collective-permute-done.4.refs_1_, bf16[2,3,256,128]{3,2,1,0:T(8,128)(2,1)S(1)} %collective-permute-done.5.refs_2_, bf16[3,1152,512]{2,1,0:T(8,128)(2,1)S(1)} %bitcast.8, ...), custom_call_target="tpu_custom_call" | custom-call | flops 905969664 | bytes 4391428 | tf_op jit(solution)/shard_map/pallas_call | solution.py:124
  (1 shorter events, 0.0 us)
Async XLA Ops:
  0.0 18.2 %copy-start.11 = (f32[128]{0:T(128)S(1)}, f32[128]{0:T(128)}, u32[]{:S(2)}) copy-start(f32[128]{0:T(128)} %param.7) | copy-start | bytes 1540
  0.0 12.4 %collective-permute-start.1 = (bf16[256,512]{1,0:T(8,128)(2,1)}, bf16[256,512]{1,0:T(8,128)(2,1)S(1)}, u32[]{:S(2)}, u32[]{:S(2)}) collective-permute-start(bf16[256,512]{1,0:T(8,128)(2,1)} %bitcast.14), channel_id=1, source_target_pairs={{24,0},{9,1},{26,2},{11,3},{28,4},{13,5},{30,6},{15,7},{0,8},{17,9... | collective-permute-start | bytes 786440 | tf_op jit(solution)/shard_map/ppermute | solution.py:19
  3.0 12.5 %collective-permute-start = (bf16[256,512]{1,0:T(8,128)(2,1)}, bf16[256,512]{1,0:T(8,128)(2,1)}, u32[]{:S(2)}, u32[]{:S(2)}) collective-permute-start(bf16[256,512]{1,0:T(8,128)(2,1)} %bitcast.15), channel_id=1, source_target_pairs={{28,0},{5,1},{30,2},{7,3},{0,4},{9,5},{2,6},{11,7},{4,8},{13,9},{6... | collective-permute-start | bytes 786440 | tf_op jit(solution)/shard_map/ppermute | solution.py:19
  4.5 2.0 %copy-start.1 = (bf16[3,3,3,128,512]{4,3,2,1,0:T(8,128)(2,1)S(1)}, bf16[3,3,3,128,512]{4,3,2,1,0:T(8,128)(2,1)}, u32[]{:S(2)}) copy-start(bf16[3,3,3,128,512]{4,3,2,1,0:T(8,128)(2,1)} %param.6) | copy-start | bytes 10616836
  6.5 0.9 %copy-start.5 = (bf16[1,4,64,512]{3,2,1,0:T(8,128)(2,1)S(1)}, bf16[1,4,64,512]{3,2,1,0:T(8,128)(2,1)}, u32[]{:S(2)}) copy-start(bf16[1,4,64,512]{3,2,1,0:T(8,128)(2,1)} %param.5) | copy-start | bytes 786436
  7.5 10.7 %copy-start.2 = (bf16[3,3,3,128,512]{4,3,2,1,0:T(8,128)(2,1)S(1)}, bf16[3,3,3,128,512]{4,3,2,1,0:T(8,128)(2,1)}, u32[]{:S(2)}) copy-start(bf16[3,3,3,128,512]{4,3,2,1,0:T(8,128)(2,1)} %param.6) | copy-start | bytes 10616836
  8.7 0.8 %copy-start.3 = (f32[3,256,128]{2,1,0:T(8,128)}, f32[3,256,128]{2,1,0:T(8,128)S(1)}, u32[]{:S(2)}) copy-start(f32[3,256,128]{2,1,0:T(8,128)S(1)} %shard_map.55.part_ref) | copy-start | bytes 1179652
  12.4 3.2 %collective-permute-start.2 = (bf16[256,512]{1,0:T(8,128)(2,1)S(1)}, bf16[256,512]{1,0:T(8,128)(2,1)S(1)}, u32[]{:S(2)}, u32[]{:S(2)}) collective-permute-start(bf16[256,512]{1,0:T(8,128)(2,1)S(1)} %collective-permute-done.1.far_ref), channel_id=1, source_target_pairs={{1,0},{0,1},{3,2},{2,3},{5,4},{4,5},{7,6},{6,7},{9,8},{8,9},{11,10... | collective-permute-start | bytes 786440 | tf_op jit(solution)/shard_map/ppermute | solution.py:19
  12.4 0.7 %copy-start.7 = (bf16[256,512]{1,0:T(8,128)(2,1)}, bf16[256,512]{1,0:T(8,128)(2,1)S(1)}, u32[]{:S(2)}) copy-start(bf16[256,512]{1,0:T(8,128)(2,1)S(1)} %collective-permute-done.1.far_ref) | copy-start | bytes 786436
  15.6 0.7 %copy-start.9 = (bf16[256,512]{1,0:T(8,128)(2,1)}, bf16[256,512]{1,0:T(8,128)(2,1)S(1)}, u32[]{:S(2)}) copy-start(bf16[256,512]{1,0:T(8,128)(2,1)S(1)} %collective-permute-done.2.their_far_ref) | copy-start | bytes 786436
  16.3 1.9 %collective-permute-start.3 = (bf16[256,512]{1,0:T(8,128)(2,1)}, bf16[256,512]{1,0:T(8,128)(2,1)}, u32[]{:S(2)}, u32[]{:S(2)}) collective-permute-start(bf16[256,512]{1,0:T(8,128)(2,1)} %collective-permute-done.near_ref), channel_id=1, source_target_pairs={{1,0},{0,1},{3,2},{2,3},{5,4},{4,5},{7,6},{6,7},{9,8},{8,9},{11,10... | collective-permute-start | bytes 786440 | tf_op jit(solution)/shard_map/ppermute | solution.py:19
  18.2 1.0 %copy-start.4 = (f32[3,256,128]{2,1,0:T(8,128)S(1)}, f32[3,256,128]{2,1,0:T(8,128)}, u32[]{:S(2)}) copy-start(f32[3,256,128]{2,1,0:T(8,128)} %copy-done.3) | copy-start | bytes 1179652
  19.2 0.9 %copy-start.8 = (bf16[256,512]{1,0:T(8,128)(2,1)S(1)}, bf16[256,512]{1,0:T(8,128)(2,1)}, u32[]{:S(2)}) copy-start(bf16[256,512]{1,0:T(8,128)(2,1)} %copy-done.7) | copy-start | bytes 786436
  20.1 0.9 %copy-start.10 = (bf16[256,512]{1,0:T(8,128)(2,1)S(1)}, bf16[256,512]{1,0:T(8,128)(2,1)}, u32[]{:S(2)}) copy-start(bf16[256,512]{1,0:T(8,128)(2,1)} %copy-done.9) | copy-start | bytes 786436
  21.1 12.3 %copy-start = (bf16[3,3,3,128,512]{4,3,2,1,0:T(8,128)(2,1)S(1)}, bf16[3,3,3,128,512]{4,3,2,1,0:T(8,128)(2,1)}, u32[]{:S(2)}) copy-start(bf16[3,3,3,128,512]{4,3,2,1,0:T(8,128)(2,1)} %param.8) | copy-start | bytes 10616836
  21.1 12.3 %copy-start.6 = (f32[128]{0:T(128)S(1)}, f32[128]{0:T(128)}, u32[]{:S(2)}) copy-start(f32[128]{0:T(128)} %param.9) | copy-start | bytes 1540
  24.5 7.0 %collective-permute-start.4 = (bf16[1,3,256,128]{3,2,1,0:T(8,128)(2,1)S(1)}, bf16[1,3,256,128]{3,2,1,0:T(8,128)(2,1)S(1)}, u32[]{:S(2)}, u32[]{:S(2)}) collective-permute-start(bf16[1,3,256,128]{3,2,1,0:T(8,128)(2,1)S(1)} %bitcast.11), channel_id=1, source_target_pairs={{2,0},{3,1},{0,2},{1,3},{6,4},{7,5},{4,6},{5,7},{10,8},{11,9},{8,1... | collective-permute-start | bytes 589832 | tf_op jit(solution)/shard_map/ppermute | solution.py:19
  31.6 1.8 %collective-permute-start.5 = (bf16[2,3,256,128]{3,2,1,0:T(8,128)(2,1)S(1)}, bf16[2,3,256,128]{3,2,1,0:T(8,128)(2,1)S(1)}, u32[]{:S(2)}, u32[]{:S(2)}) collective-permute-start(bf16[2,3,256,128]{3,2,1,0:T(8,128)(2,1)S(1)} %pad_maximum_fusion), channel_id=1, source_target_pairs={{1,0},{0,1},{3,2},{2,3},{5,4},{4,5},{7,6},{6,7},{9,8},{8,9},{11,10... | collective-permute-start | bytes 1179656 | tf_op jit(solution)/shard_map/ppermute | solution.py:19

commit v8 on v5

--- a/solution.py
+++ b/solution.py
@@ -79,9 +79,12 @@
     minus_two = jnp.where(is_odd, their_far_ref[...], far_ref[...])
     plus_one = jnp.where(is_odd, near_ref[...], their_near_ref[...])
     plus_two = jnp.where(is_odd, far_ref[...], their_far_ref[...])
-    acc_ref[0] = tap_product(minus_two, w_ref, 0) + tap_product(minus_one, w_ref, 1)
-    acc_ref[1] = tap_product(minus_one, w_ref, 0) + tap_product(plus_one, w_ref, 2)
-    acc_ref[2] = tap_product(plus_one, w_ref, 1) + tap_product(plus_two, w_ref, 2)
+    acc_ref[0] = tap_product(minus_two, w_ref, 0)
+    acc_ref[1] = tap_product(minus_one, w_ref, 0)
+    acc_ref[0] += tap_product(minus_one, w_ref, 1)
+    acc_ref[2] = tap_product(plus_one, w_ref, 1)
+    acc_ref[1] += tap_product(plus_one, w_ref, 2)
+    acc_ref[2] += tap_product(plus_two, w_ref, 2)
     bias = b_ref[...]
     for plane in range(3):
         total = spatial_sum(acc_ref, plane, rows_n, cols_n, outs) + part_ref[plane]
@@ -106,11 +109,9 @@
         bit *= 2
     for position in range(count):
         field_ref[:, :, pl.ds(position * outs, outs)] = ordered[position]
-    products = None
-    for depth_tap in range(3):
-        term = tap_product(field_ref[depth_tap], w_ref, depth_tap)
-        products = term if products is None else products + term
-    acc_ref[0] = products
+    acc_ref[0] = tap_product(field_ref[0], w_ref, 0)
+    for depth_tap in (1, 2):
+        acc_ref[0] += tap_product(field_ref[depth_tap], w_ref, depth_tap)
     total = spatial_sum(acc_ref, 0, rows_n, cols_n, outs)
     result = jnp.maximum(total + b_ref[...], 0.0)
     o_ref[0] = result.T.astype(o_ref.dtype)

time: 33.4 us -> 33.4 us (level)
  no operation moved by 1% of the time
where the time goes in v8:
time: 33.4 us; the launch traced here: 33.2 us
  waiting for transfers between devices  15 us (45%)
  Pallas kernels  6.76 us (20%)
  starting transfers between devices  6.68 us (20%)
  local copies, waits for them, and re-layouts  4.7 us (14%)
    ppermute x6, waiting for transfers between devices, gathered_from(): return lax.ppermute(block, ('space', 'chan'), pairs)  15 us
    pallas_call x3, Pallas kernels, vmem_call(): pl.pallas_call(kernel, out_shape=out_shape, in_specs=specs, out_specs=pl....  6.76 us
    ppermute x6, starting transfers between devices, gathered_from(): return lax.ppermute(block, ('space', 'chan'), pairs)  6.68 us
    unnamed x16, local copies, waits for them, and re-layouts  4.7 us
  transfers between devices with their start and end apart: 6, of which 6 were waited for; matrix products, arithmetic and copies ran while one was open for 0% of the time, Pallas kernels for 4%

profile of v8, /device:TPU:0, one launch (start us, length us, event | category | flops | bytes accessed | tf_op | source)
XLA Modules:
  0.0 33.2 jit_solution(576157156384696901)
XLA Ops:
  0.0 0.0 copy-start.7
  0.0 3.0 %collective-permute-start.1 = (bf16[256,512]{1,0:T(8,128)(2,1)}, bf16[256,512]{1,0:T(8,128)(2,1)}, u32[]{:S(2)}, u32[]{:S(2)}) collective-permute-start(bf16[256,512]{1,0:T(8,128)(2,1)} %bitcast.14), channel_id=1, source_target_pairs={{24,0},{9,1},{26,2},{11,3},{28,4},{13,5},{30,6},{15,7},{0,8},{17,9... | collective-permute-start | bytes 786440 | tf_op jit(solution)/shard_map/ppermute | solution.py:19
  3.0 1.5 %collective-permute-start = (bf16[256,512]{1,0:T(8,128)(2,1)}, bf16[256,512]{1,0:T(8,128)(2,1)}, u32[]{:S(2)}, u32[]{:S(2)}) collective-permute-start(bf16[256,512]{1,0:T(8,128)(2,1)} %bitcast.15), channel_id=1, source_target_pairs={{28,0},{5,1},{30,2},{7,3},{0,4},{9,5},{2,6},{11,7},{4,8},{13,9},{6... | collective-permute-start | bytes 786440 | tf_op jit(solution)/shard_map/ppermute | solution.py:19
  4.5 0.0 copy-start.1
  4.5 2.0 %copy-done.1 = bf16[3,3,3,128,512]{4,3,2,1,0:T(8,128)(2,1)S(1)} copy-done((bf16[3,3,3,128,512]{4,3,2,1,0:T(8,128)(2,1)S(1)}, bf16[3,3,3,128,512]{4,3,2,1,0:T(8,128)(2,1)}, u32[]{:S(2)}) %copy-start.1) | copy-done | bytes 3538968
  6.5 0.0 copy-start.5
  6.5 0.9 %copy-done.5 = bf16[1,4,64,512]{3,2,1,0:T(8,128)(2,1)S(1)} copy-done((bf16[1,4,64,512]{3,2,1,0:T(8,128)(2,1)S(1)}, bf16[1,4,64,512]{3,2,1,0:T(8,128)(2,1)}, u32[]{:S(2)}) %copy-start.5) | copy-done | bytes 262168
  7.5 0.0 copy-start.2
  7.5 1.2 %shard_map.55.part_ref = f32[3,256,128]{2,1,0:T(8,128)S(1)} custom-call(bf16[256,512]{1,0:T(8,128)(2,1)S(1)} %bitcast.16, bf16[3,1152,512]{2,1,0:T(8,128)(2,1)S(1)} %bitcast.9), custom_call_target="tpu_custom_call" | custom-call | flops 905969664 | bytes 4194304 | tf_op jit(solution)/shard_map/pallas_call | solution.py:125
  8.7 0.0 copy-start.3
  8.7 0.7 %copy-done.3 = f32[3,256,128]{2,1,0:T(8,128)} copy-done((f32[3,256,128]{2,1,0:T(8,128)}, f32[3,256,128]{2,1,0:T(8,128)S(1)}, u32[]{:S(2)}) %copy-start.3) | copy-done | bytes 393240
  9.4 3.0 %collective-permute-done.1.far_ref = bf16[256,512]{1,0:T(8,128)(2,1)} collective-permute-done((bf16[256,512]{1,0:T(8,128)(2,1)}, bf16[256,512]{1,0:T(8,128)(2,1)}, u32[]{:S(2)}, u32[]{:S(2)}) %collective-permute-start.1) | collective-permute-done | bytes 262176 | tf_op jit(solution)/shard_map/ppermute | solution.py:19
  12.5 3.1 %collective-permute-done.near_ref = bf16[256,512]{1,0:T(8,128)(2,1)} collective-permute-done((bf16[256,512]{1,0:T(8,128)(2,1)}, bf16[256,512]{1,0:T(8,128)(2,1)}, u32[]{:S(2)}, u32[]{:S(2)}) %collective-permute-start) | collective-permute-done | bytes 262176 | tf_op jit(solution)/shard_map/ppermute | solution.py:19
  15.6 0.0 collective-permute-start.2
  15.6 0.5 %collective-permute-start.3 = (bf16[256,512]{1,0:T(8,128)(2,1)}, bf16[256,512]{1,0:T(8,128)(2,1)}, u32[]{:S(2)}, u32[]{:S(2)}) collective-permute-start(bf16[256,512]{1,0:T(8,128)(2,1)} %collective-permute-done.1.far_ref), channel_id=1, source_target_pairs={{1,0},{0,1},{3,2},{2,3},{5,4},{4,5},{7,6},{6,7},{9,8},{8,9},{11,10... | collective-permute-start | bytes 786440 | tf_op jit(solution)/shard_map/ppermute | solution.py:19
  16.1 1.4 %collective-permute-done.2.their_near_ref = bf16[256,512]{1,0:T(8,128)(2,1)} collective-permute-done((bf16[256,512]{1,0:T(8,128)(2,1)}, bf16[256,512]{1,0:T(8,128)(2,1)}, u32[]{:S(2)}, u32[]{:S(2)}) %collective-permute-start.2) | collective-permute-done | bytes 262176 | tf_op jit(solution)/shard_map/ppermute | solution.py:19
  17.5 0.4 %collective-permute-done.3.their_far_ref = bf16[256,512]{1,0:T(8,128)(2,1)} collective-permute-done((bf16[256,512]{1,0:T(8,128)(2,1)}, bf16[256,512]{1,0:T(8,128)(2,1)}, u32[]{:S(2)}, u32[]{:S(2)}) %collective-permute-start.3) | collective-permute-done | bytes 262176 | tf_op jit(solution)/shard_map/ppermute | solution.py:19
  17.8 0.0 copy-done.7
  17.8 0.0 copy-done.2
  17.8 0.0 copy-start.4
  17.8 1.0 %copy-done.4 = f32[3,256,128]{2,1,0:T(8,128)S(1)} copy-done((f32[3,256,128]{2,1,0:T(8,128)S(1)}, f32[3,256,128]{2,1,0:T(8,128)}, u32[]{:S(2)}) %copy-start.4) | copy-done | bytes 393240
  18.8 0.0 copy-start
  18.8 0.0 copy-start.6
  18.8 3.6 %shard_map.56 = bf16[3,256,128]{2,1,0:T(8,128)(2,1)S(1)} custom-call(s32[1]{0:T(128)} %bitcast.1.odd_ref, bf16[256,512]{1,0:T(8,128)(2,1)} %collective-permute-done.near_ref, bf16[256,512]{1,0:T(8,128)(2,1)} %collective-permute-done.1.far_ref, bf16[256,512]{1,0:T(8,128)(2,1)} %collective-permute-done.2.their_near_ref, ...), custom_call_target="tpu_custom_call" | custom-call | flops 1811939328 | bytes 5177860 | tf_op jit(solution)/shard_map/pallas_call | solution.py:125
  22.4 1.6 %collective-permute-start.4 = (bf16[1,3,256,128]{3,2,1,0:T(8,128)(2,1)S(1)}, bf16[1,3,256,128]{3,2,1,0:T(8,128)(2,1)S(1)}, u32[]{:S(2)}, u32[]{:S(2)}) collective-permute-start(bf16[1,3,256,128]{3,2,1,0:T(8,128)(2,1)S(1)} %bitcast.11), channel_id=1, source_target_pairs={{2,0},{3,1},{0,2},{1,3},{6,4},{7,5},{4,6},{5,7},{10,8},{11,9},{8,1... | collective-permute-start | bytes 589832 | tf_op jit(solution)/shard_map/ppermute | solution.py:19
  24.0 5.4 %collective-permute-done.4.refs_1_ = bf16[1,3,256,128]{3,2,1,0:T(8,128)(2,1)S(1)} collective-permute-done((bf16[1,3,256,128]{3,2,1,0:T(8,128)(2,1)S(1)}, bf16[1,3,256,128]{3,2,1,0:T(8,128)(2,1)S(1)}, u32[]{:S(2)}, u32[]{:S(2)}) %collective-permute-start.4) | collective-permute-done | bytes 196640 | tf_op jit(solution)/shard_map/ppermute | solution.py:19
  29.5 0.1 collective-permute-start.5
  29.6 1.7 %collective-permute-done.5.refs_2_ = bf16[2,3,256,128]{3,2,1,0:T(8,128)(2,1)S(1)} collective-permute-done((bf16[2,3,256,128]{3,2,1,0:T(8,128)(2,1)S(1)}, bf16[2,3,256,128]{3,2,1,0:T(8,128)(2,1)S(1)}, u32[]{:S(2)}, u32[]{:S(2)}) %collective-permute-start.5) | collective-permute-done | bytes 393248 | tf_op jit(solution)/shard_map/ppermute | solution.py:19
  31.3 0.0 copy-done
  31.3 0.0 copy-done.6
  31.3 2.0 %shard_map.57 = bf16[1,128,256]{2,1,0:T(8,128)(2,1)} custom-call(s32[1]{0:T(128)} %bitcast.me_ref, bf16[1,3,256,128]{3,2,1,0:T(8,128)(2,1)S(1)} %bitcast.13, bf16[1,3,256,128]{3,2,1,0:T(8,128)(2,1)S(1)} %collective-permute-done.4.refs_1_, bf16[2,3,256,128]{3,2,1,0:T(8,128)(2,1)S(1)} %collective-permute-done.5.refs_2_, bf16[3,1152,512]{2,1,0:T(8,128)(2,1)S(1)} %bitcast.8, ...), custom_call_target="tpu_custom_call" | custom-call | flops 905969664 | bytes 4391428 | tf_op jit(solution)/shard_map/pallas_call | solution.py:125
  (1 shorter events, 0.0 us)
Async XLA Ops:
  0.0 17.8 %copy-start.7 = (f32[128]{0:T(128)S(1)}, f32[128]{0:T(128)}, u32[]{:S(2)}) copy-start(f32[128]{0:T(128)} %param.7) | copy-start | bytes 1540
  0.0 12.5 %collective-permute-start.1 = (bf16[256,512]{1,0:T(8,128)(2,1)}, bf16[256,512]{1,0:T(8,128)(2,1)}, u32[]{:S(2)}, u32[]{:S(2)}) collective-permute-start(bf16[256,512]{1,0:T(8,128)(2,1)} %bitcast.14), channel_id=1, source_target_pairs={{24,0},{9,1},{26,2},{11,3},{28,4},{13,5},{30,6},{15,7},{0,8},{17,9... | collective-permute-start | bytes 786440 | tf_op jit(solution)/shard_map/ppermute | solution.py:19
  3.0 12.5 %collective-permute-start = (bf16[256,512]{1,0:T(8,128)(2,1)}, bf16[256,512]{1,0:T(8,128)(2,1)}, u32[]{:S(2)}, u32[]{:S(2)}) collective-permute-start(bf16[256,512]{1,0:T(8,128)(2,1)} %bitcast.15), channel_id=1, source_target_pairs={{28,0},{5,1},{30,2},{7,3},{0,4},{9,5},{2,6},{11,7},{4,8},{13,9},{6... | collective-permute-start | bytes 786440 | tf_op jit(solution)/shard_map/ppermute | solution.py:19
  4.5 2.0 %copy-start.1 = (bf16[3,3,3,128,512]{4,3,2,1,0:T(8,128)(2,1)S(1)}, bf16[3,3,3,128,512]{4,3,2,1,0:T(8,128)(2,1)}, u32[]{:S(2)}) copy-start(bf16[3,3,3,128,512]{4,3,2,1,0:T(8,128)(2,1)} %param.6) | copy-start | bytes 10616836
  6.5 0.9 %copy-start.5 = (bf16[1,4,64,512]{3,2,1,0:T(8,128)(2,1)S(1)}, bf16[1,4,64,512]{3,2,1,0:T(8,128)(2,1)}, u32[]{:S(2)}) copy-start(bf16[1,4,64,512]{3,2,1,0:T(8,128)(2,1)} %param.5) | copy-start | bytes 786436
  7.5 10.4 %copy-start.2 = (bf16[3,3,3,128,512]{4,3,2,1,0:T(8,128)(2,1)S(1)}, bf16[3,3,3,128,512]{4,3,2,1,0:T(8,128)(2,1)}, u32[]{:S(2)}) copy-start(bf16[3,3,3,128,512]{4,3,2,1,0:T(8,128)(2,1)} %param.6) | copy-start | bytes 10616836
  8.7 0.7 %copy-start.3 = (f32[3,256,128]{2,1,0:T(8,128)}, f32[3,256,128]{2,1,0:T(8,128)S(1)}, u32[]{:S(2)}) copy-start(f32[3,256,128]{2,1,0:T(8,128)S(1)} %shard_map.55.part_ref) | copy-start | bytes 1179652
  15.6 1.9 %collective-permute-start.2 = (bf16[256,512]{1,0:T(8,128)(2,1)}, bf16[256,512]{1,0:T(8,128)(2,1)}, u32[]{:S(2)}, u32[]{:S(2)}) collective-permute-start(bf16[256,512]{1,0:T(8,128)(2,1)} %collective-permute-done.near_ref), channel_id=1, source_target_pairs={{1,0},{0,1},{3,2},{2,3},{5,4},{4,5},{7,6},{6,7},{9,8},{8,9},{11,10... | collective-permute-start | bytes 786440 | tf_op jit(solution)/shard_map/ppermute | solution.py:19
  15.6 2.2 %collective-permute-start.3 = (bf16[256,512]{1,0:T(8,128)(2,1)}, bf16[256,512]{1,0:T(8,128)(2,1)}, u32[]{:S(2)}, u32[]{:S(2)}) collective-permute-start(bf16[256,512]{1,0:T(8,128)(2,1)} %collective-permute-done.1.far_ref), channel_id=1, source_target_pairs={{1,0},{0,1},{3,2},{2,3},{5,4},{4,5},{7,6},{6,7},{9,8},{8,9},{11,10... | collective-permute-start | bytes 786440 | tf_op jit(solution)/shard_map/ppermute | solution.py:19
  17.8 1.0 %copy-start.4 = (f32[3,256,128]{2,1,0:T(8,128)S(1)}, f32[3,256,128]{2,1,0:T(8,128)}, u32[]{:S(2)}) copy-start(f32[3,256,128]{2,1,0:T(8,128)} %copy-done.3) | copy-start | bytes 1179652
  18.8 12.4 %copy-start = (bf16[3,3,3,128,512]{4,3,2,1,0:T(8,128)(2,1)S(1)}, bf16[3,3,3,128,512]{4,3,2,1,0:T(8,128)(2,1)}, u32[]{:S(2)}) copy-start(bf16[3,3,3,128,512]{4,3,2,1,0:T(8,128)(2,1)} %param.8) | copy-start | bytes 10616836
  18.8 12.4 %copy-start.6 = (f32[128]{0:T(128)S(1)}, f32[128]{0:T(128)}, u32[]{:S(2)}) copy-start(f32[128]{0:T(128)} %param.9) | copy-start | bytes 1540
  22.4 7.0 %collective-permute-start.4 = (bf16[1,3,256,128]{3,2,1,0:T(8,128)(2,1)S(1)}, bf16[1,3,256,128]{3,2,1,0:T(8,128)(2,1)S(1)}, u32[]{:S(2)}, u32[]{:S(2)}) collective-permute-start(bf16[1,3,256,128]{3,2,1,0:T(8,128)(2,1)S(1)} %bitcast.11), channel_id=1, source_target_pairs={{2,0},{3,1},{0,2},{1,3},{6,4},{7,5},{4,6},{5,7},{10,8},{11,9},{8,1... | collective-permute-start | bytes 589832 | tf_op jit(solution)/shard_map/ppermute | solution.py:19
  29.5 1.8 %collective-permute-start.5 = (bf16[2,3,256,128]{3,2,1,0:T(8,128)(2,1)S(1)}, bf16[2,3,256,128]{3,2,1,0:T(8,128)(2,1)S(1)}, u32[]{:S(2)}, u32[]{:S(2)}) collective-permute-start(bf16[2,3,256,128]{3,2,1,0:T(8,128)(2,1)S(1)} %pad_maximum_fusion), channel_id=1, source_target_pairs={{1,0},{0,1},{3,2},{2,3},{5,4},{4,5},{7,6},{6,7},{9,8},{8,9},{11,10... | collective-permute-start | bytes 1179656 | tf_op jit(solution)/shard_map/ppermute | solution.py:19

commit v9 on v8

--- a/solution.py
+++ b/solution.py
@@ -35,7 +35,10 @@
         shifted = None
         for row_tap in range(3):
             tap = row_tap * 3 + col_tap
-            part = acc_ref[plane, :, pl.ds(tap * outs, outs)]
+            if len(acc_ref.shape) == 3:
+                part = acc_ref[plane, :, pl.ds(tap * outs, outs)]
+            else:
+                part = acc_ref[pl.ds(plane * cells, cells), pl.ds(tap * outs, outs)]
             amount = ((1 - row_tap) * cols_n) % cells
             if amount:
                 part = pltpu.roll(part, amount, 0)
@@ -65,29 +68,32 @@
 def own_plane_kernel(rows_n, cols_n, x_ref, w_ref, o_ref, acc_ref):
     outs = o_ref.shape[2]
     x = x_ref[...]
-    for plane in range(3):
-        acc_ref[plane] = tap_product(x, w_ref, 2 - plane)
-    for plane in range(3):
-        o_ref[plane] = spatial_sum(acc_ref, plane, rows_n, cols_n, outs)
-
-
-def neighbour_kernel(rows_n, cols_n, odd_ref, near_ref, far_ref, their_near_ref, their_far_ref, part_ref,
-                     w_ref, b_ref, o_ref, acc_ref):
+    for index, depth_tap in enumerate((2, 0)):
+        acc_ref[index] = tap_product(x, w_ref, depth_tap)
+    for index in range(2):
+        o_ref[index] = spatial_sum(acc_ref, index, rows_n, cols_n, outs)
+
+
+def neighbour_kernel(rows_n, cols_n, odd_ref, own_ref, near_ref, far_ref, their_near_ref, their_far_ref,
+                     part_ref, w_ref, b_ref, o_ref, field_ref, acc_ref):
     outs = o_ref.shape[2]
+    cells = rows_n * cols_n
     is_odd = odd_ref[0] != 0
-    minus_one = jnp.where(is_odd, their_near_ref[...], near_ref[...])
-    minus_two = jnp.where(is_odd, their_far_ref[...], far_ref[...])
-    plus_one = jnp.where(is_odd, near_ref[...], their_near_ref[...])
-    plus_two = jnp.where(is_odd, far_ref[...], their_far_ref[...])
-    acc_ref[0] = tap_product(minus_two, w_ref, 0)
-    acc_ref[1] = tap_product(minus_one, w_ref, 0)
-    acc_ref[0] += tap_product(minus_one, w_ref, 1)
-    acc_ref[2] = tap_product(plus_one, w_ref, 1)
-    acc_ref[1] += tap_product(plus_one, w_ref, 2)
-    acc_ref[2] += tap_product(plus_two, w_ref, 2)
+    field_ref[pl.ds(0, cells)] = jnp.where(is_odd, their_far_ref[...], far_ref[...])
+    field_ref[pl.ds(cells, cells)] = jnp.where(is_odd, their_near_ref[...], near_ref[...])
+    field_ref[pl.ds(2 * cells, cells)] = own_ref[...]
+    field_ref[pl.ds(3 * cells, cells)] = jnp.where(is_odd, near_ref[...], their_near_ref[...])
+    field_ref[pl.ds(4 * cells, cells)] = jnp.where(is_odd, far_ref[...], their_far_ref[...])
+    acc_ref[pl.ds(0, 2 * cells)] = tap_product(field_ref[pl.ds(0, 2 * cells)], w_ref, 0)
+    upper = tap_product(field_ref[pl.ds(3 * cells, 2 * cells)], w_ref, 2)
+    acc_ref[pl.ds(2 * cells, cells)] = upper[cells:]
+    acc_ref[pl.ds(cells, cells)] += upper[:cells]
+    acc_ref[...] += tap_product(field_ref[pl.ds(cells, 3 * cells)], w_ref, 1)
     bias = b_ref[...]
     for plane in range(3):
-        total = spatial_sum(acc_ref, plane, rows_n, cols_n, outs) + part_ref[plane]
+        total = spatial_sum(acc_ref, plane, rows_n, cols_n, outs)
+        if plane != 1:
+            total = total + part_ref[plane // 2]
         o_ref[plane] = jnp.maximum(total + bias, 0.0).astype(o_ref.dtype)
 
 
@@ -148,10 +154,10 @@
     near, far = from_side(flat, 1), from_side(flat, 2)
     own_terms = vmem_call(
         functools.partial(own_plane_kernel, rows_n, cols_n),
-        jax.ShapeDtypeStruct((3, cells, outs), jnp.float32),
+        jax.ShapeDtypeStruct((2, cells, outs), jnp.float32),
         [flat, one_stack],
-        [pltpu.VMEM((3, cells, 9 * outs), jnp.float32)],
-        3 * tap_flops,
+        [pltpu.VMEM((2, cells, 9 * outs), jnp.float32)],
+        2 * tap_flops,
     )
     near, far, own_terms = lax.optimization_barrier((near, far, own_terms))
     their_near, their_far = from_chan_partner(near, 1), from_chan_partner(far, 1)
@@ -159,9 +165,9 @@
     hidden = vmem_call(
         functools.partial(neighbour_kernel, rows_n, cols_n),
         jax.ShapeDtypeStruct((3, cells, outs), jnp.bfloat16),
-        [odd, near, far, their_near, their_far, own_terms, one_stack, bias_one.reshape(1, outs)],
-        [pltpu.VMEM((3, cells, 9 * outs), jnp.float32)],
-        6 * tap_flops,
+        [odd, flat, near, far, their_near, their_far, own_terms, one_stack, bias_one.reshape(1, outs)],
+        [pltpu.VMEM((5 * cells, count_in), jnp.bfloat16), pltpu.VMEM((3 * cells, 9 * outs), jnp.float32)],
+        7 * tap_flops,
         smem_first=True,
     )
 

time: 33.4 us -> 34.7 us (1.039)
  local copies, waits for them, and re-layouts: 4.7 us -> 5.58 us
  waiting for transfers between devices: 15 us -> 15.4 us
    unnamed x16 -> x18, local copies, waits for them, and re-layouts: 4.7 us -> 5.58 us
    ppermute x6, waiting for transfers between devices: 15 us -> 15.4 us  [gathered_from(): return lax.ppermute(block, ('space', 'chan'), pairs)]
  transfers between devices with their start and end apart: 6 -> 6, of which waited for: 6 -> 6; matrix products, arithmetic and copies ran while one was open for 0% -> 0% of each run, Pallas kernels for 4% -> 3%
where the time goes in v9:
time: 34.7 us; the launch traced here: 34.5 us
  waiting for transfers between devices  15.4 us (44%)
  Pallas kernels  6.76 us (19%)
  starting transfers between devices  6.68 us (19%)
  local copies, waits for them, and re-layouts  5.58 us (16%)
    ppermute x6, waiting for transfers between devices, gathered_from(): return lax.ppermute(block, ('space', 'chan'), pairs)  15.4 us
    pallas_call x3, Pallas kernels, vmem_call(): pl.pallas_call(kernel, out_shape=out_shape, in_specs=specs, out_specs=pl....  6.76 us
    ppermute x6, starting transfers between devices, gathered_from(): return lax.ppermute(block, ('space', 'chan'), pairs)  6.68 us
    unnamed x18, local copies, waits for them, and re-layouts  5.58 us
  transfers between devices with their start and end apart: 6, of which 6 were waited for; matrix products, arithmetic and copies ran while one was open for 0% of the time, Pallas kernels for 3%

profile of v9, /device:TPU:0, one launch (start us, length us, event | category | flops | bytes accessed | tf_op | source)
XLA Modules:
  0.0 34.5 jit_solution(12769959452495946298)
XLA Ops:
  0.0 0.0 copy-start.8
  0.0 3.0 %collective-permute-start.1 = (bf16[256,512]{1,0:T(8,128)(2,1)}, bf16[256,512]{1,0:T(8,128)(2,1)}, u32[]{:S(2)}, u32[]{:S(2)}) collective-permute-start(bf16[256,512]{1,0:T(8,128)(2,1)} %bitcast.14), channel_id=1, source_target_pairs={{24,0},{9,1},{26,2},{11,3},{28,4},{13,5},{30,6},{15,7},{0,8},{17,9... | collective-permute-start | bytes 786440 | tf_op jit(solution)/shard_map/ppermute | solution.py:19
  3.0 1.5 %collective-permute-start = (bf16[256,512]{1,0:T(8,128)(2,1)}, bf16[256,512]{1,0:T(8,128)(2,1)}, u32[]{:S(2)}, u32[]{:S(2)}) collective-permute-start(bf16[256,512]{1,0:T(8,128)(2,1)} %bitcast.15), channel_id=1, source_target_pairs={{28,0},{5,1},{30,2},{7,3},{0,4},{9,5},{2,6},{11,7},{4,8},{13,9},{6... | collective-permute-start | bytes 786440 | tf_op jit(solution)/shard_map/ppermute | solution.py:19
  4.5 0.0 copy-start.1
  4.5 2.0 %copy-done.1 = bf16[3,3,3,128,512]{4,3,2,1,0:T(8,128)(2,1)S(1)} copy-done((bf16[3,3,3,128,512]{4,3,2,1,0:T(8,128)(2,1)S(1)}, bf16[3,3,3,128,512]{4,3,2,1,0:T(8,128)(2,1)}, u32[]{:S(2)}) %copy-start.1) | copy-done | bytes 3538968
  6.5 0.0 copy-start.3
  6.5 0.9 %copy-done.3 = bf16[1,4,64,512]{3,2,1,0:T(8,128)(2,1)S(1)} copy-done((bf16[1,4,64,512]{3,2,1,0:T(8,128)(2,1)S(1)}, bf16[1,4,64,512]{3,2,1,0:T(8,128)(2,1)}, u32[]{:S(2)}) %copy-start.3) | copy-done | bytes 262168
  7.5 0.0 copy-start.2
  7.5 0.9 %shard_map.55.part_ref = f32[2,256,128]{2,1,0:T(8,128)S(1)} custom-call(bf16[256,512]{1,0:T(8,128)(2,1)S(1)} %bitcast.16, bf16[3,1152,512]{2,1,0:T(8,128)(2,1)S(1)} %bitcast.9), custom_call_target="tpu_custom_call" | custom-call | flops 603979776 | bytes 4063232 | tf_op jit(solution)/shard_map/pallas_call | solution.py:131
  8.4 0.0 copy-start.5
  8.4 0.7 %copy-done.5 = f32[2,256,128]{2,1,0:T(8,128)} copy-done((f32[2,256,128]{2,1,0:T(8,128)}, f32[2,256,128]{2,1,0:T(8,128)S(1)}, u32[]{:S(2)}) %copy-start.5) | copy-done | bytes 262168
  9.1 3.4 %collective-permute-done.1.far_ref = bf16[256,512]{1,0:T(8,128)(2,1)} collective-permute-done((bf16[256,512]{1,0:T(8,128)(2,1)}, bf16[256,512]{1,0:T(8,128)(2,1)}, u32[]{:S(2)}, u32[]{:S(2)}) %collective-permute-start.1) | collective-permute-done | bytes 262176 | tf_op jit(solution)/shard_map/ppermute | solution.py:19
  12.5 3.1 %collective-permute-done.near_ref = bf16[256,512]{1,0:T(8,128)(2,1)} collective-permute-done((bf16[256,512]{1,0:T(8,128)(2,1)}, bf16[256,512]{1,0:T(8,128)(2,1)}, u32[]{:S(2)}, u32[]{:S(2)}) %collective-permute-start) | collective-permute-done | bytes 262176 | tf_op jit(solution)/shard_map/ppermute | solution.py:19
  15.6 0.0 collective-permute-start.2
  15.6 0.5 %collective-permute-start.3 = (bf16[256,512]{1,0:T(8,128)(2,1)}, bf16[256,512]{1,0:T(8,128)(2,1)}, u32[]{:S(2)}, u32[]{:S(2)}) collective-permute-start(bf16[256,512]{1,0:T(8,128)(2,1)} %collective-permute-done.1.far_ref), channel_id=1, source_target_pairs={{1,0},{0,1},{3,2},{2,3},{5,4},{4,5},{7,6},{6,7},{9,8},{8,9},{11,10... | collective-permute-start | bytes 786440 | tf_op jit(solution)/shard_map/ppermute | solution.py:19
  16.1 1.4 %collective-permute-done.2.their_near_ref = bf16[256,512]{1,0:T(8,128)(2,1)} collective-permute-done((bf16[256,512]{1,0:T(8,128)(2,1)}, bf16[256,512]{1,0:T(8,128)(2,1)}, u32[]{:S(2)}, u32[]{:S(2)}) %collective-permute-start.2) | collective-permute-done | bytes 262176 | tf_op jit(solution)/shard_map/ppermute | solution.py:19
  17.5 0.4 %collective-permute-done.3.their_far_ref = bf16[256,512]{1,0:T(8,128)(2,1)} collective-permute-done((bf16[256,512]{1,0:T(8,128)(2,1)}, bf16[256,512]{1,0:T(8,128)(2,1)}, u32[]{:S(2)}, u32[]{:S(2)}) %collective-permute-start.3) | collective-permute-done | bytes 262176 | tf_op jit(solution)/shard_map/ppermute | solution.py:19
  17.8 0.0 copy-done.8
  17.8 0.0 copy-done.2
  17.8 0.0 copy-start.4
  17.8 0.9 %copy-done.4 = bf16[1,4,64,512]{3,2,1,0:T(8,128)(2,1)S(1)} copy-done((bf16[1,4,64,512]{3,2,1,0:T(8,128)(2,1)S(1)}, bf16[1,4,64,512]{3,2,1,0:T(8,128)(2,1)}, u32[]{:S(2)}) %copy-start.4) | copy-done | bytes 262168
  18.8 0.0 copy-start.6
  18.8 0.9 %copy-done.6 = f32[2,256,128]{2,1,0:T(8,128)S(1)} copy-done((f32[2,256,128]{2,1,0:T(8,128)S(1)}, f32[2,256,128]{2,1,0:T(8,128)}, u32[]{:S(2)}) %copy-start.6) | copy-done | bytes 262168
  19.7 0.0 copy-start
  19.7 0.0 copy-start.7
  19.7 3.9 %shard_map.56 = bf16[3,256,128]{2,1,0:T(8,128)(2,1)S(1)} custom-call(s32[1]{0:T(128)} %bitcast.1.odd_ref, bf16[256,512]{1,0:T(8,128)(2,1)S(1)} %bitcast.17, bf16[256,512]{1,0:T(8,128)(2,1)} %collective-permute-done.near_ref, bf16[256,512]{1,0:T(8,128)(2,1)} %collective-permute-done.1.far_ref, bf16[256,512]{1,0:T(8,128)(2,1)} %collective-permute-done.2.their_near_ref, ...), custom_call_target="tpu_custom_call" | custom-call | flops 2113929216 | bytes 5308932 | tf_op jit(solution)/shard_map/pallas_call | solution.py:131
  23.7 1.6 %collective-permute-start.4 = (bf16[1,3,256,128]{3,2,1,0:T(8,128)(2,1)S(1)}, bf16[1,3,256,128]{3,2,1,0:T(8,128)(2,1)S(1)}, u32[]{:S(2)}, u32[]{:S(2)}) collective-permute-start(bf16[1,3,256,128]{3,2,1,0:T(8,128)(2,1)S(1)} %bitcast.11), channel_id=1, source_target_pairs={{2,0},{3,1},{0,2},{1,3},{6,4},{7,5},{4,6},{5,7},{10,8},{11,9},{8,1... | collective-permute-start | bytes 589832 | tf_op jit(solution)/shard_map/ppermute | solution.py:19
  25.3 5.4 %collective-permute-done.4.refs_1_ = bf16[1,3,256,128]{3,2,1,0:T(8,128)(2,1)S(1)} collective-permute-done((bf16[1,3,256,128]{3,2,1,0:T(8,128)(2,1)S(1)}, bf16[1,3,256,128]{3,2,1,0:T(8,128)(2,1)S(1)}, u32[]{:S(2)}, u32[]{:S(2)}) %collective-permute-start.4) | collective-permute-done | bytes 196640 | tf_op jit(solution)/shard_map/ppermute | solution.py:19
  30.7 0.1 collective-permute-start.5
  30.8 1.7 %collective-permute-done.5.refs_2_ = bf16[2,3,256,128]{3,2,1,0:T(8,128)(2,1)S(1)} collective-permute-done((bf16[2,3,256,128]{3,2,1,0:T(8,128)(2,1)S(1)}, bf16[2,3,256,128]{3,2,1,0:T(8,128)(2,1)S(1)}, u32[]{:S(2)}, u32[]{:S(2)}) %collective-permute-start.5) | collective-permute-done | bytes 393248 | tf_op jit(solution)/shard_map/ppermute | solution.py:19
  32.5 0.0 copy-done
  32.5 0.0 copy-done.7
  32.5 2.0 %shard_map.57 = bf16[1,128,256]{2,1,0:T(8,128)(2,1)} custom-call(s32[1]{0:T(128)} %bitcast.me_ref, bf16[1,3,256,128]{3,2,1,0:T(8,128)(2,1)S(1)} %bitcast.13, bf16[1,3,256,128]{3,2,1,0:T(8,128)(2,1)S(1)} %collective-permute-done.4.refs_1_, bf16[2,3,256,128]{3,2,1,0:T(8,128)(2,1)S(1)} %collective-permute-done.5.refs_2_, bf16[3,1152,512]{2,1,0:T(8,128)(2,1)S(1)} %bitcast.8, ...), custom_call_target="tpu_custom_call" | custom-call | flops 905969664 | bytes 4391428 | tf_op jit(solution)/shard_map/pallas_call | solution.py:131
  (1 shorter events, 0.0 us)
Async XLA Ops:
  0.0 17.8 %copy-start.8 = (f32[128]{0:T(128)S(1)}, f32[128]{0:T(128)}, u32[]{:S(2)}) copy-start(f32[128]{0:T(128)} %param.7) | copy-start | bytes 1540
  0.0 12.5 %collective-permute-start.1 = (bf16[256,512]{1,0:T(8,128)(2,1)}, bf16[256,512]{1,0:T(8,128)(2,1)}, u32[]{:S(2)}, u32[]{:S(2)}) collective-permute-start(bf16[256,512]{1,0:T(8,128)(2,1)} %bitcast.14), channel_id=1, source_target_pairs={{24,0},{9,1},{26,2},{11,3},{28,4},{13,5},{30,6},{15,7},{0,8},{17,9... | collective-permute-start | bytes 786440 | tf_op jit(solution)/shard_map/ppermute | solution.py:19
  3.0 12.5 %collective-permute-start = (bf16[256,512]{1,0:T(8,128)(2,1)}, bf16[256,512]{1,0:T(8,128)(2,1)}, u32[]{:S(2)}, u32[]{:S(2)}) collective-permute-start(bf16[256,512]{1,0:T(8,128)(2,1)} %bitcast.15), channel_id=1, source_target_pairs={{28,0},{5,1},{30,2},{7,3},{0,4},{9,5},{2,6},{11,7},{4,8},{13,9},{6... | collective-permute-start | bytes 786440 | tf_op jit(solution)/shard_map/ppermute | solution.py:19
  4.5 2.0 %copy-start.1 = (bf16[3,3,3,128,512]{4,3,2,1,0:T(8,128)(2,1)S(1)}, bf16[3,3,3,128,512]{4,3,2,1,0:T(8,128)(2,1)}, u32[]{:S(2)}) copy-start(bf16[3,3,3,128,512]{4,3,2,1,0:T(8,128)(2,1)} %param.6) | copy-start | bytes 10616836
  6.5 0.9 %copy-start.3 = (bf16[1,4,64,512]{3,2,1,0:T(8,128)(2,1)S(1)}, bf16[1,4,64,512]{3,2,1,0:T(8,128)(2,1)}, u32[]{:S(2)}) copy-start(bf16[1,4,64,512]{3,2,1,0:T(8,128)(2,1)} %param.5) | copy-start | bytes 786436
  7.5 10.4 %copy-start.2 = (bf16[3,3,3,128,512]{4,3,2,1,0:T(8,128)(2,1)S(1)}, bf16[3,3,3,128,512]{4,3,2,1,0:T(8,128)(2,1)}, u32[]{:S(2)}) copy-start(bf16[3,3,3,128,512]{4,3,2,1,0:T(8,128)(2,1)} %param.6) | copy-start | bytes 10616836
  8.4 0.7 %copy-start.5 = (f32[2,256,128]{2,1,0:T(8,128)}, f32[2,256,128]{2,1,0:T(8,128)S(1)}, u32[]{:S(2)}) copy-start(f32[2,256,128]{2,1,0:T(8,128)S(1)} %shard_map.55.part_ref) | copy-start | bytes 786436
  15.6 1.9 %collective-permute-start.2 = (bf16[256,512]{1,0:T(8,128)(2,1)}, bf16[256,512]{1,0:T(8,128)(2,1)}, u32[]{:S(2)}, u32[]{:S(2)}) collective-permute-start(bf16[256,512]{1,0:T(8,128)(2,1)} %collective-permute-done.near_ref), channel_id=1, source_target_pairs={{1,0},{0,1},{3,2},{2,3},{5,4},{4,5},{7,6},{6,7},{9,8},{8,9},{11,10... | collective-permute-start | bytes 786440 | tf_op jit(solution)/shard_map/ppermute | solution.py:19
  15.6 2.2 %collective-permute-start.3 = (bf16[256,512]{1,0:T(8,128)(2,1)}, bf16[256,512]{1,0:T(8,128)(2,1)}, u32[]{:S(2)}, u32[]{:S(2)}) collective-permute-start(bf16[256,512]{1,0:T(8,128)(2,1)} %collective-permute-done.1.far_ref), channel_id=1, source_target_pairs={{1,0},{0,1},{3,2},{2,3},{5,4},{4,5},{7,6},{6,7},{9,8},{8,9},{11,10... | collective-permute-start | bytes 786440 | tf_op jit(solution)/shard_map/ppermute | solution.py:19
  17.8 1.0 %copy-start.4 = (bf16[1,4,64,512]{3,2,1,0:T(8,128)(2,1)S(1)}, bf16[1,4,64,512]{3,2,1,0:T(8,128)(2,1)}, u32[]{:S(2)}) copy-start(bf16[1,4,64,512]{3,2,1,0:T(8,128)(2,1)} %param.5) | copy-start | bytes 786436
  18.8 0.9 %copy-start.6 = (f32[2,256,128]{2,1,0:T(8,128)S(1)}, f32[2,256,128]{2,1,0:T(8,128)}, u32[]{:S(2)}) copy-start(f32[2,256,128]{2,1,0:T(8,128)} %copy-done.5) | copy-start | bytes 786436
  19.7 12.8 %copy-start = (bf16[3,3,3,128,512]{4,3,2,1,0:T(8,128)(2,1)S(1)}, bf16[3,3,3,128,512]{4,3,2,1,0:T(8,128)(2,1)}, u32[]{:S(2)}) copy-start(bf16[3,3,3,128,512]{4,3,2,1,0:T(8,128)(2,1)} %param.8) | copy-start | bytes 10616836
  19.7 12.8 %copy-start.7 = (f32[128]{0:T(128)S(1)}, f32[128]{0:T(128)}, u32[]{:S(2)}) copy-start(f32[128]{0:T(128)} %param.9) | copy-start | bytes 1540
  23.7 7.0 %collective-permute-start.4 = (bf16[1,3,256,128]{3,2,1,0:T(8,128)(2,1)S(1)}, bf16[1,3,256,128]{3,2,1,0:T(8,128)(2,1)S(1)}, u32[]{:S(2)}, u32[]{:S(2)}) collective-permute-start(bf16[1,3,256,128]{3,2,1,0:T(8,128)(2,1)S(1)} %bitcast.11), channel_id=1, source_target_pairs={{2,0},{3,1},{0,2},{1,3},{6,4},{7,5},{4,6},{5,7},{10,8},{11,9},{8,1... | collective-permute-start | bytes 589832 | tf_op jit(solution)/shard_map/ppermute | solution.py:19
  30.7 1.8 %collective-permute-start.5 = (bf16[2,3,256,128]{3,2,1,0:T(8,128)(2,1)S(1)}, bf16[2,3,256,128]{3,2,1,0:T(8,128)(2,1)S(1)}, u32[]{:S(2)}, u32[]{:S(2)}) collective-permute-start(bf16[2,3,256,128]{3,2,1,0:T(8,128)(2,1)S(1)} %pad_maximum_fusion), channel_id=1, source_target_pairs={{1,0},{0,1},{3,2},{2,3},{5,4},{4,5},{7,6},{6,7},{9,8},{8,9},{11,10... | collective-permute-start | bytes 1179656 | tf_op jit(solution)/shard_map/ppermute | solution.py:19

commit v10 on v5

--- a/solution.py
+++ b/solution.py
@@ -164,18 +164,22 @@
         smem_first=True,
     )
 
-    held = [(hidden[None], (0,))]
+    held = [(hidden[None], (0,)), (from_chan_partner(hidden, 1)[None], (1,))]
+    remote = [(hidden[None], (0,))]
     offsets = [0]
-    bit = 1
+    bit = 2
     while bit < chans:
+        sent = jnp.stack([arr[i] for arr, offs in remote for i in range(len(offs))])
+        got = from_chan_partner(sent, bit)
+        remote.append((got, tuple(j ^ bit for j in offsets)))
+        offsets = offsets + [j ^ bit for j in offsets]
         bit *= 2
-    bit //= 2
-    while bit >= 1:
-        sent = jnp.stack([arr[i] for arr, offs in held for i in range(len(offs))])
-        got = from_chan_partner(sent, bit)
-        held.append((got, tuple(j ^ bit for j in offsets)))
-        offsets = offsets + [j ^ bit for j in offsets]
-        bit //= 2
+    if len(remote) > 1:
+        received = [(arr, offs) for arr, offs in remote[1:]]
+        held.extend(received)
+        sent = jnp.stack([arr[i] for arr, offs in received for i in range(len(offs))])
+        forwarded = from_chan_partner(sent, 1)
+        held.append((forwarded, tuple(j ^ 1 for _, offs in received for j in offs)))
     layout = tuple(offs for _, offs in held)
     me_flag = me.astype(jnp.int32).reshape(1)
     output = vmem_call(

time: 33.4 us -> 35 us (1.048)
  local copies, waits for them, and re-layouts: 4.7 us -> 6.69 us
    unnamed x16, local copies, waits for them, and re-layouts: 4.7 us -> 6.69 us
    ppermute x6 -> x7, waiting for transfers between devices: 15 us -> 14.7 us  [gathered_from(): return lax.ppermute(block, ('space', 'chan'), pairs)]
    ppermute x6 -> x7, starting transfers between devices: 6.68 us -> 6.61 us  [gathered_from(): return lax.ppermute(block, ('space', 'chan'), pairs)]
  transfers between devices with their start and end apart: 6 -> 7, of which waited for: 6 -> 6; matrix products, arithmetic and copies ran while one was open for 0% -> 0% of each run, Pallas kernels for 4% -> 4%
where the time goes in v10:
time: 35 us; the launch traced here: 34.7 us
  waiting for transfers between devices  14.7 us (42%)
  local copies, waits for them, and re-layouts  6.69 us (19%)
  Pallas kernels  6.62 us (19%)
  starting transfers between devices  6.61 us (19%)
    ppermute x7, waiting for transfers between devices, gathered_from(): return lax.ppermute(block, ('space', 'chan'), pairs)  14.7 us
    unnamed x16, local copies, waits for them, and re-layouts  6.69 us
    pallas_call x3, Pallas kernels, vmem_call(): pl.pallas_call(kernel, out_shape=out_shape, in_specs=specs, out_specs=pl....  6.62 us
    ppermute x7, starting transfers between devices, gathered_from(): return lax.ppermute(block, ('space', 'chan'), pairs)  6.61 us
  transfers between devices with their start and end apart: 7, of which 6 were waited for; matrix products, arithmetic and copies ran while one was open for 0% of the time, Pallas kernels for 4%

profile of v10, /device:TPU:0, one launch (start us, length us, event | category | flops | bytes accessed | tf_op | source)
XLA Modules:
  0.0 34.7 jit_solution(5141038243293569066)
XLA Ops:
  0.0 0.0 copy-start.7
  0.0 3.0 %collective-permute-start.1 = (bf16[256,512]{1,0:T(8,128)(2,1)}, bf16[256,512]{1,0:T(8,128)(2,1)}, u32[]{:S(2)}, u32[]{:S(2)}) collective-permute-start(bf16[256,512]{1,0:T(8,128)(2,1)} %bitcast.12), channel_id=1, source_target_pairs={{24,0},{9,1},{26,2},{11,3},{28,4},{13,5},{30,6},{15,7},{0,8},{17,9... | collective-permute-start | bytes 786440 | tf_op jit(solution)/shard_map/ppermute | solution.py:19
  3.0 1.5 %collective-permute-start = (bf16[256,512]{1,0:T(8,128)(2,1)}, bf16[256,512]{1,0:T(8,128)(2,1)}, u32[]{:S(2)}, u32[]{:S(2)}) collective-permute-start(bf16[256,512]{1,0:T(8,128)(2,1)} %bitcast.13), channel_id=1, source_target_pairs={{28,0},{5,1},{30,2},{7,3},{0,4},{9,5},{2,6},{11,7},{4,8},{13,9},{6... | collective-permute-start | bytes 786440 | tf_op jit(solution)/shard_map/ppermute | solution.py:19
  4.5 0.0 copy-start.1
  4.5 2.0 %copy-done.1 = bf16[3,3,3,128,512]{4,3,2,1,0:T(8,128)(2,1)S(1)} copy-done((bf16[3,3,3,128,512]{4,3,2,1,0:T(8,128)(2,1)S(1)}, bf16[3,3,3,128,512]{4,3,2,1,0:T(8,128)(2,1)}, u32[]{:S(2)}) %copy-start.1) | copy-done | bytes 3538968
  6.5 0.0 copy-start.5
  6.5 0.9 %copy-done.5 = bf16[1,4,64,512]{3,2,1,0:T(8,128)(2,1)S(1)} copy-done((bf16[1,4,64,512]{3,2,1,0:T(8,128)(2,1)S(1)}, bf16[1,4,64,512]{3,2,1,0:T(8,128)(2,1)}, u32[]{:S(2)}) %copy-start.5) | copy-done | bytes 262168
  7.5 0.0 copy-start.6
  7.5 1.2 %shard_map.55.part_ref = f32[3,256,128]{2,1,0:T(8,128)S(1)} custom-call(bf16[256,512]{1,0:T(8,128)(2,1)S(1)} %bitcast.14, bf16[3,1152,512]{2,1,0:T(8,128)(2,1)S(1)} %bitcast.10), custom_call_target="tpu_custom_call" | custom-call | flops 905969664 | bytes 4194304 | tf_op jit(solution)/shard_map/pallas_call | solution.py:124
  8.7 0.0 copy-start.3
  8.7 0.7 %copy-done.3 = f32[3,256,128]{2,1,0:T(8,128)} copy-done((f32[3,256,128]{2,1,0:T(8,128)}, f32[3,256,128]{2,1,0:T(8,128)S(1)}, u32[]{:S(2)}) %copy-start.3) | copy-done | bytes 393240
  9.4 0.0 copy-start
  9.4 3.0 %collective-permute-done.1.far_ref = bf16[256,512]{1,0:T(8,128)(2,1)} collective-permute-done((bf16[256,512]{1,0:T(8,128)(2,1)}, bf16[256,512]{1,0:T(8,128)(2,1)}, u32[]{:S(2)}, u32[]{:S(2)}) %collective-permute-start.1) | collective-permute-done | bytes 262176 | tf_op jit(solution)/shard_map/ppermute | solution.py:19
  12.5 3.1 %collective-permute-done.near_ref = bf16[256,512]{1,0:T(8,128)(2,1)} collective-permute-done((bf16[256,512]{1,0:T(8,128)(2,1)}, bf16[256,512]{1,0:T(8,128)(2,1)}, u32[]{:S(2)}, u32[]{:S(2)}) %collective-permute-start) | collective-permute-done | bytes 262176 | tf_op jit(solution)/shard_map/ppermute | solution.py:19
  15.6 0.0 collective-permute-start.2
  15.6 0.5 %collective-permute-start.3 = (bf16[256,512]{1,0:T(8,128)(2,1)}, bf16[256,512]{1,0:T(8,128)(2,1)}, u32[]{:S(2)}, u32[]{:S(2)}) collective-permute-start(bf16[256,512]{1,0:T(8,128)(2,1)} %collective-permute-done.1.far_ref), channel_id=1, source_target_pairs={{1,0},{0,1},{3,2},{2,3},{5,4},{4,5},{7,6},{6,7},{9,8},{8,9},{11,10... | collective-permute-start | bytes 786440 | tf_op jit(solution)/shard_map/ppermute | solution.py:19
  16.1 1.4 %collective-permute-done.2.their_near_ref = bf16[256,512]{1,0:T(8,128)(2,1)} collective-permute-done((bf16[256,512]{1,0:T(8,128)(2,1)}, bf16[256,512]{1,0:T(8,128)(2,1)}, u32[]{:S(2)}, u32[]{:S(2)}) %collective-permute-start.2) | collective-permute-done | bytes 262176 | tf_op jit(solution)/shard_map/ppermute | solution.py:19
  17.5 0.4 %collective-permute-done.3.their_far_ref = bf16[256,512]{1,0:T(8,128)(2,1)} collective-permute-done((bf16[256,512]{1,0:T(8,128)(2,1)}, bf16[256,512]{1,0:T(8,128)(2,1)}, u32[]{:S(2)}, u32[]{:S(2)}) %collective-permute-start.3) | collective-permute-done | bytes 262176 | tf_op jit(solution)/shard_map/ppermute | solution.py:19
  17.8 0.0 copy-done.7
  17.8 0.0 copy-start.2
  17.8 2.0 %copy-done.2 = bf16[3,3,3,128,512]{4,3,2,1,0:T(8,128)(2,1)S(1)} copy-done((bf16[3,3,3,128,512]{4,3,2,1,0:T(8,128)(2,1)S(1)}, bf16[3,3,3,128,512]{4,3,2,1,0:T(8,128)(2,1)}, u32[]{:S(2)}) %copy-start.2) | copy-done | bytes 3538968
  19.8 0.0 copy-start.4
  19.8 1.0 %copy-done.4 = f32[3,256,128]{2,1,0:T(8,128)S(1)} copy-done((f32[3,256,128]{2,1,0:T(8,128)S(1)}, f32[3,256,128]{2,1,0:T(8,128)}, u32[]{:S(2)}) %copy-start.4) | copy-done | bytes 393240
  20.8 3.4 %shard_map.56 = bf16[3,256,128]{2,1,0:T(8,128)(2,1)S(1)} custom-call(s32[1]{0:T(128)} %bitcast.1.odd_ref, bf16[256,512]{1,0:T(8,128)(2,1)} %collective-permute-done.near_ref, bf16[256,512]{1,0:T(8,128)(2,1)} %collective-permute-done.1.far_ref, bf16[256,512]{1,0:T(8,128)(2,1)} %collective-permute-done.2.their_near_ref, ...), custom_call_target="tpu_custom_call" | custom-call | flops 1811939328 | bytes 5177860 | tf_op jit(solution)/shard_map/pallas_call | solution.py:124
  24.3 1.6 %collective-permute-start.5 = (bf16[1,3,256,128]{3,2,1,0:T(8,128)(2,1)S(1)}, bf16[1,3,256,128]{3,2,1,0:T(8,128)(2,1)S(1)}, u32[]{:S(2)}, u32[]{:S(2)}) collective-permute-start(bf16[1,3,256,128]{3,2,1,0:T(8,128)(2,1)S(1)} %bitcast.15), channel_id=1, source_target_pairs={{2,0},{3,1},{0,2},{1,3},{6,4},{7,5},{4,6},{5,7},{10,8},{11,9},{8,1... | collective-permute-start | bytes 589832 | tf_op jit(solution)/shard_map/ppermute | solution.py:19
  25.9 0.0 collective-permute-start.4
  25.9 5.4 %collective-permute-done.5.refs_2_ = bf16[1,3,256,128]{3,2,1,0:T(8,128)(2,1)S(1)} collective-permute-done((bf16[1,3,256,128]{3,2,1,0:T(8,128)(2,1)S(1)}, bf16[1,3,256,128]{3,2,1,0:T(8,128)(2,1)S(1)}, u32[]{:S(2)}, u32[]{:S(2)}) %collective-permute-start.5) | collective-permute-done | bytes 196640 | tf_op jit(solution)/shard_map/ppermute | solution.py:19
  31.3 0.0 collective-permute-start.6
  31.3 0.0 collective-permute-done.4
  31.3 1.4 %collective-permute-done.6.refs_3_ = bf16[1,3,256,128]{3,2,1,0:T(8,128)(2,1)S(1)} collective-permute-done((bf16[1,3,256,128]{3,2,1,0:T(8,128)(2,1)S(1)}, bf16[1,3,256,128]{3,2,1,0:T(8,128)(2,1)S(1)}, u32[]{:S(2)}, u32[]{:S(2)}) %collective-permute-start.6) | collective-permute-done | bytes 196640 | tf_op jit(solution)/shard_map/ppermute | solution.py:19
  32.7 0.0 copy-done.6
  32.7 0.0 copy-done
  32.7 2.0 %shard_map.57 = bf16[1,128,256]{2,1,0:T(8,128)(2,1)} custom-call(s32[1]{0:T(128)} %bitcast.me_ref, bf16[1,3,256,128]{3,2,1,0:T(8,128)(2,1)S(1)} %bitcast.16, bf16[1,3,256,128]{3,2,1,0:T(8,128)(2,1)S(1)} %bitcast.17, bf16[1,3,256,128]{3,2,1,0:T(8,128)(2,1)S(1)} %collective-permute-done.5.refs_2_, bf16[1,3,256,128]{3,2,1,0:T(8,128)(2,1)S(1)} %collective-permute-done.6.refs_3_, ...), custom_call_target="tpu_custom_call" | custom-call | flops 905969664 | bytes 4391428 | tf_op jit(solution)/shard_map/pallas_call | solution.py:124
Async XLA Ops:
  0.0 17.8 %copy-start.7 = (f32[128]{0:T(128)S(1)}, f32[128]{0:T(128)}, u32[]{:S(2)}) copy-start(f32[128]{0:T(128)} %param.7) | copy-start | bytes 1540
  0.0 12.5 %collective-permute-start.1 = (bf16[256,512]{1,0:T(8,128)(2,1)}, bf16[256,512]{1,0:T(8,128)(2,1)}, u32[]{:S(2)}, u32[]{:S(2)}) collective-permute-start(bf16[256,512]{1,0:T(8,128)(2,1)} %bitcast.12), channel_id=1, source_target_pairs={{24,0},{9,1},{26,2},{11,3},{28,4},{13,5},{30,6},{15,7},{0,8},{17,9... | collective-permute-start | bytes 786440 | tf_op jit(solution)/shard_map/ppermute | solution.py:19
  3.0 12.5 %collective-permute-start = (bf16[256,512]{1,0:T(8,128)(2,1)}, bf16[256,512]{1,0:T(8,128)(2,1)}, u32[]{:S(2)}, u32[]{:S(2)}) collective-permute-start(bf16[256,512]{1,0:T(8,128)(2,1)} %bitcast.13), channel_id=1, source_target_pairs={{28,0},{5,1},{30,2},{7,3},{0,4},{9,5},{2,6},{11,7},{4,8},{13,9},{6... | collective-permute-start | bytes 786440 | tf_op jit(solution)/shard_map/ppermute | solution.py:19
  4.5 2.0 %copy-start.1 = (bf16[3,3,3,128,512]{4,3,2,1,0:T(8,128)(2,1)S(1)}, bf16[3,3,3,128,512]{4,3,2,1,0:T(8,128)(2,1)}, u32[]{:S(2)}) copy-start(bf16[3,3,3,128,512]{4,3,2,1,0:T(8,128)(2,1)} %param.6) | copy-start | bytes 10616836
  6.5 0.9 %copy-start.5 = (bf16[1,4,64,512]{3,2,1,0:T(8,128)(2,1)S(1)}, bf16[1,4,64,512]{3,2,1,0:T(8,128)(2,1)}, u32[]{:S(2)}) copy-start(bf16[1,4,64,512]{3,2,1,0:T(8,128)(2,1)} %param.5) | copy-start | bytes 786436
  7.5 25.2 %copy-start.6 = (f32[128]{0:T(128)S(1)}, f32[128]{0:T(128)}, u32[]{:S(2)}) copy-start(f32[128]{0:T(128)} %param.9) | copy-start | bytes 1540
  8.7 0.7 %copy-start.3 = (f32[3,256,128]{2,1,0:T(8,128)}, f32[3,256,128]{2,1,0:T(8,128)S(1)}, u32[]{:S(2)}) copy-start(f32[3,256,128]{2,1,0:T(8,128)S(1)} %shard_map.55.part_ref) | copy-start | bytes 1179652
  9.4 23.3 %copy-start = (bf16[3,3,3,128,512]{4,3,2,1,0:T(8,128)(2,1)S(1)}, bf16[3,3,3,128,512]{4,3,2,1,0:T(8,128)(2,1)}, u32[]{:S(2)}) copy-start(bf16[3,3,3,128,512]{4,3,2,1,0:T(8,128)(2,1)} %param.8) | copy-start | bytes 10616836
  15.6 1.9 %collective-permute-start.2 = (bf16[256,512]{1,0:T(8,128)(2,1)}, bf16[256,512]{1,0:T(8,128)(2,1)}, u32[]{:S(2)}, u32[]{:S(2)}) collective-permute-start(bf16[256,512]{1,0:T(8,128)(2,1)} %collective-permute-done.near_ref), channel_id=1, source_target_pairs={{1,0},{0,1},{3,2},{2,3},{5,4},{4,5},{7,6},{6,7},{9,8},{8,9},{11,10... | collective-permute-start | bytes 786440 | tf_op jit(solution)/shard_map/ppermute | solution.py:19
  15.6 2.2 %collective-permute-start.3 = (bf16[256,512]{1,0:T(8,128)(2,1)}, bf16[256,512]{1,0:T(8,128)(2,1)}, u32[]{:S(2)}, u32[]{:S(2)}) collective-permute-start(bf16[256,512]{1,0:T(8,128)(2,1)} %collective-permute-done.1.far_ref), channel_id=1, source_target_pairs={{1,0},{0,1},{3,2},{2,3},{5,4},{4,5},{7,6},{6,7},{9,8},{8,9},{11,10... | collective-permute-start | bytes 786440 | tf_op jit(solution)/shard_map/ppermute | solution.py:19
  17.8 2.0 %copy-start.2 = (bf16[3,3,3,128,512]{4,3,2,1,0:T(8,128)(2,1)S(1)}, bf16[3,3,3,128,512]{4,3,2,1,0:T(8,128)(2,1)}, u32[]{:S(2)}) copy-start(bf16[3,3,3,128,512]{4,3,2,1,0:T(8,128)(2,1)} %param.6) | copy-start | bytes 10616836
  19.8 1.0 %copy-start.4 = (f32[3,256,128]{2,1,0:T(8,128)S(1)}, f32[3,256,128]{2,1,0:T(8,128)}, u32[]{:S(2)}) copy-start(f32[3,256,128]{2,1,0:T(8,128)} %copy-done.3) | copy-start | bytes 1179652
  24.3 7.0 %collective-permute-start.5 = (bf16[1,3,256,128]{3,2,1,0:T(8,128)(2,1)S(1)}, bf16[1,3,256,128]{3,2,1,0:T(8,128)(2,1)S(1)}, u32[]{:S(2)}, u32[]{:S(2)}) collective-permute-start(bf16[1,3,256,128]{3,2,1,0:T(8,128)(2,1)S(1)} %bitcast.15), channel_id=1, source_target_pairs={{2,0},{3,1},{0,2},{1,3},{6,4},{7,5},{4,6},{5,7},{10,8},{11,9},{8,1... | collective-permute-start | bytes 589832 | tf_op jit(solution)/shard_map/ppermute | solution.py:19
  25.9 5.4 %collective-permute-start.4 = (bf16[3,256,128]{2,1,0:T(8,128)(2,1)S(1)}, bf16[3,256,128]{2,1,0:T(8,128)(2,1)S(1)}, u32[]{:S(2)}, u32[]{:S(2)}) collective-permute-start(bf16[3,256,128]{2,1,0:T(8,128)(2,1)S(1)} %shard_map.56), channel_id=1, source_target_pairs={{1,0},{0,1},{3,2},{2,3},{5,4},{4,5},{7,6},{6,7},{9,8},{8,9},{11,10... | collective-permute-start | bytes 589832 | tf_op jit(solution)/shard_map/ppermute | solution.py:19
  31.3 1.4 %collective-permute-start.6 = (bf16[1,3,256,128]{3,2,1,0:T(8,128)(2,1)S(1)}, bf16[1,3,256,128]{3,2,1,0:T(8,128)(2,1)S(1)}, u32[]{:S(2)}, u32[]{:S(2)}) collective-permute-start(bf16[1,3,256,128]{3,2,1,0:T(8,128)(2,1)S(1)} %collective-permute-done.5.refs_2_), channel_id=1, source_target_pairs={{1,0},{0,1},{3,2},{2,3},{5,4},{4,5},{7,6},{6,7},{9,8},{8,9},{11,10... | collective-permute-start | bytes 589832 | tf_op jit(solution)/shard_map/ppermute | solution.py:19

commit v11 on v7

--- a/solution.py
+++ b/solution.py
@@ -62,29 +62,34 @@
     )
 
 
-def own_plane_kernel(rows_n, cols_n, x_ref, w_ref, o_ref, acc_ref):
+def own_plane_kernel(rows_n, cols_n, x_ref, w_ref, o_ref, send_ref, acc_ref):
     outs = o_ref.shape[2]
     x = x_ref[...]
     for plane in range(3):
         acc_ref[plane] = tap_product(x, w_ref, 2 - plane)
     for plane in range(3):
-        o_ref[plane] = spatial_sum(acc_ref, plane, rows_n, cols_n, outs)
-
-
-def neighbour_kernel(rows_n, cols_n, odd_ref, near_ref, far_ref, their_near_ref, their_far_ref, part_ref,
+        terms = spatial_sum(acc_ref, plane, rows_n, cols_n, outs)
+        o_ref[plane] = terms
+        if plane != 1:
+            send_ref[plane // 2] = terms
+
+
+def neighbour_kernel(rows_n, cols_n, odd_ref, near_ref, their_near_ref, below_ref, above_ref, part_ref,
                      w_ref, b_ref, o_ref, acc_ref):
     outs = o_ref.shape[2]
     is_odd = odd_ref[0] != 0
     minus_one = jnp.where(is_odd, their_near_ref[...], near_ref[...])
-    minus_two = jnp.where(is_odd, their_far_ref[...], far_ref[...])
     plus_one = jnp.where(is_odd, near_ref[...], their_near_ref[...])
-    plus_two = jnp.where(is_odd, far_ref[...], their_far_ref[...])
-    acc_ref[0] = tap_product(minus_two, w_ref, 0) + tap_product(minus_one, w_ref, 1)
-    acc_ref[1] = tap_product(minus_one, w_ref, 0) + tap_product(plus_one, w_ref, 2)
-    acc_ref[2] = tap_product(plus_one, w_ref, 1) + tap_product(plus_two, w_ref, 2)
+    acc_ref[0] = tap_product(minus_one, w_ref, 1)
+    acc_ref[1] = tap_product(minus_one, w_ref, 0)
+    acc_ref[1] += tap_product(plus_one, w_ref, 2)
+    acc_ref[2] = tap_product(plus_one, w_ref, 1)
     bias = b_ref[...]
+    far = {0: below_ref, 2: above_ref}
     for plane in range(3):
         total = spatial_sum(acc_ref, plane, rows_n, cols_n, outs) + part_ref[plane]
+        if plane in far:
+            total = total + far[plane][...]
         o_ref[plane] = jnp.maximum(total + bias, 0.0).astype(o_ref.dtype)
 
 
@@ -120,12 +125,14 @@
     specs = [pl.BlockSpec(memory_space=pltpu.VMEM) for _ in operands]
     if smem_first:
         specs[0] = pl.BlockSpec(memory_space=pltpu.SMEM)
-    moved = sum(x.size * x.dtype.itemsize for x in operands) + out_shape.size * out_shape.dtype.itemsize
+    outs_list = out_shape if isinstance(out_shape, tuple) else (out_shape,)
+    moved = sum(x.size * x.dtype.itemsize for x in operands) + sum(o.size * o.dtype.itemsize for o in outs_list)
     return pl.pallas_call(
         kernel,
         out_shape=out_shape,
         in_specs=specs,
-        out_specs=pl.BlockSpec(memory_space=pltpu.VMEM),
+        out_specs=tuple(pl.BlockSpec(memory_space=pltpu.VMEM) for _ in outs_list)
+        if isinstance(out_shape, tuple) else pl.BlockSpec(memory_space=pltpu.VMEM),
         scratch_shapes=scratch,
         compiler_params=pltpu.CompilerParams(vmem_limit_bytes=48 * 1024 * 1024),
         cost_estimate=pl.CostEstimate(flops=flops, transcendentals=0, bytes_accessed=moved),
@@ -144,25 +151,25 @@
     tap_flops = 2 * cells * count_in * 9 * outs
 
     flat = plane.reshape(cells, count_in)
-    near, far = from_side(flat, 1), from_side(flat, 2)
-    own_terms = vmem_call(
+    near = from_side(flat, 1)
+    own_terms, sent = vmem_call(
         functools.partial(own_plane_kernel, rows_n, cols_n),
-        jax.ShapeDtypeStruct((3, cells, outs), jnp.float32),
+        (jax.ShapeDtypeStruct((3, cells, outs), jnp.float32), jax.ShapeDtypeStruct((2, cells, outs), jnp.float32)),
         [flat, one_stack],
         [pltpu.VMEM((3, cells, 9 * outs), jnp.float32)],
         3 * tap_flops,
     )
-    far, own_terms = lax.optimization_barrier((far, own_terms))
-    their_far = from_chan_partner(far, 1)
-    near, own_terms, their_far = lax.optimization_barrier((near, own_terms, their_far))
+    below = gathered_from(sent[1], lambda s, c: (s - 2, c))
+    above = gathered_from(sent[0], lambda s, c: (s + 2, c))
+    near, below, above = lax.optimization_barrier((near, below, above))
     their_near = from_chan_partner(near, 1)
     odd = (me % 2).astype(jnp.int32).reshape(1)
     hidden = vmem_call(
         functools.partial(neighbour_kernel, rows_n, cols_n),
         jax.ShapeDtypeStruct((3, cells, outs), jnp.bfloat16),
-        [odd, near, far, their_near, their_far, own_terms, one_stack, bias_one.reshape(1, outs)],
+        [odd, near, their_near, below, above, own_terms, one_stack, bias_one.reshape(1, outs)],
         [pltpu.VMEM((3, cells, 9 * outs), jnp.float32)],
-        6 * tap_flops,
+        4 * tap_flops,
         smem_first=True,
     )
 

time: 35.6 us -> 37.3 us (1.048)
  starting transfers between devices: 6.18 us -> 8.25 us
  Pallas kernels: 6.65 us -> 5.78 us
  waiting for transfers between devices: 14.4 us -> 15.1 us
    ppermute x6, starting transfers between devices: 6.18 us -> 8.25 us  [gathered_from(): return lax.ppermute(block, ('space', 'chan'), pairs)]
    pallas_call x3, Pallas kernels: 6.65 us -> 5.78 us  [vmem_call(): pl.pallas_call(kernel, out_shape=out_shape, in_specs=specs, out_specs=tup...]
    ppermute x6, waiting for transfers between devices: 14.4 us -> 15.1 us  [gathered_from(): return lax.ppermute(block, ('space', 'chan'), pairs)]
where the time goes in v11:
time: 37.3 us; the launch traced here: 37.1 us
  waiting for transfers between devices  15.1 us (40%)
  starting transfers between devices  8.25 us (22%)
  local copies, waits for them, and re-layouts  7.81 us (21%)
  Pallas kernels  5.78 us (15%)
    ppermute x6, waiting for transfers between devices, gathered_from(): return lax.ppermute(block, ('space', 'chan'), pairs)  15.1 us
    ppermute x6, starting transfers between devices, gathered_from(): return lax.ppermute(block, ('space', 'chan'), pairs)  8.25 us
    unnamed x24, local copies, waits for them, and re-layouts  7.79 us
    pallas_call x3, Pallas kernels, vmem_call(): pl.pallas_call(kernel, out_shape=out_shape, in_specs=specs, out_specs=tup...  5.78 us
  transfers between devices with their start and end apart: 6, of which 5 were waited for; matrix products, arithmetic and copies ran while one was open for 0% of the time, Pallas kernels for 3%

profile of v11, /device:TPU:0, one launch (start us, length us, event | category | flops | bytes accessed | tf_op | source)
XLA Modules:
  0.0 37.1 jit_solution(10186318206891768080)
XLA Ops:
  0.0 0.0 copy-start.11
  0.0 2.9 %collective-permute-start = (bf16[256,512]{1,0:T(8,128)(2,1)}, bf16[256,512]{1,0:T(8,128)(2,1)}, u32[]{:S(2)}, u32[]{:S(2)}) collective-permute-start(bf16[256,512]{1,0:T(8,128)(2,1)} %bitcast.18), channel_id=1, source_target_pairs={{28,0},{5,1},{30,2},{7,3},{0,4},{9,5},{2,6},{11,7},{4,8},{13,9},{6... | collective-permute-start | bytes 786440 | tf_op jit(solution)/shard_map/ppermute | solution.py:19
  2.9 0.0 copy-start
  2.9 2.0 %copy-done = bf16[3,3,3,128,512]{4,3,2,1,0:T(8,128)(2,1)S(1)} copy-done((bf16[3,3,3,128,512]{4,3,2,1,0:T(8,128)(2,1)S(1)}, bf16[3,3,3,128,512]{4,3,2,1,0:T(8,128)(2,1)}, u32[]{:S(2)}) %copy-start) | copy-done | bytes 3538968
  4.9 0.0 copy-start.5
  4.9 0.9 %copy-done.5 = bf16[1,4,64,512]{3,2,1,0:T(8,128)(2,1)S(1)} copy-done((bf16[1,4,64,512]{3,2,1,0:T(8,128)(2,1)S(1)}, bf16[1,4,64,512]{3,2,1,0:T(8,128)(2,1)}, u32[]{:S(2)}) %copy-start.5) | copy-done | bytes 262168
  5.9 0.0 copy-start.1
  5.9 1.2 %shard_map.55 = (f32[3,256,128]{2,1,0:T(8,128)S(1)}, f32[2,256,128]{2,1,0:T(8,128)S(1)}) custom-call(bf16[256,512]{1,0:T(8,128)(2,1)S(1)} %bitcast.19, bf16[3,1152,512]{2,1,0:T(8,128)(2,1)S(1)} %bitcast.12), custom_call_target="tpu_custom_call" | custom-call | flops 905969664 | bytes 4456448 | tf_op jit(solution)/shard_map/pallas_call | solution.py:130
  7.1 0.0 copy-start.3
  7.1 0.7 %copy-done.3 = f32[3,256,128]{2,1,0:T(8,128)} copy-done((f32[3,256,128]{2,1,0:T(8,128)}, f32[3,256,128]{2,1,0:T(8,128)S(1)}, u32[]{:S(2)}) %copy-start.3) | copy-done | bytes 393240
  7.9 0.0 copy-start.10
  7.9 3.7 %collective-permute-start.2 = (f32[256,128]{1,0:T(8,128)S(1)}, f32[256,128]{1,0:T(8,128)S(1)}, u32[]{:S(2)}, u32[]{:S(2)}) collective-permute-start(f32[256,128]{1,0:T(8,128)S(1)} %get-tuple-element.15), channel_id=1, source_target_pairs={{8,0},{9,1},{10,2},{11,3},{12,4},{13,5},{14,6},{15,7},{16,8},{17,9... | collective-permute-start | bytes 393224 | tf_op jit(solution)/shard_map/ppermute | solution.py:19
  11.6 0.0 collective-permute-start.1
  11.6 3.8 %collective-permute-done.2.above_ref = f32[256,128]{1,0:T(8,128)S(1)} collective-permute-done((f32[256,128]{1,0:T(8,128)S(1)}, f32[256,128]{1,0:T(8,128)S(1)}, u32[]{:S(2)}, u32[]{:S(2)}) %collective-permute-start.2) | collective-permute-done | bytes 131104 | tf_op jit(solution)/shard_map/ppermute | solution.py:19
  15.3 0.0 copy-start.6
  15.3 0.7 %copy-done.6 = f32[256,128]{1,0:T(8,128)} copy-done((f32[256,128]{1,0:T(8,128)}, f32[256,128]{1,0:T(8,128)S(1)}, u32[]{:S(2)}) %copy-start.6) | copy-done | bytes 131096
  16.0 2.3 %collective-permute-done.1.below_ref = f32[256,128]{1,0:T(8,128)S(1)} collective-permute-done((f32[256,128]{1,0:T(8,128)S(1)}, f32[256,128]{1,0:T(8,128)S(1)}, u32[]{:S(2)}, u32[]{:S(2)}) %collective-permute-start.1) | collective-permute-done | bytes 131104 | tf_op jit(solution)/shard_map/ppermute | solution.py:19
  18.3 0.0 copy-start.8
  18.3 0.6 %copy-done.8 = f32[256,128]{1,0:T(8,128)} copy-done((f32[256,128]{1,0:T(8,128)}, f32[256,128]{1,0:T(8,128)S(1)}, u32[]{:S(2)}) %copy-start.8) | copy-done | bytes 131096
  19.0 0.0 collective-permute-done.near_ref
  19.0 0.0 collective-permute-start.3
  19.0 0.0 copy-start.2
  19.0 1.9 %collective-permute-done.3.their_near_ref = bf16[256,512]{1,0:T(8,128)(2,1)} collective-permute-done((bf16[256,512]{1,0:T(8,128)(2,1)}, bf16[256,512]{1,0:T(8,128)(2,1)}, u32[]{:S(2)}, u32[]{:S(2)}) %collective-permute-start.3) | collective-permute-done | bytes 262176 | tf_op jit(solution)/shard_map/ppermute | solution.py:19
  20.8 0.0 copy-done.11
  20.8 0.0 copy-done.1
  20.8 0.0 copy-start.4
  20.8 1.0 %copy-done.4 = f32[3,256,128]{2,1,0:T(8,128)S(1)} copy-done((f32[3,256,128]{2,1,0:T(8,128)S(1)}, f32[3,256,128]{2,1,0:T(8,128)}, u32[]{:S(2)}) %copy-start.4) | copy-done | bytes 393240
  21.8 0.0 copy-start.7
  21.8 0.9 %copy-done.7 = f32[256,128]{1,0:T(8,128)S(1)} copy-done((f32[256,128]{1,0:T(8,128)S(1)}, f32[256,128]{1,0:T(8,128)}, u32[]{:S(2)}) %copy-start.7) | copy-done | bytes 131096
  22.7 0.0 copy-start.9
  22.7 0.9 %copy-done.9 = f32[256,128]{1,0:T(8,128)S(1)} copy-done((f32[256,128]{1,0:T(8,128)S(1)}, f32[256,128]{1,0:T(8,128)}, u32[]{:S(2)}) %copy-start.9) | copy-done | bytes 131096
  23.6 2.6 %shard_map.56 = bf16[3,256,128]{2,1,0:T(8,128)(2,1)S(1)} custom-call(s32[1]{0:T(128)} %bitcast.1.odd_ref, bf16[256,512]{1,0:T(8,128)(2,1)} %collective-permute-done.near_ref, bf16[256,512]{1,0:T(8,128)(2,1)} %collective-permute-done.3.their_near_ref, f32[256,128]{1,0:T(8,128)S(1)} %copy-done.9, f32[256,128]{1,0:T(8,128)S(1)} %copy-done.7, ...), custom_call_target="tpu_custom_call" | custom-call | flops 1207959552 | bytes 4915716 | tf_op jit(solution)/shard_map/pallas_call | solution.py:130
  26.3 1.6 %collective-permute-start.4 = (bf16[1,3,256,128]{3,2,1,0:T(8,128)(2,1)S(1)}, bf16[1,3,256,128]{3,2,1,0:T(8,128)(2,1)S(1)}, u32[]{:S(2)}, u32[]{:S(2)}) collective-permute-start(bf16[1,3,256,128]{3,2,1,0:T(8,128)(2,1)S(1)} %bitcast.15), channel_id=1, source_target_pairs={{2,0},{3,1},{0,2},{1,3},{6,4},{7,5},{4,6},{5,7},{10,8},{11,9},{8,1... | collective-permute-start | bytes 589832 | tf_op jit(solution)/shard_map/ppermute | solution.py:19
  27.8 5.4 %collective-permute-done.4.refs_1_ = bf16[1,3,256,128]{3,2,1,0:T(8,128)(2,1)S(1)} collective-permute-done((bf16[1,3,256,128]{3,2,1,0:T(8,128)(2,1)S(1)}, bf16[1,3,256,128]{3,2,1,0:T(8,128)(2,1)S(1)}, u32[]{:S(2)}, u32[]{:S(2)}) %collective-permute-start.4) | collective-permute-done | bytes 196640 | tf_op jit(solution)/shard_map/ppermute | solution.py:19
  33.3 0.1 collective-permute-start.5
  33.4 1.7 %collective-permute-done.5.refs_2_ = bf16[2,3,256,128]{3,2,1,0:T(8,128)(2,1)S(1)} collective-permute-done((bf16[2,3,256,128]{3,2,1,0:T(8,128)(2,1)S(1)}, bf16[2,3,256,128]{3,2,1,0:T(8,128)(2,1)S(1)}, u32[]{:S(2)}, u32[]{:S(2)}) %collective-permute-start.5) | collective-permute-done | bytes 393248 | tf_op jit(solution)/shard_map/ppermute | solution.py:19
  35.1 0.0 copy-done.10
  35.1 0.0 copy-done.2
  35.1 2.0 %shard_map.57 = bf16[1,128,256]{2,1,0:T(8,128)(2,1)} custom-call(s32[1]{0:T(128)} %bitcast.me_ref, bf16[1,3,256,128]{3,2,1,0:T(8,128)(2,1)S(1)} %bitcast.17, bf16[1,3,256,128]{3,2,1,0:T(8,128)(2,1)S(1)} %collective-permute-done.4.refs_1_, bf16[2,3,256,128]{3,2,1,0:T(8,128)(2,1)S(1)} %collective-permute-done.5.refs_2_, bf16[3,1152,512]{2,1,0:T(8,128)(2,1)S(1)} %bitcast.14, ...), custom_call_target="tpu_custom_call" | custom-call | flops 905969664 | bytes 4391428 | tf_op jit(solution)/shard_map/pallas_call | solution.py:130
  (2 shorter events, 0.1 us)
Async XLA Ops:
  0.0 20.8 %copy-start.11 = (f32[128]{0:T(128)S(1)}, f32[128]{0:T(128)}, u32[]{:S(2)}) copy-start(f32[128]{0:T(128)} %param.7) | copy-start | bytes 1540
  0.0 19.0 %collective-permute-start = (bf16[256,512]{1,0:T(8,128)(2,1)}, bf16[256,512]{1,0:T(8,128)(2,1)}, u32[]{:S(2)}, u32[]{:S(2)}) collective-permute-start(bf16[256,512]{1,0:T(8,128)(2,1)} %bitcast.18), channel_id=1, source_target_pairs={{28,0},{5,1},{30,2},{7,3},{0,4},{9,5},{2,6},{11,7},{4,8},{13,9},{6... | collective-permute-start | bytes 786440 | tf_op jit(solution)/shard_map/ppermute | solution.py:19
  2.9 2.0 %copy-start = (bf16[3,3,3,128,512]{4,3,2,1,0:T(8,128)(2,1)S(1)}, bf16[3,3,3,128,512]{4,3,2,1,0:T(8,128)(2,1)}, u32[]{:S(2)}) copy-start(bf16[3,3,3,128,512]{4,3,2,1,0:T(8,128)(2,1)} %param.6) | copy-start | bytes 10616836
  4.9 0.9 %copy-start.5 = (bf16[1,4,64,512]{3,2,1,0:T(8,128)(2,1)S(1)}, bf16[1,4,64,512]{3,2,1,0:T(8,128)(2,1)}, u32[]{:S(2)}) copy-start(bf16[1,4,64,512]{3,2,1,0:T(8,128)(2,1)} %param.5) | copy-start | bytes 786436
  5.9 14.9 %copy-start.1 = (bf16[3,3,3,128,512]{4,3,2,1,0:T(8,128)(2,1)S(1)}, bf16[3,3,3,128,512]{4,3,2,1,0:T(8,128)(2,1)}, u32[]{:S(2)}) copy-start(bf16[3,3,3,128,512]{4,3,2,1,0:T(8,128)(2,1)} %param.6) | copy-start | bytes 10616836
  7.1 0.7 %copy-start.3 = (f32[3,256,128]{2,1,0:T(8,128)}, f32[3,256,128]{2,1,0:T(8,128)S(1)}, u32[]{:S(2)}) copy-start(f32[3,256,128]{2,1,0:T(8,128)S(1)} %get-tuple-element.14.part_ref) | copy-start | bytes 1179652
  7.9 27.2 %copy-start.10 = (f32[128]{0:T(128)S(1)}, f32[128]{0:T(128)}, u32[]{:S(2)}) copy-start(f32[128]{0:T(128)} %param.9) | copy-start | bytes 1540
  7.9 7.4 %collective-permute-start.2 = (f32[256,128]{1,0:T(8,128)S(1)}, f32[256,128]{1,0:T(8,128)S(1)}, u32[]{:S(2)}, u32[]{:S(2)}) collective-permute-start(f32[256,128]{1,0:T(8,128)S(1)} %get-tuple-element.15), channel_id=1, source_target_pairs={{8,0},{9,1},{10,2},{11,3},{12,4},{13,5},{14,6},{15,7},{16,8},{17,9... | collective-permute-start | bytes 393224 | tf_op jit(solution)/shard_map/ppermute | solution.py:19
  11.6 6.8 %collective-permute-start.1 = (f32[256,128]{1,0:T(8,128)S(1)}, f32[256,128]{1,0:T(8,128)S(1)}, u32[]{:S(2)}, u32[]{:S(2)}) collective-permute-start(f32[256,128]{1,0:T(8,128)S(1)} %get-tuple-element.16), channel_id=1, source_target_pairs={{24,0},{25,1},{26,2},{27,3},{28,4},{29,5},{30,6},{31,7},{0,8},{1,9... | collective-permute-start | bytes 393224 | tf_op jit(solution)/shard_map/ppermute | solution.py:19
  15.3 0.7 %copy-start.6 = (f32[256,128]{1,0:T(8,128)}, f32[256,128]{1,0:T(8,128)S(1)}, u32[]{:S(2)}) copy-start(f32[256,128]{1,0:T(8,128)S(1)} %collective-permute-done.2.above_ref) | copy-start | bytes 393220
  18.3 0.6 %copy-start.8 = (f32[256,128]{1,0:T(8,128)}, f32[256,128]{1,0:T(8,128)S(1)}, u32[]{:S(2)}) copy-start(f32[256,128]{1,0:T(8,128)S(1)} %collective-permute-done.1.below_ref) | copy-start | bytes 393220
  19.0 1.9 %collective-permute-start.3 = (bf16[256,512]{1,0:T(8,128)(2,1)}, bf16[256,512]{1,0:T(8,128)(2,1)}, u32[]{:S(2)}, u32[]{:S(2)}) collective-permute-start(bf16[256,512]{1,0:T(8,128)(2,1)} %collective-permute-done.near_ref), channel_id=1, source_target_pairs={{1,0},{0,1},{3,2},{2,3},{5,4},{4,5},{7,6},{6,7},{9,8},{8,9},{11,10... | collective-permute-start | bytes 786440 | tf_op jit(solution)/shard_map/ppermute | solution.py:19
  19.0 16.1 %copy-start.2 = (bf16[3,3,3,128,512]{4,3,2,1,0:T(8,128)(2,1)S(1)}, bf16[3,3,3,128,512]{4,3,2,1,0:T(8,128)(2,1)}, u32[]{:S(2)}) copy-start(bf16[3,3,3,128,512]{4,3,2,1,0:T(8,128)(2,1)} %param.8) | copy-start | bytes 10616836
  20.8 1.0 %copy-start.4 = (f32[3,256,128]{2,1,0:T(8,128)S(1)}, f32[3,256,128]{2,1,0:T(8,128)}, u32[]{:S(2)}) copy-start(f32[3,256,128]{2,1,0:T(8,128)} %copy-done.3) | copy-start | bytes 1179652
  21.8 0.9 %copy-start.7 = (f32[256,128]{1,0:T(8,128)S(1)}, f32[256,128]{1,0:T(8,128)}, u32[]{:S(2)}) copy-start(f32[256,128]{1,0:T(8,128)} %copy-done.6) | copy-start | bytes 393220
  22.7 0.9 %copy-start.9 = (f32[256,128]{1,0:T(8,128)S(1)}, f32[256,128]{1,0:T(8,128)}, u32[]{:S(2)}) copy-start(f32[256,128]{1,0:T(8,128)} %copy-done.8) | copy-start | bytes 393220
  26.3 7.0 %collective-permute-start.4 = (bf16[1,3,256,128]{3,2,1,0:T(8,128)(2,1)S(1)}, bf16[1,3,256,128]{3,2,1,0:T(8,128)(2,1)S(1)}, u32[]{:S(2)}, u32[]{:S(2)}) collective-permute-start(bf16[1,3,256,128]{3,2,1,0:T(8,128)(2,1)S(1)} %bitcast.15), channel_id=1, source_target_pairs={{2,0},{3,1},{0,2},{1,3},{6,4},{7,5},{4,6},{5,7},{10,8},{11,9},{8,1... | collective-permute-start | bytes 589832 | tf_op jit(solution)/shard_map/ppermute | solution.py:19
  33.3 1.8 %collective-permute-start.5 = (bf16[2,3,256,128]{3,2,1,0:T(8,128)(2,1)S(1)}, bf16[2,3,256,128]{3,2,1,0:T(8,128)(2,1)S(1)}, u32[]{:S(2)}, u32[]{:S(2)}) collective-permute-start(bf16[2,3,256,128]{3,2,1,0:T(8,128)(2,1)S(1)} %pad_maximum_fusion), channel_id=1, source_target_pairs={{1,0},{0,1},{3,2},{2,3},{5,4},{4,5},{7,6},{6,7},{9,8},{8,9},{11,10... | collective-permute-start | bytes 1179656 | tf_op jit(solution)/shard_map/ppermute | solution.py:19

commit v12 on v5

--- a/solution.py
+++ b/solution.py
@@ -71,21 +71,46 @@
         o_ref[plane] = spatial_sum(acc_ref, plane, rows_n, cols_n, outs)
 
 
-def neighbour_kernel(rows_n, cols_n, odd_ref, near_ref, far_ref, their_near_ref, their_far_ref, part_ref,
+def side_products(acc_ref, first_ref, second_ref, w_ref, minus):
+    if minus:
+        acc_ref[0] = tap_product(second_ref[...], w_ref, 0)
+        acc_ref[0] += tap_product(first_ref[...], w_ref, 1)
+        acc_ref[1] = tap_product(first_ref[...], w_ref, 0)
+        return (0, 1)
+    acc_ref[1] = tap_product(first_ref[...], w_ref, 2)
+    acc_ref[2] = tap_product(first_ref[...], w_ref, 1)
+    acc_ref[2] += tap_product(second_ref[...], w_ref, 2)
+    return (1, 2)
+
+
+def fetched_side_kernel(rows_n, cols_n, odd_ref, near_ref, far_ref, w_ref, o_ref, acc_ref):
+    outs = o_ref.shape[2]
+    for minus in (True, False):
+
+        @pl.when((odd_ref[0] == 0) == minus)
+        def _():
+            touched = side_products(acc_ref, near_ref, far_ref, w_ref, minus)
+            for plane in range(3):
+                if plane in touched:
+                    o_ref[plane] = spatial_sum(acc_ref, plane, rows_n, cols_n, outs)
+                else:
+                    o_ref[plane] = jnp.zeros(o_ref.shape[1:], o_ref.dtype)
+
+
+def neighbour_kernel(rows_n, cols_n, odd_ref, their_near_ref, their_far_ref, fetched_ref, part_ref,
                      w_ref, b_ref, o_ref, acc_ref):
     outs = o_ref.shape[2]
-    is_odd = odd_ref[0] != 0
-    minus_one = jnp.where(is_odd, their_near_ref[...], near_ref[...])
-    minus_two = jnp.where(is_odd, their_far_ref[...], far_ref[...])
-    plus_one = jnp.where(is_odd, near_ref[...], their_near_ref[...])
-    plus_two = jnp.where(is_odd, far_ref[...], their_far_ref[...])
-    acc_ref[0] = tap_product(minus_two, w_ref, 0) + tap_product(minus_one, w_ref, 1)
-    acc_ref[1] = tap_product(minus_one, w_ref, 0) + tap_product(plus_one, w_ref, 2)
-    acc_ref[2] = tap_product(plus_one, w_ref, 1) + tap_product(plus_two, w_ref, 2)
     bias = b_ref[...]
-    for plane in range(3):
-        total = spatial_sum(acc_ref, plane, rows_n, cols_n, outs) + part_ref[plane]
-        o_ref[plane] = jnp.maximum(total + bias, 0.0).astype(o_ref.dtype)
+    for minus in (True, False):
+
+        @pl.when((odd_ref[0] != 0) == minus)
+        def _():
+            touched = side_products(acc_ref, their_near_ref, their_far_ref, w_ref, minus)
+            for plane in range(3):
+                total = fetched_ref[plane] + part_ref[plane]
+                if plane in touched:
+                    total = total + spatial_sum(acc_ref, plane, rows_n, cols_n, outs)
+                o_ref[plane] = jnp.maximum(total + bias, 0.0).astype(o_ref.dtype)
 
 
 def second_kernel(rows_n, cols_n, layout, me_ref, *refs):
@@ -155,12 +180,20 @@
     near, far, own_terms = lax.optimization_barrier((near, far, own_terms))
     their_near, their_far = from_chan_partner(near, 1), from_chan_partner(far, 1)
     odd = (me % 2).astype(jnp.int32).reshape(1)
+    fetched_terms = vmem_call(
+        functools.partial(fetched_side_kernel, rows_n, cols_n),
+        jax.ShapeDtypeStruct((3, cells, outs), jnp.float32),
+        [odd, near, far, one_stack],
+        [pltpu.VMEM((3, cells, 9 * outs), jnp.float32)],
+        3 * tap_flops,
+        smem_first=True,
+    )
     hidden = vmem_call(
         functools.partial(neighbour_kernel, rows_n, cols_n),
         jax.ShapeDtypeStruct((3, cells, outs), jnp.bfloat16),
-        [odd, near, far, their_near, their_far, own_terms, one_stack, bias_one.reshape(1, outs)],
+        [odd, their_near, their_far, fetched_terms, own_terms, one_stack, bias_one.reshape(1, outs)],
         [pltpu.VMEM((3, cells, 9 * outs), jnp.float32)],
-        6 * tap_flops,
+        3 * tap_flops,
         smem_first=True,
     )
 

time: 33.4 us -> 30.7 us (0.919)
  waiting for transfers between devices: 15 us -> 12.1 us
  Pallas kernels: 6.76 us -> 7.91 us
  local copies, waits for them, and re-layouts: 4.7 us -> 3.71 us
    ppermute x6, waiting for transfers between devices: 15 us -> 12.1 us  [gathered_from(): return lax.ppermute(block, ('space', 'chan'), pairs)]
    pallas_call x3 -> x4, Pallas kernels: 6.76 us -> 7.91 us  [vmem_call(): pl.pallas_call(kernel, out_shape=out_shape, in_specs=specs, out_specs=pl....]
    unnamed x16, local copies, waits for them, and re-layouts: 4.7 us -> 3.71 us
  transfers between devices with their start and end apart: 6 -> 6, of which waited for: 6 -> 4; matrix products, arithmetic and copies ran while one was open for 0% -> 0% of each run, Pallas kernels for 4% -> 12%
where the time goes in v12:
time: 30.7 us; the launch traced here: 30.5 us
  waiting for transfers between devices  12.1 us (39%)
  Pallas kernels  7.91 us (26%)
  starting transfers between devices  6.68 us (22%)
  local copies, waits for them, and re-layouts  3.71 us (12%)
    ppermute x6, waiting for transfers between devices, gathered_from(): return lax.ppermute(block, ('space', 'chan'), pairs)  12.1 us
    pallas_call x4, Pallas kernels, vmem_call(): pl.pallas_call(kernel, out_shape=out_shape, in_specs=specs, out_specs=pl....  7.91 us
    ppermute x6, starting transfers between devices, gathered_from(): return lax.ppermute(block, ('space', 'chan'), pairs)  6.68 us
    unnamed x16, local copies, waits for them, and re-layouts  3.71 us
  transfers between devices with their start and end apart: 6, of which 4 were waited for; matrix products, arithmetic and copies ran while one was open for 0% of the time, Pallas kernels for 12%

profile of v12, /device:TPU:0, one launch (start us, length us, event | category | flops | bytes accessed | tf_op | source)
XLA Modules:
  0.0 30.5 jit_solution(12919413424772147369)
XLA Ops:
  0.0 2.9 %collective-permute-start = (bf16[256,512]{1,0:T(8,128)(2,1)}, bf16[256,512]{1,0:T(8,128)(2,1)}, u32[]{:S(2)}, u32[]{:S(2)}) collective-permute-start(bf16[256,512]{1,0:T(8,128)(2,1)} %bitcast.15), channel_id=1, source_target_pairs={{28,0},{5,1},{30,2},{7,3},{0,4},{9,5},{2,6},{11,7},{4,8},{13,9},{6... | collective-permute-start | bytes 786440 | tf_op jit(solution)/shard_map/ppermute | solution.py:19
  2.9 1.6 %collective-permute-start.1 = (bf16[256,512]{1,0:T(8,128)(2,1)}, bf16[256,512]{1,0:T(8,128)(2,1)}, u32[]{:S(2)}, u32[]{:S(2)}) collective-permute-start(bf16[256,512]{1,0:T(8,128)(2,1)} %bitcast.16), channel_id=1, source_target_pairs={{24,0},{9,1},{26,2},{11,3},{28,4},{13,5},{30,6},{15,7},{0,8},{17,9... | collective-permute-start | bytes 786440 | tf_op jit(solution)/shard_map/ppermute | solution.py:19
  4.5 0.0 copy-start
  4.5 2.0 %copy-done = bf16[3,3,3,128,512]{4,3,2,1,0:T(8,128)(2,1)S(1)} copy-done((bf16[3,3,3,128,512]{4,3,2,1,0:T(8,128)(2,1)S(1)}, bf16[3,3,3,128,512]{4,3,2,1,0:T(8,128)(2,1)}, u32[]{:S(2)}) %copy-start) | copy-done | bytes 3538968
  6.5 0.0 copy-start.5
  6.5 0.9 %copy-done.5 = bf16[1,4,64,512]{3,2,1,0:T(8,128)(2,1)S(1)} copy-done((bf16[1,4,64,512]{3,2,1,0:T(8,128)(2,1)S(1)}, bf16[1,4,64,512]{3,2,1,0:T(8,128)(2,1)}, u32[]{:S(2)}) %copy-start.5) | copy-done | bytes 262168
  7.5 0.0 copy-start.1
  7.5 0.0 copy-start.6
  7.5 1.2 %shard_map.55.part_ref = f32[3,256,128]{2,1,0:T(8,128)S(1)} custom-call(bf16[256,512]{1,0:T(8,128)(2,1)S(1)} %bitcast.17, bf16[3,1152,512]{2,1,0:T(8,128)(2,1)S(1)} %bitcast.8), custom_call_target="tpu_custom_call" | custom-call | flops 905969664 | bytes 4194304 | tf_op jit(solution)/shard_map/pallas_call | solution.py:149
  8.7 0.0 copy-start.3
  8.7 0.7 %copy-done.3 = f32[3,256,128]{2,1,0:T(8,128)} copy-done((f32[3,256,128]{2,1,0:T(8,128)}, f32[3,256,128]{2,1,0:T(8,128)S(1)}, u32[]{:S(2)}) %copy-start.3) | copy-done | bytes 393240
  9.4 3.6 %collective-permute-done.near_ref = bf16[256,512]{1,0:T(8,128)(2,1)} collective-permute-done((bf16[256,512]{1,0:T(8,128)(2,1)}, bf16[256,512]{1,0:T(8,128)(2,1)}, u32[]{:S(2)}, u32[]{:S(2)}) %collective-permute-start) | collective-permute-done | bytes 262176 | tf_op jit(solution)/shard_map/ppermute | solution.py:19
  13.0 1.3 %collective-permute-done.1.far_ref = bf16[256,512]{1,0:T(8,128)(2,1)} collective-permute-done((bf16[256,512]{1,0:T(8,128)(2,1)}, bf16[256,512]{1,0:T(8,128)(2,1)}, u32[]{:S(2)}, u32[]{:S(2)}) %collective-permute-start.1) | collective-permute-done | bytes 262176 | tf_op jit(solution)/shard_map/ppermute | solution.py:19
  14.3 0.2 collective-permute-start.2
  14.5 0.3 %collective-permute-start.3 = (bf16[256,512]{1,0:T(8,128)(2,1)}, bf16[256,512]{1,0:T(8,128)(2,1)}, u32[]{:S(2)}, u32[]{:S(2)}) collective-permute-start(bf16[256,512]{1,0:T(8,128)(2,1)} %collective-permute-done.1.far_ref), channel_id=1, source_target_pairs={{1,0},{0,1},{3,2},{2,3},{5,4},{4,5},{7,6},{6,7},{9,8},{8,9},{11,10... | collective-permute-start | bytes 786440 | tf_op jit(solution)/shard_map/ppermute | solution.py:19
  14.8 0.0 copy-start.4
  14.8 0.0 copy-done.1
  14.8 2.3 %shard_map.56.fetched_ref = f32[3,256,128]{2,1,0:T(8,128)S(1)} custom-call(s32[1]{0:T(128)} %bitcast.1.odd_ref, bf16[256,512]{1,0:T(8,128)(2,1)} %collective-permute-done.near_ref, bf16[256,512]{1,0:T(8,128)(2,1)} %collective-permute-done.1.far_ref, bf16[3,1152,512]{2,1,0:T(8,128)(2,1)S(1)} %bitcast.9), custom_call_target="tpu_custom_call" | custom-call | flops 905969664 | bytes 4456452 | tf_op jit(solution)/shard_map/pallas_call | solution.py:149
  17.1 0.0 copy-start.2
  17.1 0.0 copy-start.7
  17.2 0.0 collective-permute-done.2.their_near_ref
  17.2 0.0 collective-permute-done.3.their_far_ref
  17.2 0.0 copy-done.6
  17.2 0.0 copy-done.4
  17.2 2.4 %shard_map.57 = bf16[3,256,128]{2,1,0:T(8,128)(2,1)S(1)} custom-call(s32[1]{0:T(128)} %bitcast.1.odd_ref, bf16[256,512]{1,0:T(8,128)(2,1)} %collective-permute-done.2.their_near_ref, bf16[256,512]{1,0:T(8,128)(2,1)} %collective-permute-done.3.their_far_ref, f32[3,256,128]{2,1,0:T(8,128)S(1)} %shard_map.56.fetched_ref, f32[3,256,128]{2,1,0:T(8,128)S(1)} %copy-done.4, ...), custom_call_target="tpu_custom_call" | custom-call | flops 905969664 | bytes 5046788 | tf_op jit(solution)/shard_map/pallas_call | solution.py:149
  19.6 1.6 %collective-permute-start.4 = (bf16[1,3,256,128]{3,2,1,0:T(8,128)(2,1)S(1)}, bf16[1,3,256,128]{3,2,1,0:T(8,128)(2,1)S(1)}, u32[]{:S(2)}, u32[]{:S(2)}) collective-permute-start(bf16[1,3,256,128]{3,2,1,0:T(8,128)(2,1)S(1)} %bitcast.12), channel_id=1, source_target_pairs={{2,0},{3,1},{0,2},{1,3},{6,4},{7,5},{4,6},{5,7},{10,8},{11,9},{8,1... | collective-permute-start | bytes 589832 | tf_op jit(solution)/shard_map/ppermute | solution.py:19
  21.2 5.5 %collective-permute-done.4.refs_1_ = bf16[1,3,256,128]{3,2,1,0:T(8,128)(2,1)S(1)} collective-permute-done((bf16[1,3,256,128]{3,2,1,0:T(8,128)(2,1)S(1)}, bf16[1,3,256,128]{3,2,1,0:T(8,128)(2,1)S(1)}, u32[]{:S(2)}, u32[]{:S(2)}) %collective-permute-start.4) | collective-permute-done | bytes 196640 | tf_op jit(solution)/shard_map/ppermute | solution.py:19
  26.8 0.1 collective-permute-start.5
  26.8 1.7 %collective-permute-done.5.refs_2_ = bf16[2,3,256,128]{3,2,1,0:T(8,128)(2,1)S(1)} collective-permute-done((bf16[2,3,256,128]{3,2,1,0:T(8,128)(2,1)S(1)}, bf16[2,3,256,128]{3,2,1,0:T(8,128)(2,1)S(1)}, u32[]{:S(2)}, u32[]{:S(2)}) %collective-permute-start.5) | collective-permute-done | bytes 393248 | tf_op jit(solution)/shard_map/ppermute | solution.py:19
  28.5 0.0 copy-done.2
  28.5 0.0 copy-done.7
  28.5 2.0 %shard_map.58 = bf16[1,128,256]{2,1,0:T(8,128)(2,1)} custom-call(s32[1]{0:T(128)} %bitcast.me_ref, bf16[1,3,256,128]{3,2,1,0:T(8,128)(2,1)S(1)} %bitcast.14, bf16[1,3,256,128]{3,2,1,0:T(8,128)(2,1)S(1)} %collective-permute-done.4.refs_1_, bf16[2,3,256,128]{3,2,1,0:T(8,128)(2,1)S(1)} %collective-permute-done.5.refs_2_, bf16[3,1152,512]{2,1,0:T(8,128)(2,1)S(1)} %bitcast.11, ...), custom_call_target="tpu_custom_call" | custom-call | flops 905969664 | bytes 4391428 | tf_op jit(solution)/shard_map/pallas_call | solution.py:149
  (1 shorter events, 0.0 us)
Async XLA Ops:
  0.0 13.0 %collective-permute-start = (bf16[256,512]{1,0:T(8,128)(2,1)}, bf16[256,512]{1,0:T(8,128)(2,1)}, u32[]{:S(2)}, u32[]{:S(2)}) collective-permute-start(bf16[256,512]{1,0:T(8,128)(2,1)} %bitcast.15), channel_id=1, source_target_pairs={{28,0},{5,1},{30,2},{7,3},{0,4},{9,5},{2,6},{11,7},{4,8},{13,9},{6... | collective-permute-start | bytes 786440 | tf_op jit(solution)/shard_map/ppermute | solution.py:19
  2.9 11.4 %collective-permute-start.1 = (bf16[256,512]{1,0:T(8,128)(2,1)}, bf16[256,512]{1,0:T(8,128)(2,1)}, u32[]{:S(2)}, u32[]{:S(2)}) collective-permute-start(bf16[256,512]{1,0:T(8,128)(2,1)} %bitcast.16), channel_id=1, source_target_pairs={{24,0},{9,1},{26,2},{11,3},{28,4},{13,5},{30,6},{15,7},{0,8},{17,9... | collective-permute-start | bytes 786440 | tf_op jit(solution)/shard_map/ppermute | solution.py:19
  4.5 2.0 %copy-start = (bf16[3,3,3,128,512]{4,3,2,1,0:T(8,128)(2,1)S(1)}, bf16[3,3,3,128,512]{4,3,2,1,0:T(8,128)(2,1)}, u32[]{:S(2)}) copy-start(bf16[3,3,3,128,512]{4,3,2,1,0:T(8,128)(2,1)} %param.6) | copy-start | bytes 10616836
  6.5 0.9 %copy-start.5 = (bf16[1,4,64,512]{3,2,1,0:T(8,128)(2,1)S(1)}, bf16[1,4,64,512]{3,2,1,0:T(8,128)(2,1)}, u32[]{:S(2)}) copy-start(bf16[1,4,64,512]{3,2,1,0:T(8,128)(2,1)} %param.5) | copy-start | bytes 786436
  7.5 7.3 %copy-start.1 = (bf16[3,3,3,128,512]{4,3,2,1,0:T(8,128)(2,1)S(1)}, bf16[3,3,3,128,512]{4,3,2,1,0:T(8,128)(2,1)}, u32[]{:S(2)}) copy-start(bf16[3,3,3,128,512]{4,3,2,1,0:T(8,128)(2,1)} %param.6) | copy-start | bytes 10616836
  7.5 9.7 %copy-start.6 = (f32[128]{0:T(128)S(1)}, f32[128]{0:T(128)}, u32[]{:S(2)}) copy-start(f32[128]{0:T(128)} %param.7) | copy-start | bytes 1540
  8.7 0.7 %copy-start.3 = (f32[3,256,128]{2,1,0:T(8,128)}, f32[3,256,128]{2,1,0:T(8,128)S(1)}, u32[]{:S(2)}) copy-start(f32[3,256,128]{2,1,0:T(8,128)S(1)} %shard_map.55.part_ref) | copy-start | bytes 1179652
  14.3 2.9 %collective-permute-start.2 = (bf16[256,512]{1,0:T(8,128)(2,1)}, bf16[256,512]{1,0:T(8,128)(2,1)}, u32[]{:S(2)}, u32[]{:S(2)}) collective-permute-start(bf16[256,512]{1,0:T(8,128)(2,1)} %collective-permute-done.near_ref), channel_id=1, source_target_pairs={{1,0},{0,1},{3,2},{2,3},{5,4},{4,5},{7,6},{6,7},{9,8},{8,9},{11,10... | collective-permute-start | bytes 786440 | tf_op jit(solution)/shard_map/ppermute | solution.py:19
  14.5 2.7 %collective-permute-start.3 = (bf16[256,512]{1,0:T(8,128)(2,1)}, bf16[256,512]{1,0:T(8,128)(2,1)}, u32[]{:S(2)}, u32[]{:S(2)}) collective-permute-start(bf16[256,512]{1,0:T(8,128)(2,1)} %collective-permute-done.1.far_ref), channel_id=1, source_target_pairs={{1,0},{0,1},{3,2},{2,3},{5,4},{4,5},{7,6},{6,7},{9,8},{8,9},{11,10... | collective-permute-start | bytes 786440 | tf_op jit(solution)/shard_map/ppermute | solution.py:19
  14.8 2.4 %copy-start.4 = (f32[3,256,128]{2,1,0:T(8,128)S(1)}, f32[3,256,128]{2,1,0:T(8,128)}, u32[]{:S(2)}) copy-start(f32[3,256,128]{2,1,0:T(8,128)} %copy-done.3) | copy-start | bytes 1179652
  17.1 11.4 %copy-start.2 = (bf16[3,3,3,128,512]{4,3,2,1,0:T(8,128)(2,1)S(1)}, bf16[3,3,3,128,512]{4,3,2,1,0:T(8,128)(2,1)}, u32[]{:S(2)}) copy-start(bf16[3,3,3,128,512]{4,3,2,1,0:T(8,128)(2,1)} %param.8) | copy-start | bytes 10616836
  17.1 11.4 %copy-start.7 = (f32[128]{0:T(128)S(1)}, f32[128]{0:T(128)}, u32[]{:S(2)}) copy-start(f32[128]{0:T(128)} %param.9) | copy-start | bytes 1540
  19.6 7.1 %collective-permute-start.4 = (bf16[1,3,256,128]{3,2,1,0:T(8,128)(2,1)S(1)}, bf16[1,3,256,128]{3,2,1,0:T(8,128)(2,1)S(1)}, u32[]{:S(2)}, u32[]{:S(2)}) collective-permute-start(bf16[1,3,256,128]{3,2,1,0:T(8,128)(2,1)S(1)} %bitcast.12), channel_id=1, source_target_pairs={{2,0},{3,1},{0,2},{1,3},{6,4},{7,5},{4,6},{5,7},{10,8},{11,9},{8,1... | collective-permute-start | bytes 589832 | tf_op jit(solution)/shard_map/ppermute | solution.py:19
  26.8 1.8 %collective-permute-start.5 = (bf16[2,3,256,128]{3,2,1,0:T(8,128)(2,1)S(1)}, bf16[2,3,256,128]{3,2,1,0:T(8,128)(2,1)S(1)}, u32[]{:S(2)}, u32[]{:S(2)}) collective-permute-start(bf16[2,3,256,128]{3,2,1,0:T(8,128)(2,1)S(1)} %pad_maximum_fusion), channel_id=1, source_target_pairs={{1,0},{0,1},{3,2},{2,3},{5,4},{4,5},{7,6},{6,7},{9,8},{8,9},{11,10... | collective-permute-start | bytes 1179656 | tf_op jit(solution)/shard_map/ppermute | solution.py:19

commit v13 on v12

--- a/solution.py
+++ b/solution.py
@@ -113,30 +113,61 @@
                 o_ref[plane] = jnp.maximum(total + bias, 0.0).astype(o_ref.dtype)
 
 
-def second_kernel(rows_n, cols_n, layout, me_ref, *refs):
-    inputs = refs[:len(layout)]
-    w_ref, b_ref, o_ref, field_ref, acc_ref = refs[len(layout):]
-    outs = b_ref.shape[1]
-    me = me_ref[0]
+def pair_products(acc_ref, blocks, me, pairs, w_ref, field_ref, outs, first):
+    width = 2 * outs
+    chans = len(blocks)
+    for index in range(chans):
+
+        @pl.when(me == index)
+        def _():
+            started = not first
+            for pair in pairs(index):
+                for half in range(2):
+                    ref, position = blocks[index ^ (2 * pair + half)]
+                    field_ref[:, :, pl.ds(half * outs, outs)] = ref[position]
+                for depth_tap in range(3):
+                    term = lax.dot_general(
+                        field_ref[depth_tap], w_ref[depth_tap, :, pl.ds(pair * width, width)],
+                        (((1,), (1,)), ((), ())), preferred_element_type=jnp.float32,
+                    )
+                    if started:
+                        acc_ref[0] += term
+                    else:
+                        acc_ref[0] = term
+                        started = True
+
+
+def held_blocks(inputs, layout):
     blocks = {}
     for ref, offsets in zip(inputs, layout):
         for position, j in enumerate(offsets):
-            blocks[j] = ref[position]
-    count = len(blocks)
-    ordered = [blocks[j] for j in range(count)]
-    bit = 1
-    while bit < count:
-        flip = (me & bit) != 0
-        ordered = [jnp.where(flip, ordered[j ^ bit], ordered[j]) for j in range(count)]
-        bit *= 2
-    for position in range(count):
-        field_ref[:, :, pl.ds(position * outs, outs)] = ordered[position]
-    products = None
-    for depth_tap in range(3):
-        term = tap_product(field_ref[depth_tap], w_ref, depth_tap)
-        products = term if products is None else products + term
-    acc_ref[0] = products
-    total = spatial_sum(acc_ref, 0, rows_n, cols_n, outs)
+            blocks[j] = (ref, position)
+    return blocks
+
+
+def own_pair_kernel(rows_n, cols_n, count, layout, me_ref, *refs):
+    inputs = refs[:len(layout)]
+    w_ref, o_ref, field_ref, acc_ref = refs[len(layout):]
+    outs = o_ref.shape[2]
+    me = me_ref[0]
+    blocks = held_blocks(inputs, layout)
+    full = {j: None for j in range(count)}
+    full.update(blocks)
+    pair_products(acc_ref, full, me, lambda index: [index // 2], w_ref, field_ref, outs, True)
+    o_ref[0] = spatial_sum(acc_ref, 0, rows_n, cols_n, outs)
+
+
+def second_kernel(rows_n, cols_n, count, layout, me_ref, *refs):
+    inputs = refs[:len(layout)]
+    part_ref, w_ref, b_ref, o_ref, field_ref, acc_ref = refs[len(layout):]
+    outs = b_ref.shape[1]
+    me = me_ref[0]
+    blocks = held_blocks(inputs, layout)
+    full = {j: None for j in range(count)}
+    full.update(blocks)
+    pairs = lambda index: [pair for pair in range(count // 2) if pair != index // 2]
+    pair_products(acc_ref, full, me, pairs, w_ref, field_ref, outs, True)
+    total = spatial_sum(acc_ref, 0, rows_n, cols_n, outs) + part_ref[0]
     result = jnp.maximum(total + b_ref[...], 0.0)
     o_ref[0] = result.T.astype(o_ref.dtype)
 
@@ -197,26 +228,38 @@
         smem_first=True,
     )
 
-    held = [(hidden[None], (0,))]
+    partner = from_chan_partner(hidden, 1)
+    remote = [(hidden[None], (0,))]
     offsets = [0]
-    bit = 1
+    bit = 2
     while bit < chans:
+        sent = jnp.stack([arr[i] for arr, offs in remote for i in range(len(offs))])
+        got = from_chan_partner(sent, bit)
+        remote.append((got, tuple(j ^ bit for j in offsets)))
+        offsets = offsets + [j ^ bit for j in offsets]
         bit *= 2
-    bit //= 2
-    while bit >= 1:
-        sent = jnp.stack([arr[i] for arr, offs in held for i in range(len(offs))])
-        got = from_chan_partner(sent, bit)
-        held.append((got, tuple(j ^ bit for j in offsets)))
-        offsets = offsets + [j ^ bit for j in offsets]
-        bit //= 2
+    me_flag = me.astype(jnp.int32).reshape(1)
+    own_pair = vmem_call(
+        functools.partial(own_pair_kernel, rows_n, cols_n, chans, ((0,), (1,))),
+        jax.ShapeDtypeStruct((1, cells, outs), jnp.float32),
+        [me_flag, hidden[None], partner[None], two_stack],
+        [pltpu.VMEM((3, cells, 2 * outs), jnp.bfloat16), pltpu.VMEM((1, cells, 9 * outs), jnp.float32)],
+        2 * tap_flops // chans,
+        smem_first=True,
+    )
+    received = remote[1:]
+    arrived, own_pair = lax.optimization_barrier(([arr for arr, _ in received], own_pair))
+    received = [(arr, offs) for arr, (_, offs) in zip(arrived, received)]
+    sent = jnp.stack([arr[i] for arr, offs in received for i in range(len(offs))])
+    forwarded = from_chan_partner(sent, 1)
+    held = received + [(forwarded, tuple(j ^ 1 for _, offs in received for j in offs))]
     layout = tuple(offs for _, offs in held)
-    me_flag = me.astype(jnp.int32).reshape(1)
     output = vmem_call(
-        functools.partial(second_kernel, rows_n, cols_n, layout),
+        functools.partial(second_kernel, rows_n, cols_n, chans, layout),
         jax.ShapeDtypeStruct((1, outs, cells), jnp.bfloat16),
-        [me_flag] + [arr for arr, _ in held] + [two_stack, bias_two.reshape(1, outs)],
-        [pltpu.VMEM((3, cells, count_in), jnp.bfloat16), pltpu.VMEM((1, cells, 9 * outs), jnp.float32)],
-        3 * tap_flops,
+        [me_flag] + [arr for arr, _ in held] + [own_pair, two_stack, bias_two.reshape(1, outs)],
+        [pltpu.VMEM((3, cells, 2 * outs), jnp.bfloat16), pltpu.VMEM((1, cells, 9 * outs), jnp.float32)],
+        3 * tap_flops - 2 * tap_flops // chans,
         smem_first=True,
     )
     return output

time: 30.7 us -> 30.2 us (0.984)
  waiting for transfers between devices: 12.1 us -> 11.1 us
  Pallas kernels: 7.91 us -> 8.23 us
    ppermute x6 -> x7, waiting for transfers between devices: 12.1 us -> 11.1 us  [gathered_from(): return lax.ppermute(block, ('space', 'chan'), pairs)]
    pallas_call x4 -> x5, Pallas kernels: 7.91 us -> 8.23 us  [vmem_call(): pl.pallas_call(kernel, out_shape=out_shape, in_specs=specs, out_specs=pl....]
    ppermute x6 -> x7, starting transfers between devices: 6.68 us -> 6.81 us  [gathered_from(): return lax.ppermute(block, ('space', 'chan'), pairs)]
  transfers between devices with their start and end apart: 6 -> 7, of which waited for: 4 -> 4; matrix products, arithmetic and copies ran while one was open for 0% -> 0% of each run, Pallas kernels for 12% -> 14%
where the time goes in v13:
time: 30.2 us; the launch traced here: 30 us
  waiting for transfers between devices  11.1 us (37%)
  Pallas kernels  8.23 us (27%)
  starting transfers between devices  6.81 us (23%)
  local copies, waits for them, and re-layouts  3.71 us (12%)
    ppermute x7, waiting for transfers between devices, gathered_from(): return lax.ppermute(block, ('space', 'chan'), pairs)  11.1 us
    pallas_call x5, Pallas kernels, vmem_call(): pl.pallas_call(kernel, out_shape=out_shape, in_specs=specs, out_specs=pl....  8.23 us
    ppermute x7, starting transfers between devices, gathered_from(): return lax.ppermute(block, ('space', 'chan'), pairs)  6.81 us
    unnamed x16, local copies, waits for them, and re-layouts  3.71 us
  transfers between devices with their start and end apart: 7, of which 4 were waited for; matrix products, arithmetic and copies ran while one was open for 0% of the time, Pallas kernels for 14%

profile of v13, /device:TPU:0, one launch (start us, length us, event | category | flops | bytes accessed | tf_op | source)
XLA Modules:
  0.0 30.0 jit_solution(12090072436795018886)
XLA Ops:
  0.0 2.9 %collective-permute-start = (bf16[256,512]{1,0:T(8,128)(2,1)}, bf16[256,512]{1,0:T(8,128)(2,1)}, u32[]{:S(2)}, u32[]{:S(2)}) collective-permute-start(bf16[256,512]{1,0:T(8,128)(2,1)} %bitcast.16), channel_id=1, source_target_pairs={{28,0},{5,1},{30,2},{7,3},{0,4},{9,5},{2,6},{11,7},{4,8},{13,9},{6... | collective-permute-start | bytes 786440 | tf_op jit(solution)/shard_map/ppermute | solution.py:19
  2.9 1.6 %collective-permute-start.1 = (bf16[256,512]{1,0:T(8,128)(2,1)}, bf16[256,512]{1,0:T(8,128)(2,1)}, u32[]{:S(2)}, u32[]{:S(2)}) collective-permute-start(bf16[256,512]{1,0:T(8,128)(2,1)} %bitcast.17), channel_id=1, source_target_pairs={{24,0},{9,1},{26,2},{11,3},{28,4},{13,5},{30,6},{15,7},{0,8},{17,9... | collective-permute-start | bytes 786440 | tf_op jit(solution)/shard_map/ppermute | solution.py:19
  4.5 0.0 copy-start
  4.5 2.0 %copy-done = bf16[3,3,3,128,512]{4,3,2,1,0:T(8,128)(2,1)S(1)} copy-done((bf16[3,3,3,128,512]{4,3,2,1,0:T(8,128)(2,1)S(1)}, bf16[3,3,3,128,512]{4,3,2,1,0:T(8,128)(2,1)}, u32[]{:S(2)}) %copy-start) | copy-done | bytes 3538968
  6.5 0.0 copy-start.5
  6.5 0.9 %copy-done.5 = bf16[1,4,64,512]{3,2,1,0:T(8,128)(2,1)S(1)} copy-done((bf16[1,4,64,512]{3,2,1,0:T(8,128)(2,1)S(1)}, bf16[1,4,64,512]{3,2,1,0:T(8,128)(2,1)}, u32[]{:S(2)}) %copy-start.5) | copy-done | bytes 262168
  7.5 0.0 copy-start.1
  7.5 0.0 copy-start.6
  7.5 1.2 %shard_map.55.part_ref = f32[3,256,128]{2,1,0:T(8,128)S(1)} custom-call(bf16[256,512]{1,0:T(8,128)(2,1)S(1)} %bitcast.18, bf16[3,1152,512]{2,1,0:T(8,128)(2,1)S(1)} %bitcast.9), custom_call_target="tpu_custom_call" | custom-call | flops 905969664 | bytes 4194304 | tf_op jit(solution)/shard_map/pallas_call | solution.py:180
  8.7 0.0 copy-start.3
  8.7 0.7 %copy-done.3 = f32[3,256,128]{2,1,0:T(8,128)} copy-done((f32[3,256,128]{2,1,0:T(8,128)}, f32[3,256,128]{2,1,0:T(8,128)S(1)}, u32[]{:S(2)}) %copy-start.3) | copy-done | bytes 393240
  9.4 3.6 %collective-permute-done.near_ref = bf16[256,512]{1,0:T(8,128)(2,1)} collective-permute-done((bf16[256,512]{1,0:T(8,128)(2,1)}, bf16[256,512]{1,0:T(8,128)(2,1)}, u32[]{:S(2)}, u32[]{:S(2)}) %collective-permute-start) | collective-permute-done | bytes 262176 | tf_op jit(solution)/shard_map/ppermute | solution.py:19
  13.0 1.3 %collective-permute-done.1.far_ref = bf16[256,512]{1,0:T(8,128)(2,1)} collective-permute-done((bf16[256,512]{1,0:T(8,128)(2,1)}, bf16[256,512]{1,0:T(8,128)(2,1)}, u32[]{:S(2)}, u32[]{:S(2)}) %collective-permute-start.1) | collective-permute-done | bytes 262176 | tf_op jit(solution)/shard_map/ppermute | solution.py:19
  14.3 0.2 collective-permute-start.2
  14.5 0.3 %collective-permute-start.3 = (bf16[256,512]{1,0:T(8,128)(2,1)}, bf16[256,512]{1,0:T(8,128)(2,1)}, u32[]{:S(2)}, u32[]{:S(2)}) collective-permute-start(bf16[256,512]{1,0:T(8,128)(2,1)} %collective-permute-done.1.far_ref), channel_id=1, source_target_pairs={{1,0},{0,1},{3,2},{2,3},{5,4},{4,5},{7,6},{6,7},{9,8},{8,9},{11,10... | collective-permute-start | bytes 786440 | tf_op jit(solution)/shard_map/ppermute | solution.py:19
  14.8 0.0 copy-start.4
  14.8 0.0 copy-done.1
  14.8 2.3 %shard_map.56.fetched_ref = f32[3,256,128]{2,1,0:T(8,128)S(1)} custom-call(s32[1]{0:T(128)} %bitcast.1.odd_ref, bf16[256,512]{1,0:T(8,128)(2,1)} %collective-permute-done.near_ref, bf16[256,512]{1,0:T(8,128)(2,1)} %collective-permute-done.1.far_ref, bf16[3,1152,512]{2,1,0:T(8,128)(2,1)S(1)} %bitcast.10), custom_call_target="tpu_custom_call" | custom-call | flops 905969664 | bytes 4456452 | tf_op jit(solution)/shard_map/pallas_call | solution.py:180
  17.1 0.0 copy-start.2
  17.1 0.0 collective-permute-done.2.their_near_ref
  17.2 0.0 collective-permute-done.3.their_far_ref
  17.2 0.0 copy-done.6
  17.2 0.0 copy-done.4
  17.2 0.0 copy-start.7
  17.2 2.4 %shard_map.57 = bf16[3,256,128]{2,1,0:T(8,128)(2,1)S(1)} custom-call(s32[1]{0:T(128)} %bitcast.1.odd_ref, bf16[256,512]{1,0:T(8,128)(2,1)} %collective-permute-done.2.their_near_ref, bf16[256,512]{1,0:T(8,128)(2,1)} %collective-permute-done.3.their_far_ref, f32[3,256,128]{2,1,0:T(8,128)S(1)} %shard_map.56.fetched_ref, f32[3,256,128]{2,1,0:T(8,128)S(1)} %copy-done.4, ...), custom_call_target="tpu_custom_call" | custom-call | flops 905969664 | bytes 5046788 | tf_op jit(solution)/shard_map/pallas_call | solution.py:180
  19.6 0.3 collective-permute-start.5
  19.9 1.5 %collective-permute-start.4 = (bf16[1,3,256,128]{3,2,1,0:T(8,128)(2,1)S(1)}, bf16[1,3,256,128]{3,2,1,0:T(8,128)(2,1)S(1)}, u32[]{:S(2)}, u32[]{:S(2)}) collective-permute-start(bf16[1,3,256,128]{3,2,1,0:T(8,128)(2,1)S(1)} %bitcast.14), channel_id=1, source_target_pairs={{2,0},{3,1},{0,2},{1,3},{6,4},{7,5},{4,6},{5,7},{10,8},{11,9},{8,1... | collective-permute-start | bytes 589832 | tf_op jit(solution)/shard_map/ppermute | solution.py:19
  21.4 0.0 collective-permute-done.5
  21.4 0.0 copy-done.2
  21.4 0.8 %shard_map.58.refs_2_ = f32[1,256,128]{2,1,0:T(8,128)S(1)} custom-call(s32[1]{0:T(128)} %bitcast.me_ref, bf16[1,3,256,128]{3,2,1,0:T(8,128)(2,1)S(1)} %bitcast.15, bf16[1,3,256,128]{3,2,1,0:T(8,128)(2,1)S(1)} %bitcast.19, bf16[3,1152,512]{2,1,0:T(8,128)(2,1)S(1)} %bitcast.12), custom_call_target="tpu_custom_call" | custom-call | flops 150994944 | bytes 4063236 | tf_op jit(solution)/shard_map/pallas_call | solution.py:180
  22.2 4.8 %collective-permute-done.4.refs_0_ = bf16[1,3,256,128]{3,2,1,0:T(8,128)(2,1)S(1)} collective-permute-done((bf16[1,3,256,128]{3,2,1,0:T(8,128)(2,1)S(1)}, bf16[1,3,256,128]{3,2,1,0:T(8,128)(2,1)S(1)}, u32[]{:S(2)}, u32[]{:S(2)}) %collective-permute-start.4) | collective-permute-done | bytes 196640 | tf_op jit(solution)/shard_map/ppermute | solution.py:19
  27.0 0.0 collective-permute-start.6
  27.0 1.4 %collective-permute-done.6.refs_1_ = bf16[1,3,256,128]{3,2,1,0:T(8,128)(2,1)S(1)} collective-permute-done((bf16[1,3,256,128]{3,2,1,0:T(8,128)(2,1)S(1)}, bf16[1,3,256,128]{3,2,1,0:T(8,128)(2,1)S(1)}, u32[]{:S(2)}, u32[]{:S(2)}) %collective-permute-start.6) | collective-permute-done | bytes 196640 | tf_op jit(solution)/shard_map/ppermute | solution.py:19
  28.5 0.0 copy-done.7
  28.5 1.5 %shard_map.59 = bf16[1,128,256]{2,1,0:T(8,128)(2,1)} custom-call(s32[1]{0:T(128)} %bitcast.me_ref, bf16[1,3,256,128]{3,2,1,0:T(8,128)(2,1)S(1)} %collective-permute-done.4.refs_0_, bf16[1,3,256,128]{3,2,1,0:T(8,128)(2,1)S(1)} %collective-permute-done.6.refs_1_, f32[1,256,128]{2,1,0:T(8,128)S(1)} %shard_map.58.refs_2_, bf16[3,1152,512]{2,1,0:T(8,128)(2,1)S(1)} %bitcast.13, ...), custom_call_target="tpu_custom_call" | custom-call | flops 754974720 | bytes 4129284 | tf_op jit(solution)/shard_map/pallas_call | solution.py:180
Async XLA Ops:
  0.0 13.0 %collective-permute-start = (bf16[256,512]{1,0:T(8,128)(2,1)}, bf16[256,512]{1,0:T(8,128)(2,1)}, u32[]{:S(2)}, u32[]{:S(2)}) collective-permute-start(bf16[256,512]{1,0:T(8,128)(2,1)} %bitcast.16), channel_id=1, source_target_pairs={{28,0},{5,1},{30,2},{7,3},{0,4},{9,5},{2,6},{11,7},{4,8},{13,9},{6... | collective-permute-start | bytes 786440 | tf_op jit(solution)/shard_map/ppermute | solution.py:19
  2.9 11.4 %collective-permute-start.1 = (bf16[256,512]{1,0:T(8,128)(2,1)}, bf16[256,512]{1,0:T(8,128)(2,1)}, u32[]{:S(2)}, u32[]{:S(2)}) collective-permute-start(bf16[256,512]{1,0:T(8,128)(2,1)} %bitcast.17), channel_id=1, source_target_pairs={{24,0},{9,1},{26,2},{11,3},{28,4},{13,5},{30,6},{15,7},{0,8},{17,9... | collective-permute-start | bytes 786440 | tf_op jit(solution)/shard_map/ppermute | solution.py:19
  4.5 2.0 %copy-start = (bf16[3,3,3,128,512]{4,3,2,1,0:T(8,128)(2,1)S(1)}, bf16[3,3,3,128,512]{4,3,2,1,0:T(8,128)(2,1)}, u32[]{:S(2)}) copy-start(bf16[3,3,3,128,512]{4,3,2,1,0:T(8,128)(2,1)} %param.6) | copy-start | bytes 10616836
  6.5 0.9 %copy-start.5 = (bf16[1,4,64,512]{3,2,1,0:T(8,128)(2,1)S(1)}, bf16[1,4,64,512]{3,2,1,0:T(8,128)(2,1)}, u32[]{:S(2)}) copy-start(bf16[1,4,64,512]{3,2,1,0:T(8,128)(2,1)} %param.5) | copy-start | bytes 786436
  7.5 7.3 %copy-start.1 = (bf16[3,3,3,128,512]{4,3,2,1,0:T(8,128)(2,1)S(1)}, bf16[3,3,3,128,512]{4,3,2,1,0:T(8,128)(2,1)}, u32[]{:S(2)}) copy-start(bf16[3,3,3,128,512]{4,3,2,1,0:T(8,128)(2,1)} %param.6) | copy-start | bytes 10616836
  7.5 9.7 %copy-start.6 = (f32[128]{0:T(128)S(1)}, f32[128]{0:T(128)}, u32[]{:S(2)}) copy-start(f32[128]{0:T(128)} %param.7) | copy-start | bytes 1540
  8.7 0.7 %copy-start.3 = (f32[3,256,128]{2,1,0:T(8,128)}, f32[3,256,128]{2,1,0:T(8,128)S(1)}, u32[]{:S(2)}) copy-start(f32[3,256,128]{2,1,0:T(8,128)S(1)} %shard_map.55.part_ref) | copy-start | bytes 1179652
  14.3 2.8 %collective-permute-start.2 = (bf16[256,512]{1,0:T(8,128)(2,1)}, bf16[256,512]{1,0:T(8,128)(2,1)}, u32[]{:S(2)}, u32[]{:S(2)}) collective-permute-start(bf16[256,512]{1,0:T(8,128)(2,1)} %collective-permute-done.near_ref), channel_id=1, source_target_pairs={{1,0},{0,1},{3,2},{2,3},{5,4},{4,5},{7,6},{6,7},{9,8},{8,9},{11,10... | collective-permute-start | bytes 786440 | tf_op jit(solution)/shard_map/ppermute | solution.py:19
  14.5 2.7 %collective-permute-start.3 = (bf16[256,512]{1,0:T(8,128)(2,1)}, bf16[256,512]{1,0:T(8,128)(2,1)}, u32[]{:S(2)}, u32[]{:S(2)}) collective-permute-start(bf16[256,512]{1,0:T(8,128)(2,1)} %collective-permute-done.1.far_ref), channel_id=1, source_target_pairs={{1,0},{0,1},{3,2},{2,3},{5,4},{4,5},{7,6},{6,7},{9,8},{8,9},{11,10... | collective-permute-start | bytes 786440 | tf_op jit(solution)/shard_map/ppermute | solution.py:19
  14.8 2.4 %copy-start.4 = (f32[3,256,128]{2,1,0:T(8,128)S(1)}, f32[3,256,128]{2,1,0:T(8,128)}, u32[]{:S(2)}) copy-start(f32[3,256,128]{2,1,0:T(8,128)} %copy-done.3) | copy-start | bytes 1179652
  17.1 4.3 %copy-start.2 = (bf16[3,3,3,128,512]{4,3,2,1,0:T(8,128)(2,1)S(1)}, bf16[3,3,3,128,512]{4,3,2,1,0:T(8,128)(2,1)}, u32[]{:S(2)}) copy-start(bf16[3,3,3,128,512]{4,3,2,1,0:T(8,128)(2,1)} %param.8) | copy-start | bytes 10616836
  17.2 11.3 %copy-start.7 = (f32[128]{0:T(128)S(1)}, f32[128]{0:T(128)}, u32[]{:S(2)}) copy-start(f32[128]{0:T(128)} %param.9) | copy-start | bytes 1540
  19.6 1.8 %collective-permute-start.5 = (bf16[3,256,128]{2,1,0:T(8,128)(2,1)S(1)}, bf16[3,256,128]{2,1,0:T(8,128)(2,1)S(1)}, u32[]{:S(2)}, u32[]{:S(2)}) collective-permute-start(bf16[3,256,128]{2,1,0:T(8,128)(2,1)S(1)} %shard_map.57), channel_id=1, source_target_pairs={{1,0},{0,1},{3,2},{2,3},{5,4},{4,5},{7,6},{6,7},{9,8},{8,9},{11,10... | collective-permute-start | bytes 589832 | tf_op jit(solution)/shard_map/ppermute | solution.py:19
  19.9 7.1 %collective-permute-start.4 = (bf16[1,3,256,128]{3,2,1,0:T(8,128)(2,1)S(1)}, bf16[1,3,256,128]{3,2,1,0:T(8,128)(2,1)S(1)}, u32[]{:S(2)}, u32[]{:S(2)}) collective-permute-start(bf16[1,3,256,128]{3,2,1,0:T(8,128)(2,1)S(1)} %bitcast.14), channel_id=1, source_target_pairs={{2,0},{3,1},{0,2},{1,3},{6,4},{7,5},{4,6},{5,7},{10,8},{11,9},{8,1... | collective-permute-start | bytes 589832 | tf_op jit(solution)/shard_map/ppermute | solution.py:19
  27.0 1.4 %collective-permute-start.6 = (bf16[1,3,256,128]{3,2,1,0:T(8,128)(2,1)S(1)}, bf16[1,3,256,128]{3,2,1,0:T(8,128)(2,1)S(1)}, u32[]{:S(2)}, u32[]{:S(2)}) collective-permute-start(bf16[1,3,256,128]{3,2,1,0:T(8,128)(2,1)S(1)} %collective-permute-done.4.refs_0_), channel_id=1, source_target_pairs={{1,0},{0,1},{3,2},{2,3},{5,4},{4,5},{7,6},{6,7},{9,8},{8,9},{11,10... | collective-permute-start | bytes 589832 | tf_op jit(solution)/shard_map/ppermute | solution.py:19

commit v14 on v13

--- a/solution.py
+++ b/solution.py
@@ -71,46 +71,38 @@
         o_ref[plane] = spatial_sum(acc_ref, plane, rows_n, cols_n, outs)
 
 
-def side_products(acc_ref, first_ref, second_ref, w_ref, minus):
-    if minus:
-        acc_ref[0] = tap_product(second_ref[...], w_ref, 0)
-        acc_ref[0] += tap_product(first_ref[...], w_ref, 1)
-        acc_ref[1] = tap_product(first_ref[...], w_ref, 0)
-        return (0, 1)
-    acc_ref[1] = tap_product(first_ref[...], w_ref, 2)
-    acc_ref[2] = tap_product(first_ref[...], w_ref, 1)
-    acc_ref[2] += tap_product(second_ref[...], w_ref, 2)
-    return (1, 2)
+def side_terms(acc_ref, near_ref, far_ref, w_ref, outer_tap, rows_n, cols_n, outs):
+    near = near_ref[...]
+    acc_ref[0] = tap_product(near, w_ref, 1)
+    acc_ref[0] += tap_product(far_ref[...], w_ref, outer_tap)
+    acc_ref[1] = tap_product(near, w_ref, outer_tap)
+    return [spatial_sum(acc_ref, plane, rows_n, cols_n, outs) for plane in range(2)]
 
 
 def fetched_side_kernel(rows_n, cols_n, odd_ref, near_ref, far_ref, w_ref, o_ref, acc_ref):
     outs = o_ref.shape[2]
-    for minus in (True, False):
-
-        @pl.when((odd_ref[0] == 0) == minus)
-        def _():
-            touched = side_products(acc_ref, near_ref, far_ref, w_ref, minus)
-            for plane in range(3):
-                if plane in touched:
-                    o_ref[plane] = spatial_sum(acc_ref, plane, rows_n, cols_n, outs)
-                else:
-                    o_ref[plane] = jnp.zeros(o_ref.shape[1:], o_ref.dtype)
+    outer_tap = 2 * odd_ref[0]
+    terms = side_terms(acc_ref, near_ref, far_ref, w_ref, outer_tap, rows_n, cols_n, outs)
+    for plane in range(2):
+        o_ref[plane] = terms[plane]
 
 
 def neighbour_kernel(rows_n, cols_n, odd_ref, their_near_ref, their_far_ref, fetched_ref, part_ref,
                      w_ref, b_ref, o_ref, acc_ref):
     outs = o_ref.shape[2]
     bias = b_ref[...]
-    for minus in (True, False):
-
-        @pl.when((odd_ref[0] != 0) == minus)
-        def _():
-            touched = side_products(acc_ref, their_near_ref, their_far_ref, w_ref, minus)
-            for plane in range(3):
-                total = fetched_ref[plane] + part_ref[plane]
-                if plane in touched:
-                    total = total + spatial_sum(acc_ref, plane, rows_n, cols_n, outs)
-                o_ref[plane] = jnp.maximum(total + bias, 0.0).astype(o_ref.dtype)
+    is_odd = odd_ref[0] != 0
+    outer_tap = 2 - 2 * odd_ref[0]
+    outer, centre = side_terms(acc_ref, their_near_ref, their_far_ref, w_ref, outer_tap, rows_n, cols_n, outs)
+    fetched_outer = fetched_ref[0]
+    planes = [
+        jnp.where(is_odd, outer, fetched_outer),
+        centre + fetched_ref[1],
+        jnp.where(is_odd, fetched_outer, outer),
+    ]
+    for plane in range(3):
+        total = planes[plane] + part_ref[plane]
+        o_ref[plane] = jnp.maximum(total + bias, 0.0).astype(o_ref.dtype)
 
 
 def pair_products(acc_ref, blocks, me, pairs, w_ref, field_ref, outs, first):
@@ -213,9 +205,9 @@
     odd = (me % 2).astype(jnp.int32).reshape(1)
     fetched_terms = vmem_call(
         functools.partial(fetched_side_kernel, rows_n, cols_n),
-        jax.ShapeDtypeStruct((3, cells, outs), jnp.float32),
+        jax.ShapeDtypeStruct((2, cells, outs), jnp.float32),
         [odd, near, far, one_stack],
-        [pltpu.VMEM((3, cells, 9 * outs), jnp.float32)],
+        [pltpu.VMEM((2, cells, 9 * outs), jnp.float32)],
         3 * tap_flops,
         smem_first=True,
     )
@@ -223,7 +215,7 @@
         functools.partial(neighbour_kernel, rows_n, cols_n),
         jax.ShapeDtypeStruct((3, cells, outs), jnp.bfloat16),
         [odd, their_near, their_far, fetched_terms, own_terms, one_stack, bias_one.reshape(1, outs)],
-        [pltpu.VMEM((3, cells, 9 * outs), jnp.float32)],
+        [pltpu.VMEM((2, cells, 9 * outs), jnp.float32)],
         3 * tap_flops,
         smem_first=True,
     )

time: 30.2 us -> 31.4 us (1.040)
  waiting for transfers between devices: 11.1 us -> 12.5 us
    ppermute x7, waiting for transfers between devices: 11.1 us -> 12.5 us  [gathered_from(): return lax.ppermute(block, ('space', 'chan'), pairs)]
where the time goes in v14:
time: 31.4 us; the launch traced here: 31.2 us
  waiting for transfers between devices  12.5 us (40%)
  Pallas kernels  8.21 us (26%)
  starting transfers between devices  6.69 us (21%)
  local copies, waits for them, and re-layouts  3.71 us (12%)
    ppermute x7, waiting for transfers between devices, gathered_from(): return lax.ppermute(block, ('space', 'chan'), pairs)  12.5 us
    pallas_call x5, Pallas kernels, vmem_call(): pl.pallas_call(kernel, out_shape=out_shape, in_specs=specs, out_specs=pl....  8.21 us
    ppermute x7, starting transfers between devices, gathered_from(): return lax.ppermute(block, ('space', 'chan'), pairs)  6.69 us
    unnamed x16, local copies, waits for them, and re-layouts  3.71 us
  transfers between devices with their start and end apart: 7, of which 4 were waited for; matrix products, arithmetic and copies ran while one was open for 0% of the time, Pallas kernels for 14%

profile of v14, /device:TPU:0, one launch (start us, length us, event | category | flops | bytes accessed | tf_op | source)
XLA Modules:
  0.0 31.2 jit_solution(5376320397874227481)
XLA Ops:
  0.0 3.0 %collective-permute-start.1 = (bf16[256,512]{1,0:T(8,128)(2,1)}, bf16[256,512]{1,0:T(8,128)(2,1)}, u32[]{:S(2)}, u32[]{:S(2)}) collective-permute-start(bf16[256,512]{1,0:T(8,128)(2,1)} %bitcast.16), channel_id=1, source_target_pairs={{24,0},{9,1},{26,2},{11,3},{28,4},{13,5},{30,6},{15,7},{0,8},{17,9... | collective-permute-start | bytes 786440 | tf_op jit(solution)/shard_map/ppermute | solution.py:19
  3.0 1.5 %collective-permute-start = (bf16[256,512]{1,0:T(8,128)(2,1)}, bf16[256,512]{1,0:T(8,128)(2,1)}, u32[]{:S(2)}, u32[]{:S(2)}) collective-permute-start(bf16[256,512]{1,0:T(8,128)(2,1)} %bitcast.17), channel_id=1, source_target_pairs={{28,0},{5,1},{30,2},{7,3},{0,4},{9,5},{2,6},{11,7},{4,8},{13,9},{6... | collective-permute-start | bytes 786440 | tf_op jit(solution)/shard_map/ppermute | solution.py:19
  4.5 0.0 copy-start
  4.5 2.0 %copy-done = bf16[3,3,3,128,512]{4,3,2,1,0:T(8,128)(2,1)S(1)} copy-done((bf16[3,3,3,128,512]{4,3,2,1,0:T(8,128)(2,1)S(1)}, bf16[3,3,3,128,512]{4,3,2,1,0:T(8,128)(2,1)}, u32[]{:S(2)}) %copy-start) | copy-done | bytes 3538968
  6.5 0.0 copy-start.5
  6.5 0.9 %copy-done.5 = bf16[1,4,64,512]{3,2,1,0:T(8,128)(2,1)S(1)} copy-done((bf16[1,4,64,512]{3,2,1,0:T(8,128)(2,1)S(1)}, bf16[1,4,64,512]{3,2,1,0:T(8,128)(2,1)}, u32[]{:S(2)}) %copy-start.5) | copy-done | bytes 262168
  7.5 0.0 copy-start.1
  7.5 0.0 copy-start.7
  7.5 1.2 %shard_map.55.part_ref = f32[3,256,128]{2,1,0:T(8,128)S(1)} custom-call(bf16[256,512]{1,0:T(8,128)(2,1)S(1)} %bitcast.18, bf16[3,1152,512]{2,1,0:T(8,128)(2,1)S(1)} %bitcast.9), custom_call_target="tpu_custom_call" | custom-call | flops 905969664 | bytes 4194304 | tf_op jit(solution)/shard_map/pallas_call | solution.py:172
  8.7 0.0 copy-start.3
  8.7 0.7 %copy-done.3 = f32[3,256,128]{2,1,0:T(8,128)} copy-done((f32[3,256,128]{2,1,0:T(8,128)}, f32[3,256,128]{2,1,0:T(8,128)S(1)}, u32[]{:S(2)}) %copy-start.3) | copy-done | bytes 393240
  9.4 3.0 %collective-permute-done.1.far_ref = bf16[256,512]{1,0:T(8,128)(2,1)} collective-permute-done((bf16[256,512]{1,0:T(8,128)(2,1)}, bf16[256,512]{1,0:T(8,128)(2,1)}, u32[]{:S(2)}, u32[]{:S(2)}) %collective-permute-start.1) | collective-permute-done | bytes 262176 | tf_op jit(solution)/shard_map/ppermute | solution.py:19
  12.5 3.1 %collective-permute-done.near_ref = bf16[256,512]{1,0:T(8,128)(2,1)} collective-permute-done((bf16[256,512]{1,0:T(8,128)(2,1)}, bf16[256,512]{1,0:T(8,128)(2,1)}, u32[]{:S(2)}, u32[]{:S(2)}) %collective-permute-start) | collective-permute-done | bytes 262176 | tf_op jit(solution)/shard_map/ppermute | solution.py:19
  15.6 0.0 collective-permute-start.2
  15.6 0.5 %collective-permute-start.3 = (bf16[256,512]{1,0:T(8,128)(2,1)}, bf16[256,512]{1,0:T(8,128)(2,1)}, u32[]{:S(2)}, u32[]{:S(2)}) collective-permute-start(bf16[256,512]{1,0:T(8,128)(2,1)} %collective-permute-done.1.far_ref), channel_id=1, source_target_pairs={{1,0},{0,1},{3,2},{2,3},{5,4},{4,5},{7,6},{6,7},{9,8},{8,9},{11,10... | collective-permute-start | bytes 786440 | tf_op jit(solution)/shard_map/ppermute | solution.py:19
  16.1 0.0 copy-start.4
  16.1 0.0 copy-done.1
  16.1 2.3 %shard_map.56.fetched_ref = f32[2,256,128]{2,1,0:T(8,128)S(1)} custom-call(s32[1]{0:T(128)} %bitcast.1.odd_ref, bf16[256,512]{1,0:T(8,128)(2,1)} %collective-permute-done.near_ref, bf16[256,512]{1,0:T(8,128)(2,1)} %collective-permute-done.1.far_ref, bf16[3,1152,512]{2,1,0:T(8,128)(2,1)S(1)} %bitcast.10), custom_call_target="tpu_custom_call" | custom-call | flops 905969664 | bytes 4325380 | tf_op jit(solution)/shard_map/pallas_call | solution.py:172
  18.4 0.0 copy-start.2
  18.4 0.0 collective-permute-done.2.their_near_ref
  18.4 0.0 collective-permute-done.3.their_far_ref
  18.4 0.0 copy-done.7
  18.4 0.0 copy-done.4
  18.4 0.0 copy-start.6
  18.5 2.4 %shard_map.57 = bf16[3,256,128]{2,1,0:T(8,128)(2,1)S(1)} custom-call(s32[1]{0:T(128)} %bitcast.1.odd_ref, bf16[256,512]{1,0:T(8,128)(2,1)} %collective-permute-done.2.their_near_ref, bf16[256,512]{1,0:T(8,128)(2,1)} %collective-permute-done.3.their_far_ref, f32[2,256,128]{2,1,0:T(8,128)S(1)} %shard_map.56.fetched_ref, f32[3,256,128]{2,1,0:T(8,128)S(1)} %copy-done.4, ...), custom_call_target="tpu_custom_call" | custom-call | flops 905969664 | bytes 4915716 | tf_op jit(solution)/shard_map/pallas_call | solution.py:172
  20.9 0.1 collective-permute-start.5
  21.0 1.6 %collective-permute-start.4 = (bf16[1,3,256,128]{3,2,1,0:T(8,128)(2,1)S(1)}, bf16[1,3,256,128]{3,2,1,0:T(8,128)(2,1)S(1)}, u32[]{:S(2)}, u32[]{:S(2)}) collective-permute-start(bf16[1,3,256,128]{3,2,1,0:T(8,128)(2,1)S(1)} %bitcast.14), channel_id=1, source_target_pairs={{2,0},{3,1},{0,2},{1,3},{6,4},{7,5},{4,6},{5,7},{10,8},{11,9},{8,1... | collective-permute-start | bytes 589832 | tf_op jit(solution)/shard_map/ppermute | solution.py:19
  22.6 0.0 collective-permute-done.5
  22.6 0.0 copy-done.2
  22.6 0.8 %shard_map.58.refs_2_ = f32[1,256,128]{2,1,0:T(8,128)S(1)} custom-call(s32[1]{0:T(128)} %bitcast.me_ref, bf16[1,3,256,128]{3,2,1,0:T(8,128)(2,1)S(1)} %bitcast.15, bf16[1,3,256,128]{3,2,1,0:T(8,128)(2,1)S(1)} %bitcast.19, bf16[3,1152,512]{2,1,0:T(8,128)(2,1)S(1)} %bitcast.12), custom_call_target="tpu_custom_call" | custom-call | flops 150994944 | bytes 4063236 | tf_op jit(solution)/shard_map/pallas_call | solution.py:172
  23.3 4.9 %collective-permute-done.4.refs_0_ = bf16[1,3,256,128]{3,2,1,0:T(8,128)(2,1)S(1)} collective-permute-done((bf16[1,3,256,128]{3,2,1,0:T(8,128)(2,1)S(1)}, bf16[1,3,256,128]{3,2,1,0:T(8,128)(2,1)S(1)}, u32[]{:S(2)}, u32[]{:S(2)}) %collective-permute-start.4) | collective-permute-done | bytes 196640 | tf_op jit(solution)/shard_map/ppermute | solution.py:19
  28.3 0.0 collective-permute-start.6
  28.3 1.4 %collective-permute-done.6.refs_1_ = bf16[1,3,256,128]{3,2,1,0:T(8,128)(2,1)S(1)} collective-permute-done((bf16[1,3,256,128]{3,2,1,0:T(8,128)(2,1)S(1)}, bf16[1,3,256,128]{3,2,1,0:T(8,128)(2,1)S(1)}, u32[]{:S(2)}, u32[]{:S(2)}) %collective-permute-start.6) | collective-permute-done | bytes 196640 | tf_op jit(solution)/shard_map/ppermute | solution.py:19
  29.7 0.0 copy-done.6
  29.7 1.5 %shard_map.59 = bf16[1,128,256]{2,1,0:T(8,128)(2,1)} custom-call(s32[1]{0:T(128)} %bitcast.me_ref, bf16[1,3,256,128]{3,2,1,0:T(8,128)(2,1)S(1)} %collective-permute-done.4.refs_0_, bf16[1,3,256,128]{3,2,1,0:T(8,128)(2,1)S(1)} %collective-permute-done.6.refs_1_, f32[1,256,128]{2,1,0:T(8,128)S(1)} %shard_map.58.refs_2_, bf16[3,1152,512]{2,1,0:T(8,128)(2,1)S(1)} %bitcast.13, ...), custom_call_target="tpu_custom_call" | custom-call | flops 754974720 | bytes 4129284 | tf_op jit(solution)/shard_map/pallas_call | solution.py:172
Async XLA Ops:
  0.0 12.5 %collective-permute-start.1 = (bf16[256,512]{1,0:T(8,128)(2,1)}, bf16[256,512]{1,0:T(8,128)(2,1)}, u32[]{:S(2)}, u32[]{:S(2)}) collective-permute-start(bf16[256,512]{1,0:T(8,128)(2,1)} %bitcast.16), channel_id=1, source_target_pairs={{24,0},{9,1},{26,2},{11,3},{28,4},{13,5},{30,6},{15,7},{0,8},{17,9... | collective-permute-start | bytes 786440 | tf_op jit(solution)/shard_map/ppermute | solution.py:19
  3.0 12.5 %collective-permute-start = (bf16[256,512]{1,0:T(8,128)(2,1)}, bf16[256,512]{1,0:T(8,128)(2,1)}, u32[]{:S(2)}, u32[]{:S(2)}) collective-permute-start(bf16[256,512]{1,0:T(8,128)(2,1)} %bitcast.17), channel_id=1, source_target_pairs={{28,0},{5,1},{30,2},{7,3},{0,4},{9,5},{2,6},{11,7},{4,8},{13,9},{6... | collective-permute-start | bytes 786440 | tf_op jit(solution)/shard_map/ppermute | solution.py:19
  4.5 2.0 %copy-start = (bf16[3,3,3,128,512]{4,3,2,1,0:T(8,128)(2,1)S(1)}, bf16[3,3,3,128,512]{4,3,2,1,0:T(8,128)(2,1)}, u32[]{:S(2)}) copy-start(bf16[3,3,3,128,512]{4,3,2,1,0:T(8,128)(2,1)} %param.6) | copy-start | bytes 10616836
  6.5 0.9 %copy-start.5 = (bf16[1,4,64,512]{3,2,1,0:T(8,128)(2,1)S(1)}, bf16[1,4,64,512]{3,2,1,0:T(8,128)(2,1)}, u32[]{:S(2)}) copy-start(bf16[1,4,64,512]{3,2,1,0:T(8,128)(2,1)} %param.5) | copy-start | bytes 786436
  7.5 8.6 %copy-start.1 = (bf16[3,3,3,128,512]{4,3,2,1,0:T(8,128)(2,1)S(1)}, bf16[3,3,3,128,512]{4,3,2,1,0:T(8,128)(2,1)}, u32[]{:S(2)}) copy-start(bf16[3,3,3,128,512]{4,3,2,1,0:T(8,128)(2,1)} %param.6) | copy-start | bytes 10616836
  7.5 11.0 %copy-start.7 = (f32[128]{0:T(128)S(1)}, f32[128]{0:T(128)}, u32[]{:S(2)}) copy-start(f32[128]{0:T(128)} %param.7) | copy-start | bytes 1540
  8.7 0.7 %copy-start.3 = (f32[3,256,128]{2,1,0:T(8,128)}, f32[3,256,128]{2,1,0:T(8,128)S(1)}, u32[]{:S(2)}) copy-start(f32[3,256,128]{2,1,0:T(8,128)S(1)} %shard_map.55.part_ref) | copy-start | bytes 1179652
  15.6 2.8 %collective-permute-start.2 = (bf16[256,512]{1,0:T(8,128)(2,1)}, bf16[256,512]{1,0:T(8,128)(2,1)}, u32[]{:S(2)}, u32[]{:S(2)}) collective-permute-start(bf16[256,512]{1,0:T(8,128)(2,1)} %collective-permute-done.near_ref), channel_id=1, source_target_pairs={{1,0},{0,1},{3,2},{2,3},{5,4},{4,5},{7,6},{6,7},{9,8},{8,9},{11,10... | collective-permute-start | bytes 786440 | tf_op jit(solution)/shard_map/ppermute | solution.py:19
  15.6 2.8 %collective-permute-start.3 = (bf16[256,512]{1,0:T(8,128)(2,1)}, bf16[256,512]{1,0:T(8,128)(2,1)}, u32[]{:S(2)}, u32[]{:S(2)}) collective-permute-start(bf16[256,512]{1,0:T(8,128)(2,1)} %collective-permute-done.1.far_ref), channel_id=1, source_target_pairs={{1,0},{0,1},{3,2},{2,3},{5,4},{4,5},{7,6},{6,7},{9,8},{8,9},{11,10... | collective-permute-start | bytes 786440 | tf_op jit(solution)/shard_map/ppermute | solution.py:19
  16.1 2.4 %copy-start.4 = (f32[3,256,128]{2,1,0:T(8,128)S(1)}, f32[3,256,128]{2,1,0:T(8,128)}, u32[]{:S(2)}) copy-start(f32[3,256,128]{2,1,0:T(8,128)} %copy-done.3) | copy-start | bytes 1179652
  18.4 4.2 %copy-start.2 = (bf16[3,3,3,128,512]{4,3,2,1,0:T(8,128)(2,1)S(1)}, bf16[3,3,3,128,512]{4,3,2,1,0:T(8,128)(2,1)}, u32[]{:S(2)}) copy-start(bf16[3,3,3,128,512]{4,3,2,1,0:T(8,128)(2,1)} %param.8) | copy-start | bytes 10616836
  18.4 11.3 %copy-start.6 = (f32[128]{0:T(128)S(1)}, f32[128]{0:T(128)}, u32[]{:S(2)}) copy-start(f32[128]{0:T(128)} %param.9) | copy-start | bytes 1540
  20.9 1.7 %collective-permute-start.5 = (bf16[3,256,128]{2,1,0:T(8,128)(2,1)S(1)}, bf16[3,256,128]{2,1,0:T(8,128)(2,1)S(1)}, u32[]{:S(2)}, u32[]{:S(2)}) collective-permute-start(bf16[3,256,128]{2,1,0:T(8,128)(2,1)S(1)} %shard_map.57), channel_id=1, source_target_pairs={{1,0},{0,1},{3,2},{2,3},{5,4},{4,5},{7,6},{6,7},{9,8},{8,9},{11,10... | collective-permute-start | bytes 589832 | tf_op jit(solution)/shard_map/ppermute | solution.py:19
  21.0 7.3 %collective-permute-start.4 = (bf16[1,3,256,128]{3,2,1,0:T(8,128)(2,1)S(1)}, bf16[1,3,256,128]{3,2,1,0:T(8,128)(2,1)S(1)}, u32[]{:S(2)}, u32[]{:S(2)}) collective-permute-start(bf16[1,3,256,128]{3,2,1,0:T(8,128)(2,1)S(1)} %bitcast.14), channel_id=1, source_target_pairs={{2,0},{3,1},{0,2},{1,3},{6,4},{7,5},{4,6},{5,7},{10,8},{11,9},{8,1... | collective-permute-start | bytes 589832 | tf_op jit(solution)/shard_map/ppermute | solution.py:19
  28.3 1.4 %collective-permute-start.6 = (bf16[1,3,256,128]{3,2,1,0:T(8,128)(2,1)S(1)}, bf16[1,3,256,128]{3,2,1,0:T(8,128)(2,1)S(1)}, u32[]{:S(2)}, u32[]{:S(2)}) collective-permute-start(bf16[1,3,256,128]{3,2,1,0:T(8,128)(2,1)S(1)} %collective-permute-done.4.refs_0_), channel_id=1, source_target_pairs={{1,0},{0,1},{3,2},{2,3},{5,4},{4,5},{7,6},{6,7},{9,8},{8,9},{11,10... | collective-permute-start | bytes 589832 | tf_op jit(solution)/shard_map/ppermute | solution.py:19

commit v15 on v13

--- a/solution.py
+++ b/solution.py
@@ -169,7 +169,7 @@
     pair_products(acc_ref, full, me, pairs, w_ref, field_ref, outs, True)
     total = spatial_sum(acc_ref, 0, rows_n, cols_n, outs) + part_ref[0]
     result = jnp.maximum(total + b_ref[...], 0.0)
-    o_ref[0] = result.T.astype(o_ref.dtype)
+    o_ref[0] = result.astype(o_ref.dtype)
 
 
 def vmem_call(kernel, out_shape, operands, scratch, flops, smem_first=False):
@@ -256,13 +256,13 @@
     layout = tuple(offs for _, offs in held)
     output = vmem_call(
         functools.partial(second_kernel, rows_n, cols_n, chans, layout),
-        jax.ShapeDtypeStruct((1, outs, cells), jnp.bfloat16),
+        jax.ShapeDtypeStruct((1, cells, outs), jnp.bfloat16),
         [me_flag] + [arr for arr, _ in held] + [own_pair, two_stack, bias_two.reshape(1, outs)],
         [pltpu.VMEM((3, cells, 2 * outs), jnp.bfloat16), pltpu.VMEM((1, cells, 9 * outs), jnp.float32)],
         3 * tap_flops - 2 * tap_flops // chans,
         smem_first=True,
     )
-    return output
+    return output.transpose(0, 2, 1)
 
 
 def solution(mesh):

time: 30.2 us -> 30.2 us (level)
  local copies, waits for them, and re-layouts: 3.71 us -> 4.45 us
  Pallas kernels: 8.23 us -> 7.54 us
    transpose x0 -> x1, local copies, waits for them, and re-layouts: none -> 0.74 us  [per_device(): return output.transpose(0, 2, 1)]
    pallas_call x5, Pallas kernels: 8.23 us -> 7.54 us  [vmem_call(): pl.pallas_call(kernel, out_shape=out_shape, in_specs=specs, out_specs=pl....]
where the time goes in v15:
time: 30.2 us; the launch traced here: 30 us
  waiting for transfers between devices  11.1 us (37%)
  Pallas kernels  7.54 us (25%)
  starting transfers between devices  6.81 us (23%)
  local copies, waits for them, and re-layouts  4.45 us (15%)
    ppermute x7, waiting for transfers between devices, gathered_from(): return lax.ppermute(block, ('space', 'chan'), pairs)  11.1 us
    pallas_call x5, Pallas kernels, vmem_call(): pl.pallas_call(kernel, out_shape=out_shape, in_specs=specs, out_specs=pl....  7.54 us
    ppermute x7, starting transfers between devices, gathered_from(): return lax.ppermute(block, ('space', 'chan'), pairs)  6.81 us
    unnamed x16, local copies, waits for them, and re-layouts  3.71 us
    transpose x1, local copies, waits for them, and re-layouts, per_device(): return output.transpose(0, 2, 1)  0.74 us
  transfers between devices with their start and end apart: 7, of which 4 were waited for; matrix products, arithmetic and copies ran while one was open for 0% of the time, Pallas kernels for 14%

profile of v15, /device:TPU:0, one launch (start us, length us, event | category | flops | bytes accessed | tf_op | source)
XLA Modules:
  0.0 30.0 jit_solution(12835153409086624326)
XLA Ops:
  0.0 2.9 %collective-permute-start = (bf16[256,512]{1,0:T(8,128)(2,1)}, bf16[256,512]{1,0:T(8,128)(2,1)}, u32[]{:S(2)}, u32[]{:S(2)}) collective-permute-start(bf16[256,512]{1,0:T(8,128)(2,1)} %bitcast.18), channel_id=1, source_target_pairs={{28,0},{5,1},{30,2},{7,3},{0,4},{9,5},{2,6},{11,7},{4,8},{13,9},{6... | collective-permute-start | bytes 786440 | tf_op jit(solution)/shard_map/ppermute | solution.py:19
  2.9 1.6 %collective-permute-start.1 = (bf16[256,512]{1,0:T(8,128)(2,1)}, bf16[256,512]{1,0:T(8,128)(2,1)}, u32[]{:S(2)}, u32[]{:S(2)}) collective-permute-start(bf16[256,512]{1,0:T(8,128)(2,1)} %bitcast.19), channel_id=1, source_target_pairs={{24,0},{9,1},{26,2},{11,3},{28,4},{13,5},{30,6},{15,7},{0,8},{17,9... | collective-permute-start | bytes 786440 | tf_op jit(solution)/shard_map/ppermute | solution.py:19
  4.5 0.0 copy-start
  4.5 2.0 %copy-done = bf16[3,3,3,128,512]{4,3,2,1,0:T(8,128)(2,1)S(1)} copy-done((bf16[3,3,3,128,512]{4,3,2,1,0:T(8,128)(2,1)S(1)}, bf16[3,3,3,128,512]{4,3,2,1,0:T(8,128)(2,1)}, u32[]{:S(2)}) %copy-start) | copy-done | bytes 3538968
  6.5 0.0 copy-start.5
  6.5 0.9 %copy-done.5 = bf16[1,4,64,512]{3,2,1,0:T(8,128)(2,1)S(1)} copy-done((bf16[1,4,64,512]{3,2,1,0:T(8,128)(2,1)S(1)}, bf16[1,4,64,512]{3,2,1,0:T(8,128)(2,1)}, u32[]{:S(2)}) %copy-start.5) | copy-done | bytes 262168
  7.5 0.0 copy-start.1
  7.5 0.0 copy-start.6
  7.5 1.2 %shard_map.55.part_ref = f32[3,256,128]{2,1,0:T(8,128)S(1)} custom-call(bf16[256,512]{1,0:T(8,128)(2,1)S(1)} %bitcast.20, bf16[3,1152,512]{2,1,0:T(8,128)(2,1)S(1)} %bitcast.10), custom_call_target="tpu_custom_call" | custom-call | flops 905969664 | bytes 4194304 | tf_op jit(solution)/shard_map/pallas_call | solution.py:180
  8.7 0.0 copy-start.3
  8.7 0.7 %copy-done.3 = f32[3,256,128]{2,1,0:T(8,128)} copy-done((f32[3,256,128]{2,1,0:T(8,128)}, f32[3,256,128]{2,1,0:T(8,128)S(1)}, u32[]{:S(2)}) %copy-start.3) | copy-done | bytes 393240
  9.4 3.6 %collective-permute-done.near_ref = bf16[256,512]{1,0:T(8,128)(2,1)} collective-permute-done((bf16[256,512]{1,0:T(8,128)(2,1)}, bf16[256,512]{1,0:T(8,128)(2,1)}, u32[]{:S(2)}, u32[]{:S(2)}) %collective-permute-start) | collective-permute-done | bytes 262176 | tf_op jit(solution)/shard_map/ppermute | solution.py:19
  13.0 1.3 %collective-permute-done.1.far_ref = bf16[256,512]{1,0:T(8,128)(2,1)} collective-permute-done((bf16[256,512]{1,0:T(8,128)(2,1)}, bf16[256,512]{1,0:T(8,128)(2,1)}, u32[]{:S(2)}, u32[]{:S(2)}) %collective-permute-start.1) | collective-permute-done | bytes 262176 | tf_op jit(solution)/shard_map/ppermute | solution.py:19
  14.3 0.2 collective-permute-start.2
  14.5 0.3 %collective-permute-start.3 = (bf16[256,512]{1,0:T(8,128)(2,1)}, bf16[256,512]{1,0:T(8,128)(2,1)}, u32[]{:S(2)}, u32[]{:S(2)}) collective-permute-start(bf16[256,512]{1,0:T(8,128)(2,1)} %collective-permute-done.1.far_ref), channel_id=1, source_target_pairs={{1,0},{0,1},{3,2},{2,3},{5,4},{4,5},{7,6},{6,7},{9,8},{8,9},{11,10... | collective-permute-start | bytes 786440 | tf_op jit(solution)/shard_map/ppermute | solution.py:19
  14.8 0.0 copy-start.4
  14.8 0.0 copy-done.1
  14.8 2.3 %shard_map.56.fetched_ref = f32[3,256,128]{2,1,0:T(8,128)S(1)} custom-call(s32[1]{0:T(128)} %bitcast.1.odd_ref, bf16[256,512]{1,0:T(8,128)(2,1)} %collective-permute-done.near_ref, bf16[256,512]{1,0:T(8,128)(2,1)} %collective-permute-done.1.far_ref, bf16[3,1152,512]{2,1,0:T(8,128)(2,1)S(1)} %bitcast.11), custom_call_target="tpu_custom_call" | custom-call | flops 905969664 | bytes 4456452 | tf_op jit(solution)/shard_map/pallas_call | solution.py:180
  17.1 0.0 copy-start.2
  17.1 0.0 collective-permute-done.2.their_near_ref
  17.2 0.0 collective-permute-done.3.their_far_ref
  17.2 0.0 copy-done.6
  17.2 0.0 copy-done.4
  17.2 0.0 copy-start.7
  17.2 2.4 %shard_map.57 = bf16[3,256,128]{2,1,0:T(8,128)(2,1)S(1)} custom-call(s32[1]{0:T(128)} %bitcast.1.odd_ref, bf16[256,512]{1,0:T(8,128)(2,1)} %collective-permute-done.2.their_near_ref, bf16[256,512]{1,0:T(8,128)(2,1)} %collective-permute-done.3.their_far_ref, f32[3,256,128]{2,1,0:T(8,128)S(1)} %shard_map.56.fetched_ref, f32[3,256,128]{2,1,0:T(8,128)S(1)} %copy-done.4, ...), custom_call_target="tpu_custom_call" | custom-call | flops 905969664 | bytes 5046788 | tf_op jit(solution)/shard_map/pallas_call | solution.py:180
  19.6 0.3 collective-permute-start.5
  19.9 1.5 %collective-permute-start.4 = (bf16[1,3,256,128]{3,2,1,0:T(8,128)(2,1)S(1)}, bf16[1,3,256,128]{3,2,1,0:T(8,128)(2,1)S(1)}, u32[]{:S(2)}, u32[]{:S(2)}) collective-permute-start(bf16[1,3,256,128]{3,2,1,0:T(8,128)(2,1)S(1)} %bitcast.15), channel_id=1, source_target_pairs={{2,0},{3,1},{0,2},{1,3},{6,4},{7,5},{4,6},{5,7},{10,8},{11,9},{8,1... | collective-permute-start | bytes 589832 | tf_op jit(solution)/shard_map/ppermute | solution.py:19
  21.4 0.0 collective-permute-done.5
  21.4 0.0 copy-done.2
  21.4 0.8 %shard_map.58.refs_2_ = f32[1,256,128]{2,1,0:T(8,128)S(1)} custom-call(s32[1]{0:T(128)} %bitcast.me_ref, bf16[1,3,256,128]{3,2,1,0:T(8,128)(2,1)S(1)} %bitcast.16, bf16[1,3,256,128]{3,2,1,0:T(8,128)(2,1)S(1)} %bitcast.21, bf16[3,1152,512]{2,1,0:T(8,128)(2,1)S(1)} %bitcast.13), custom_call_target="tpu_custom_call" | custom-call | flops 150994944 | bytes 4063236 | tf_op jit(solution)/shard_map/pallas_call | solution.py:180
  22.2 4.8 %collective-permute-done.4.refs_0_ = bf16[1,3,256,128]{3,2,1,0:T(8,128)(2,1)S(1)} collective-permute-done((bf16[1,3,256,128]{3,2,1,0:T(8,128)(2,1)S(1)}, bf16[1,3,256,128]{3,2,1,0:T(8,128)(2,1)S(1)}, u32[]{:S(2)}, u32[]{:S(2)}) %collective-permute-start.4) | collective-permute-done | bytes 196640 | tf_op jit(solution)/shard_map/ppermute | solution.py:19
  27.0 0.0 collective-permute-start.6
  27.0 1.4 %collective-permute-done.6.refs_1_ = bf16[1,3,256,128]{3,2,1,0:T(8,128)(2,1)S(1)} collective-permute-done((bf16[1,3,256,128]{3,2,1,0:T(8,128)(2,1)S(1)}, bf16[1,3,256,128]{3,2,1,0:T(8,128)(2,1)S(1)}, u32[]{:S(2)}, u32[]{:S(2)}) %collective-permute-start.6) | collective-permute-done | bytes 196640 | tf_op jit(solution)/shard_map/ppermute | solution.py:19
  28.5 0.0 copy-done.7
  28.5 0.8 %shard_map.59 = bf16[1,256,128]{2,1,0:T(8,128)(2,1)S(1)} custom-call(s32[1]{0:T(128)} %bitcast.me_ref, bf16[1,3,256,128]{3,2,1,0:T(8,128)(2,1)S(1)} %collective-permute-done.4.refs_0_, bf16[1,3,256,128]{3,2,1,0:T(8,128)(2,1)S(1)} %collective-permute-done.6.refs_1_, f32[1,256,128]{2,1,0:T(8,128)S(1)} %shard_map.58.refs_2_, ...), custom_call_target="tpu_custom_call" | custom-call | flops 754974720 | bytes 4129284 | tf_op jit(solution)/shard_map/pallas_call | solution.py:180
  29.3 0.7 %copy.6 = bf16[1,128,256]{2,1,0:T(8,128)(2,1)} copy(bf16[1,128,256]{1,2,0:T(8,128)(2,1)S(1)} %bitcast.17) | data formatting | bytes 131072 | tf_op jit(solution)/shard_map/transpose | solution.py:265
Async XLA Ops:
  0.0 13.0 %collective-permute-start = (bf16[256,512]{1,0:T(8,128)(2,1)}, bf16[256,512]{1,0:T(8,128)(2,1)}, u32[]{:S(2)}, u32[]{:S(2)}) collective-permute-start(bf16[256,512]{1,0:T(8,128)(2,1)} %bitcast.18), channel_id=1, source_target_pairs={{28,0},{5,1},{30,2},{7,3},{0,4},{9,5},{2,6},{11,7},{4,8},{13,9},{6... | collective-permute-start | bytes 786440 | tf_op jit(solution)/shard_map/ppermute | solution.py:19
  2.9 11.4 %collective-permute-start.1 = (bf16[256,512]{1,0:T(8,128)(2,1)}, bf16[256,512]{1,0:T(8,128)(2,1)}, u32[]{:S(2)}, u32[]{:S(2)}) collective-permute-start(bf16[256,512]{1,0:T(8,128)(2,1)} %bitcast.19), channel_id=1, source_target_pairs={{24,0},{9,1},{26,2},{11,3},{28,4},{13,5},{30,6},{15,7},{0,8},{17,9... | collective-permute-start | bytes 786440 | tf_op jit(solution)/shard_map/ppermute | solution.py:19
  4.5 2.0 %copy-start = (bf16[3,3,3,128,512]{4,3,2,1,0:T(8,128)(2,1)S(1)}, bf16[3,3,3,128,512]{4,3,2,1,0:T(8,128)(2,1)}, u32[]{:S(2)}) copy-start(bf16[3,3,3,128,512]{4,3,2,1,0:T(8,128)(2,1)} %param.6) | copy-start | bytes 10616836
  6.5 0.9 %copy-start.5 = (bf16[1,4,64,512]{3,2,1,0:T(8,128)(2,1)S(1)}, bf16[1,4,64,512]{3,2,1,0:T(8,128)(2,1)}, u32[]{:S(2)}) copy-start(bf16[1,4,64,512]{3,2,1,0:T(8,128)(2,1)} %param.5) | copy-start | bytes 786436
  7.5 7.3 %copy-start.1 = (bf16[3,3,3,128,512]{4,3,2,1,0:T(8,128)(2,1)S(1)}, bf16[3,3,3,128,512]{4,3,2,1,0:T(8,128)(2,1)}, u32[]{:S(2)}) copy-start(bf16[3,3,3,128,512]{4,3,2,1,0:T(8,128)(2,1)} %param.6) | copy-start | bytes 10616836
  7.5 9.7 %copy-start.6 = (f32[128]{0:T(128)S(1)}, f32[128]{0:T(128)}, u32[]{:S(2)}) copy-start(f32[128]{0:T(128)} %param.7) | copy-start | bytes 1540
  8.7 0.7 %copy-start.3 = (f32[3,256,128]{2,1,0:T(8,128)}, f32[3,256,128]{2,1,0:T(8,128)S(1)}, u32[]{:S(2)}) copy-start(f32[3,256,128]{2,1,0:T(8,128)S(1)} %shard_map.55.part_ref) | copy-start | bytes 1179652
  14.3 2.8 %collective-permute-start.2 = (bf16[256,512]{1,0:T(8,128)(2,1)}, bf16[256,512]{1,0:T(8,128)(2,1)}, u32[]{:S(2)}, u32[]{:S(2)}) collective-permute-start(bf16[256,512]{1,0:T(8,128)(2,1)} %collective-permute-done.near_ref), channel_id=1, source_target_pairs={{1,0},{0,1},{3,2},{2,3},{5,4},{4,5},{7,6},{6,7},{9,8},{8,9},{11,10... | collective-permute-start | bytes 786440 | tf_op jit(solution)/shard_map/ppermute | solution.py:19
  14.5 2.7 %collective-permute-start.3 = (bf16[256,512]{1,0:T(8,128)(2,1)}, bf16[256,512]{1,0:T(8,128)(2,1)}, u32[]{:S(2)}, u32[]{:S(2)}) collective-permute-start(bf16[256,512]{1,0:T(8,128)(2,1)} %collective-permute-done.1.far_ref), channel_id=1, source_target_pairs={{1,0},{0,1},{3,2},{2,3},{5,4},{4,5},{7,6},{6,7},{9,8},{8,9},{11,10... | collective-permute-start | bytes 786440 | tf_op jit(solution)/shard_map/ppermute | solution.py:19
  14.8 2.4 %copy-start.4 = (f32[3,256,128]{2,1,0:T(8,128)S(1)}, f32[3,256,128]{2,1,0:T(8,128)}, u32[]{:S(2)}) copy-start(f32[3,256,128]{2,1,0:T(8,128)} %copy-done.3) | copy-start | bytes 1179652
  17.1 4.3 %copy-start.2 = (bf16[3,3,3,128,512]{4,3,2,1,0:T(8,128)(2,1)S(1)}, bf16[3,3,3,128,512]{4,3,2,1,0:T(8,128)(2,1)}, u32[]{:S(2)}) copy-start(bf16[3,3,3,128,512]{4,3,2,1,0:T(8,128)(2,1)} %param.8) | copy-start | bytes 10616836
  17.2 11.3 %copy-start.7 = (f32[128]{0:T(128)S(1)}, f32[128]{0:T(128)}, u32[]{:S(2)}) copy-start(f32[128]{0:T(128)} %param.9) | copy-start | bytes 1540
  19.6 1.8 %collective-permute-start.5 = (bf16[3,256,128]{2,1,0:T(8,128)(2,1)S(1)}, bf16[3,256,128]{2,1,0:T(8,128)(2,1)S(1)}, u32[]{:S(2)}, u32[]{:S(2)}) collective-permute-start(bf16[3,256,128]{2,1,0:T(8,128)(2,1)S(1)} %shard_map.57), channel_id=1, source_target_pairs={{1,0},{0,1},{3,2},{2,3},{5,4},{4,5},{7,6},{6,7},{9,8},{8,9},{11,10... | collective-permute-start | bytes 589832 | tf_op jit(solution)/shard_map/ppermute | solution.py:19
  19.9 7.1 %collective-permute-start.4 = (bf16[1,3,256,128]{3,2,1,0:T(8,128)(2,1)S(1)}, bf16[1,3,256,128]{3,2,1,0:T(8,128)(2,1)S(1)}, u32[]{:S(2)}, u32[]{:S(2)}) collective-permute-start(bf16[1,3,256,128]{3,2,1,0:T(8,128)(2,1)S(1)} %bitcast.15), channel_id=1, source_target_pairs={{2,0},{3,1},{0,2},{1,3},{6,4},{7,5},{4,6},{5,7},{10,8},{11,9},{8,1... | collective-permute-start | bytes 589832 | tf_op jit(solution)/shard_map/ppermute | solution.py:19
  27.0 1.4 %collective-permute-start.6 = (bf16[1,3,256,128]{3,2,1,0:T(8,128)(2,1)S(1)}, bf16[1,3,256,128]{3,2,1,0:T(8,128)(2,1)S(1)}, u32[]{:S(2)}, u32[]{:S(2)}) collective-permute-start(bf16[1,3,256,128]{3,2,1,0:T(8,128)(2,1)S(1)} %collective-permute-done.4.refs_0_), channel_id=1, source_target_pairs={{1,0},{0,1},{3,2},{2,3},{5,4},{4,5},{7,6},{6,7},{9,8},{8,9},{11,10... | collective-permute-start | bytes 589832 | tf_op jit(solution)/shard_map/ppermute | solution.py:19

commit v16 on v13

--- a/solution.py
+++ b/solution.py
@@ -168,8 +168,11 @@
     pairs = lambda index: [pair for pair in range(count // 2) if pair != index // 2]
     pair_products(acc_ref, full, me, pairs, w_ref, field_ref, outs, True)
     total = spatial_sum(acc_ref, 0, rows_n, cols_n, outs) + part_ref[0]
-    result = jnp.maximum(total + b_ref[...], 0.0)
-    o_ref[0] = result.T.astype(o_ref.dtype)
+    result = jnp.maximum(total + b_ref[...], 0.0).astype(o_ref.dtype)
+    rows = lax.broadcasted_iota(jnp.int32, (outs, outs), 0)
+    eye = (rows == lax.broadcasted_iota(jnp.int32, (outs, outs), 1)).astype(o_ref.dtype)
+    flipped = lax.dot_general(eye, result, (((1,), (1,)), ((), ())), preferred_element_type=jnp.float32)
+    o_ref[0] = flipped.astype(o_ref.dtype)
 
 
 def vmem_call(kernel, out_shape, operands, scratch, flops, smem_first=False):

time: 30.2 us -> 30.2 us (level)
  no operation moved by 1% of the time
where the time goes in v16:
time: 30.2 us; the launch traced here: 30 us
  waiting for transfers between devices  11.1 us (37%)
  Pallas kernels  8.3 us (27%)
  starting transfers between devices  6.81 us (23%)
  local copies, waits for them, and re-layouts  3.71 us (12%)
    ppermute x7, waiting for transfers between devices, gathered_from(): return lax.ppermute(block, ('space', 'chan'), pairs)  11.1 us
    pallas_call x5, Pallas kernels, vmem_call(): pl.pallas_call(kernel, out_shape=out_shape, in_specs=specs, out_specs=pl....  8.3 us
    ppermute x7, starting transfers between devices, gathered_from(): return lax.ppermute(block, ('space', 'chan'), pairs)  6.81 us
    unnamed x16, local copies, waits for them, and re-layouts  3.71 us
  transfers between devices with their start and end apart: 7, of which 4 were waited for; matrix products, arithmetic and copies ran while one was open for 0% of the time, Pallas kernels for 14%

profile of v16, /device:TPU:0, one launch (start us, length us, event | category | flops | bytes accessed | tf_op | source)
XLA Modules:
  0.0 30.0 jit_solution(8925020433145131437)
XLA Ops:
  0.0 2.9 %collective-permute-start = (bf16[256,512]{1,0:T(8,128)(2,1)}, bf16[256,512]{1,0:T(8,128)(2,1)}, u32[]{:S(2)}, u32[]{:S(2)}) collective-permute-start(bf16[256,512]{1,0:T(8,128)(2,1)} %bitcast.16), channel_id=1, source_target_pairs={{28,0},{5,1},{30,2},{7,3},{0,4},{9,5},{2,6},{11,7},{4,8},{13,9},{6... | collective-permute-start | bytes 786440 | tf_op jit(solution)/shard_map/ppermute | solution.py:19
  2.9 1.6 %collective-permute-start.1 = (bf16[256,512]{1,0:T(8,128)(2,1)}, bf16[256,512]{1,0:T(8,128)(2,1)}, u32[]{:S(2)}, u32[]{:S(2)}) collective-permute-start(bf16[256,512]{1,0:T(8,128)(2,1)} %bitcast.17), channel_id=1, source_target_pairs={{24,0},{9,1},{26,2},{11,3},{28,4},{13,5},{30,6},{15,7},{0,8},{17,9... | collective-permute-start | bytes 786440 | tf_op jit(solution)/shard_map/ppermute | solution.py:19
  4.5 0.0 copy-start
  4.5 2.0 %copy-done = bf16[3,3,3,128,512]{4,3,2,1,0:T(8,128)(2,1)S(1)} copy-done((bf16[3,3,3,128,512]{4,3,2,1,0:T(8,128)(2,1)S(1)}, bf16[3,3,3,128,512]{4,3,2,1,0:T(8,128)(2,1)}, u32[]{:S(2)}) %copy-start) | copy-done | bytes 3538968
  6.5 0.0 copy-start.5
  6.5 0.9 %copy-done.5 = bf16[1,4,64,512]{3,2,1,0:T(8,128)(2,1)S(1)} copy-done((bf16[1,4,64,512]{3,2,1,0:T(8,128)(2,1)S(1)}, bf16[1,4,64,512]{3,2,1,0:T(8,128)(2,1)}, u32[]{:S(2)}) %copy-start.5) | copy-done | bytes 262168
  7.5 0.0 copy-start.1
  7.5 0.0 copy-start.6
  7.5 1.2 %shard_map.55.part_ref = f32[3,256,128]{2,1,0:T(8,128)S(1)} custom-call(bf16[256,512]{1,0:T(8,128)(2,1)S(1)} %bitcast.18, bf16[3,1152,512]{2,1,0:T(8,128)(2,1)S(1)} %bitcast.9), custom_call_target="tpu_custom_call" | custom-call | flops 905969664 | bytes 4194304 | tf_op jit(solution)/shard_map/pallas_call | solution.py:183
  8.7 0.0 copy-start.3
  8.7 0.7 %copy-done.3 = f32[3,256,128]{2,1,0:T(8,128)} copy-done((f32[3,256,128]{2,1,0:T(8,128)}, f32[3,256,128]{2,1,0:T(8,128)S(1)}, u32[]{:S(2)}) %copy-start.3) | copy-done | bytes 393240
  9.4 3.6 %collective-permute-done.near_ref = bf16[256,512]{1,0:T(8,128)(2,1)} collective-permute-done((bf16[256,512]{1,0:T(8,128)(2,1)}, bf16[256,512]{1,0:T(8,128)(2,1)}, u32[]{:S(2)}, u32[]{:S(2)}) %collective-permute-start) | collective-permute-done | bytes 262176 | tf_op jit(solution)/shard_map/ppermute | solution.py:19
  13.0 1.3 %collective-permute-done.1.far_ref = bf16[256,512]{1,0:T(8,128)(2,1)} collective-permute-done((bf16[256,512]{1,0:T(8,128)(2,1)}, bf16[256,512]{1,0:T(8,128)(2,1)}, u32[]{:S(2)}, u32[]{:S(2)}) %collective-permute-start.1) | collective-permute-done | bytes 262176 | tf_op jit(solution)/shard_map/ppermute | solution.py:19
  14.3 0.2 collective-permute-start.2
  14.5 0.3 %collective-permute-start.3 = (bf16[256,512]{1,0:T(8,128)(2,1)}, bf16[256,512]{1,0:T(8,128)(2,1)}, u32[]{:S(2)}, u32[]{:S(2)}) collective-permute-start(bf16[256,512]{1,0:T(8,128)(2,1)} %collective-permute-done.1.far_ref), channel_id=1, source_target_pairs={{1,0},{0,1},{3,2},{2,3},{5,4},{4,5},{7,6},{6,7},{9,8},{8,9},{11,10... | collective-permute-start | bytes 786440 | tf_op jit(solution)/shard_map/ppermute | solution.py:19
  14.8 0.0 copy-start.4
  14.8 0.0 copy-done.1
  14.8 2.3 %shard_map.56.fetched_ref = f32[3,256,128]{2,1,0:T(8,128)S(1)} custom-call(s32[1]{0:T(128)} %bitcast.1.odd_ref, bf16[256,512]{1,0:T(8,128)(2,1)} %collective-permute-done.near_ref, bf16[256,512]{1,0:T(8,128)(2,1)} %collective-permute-done.1.far_ref, bf16[3,1152,512]{2,1,0:T(8,128)(2,1)S(1)} %bitcast.10), custom_call_target="tpu_custom_call" | custom-call | flops 905969664 | bytes 4456452 | tf_op jit(solution)/shard_map/pallas_call | solution.py:183
  17.1 0.0 copy-start.2
  17.1 0.0 collective-permute-done.2.their_near_ref
  17.2 0.0 collective-permute-done.3.their_far_ref
  17.2 0.0 copy-done.6
  17.2 0.0 copy-done.4
  17.2 0.0 copy-start.7
  17.2 2.4 %shard_map.57 = bf16[3,256,128]{2,1,0:T(8,128)(2,1)S(1)} custom-call(s32[1]{0:T(128)} %bitcast.1.odd_ref, bf16[256,512]{1,0:T(8,128)(2,1)} %collective-permute-done.2.their_near_ref, bf16[256,512]{1,0:T(8,128)(2,1)} %collective-permute-done.3.their_far_ref, f32[3,256,128]{2,1,0:T(8,128)S(1)} %shard_map.56.fetched_ref, f32[3,256,128]{2,1,0:T(8,128)S(1)} %copy-done.4, ...), custom_call_target="tpu_custom_call" | custom-call | flops 905969664 | bytes 5046788 | tf_op jit(solution)/shard_map/pallas_call | solution.py:183
  19.6 0.3 collective-permute-start.5
  19.9 1.5 %collective-permute-start.4 = (bf16[1,3,256,128]{3,2,1,0:T(8,128)(2,1)S(1)}, bf16[1,3,256,128]{3,2,1,0:T(8,128)(2,1)S(1)}, u32[]{:S(2)}, u32[]{:S(2)}) collective-permute-start(bf16[1,3,256,128]{3,2,1,0:T(8,128)(2,1)S(1)} %bitcast.14), channel_id=1, source_target_pairs={{2,0},{3,1},{0,2},{1,3},{6,4},{7,5},{4,6},{5,7},{10,8},{11,9},{8,1... | collective-permute-start | bytes 589832 | tf_op jit(solution)/shard_map/ppermute | solution.py:19
  21.4 0.0 collective-permute-done.5
  21.4 0.0 copy-done.2
  21.4 0.8 %shard_map.58.refs_2_ = f32[1,256,128]{2,1,0:T(8,128)S(1)} custom-call(s32[1]{0:T(128)} %bitcast.me_ref, bf16[1,3,256,128]{3,2,1,0:T(8,128)(2,1)S(1)} %bitcast.15, bf16[1,3,256,128]{3,2,1,0:T(8,128)(2,1)S(1)} %bitcast.19, bf16[3,1152,512]{2,1,0:T(8,128)(2,1)S(1)} %bitcast.12), custom_call_target="tpu_custom_call" | custom-call | flops 150994944 | bytes 4063236 | tf_op jit(solution)/shard_map/pallas_call | solution.py:183
  22.2 4.8 %collective-permute-done.4.refs_0_ = bf16[1,3,256,128]{3,2,1,0:T(8,128)(2,1)S(1)} collective-permute-done((bf16[1,3,256,128]{3,2,1,0:T(8,128)(2,1)S(1)}, bf16[1,3,256,128]{3,2,1,0:T(8,128)(2,1)S(1)}, u32[]{:S(2)}, u32[]{:S(2)}) %collective-permute-start.4) | collective-permute-done | bytes 196640 | tf_op jit(solution)/shard_map/ppermute | solution.py:19
  27.0 0.0 collective-permute-start.6
  27.0 1.4 %collective-permute-done.6.refs_1_ = bf16[1,3,256,128]{3,2,1,0:T(8,128)(2,1)S(1)} collective-permute-done((bf16[1,3,256,128]{3,2,1,0:T(8,128)(2,1)S(1)}, bf16[1,3,256,128]{3,2,1,0:T(8,128)(2,1)S(1)}, u32[]{:S(2)}, u32[]{:S(2)}) %collective-permute-start.6) | collective-permute-done | bytes 196640 | tf_op jit(solution)/shard_map/ppermute | solution.py:19
  28.5 0.0 copy-done.7
  28.5 1.6 %shard_map.59 = bf16[1,128,256]{2,1,0:T(8,128)(2,1)} custom-call(s32[1]{0:T(128)} %bitcast.me_ref, bf16[1,3,256,128]{3,2,1,0:T(8,128)(2,1)S(1)} %collective-permute-done.4.refs_0_, bf16[1,3,256,128]{3,2,1,0:T(8,128)(2,1)S(1)} %collective-permute-done.6.refs_1_, f32[1,256,128]{2,1,0:T(8,128)S(1)} %shard_map.58.refs_2_, bf16[3,1152,512]{2,1,0:T(8,128)(2,1)S(1)} %bitcast.13, ...), custom_call_target="tpu_custom_call" | custom-call | flops 754974720 | bytes 4129284 | tf_op jit(solution)/shard_map/pallas_call | solution.py:183
Async XLA Ops:
  0.0 13.0 %collective-permute-start = (bf16[256,512]{1,0:T(8,128)(2,1)}, bf16[256,512]{1,0:T(8,128)(2,1)}, u32[]{:S(2)}, u32[]{:S(2)}) collective-permute-start(bf16[256,512]{1,0:T(8,128)(2,1)} %bitcast.16), channel_id=1, source_target_pairs={{28,0},{5,1},{30,2},{7,3},{0,4},{9,5},{2,6},{11,7},{4,8},{13,9},{6... | collective-permute-start | bytes 786440 | tf_op jit(solution)/shard_map/ppermute | solution.py:19
  2.9 11.4 %collective-permute-start.1 = (bf16[256,512]{1,0:T(8,128)(2,1)}, bf16[256,512]{1,0:T(8,128)(2,1)}, u32[]{:S(2)}, u32[]{:S(2)}) collective-permute-start(bf16[256,512]{1,0:T(8,128)(2,1)} %bitcast.17), channel_id=1, source_target_pairs={{24,0},{9,1},{26,2},{11,3},{28,4},{13,5},{30,6},{15,7},{0,8},{17,9... | collective-permute-start | bytes 786440 | tf_op jit(solution)/shard_map/ppermute | solution.py:19
  4.5 2.0 %copy-start = (bf16[3,3,3,128,512]{4,3,2,1,0:T(8,128)(2,1)S(1)}, bf16[3,3,3,128,512]{4,3,2,1,0:T(8,128)(2,1)}, u32[]{:S(2)}) copy-start(bf16[3,3,3,128,512]{4,3,2,1,0:T(8,128)(2,1)} %param.6) | copy-start | bytes 10616836
  6.5 0.9 %copy-start.5 = (bf16[1,4,64,512]{3,2,1,0:T(8,128)(2,1)S(1)}, bf16[1,4,64,512]{3,2,1,0:T(8,128)(2,1)}, u32[]{:S(2)}) copy-start(bf16[1,4,64,512]{3,2,1,0:T(8,128)(2,1)} %param.5) | copy-start | bytes 786436
  7.5 7.3 %copy-start.1 = (bf16[3,3,3,128,512]{4,3,2,1,0:T(8,128)(2,1)S(1)}, bf16[3,3,3,128,512]{4,3,2,1,0:T(8,128)(2,1)}, u32[]{:S(2)}) copy-start(bf16[3,3,3,128,512]{4,3,2,1,0:T(8,128)(2,1)} %param.6) | copy-start | bytes 10616836
  7.5 9.7 %copy-start.6 = (f32[128]{0:T(128)S(1)}, f32[128]{0:T(128)}, u32[]{:S(2)}) copy-start(f32[128]{0:T(128)} %param.7) | copy-start | bytes 1540
  8.7 0.7 %copy-start.3 = (f32[3,256,128]{2,1,0:T(8,128)}, f32[3,256,128]{2,1,0:T(8,128)S(1)}, u32[]{:S(2)}) copy-start(f32[3,256,128]{2,1,0:T(8,128)S(1)} %shard_map.55.part_ref) | copy-start | bytes 1179652
  14.3 2.8 %collective-permute-start.2 = (bf16[256,512]{1,0:T(8,128)(2,1)}, bf16[256,512]{1,0:T(8,128)(2,1)}, u32[]{:S(2)}, u32[]{:S(2)}) collective-permute-start(bf16[256,512]{1,0:T(8,128)(2,1)} %collective-permute-done.near_ref), channel_id=1, source_target_pairs={{1,0},{0,1},{3,2},{2,3},{5,4},{4,5},{7,6},{6,7},{9,8},{8,9},{11,10... | collective-permute-start | bytes 786440 | tf_op jit(solution)/shard_map/ppermute | solution.py:19
  14.5 2.7 %collective-permute-start.3 = (bf16[256,512]{1,0:T(8,128)(2,1)}, bf16[256,512]{1,0:T(8,128)(2,1)}, u32[]{:S(2)}, u32[]{:S(2)}) collective-permute-start(bf16[256,512]{1,0:T(8,128)(2,1)} %collective-permute-done.1.far_ref), channel_id=1, source_target_pairs={{1,0},{0,1},{3,2},{2,3},{5,4},{4,5},{7,6},{6,7},{9,8},{8,9},{11,10... | collective-permute-start | bytes 786440 | tf_op jit(solution)/shard_map/ppermute | solution.py:19
  14.8 2.4 %copy-start.4 = (f32[3,256,128]{2,1,0:T(8,128)S(1)}, f32[3,256,128]{2,1,0:T(8,128)}, u32[]{:S(2)}) copy-start(f32[3,256,128]{2,1,0:T(8,128)} %copy-done.3) | copy-start | bytes 1179652
  17.1 4.3 %copy-start.2 = (bf16[3,3,3,128,512]{4,3,2,1,0:T(8,128)(2,1)S(1)}, bf16[3,3,3,128,512]{4,3,2,1,0:T(8,128)(2,1)}, u32[]{:S(2)}) copy-start(bf16[3,3,3,128,512]{4,3,2,1,0:T(8,128)(2,1)} %param.8) | copy-start | bytes 10616836
  17.2 11.3 %copy-start.7 = (f32[128]{0:T(128)S(1)}, f32[128]{0:T(128)}, u32[]{:S(2)}) copy-start(f32[128]{0:T(128)} %param.9) | copy-start | bytes 1540
  19.6 1.8 %collective-permute-start.5 = (bf16[3,256,128]{2,1,0:T(8,128)(2,1)S(1)}, bf16[3,256,128]{2,1,0:T(8,128)(2,1)S(1)}, u32[]{:S(2)}, u32[]{:S(2)}) collective-permute-start(bf16[3,256,128]{2,1,0:T(8,128)(2,1)S(1)} %shard_map.57), channel_id=1, source_target_pairs={{1,0},{0,1},{3,2},{2,3},{5,4},{4,5},{7,6},{6,7},{9,8},{8,9},{11,10... | collective-permute-start | bytes 589832 | tf_op jit(solution)/shard_map/ppermute | solution.py:19
  19.9 7.1 %collective-permute-start.4 = (bf16[1,3,256,128]{3,2,1,0:T(8,128)(2,1)S(1)}, bf16[1,3,256,128]{3,2,1,0:T(8,128)(2,1)S(1)}, u32[]{:S(2)}, u32[]{:S(2)}) collective-permute-start(bf16[1,3,256,128]{3,2,1,0:T(8,128)(2,1)S(1)} %bitcast.14), channel_id=1, source_target_pairs={{2,0},{3,1},{0,2},{1,3},{6,4},{7,5},{4,6},{5,7},{10,8},{11,9},{8,1... | collective-permute-start | bytes 589832 | tf_op jit(solution)/shard_map/ppermute | solution.py:19
  27.0 1.4 %collective-permute-start.6 = (bf16[1,3,256,128]{3,2,1,0:T(8,128)(2,1)S(1)}, bf16[1,3,256,128]{3,2,1,0:T(8,128)(2,1)S(1)}, u32[]{:S(2)}, u32[]{:S(2)}) collective-permute-start(bf16[1,3,256,128]{3,2,1,0:T(8,128)(2,1)S(1)} %collective-permute-done.4.refs_0_), channel_id=1, source_target_pairs={{1,0},{0,1},{3,2},{2,3},{5,4},{4,5},{7,6},{6,7},{9,8},{8,9},{11,10... | collective-permute-start | bytes 589832 | tf_op jit(solution)/shard_map/ppermute | solution.py:19

commit v17 on v13

--- a/solution.py
+++ b/solution.py
@@ -56,6 +56,35 @@
     return total
 
 
+def spatial_sum_lanes(acc_ref, rows_n, cols_n, outs):
+    cells = rows_n * cols_n
+    column = lax.broadcasted_iota(jnp.int32, (outs, cells), 1) % cols_n
+    total = None
+    for col_tap in range(3):
+        shifted = None
+        for row_tap in range(3):
+            tap = row_tap * 3 + col_tap
+            part = acc_ref[pl.ds(tap * outs, outs), :]
+            amount = ((1 - row_tap) * cols_n) % cells
+            if amount:
+                part = pltpu.roll(part, amount, 1)
+            shifted = part if shifted is None else shifted + part
+        if col_tap == 0:
+            shifted = jnp.where(
+                column == 0,
+                pltpu.roll(shifted, (1 - cols_n) % cells, 1),
+                pltpu.roll(shifted, 1, 1),
+            )
+        elif col_tap == 2:
+            shifted = jnp.where(
+                column == cols_n - 1,
+                pltpu.roll(shifted, cols_n - 1, 1),
+                pltpu.roll(shifted, cells - 1, 1),
+            )
+        total = shifted if total is None else total + shifted
+    return total
+
+
 def tap_product(plane, w_ref, depth_tap):
     return lax.dot_general(
         plane, w_ref[depth_tap], (((1,), (1,)), ((), ())), preferred_element_type=jnp.float32
@@ -127,13 +156,13 @@
                     field_ref[:, :, pl.ds(half * outs, outs)] = ref[position]
                 for depth_tap in range(3):
                     term = lax.dot_general(
-                        field_ref[depth_tap], w_ref[depth_tap, :, pl.ds(pair * width, width)],
+                        w_ref[depth_tap, :, pl.ds(pair * width, width)], field_ref[depth_tap],
                         (((1,), (1,)), ((), ())), preferred_element_type=jnp.float32,
                     )
                     if started:
-                        acc_ref[0] += term
+                        acc_ref[...] += term
                     else:
-                        acc_ref[0] = term
+                        acc_ref[...] = term
                         started = True
 
 
@@ -148,28 +177,28 @@
 def own_pair_kernel(rows_n, cols_n, count, layout, me_ref, *refs):
     inputs = refs[:len(layout)]
     w_ref, o_ref, field_ref, acc_ref = refs[len(layout):]
-    outs = o_ref.shape[2]
+    outs = o_ref.shape[1]
     me = me_ref[0]
     blocks = held_blocks(inputs, layout)
     full = {j: None for j in range(count)}
     full.update(blocks)
     pair_products(acc_ref, full, me, lambda index: [index // 2], w_ref, field_ref, outs, True)
-    o_ref[0] = spatial_sum(acc_ref, 0, rows_n, cols_n, outs)
+    o_ref[0] = spatial_sum_lanes(acc_ref, rows_n, cols_n, outs)
 
 
 def second_kernel(rows_n, cols_n, count, layout, me_ref, *refs):
     inputs = refs[:len(layout)]
     part_ref, w_ref, b_ref, o_ref, field_ref, acc_ref = refs[len(layout):]
-    outs = b_ref.shape[1]
+    outs = b_ref.shape[0]
     me = me_ref[0]
     blocks = held_blocks(inputs, layout)
     full = {j: None for j in range(count)}
     full.update(blocks)
     pairs = lambda index: [pair for pair in range(count // 2) if pair != index // 2]
     pair_products(acc_ref, full, me, pairs, w_ref, field_ref, outs, True)
-    total = spatial_sum(acc_ref, 0, rows_n, cols_n, outs) + part_ref[0]
+    total = spatial_sum_lanes(acc_ref, rows_n, cols_n, outs) + part_ref[0]
     result = jnp.maximum(total + b_ref[...], 0.0)
-    o_ref[0] = result.T.astype(o_ref.dtype)
+    o_ref[0] = result.astype(o_ref.dtype)
 
 
 def vmem_call(kernel, out_shape, operands, scratch, flops, smem_first=False):
@@ -241,9 +270,9 @@
     me_flag = me.astype(jnp.int32).reshape(1)
     own_pair = vmem_call(
         functools.partial(own_pair_kernel, rows_n, cols_n, chans, ((0,), (1,))),
-        jax.ShapeDtypeStruct((1, cells, outs), jnp.float32),
+        jax.ShapeDtypeStruct((1, outs, cells), jnp.float32),
         [me_flag, hidden[None], partner[None], two_stack],
-        [pltpu.VMEM((3, cells, 2 * outs), jnp.bfloat16), pltpu.VMEM((1, cells, 9 * outs), jnp.float32)],
+        [pltpu.VMEM((3, cells, 2 * outs), jnp.bfloat16), pltpu.VMEM((9 * outs, cells), jnp.float32)],
         2 * tap_flops // chans,
         smem_first=True,
     )
@@ -257,8 +286,8 @@
     output = vmem_call(
         functools.partial(second_kernel, rows_n, cols_n, chans, layout),
         jax.ShapeDtypeStruct((1, outs, cells), jnp.bfloat16),
-        [me_flag] + [arr for arr, _ in held] + [own_pair, two_stack, bias_two.reshape(1, outs)],
-        [pltpu.VMEM((3, cells, 2 * outs), jnp.bfloat16), pltpu.VMEM((1, cells, 9 * outs), jnp.float32)],
+        [me_flag] + [arr for arr, _ in held] + [own_pair, two_stack, bias_two.reshape(outs, 1)],
+        [pltpu.VMEM((3, cells, 2 * outs), jnp.bfloat16), pltpu.VMEM((9 * outs, cells), jnp.float32)],
         3 * tap_flops - 2 * tap_flops // chans,
         smem_first=True,
     )

time: 30.2 us -> 33.8 us (1.12)
  local copies, waits for them, and re-layouts: 3.71 us -> 6.84 us
  Pallas kernels: 8.23 us -> 10.1 us
  waiting for transfers between devices: 11.1 us -> 9.72 us
    unnamed x16 -> x24, local copies, waits for them, and re-layouts: 3.71 us -> 6.1 us
    pallas_call x5, Pallas kernels: 8.23 us -> 10.1 us  [vmem_call(): pl.pallas_call(kernel, out_shape=out_shape, in_specs=specs, out_specs=pl....]
    ppermute x7, waiting for transfers between devices: 11.1 us -> 9.72 us  [gathered_from(): return lax.ppermute(block, ('space', 'chan'), pairs)]
    reshape x0 -> x1, local copies, waits for them, and re-layouts: none -> 0.74 us  [per_device(): bias_two.reshape(outs, 1)]
  transfers between devices with their start and end apart: 7 -> 7, of which waited for: 4 -> 4; matrix products, arithmetic and copies ran while one was open for 0% -> 2% of each run, Pallas kernels for 14% -> 14%
where the time goes in v17:
time: 33.8 us; the launch traced here: 33.5 us
  Pallas kernels  10.1 us (30%)
  waiting for transfers between devices  9.72 us (29%)
  local copies, waits for them, and re-layouts  6.84 us (20%)
  starting transfers between devices  6.81 us (20%)
    pallas_call x5, Pallas kernels, vmem_call(): pl.pallas_call(kernel, out_shape=out_shape, in_specs=specs, out_specs=pl....  10.1 us
    ppermute x7, waiting for transfers between devices, gathered_from(): return lax.ppermute(block, ('space', 'chan'), pairs)  9.72 us
    ppermute x7, starting transfers between devices, gathered_from(): return lax.ppermute(block, ('space', 'chan'), pairs)  6.81 us
    unnamed x24, local copies, waits for them, and re-layouts  6.1 us
    reshape x1, local copies, waits for them, and re-layouts, per_device(): bias_two.reshape(outs, 1)  0.74 us
  transfers between devices with their start and end apart: 7, of which 4 were waited for; matrix products, arithmetic and copies ran while one was open for 2% of the time, Pallas kernels for 14%

profile of v17, /device:TPU:0, one launch (start us, length us, event | category | flops | bytes accessed | tf_op | source)
XLA Modules:
  0.0 33.5 jit_solution(11276782574976878444)
XLA Ops:
  0.0 2.9 %collective-permute-start = (bf16[256,512]{1,0:T(8,128)(2,1)}, bf16[256,512]{1,0:T(8,128)(2,1)}, u32[]{:S(2)}, u32[]{:S(2)}) collective-permute-start(bf16[256,512]{1,0:T(8,128)(2,1)} %bitcast.16), channel_id=1, source_target_pairs={{28,0},{5,1},{30,2},{7,3},{0,4},{9,5},{2,6},{11,7},{4,8},{13,9},{6... | collective-permute-start | bytes 786440 | tf_op jit(solution)/shard_map/ppermute | solution.py:19
  2.9 1.6 %collective-permute-start.1 = (bf16[256,512]{1,0:T(8,128)(2,1)}, bf16[256,512]{1,0:T(8,128)(2,1)}, u32[]{:S(2)}, u32[]{:S(2)}) collective-permute-start(bf16[256,512]{1,0:T(8,128)(2,1)} %bitcast.17), channel_id=1, source_target_pairs={{24,0},{9,1},{26,2},{11,3},{28,4},{13,5},{30,6},{15,7},{0,8},{17,9... | collective-permute-start | bytes 786440 | tf_op jit(solution)/shard_map/ppermute | solution.py:19
  4.5 0.0 copy-start
  4.5 2.0 %copy-done = bf16[3,3,3,128,512]{4,3,2,1,0:T(8,128)(2,1)S(1)} copy-done((bf16[3,3,3,128,512]{4,3,2,1,0:T(8,128)(2,1)S(1)}, bf16[3,3,3,128,512]{4,3,2,1,0:T(8,128)(2,1)}, u32[]{:S(2)}) %copy-start) | copy-done | bytes 3538968
  6.5 0.0 copy-start.9
  6.5 0.9 %copy-done.9 = bf16[1,4,64,512]{3,2,1,0:T(8,128)(2,1)S(1)} copy-done((bf16[1,4,64,512]{3,2,1,0:T(8,128)(2,1)S(1)}, bf16[1,4,64,512]{3,2,1,0:T(8,128)(2,1)}, u32[]{:S(2)}) %copy-start.9) | copy-done | bytes 262168
  7.5 0.0 copy-start.1
  7.5 0.0 copy-start.10
  7.5 1.2 %shard_map.55.part_ref = f32[3,256,128]{2,1,0:T(8,128)S(1)} custom-call(bf16[256,512]{1,0:T(8,128)(2,1)S(1)} %bitcast.18, bf16[3,1152,512]{2,1,0:T(8,128)(2,1)S(1)} %bitcast.9), custom_call_target="tpu_custom_call" | custom-call | flops 905969664 | bytes 4194304 | tf_op jit(solution)/shard_map/pallas_call | solution.py:209
  8.7 0.0 copy-start.4
  8.7 0.7 %copy-done.4 = f32[3,256,128]{2,1,0:T(8,128)} copy-done((f32[3,256,128]{2,1,0:T(8,128)}, f32[3,256,128]{2,1,0:T(8,128)S(1)}, u32[]{:S(2)}) %copy-start.4) | copy-done | bytes 393240
  9.5 3.6 %collective-permute-done.near_ref = bf16[256,512]{1,0:T(8,128)(2,1)} collective-permute-done((bf16[256,512]{1,0:T(8,128)(2,1)}, bf16[256,512]{1,0:T(8,128)(2,1)}, u32[]{:S(2)}, u32[]{:S(2)}) %collective-permute-start) | collective-permute-done | bytes 262176 | tf_op jit(solution)/shard_map/ppermute | solution.py:19
  13.0 1.3 %collective-permute-done.1.far_ref = bf16[256,512]{1,0:T(8,128)(2,1)} collective-permute-done((bf16[256,512]{1,0:T(8,128)(2,1)}, bf16[256,512]{1,0:T(8,128)(2,1)}, u32[]{:S(2)}, u32[]{:S(2)}) %collective-permute-start.1) | collective-permute-done | bytes 262176 | tf_op jit(solution)/shard_map/ppermute | solution.py:19
  14.3 0.2 collective-permute-start.2
  14.5 0.3 collective-permute-start.3
  14.8 0.0 copy-start.5
  14.8 0.0 copy-done.1
  14.8 2.3 %shard_map.56.fetched_ref = f32[3,256,128]{2,1,0:T(8,128)S(1)} custom-call(s32[1]{0:T(128)} %bitcast.1.odd_ref, bf16[256,512]{1,0:T(8,128)(2,1)} %collective-permute-done.near_ref, bf16[256,512]{1,0:T(8,128)(2,1)} %collective-permute-done.1.far_ref, bf16[3,1152,512]{2,1,0:T(8,128)(2,1)S(1)} %bitcast.10), custom_call_target="tpu_custom_call" | custom-call | flops 905969664 | bytes 4456452 | tf_op jit(solution)/shard_map/pallas_call | solution.py:209
  17.1 0.0 copy-start.2
  17.1 0.0 collective-permute-done.2.their_near_ref
  17.2 0.0 collective-permute-done.3.their_far_ref
  17.2 0.0 copy-done.10
  17.2 0.0 copy-done.5
  17.2 0.0 copy-start.11
  17.2 2.4 %shard_map.57 = bf16[3,256,128]{2,1,0:T(8,128)(2,1)S(1)} custom-call(s32[1]{0:T(128)} %bitcast.1.odd_ref, bf16[256,512]{1,0:T(8,128)(2,1)} %collective-permute-done.2.their_near_ref, bf16[256,512]{1,0:T(8,128)(2,1)} %collective-permute-done.3.their_far_ref, f32[3,256,128]{2,1,0:T(8,128)S(1)} %shard_map.56.fetched_ref, f32[3,256,128]{2,1,0:T(8,128)S(1)} %copy-done.5, ...), custom_call_target="tpu_custom_call" | custom-call | flops 905969664 | bytes 5046788 | tf_op jit(solution)/shard_map/pallas_call | solution.py:209
  19.6 0.0 copy-start.3
  19.6 0.3 collective-permute-start.5
  19.9 1.5 %collective-permute-start.4 = (bf16[1,3,256,128]{3,2,1,0:T(8,128)(2,1)S(1)}, bf16[1,3,256,128]{3,2,1,0:T(8,128)(2,1)}, u32[]{:S(2)}, u32[]{:S(2)}) collective-permute-start(bf16[1,3,256,128]{3,2,1,0:T(8,128)(2,1)S(1)} %bitcast.14), channel_id=1, source_target_pairs={{2,0},{3,1},{0,2},{1,3},{6,4},{7,5},{4,6},{5,7},{10,8},{11,9},{8,1... | collective-permute-start | bytes 589832 | tf_op jit(solution)/shard_map/ppermute | solution.py:19
  21.4 0.0 collective-permute-done.5
  21.4 0.0 copy-done.2
  21.4 1.2 %shard_map.58.refs_2_ = f32[1,128,256]{2,1,0:T(8,128)S(1)} custom-call(s32[1]{0:T(128)} %bitcast.me_ref, bf16[1,3,256,128]{3,2,1,0:T(8,128)(2,1)S(1)} %bitcast.15, bf16[1,3,256,128]{3,2,1,0:T(8,128)(2,1)S(1)} %bitcast.19, bf16[3,1152,512]{2,1,0:T(8,128)(2,1)S(1)} %bitcast.12), custom_call_target="tpu_custom_call" | custom-call | flops 150994944 | bytes 4063236 | tf_op jit(solution)/shard_map/pallas_call | solution.py:209
  22.7 0.0 copy-start.6
  22.7 0.6 %copy-done.6 = f32[1,128,256]{2,1,0:T(8,128)} copy-done((f32[1,128,256]{2,1,0:T(8,128)}, f32[1,128,256]{2,1,0:T(8,128)S(1)}, u32[]{:S(2)}) %copy-start.6) | copy-done | bytes 131096
  23.3 3.8 %collective-permute-done.4.refs_0_ = bf16[1,3,256,128]{3,2,1,0:T(8,128)(2,1)} collective-permute-done((bf16[1,3,256,128]{3,2,1,0:T(8,128)(2,1)S(1)}, bf16[1,3,256,128]{3,2,1,0:T(8,128)(2,1)}, u32[]{:S(2)}, u32[]{:S(2)}) %collective-permute-start.4) | collective-permute-done | bytes 196640 | tf_op jit(solution)/shard_map/ppermute | solution.py:19
  27.1 0.0 collective-permute-start.6
  27.1 0.0 copy-done.11
  27.1 0.7 %copy.6.refs_4_ = f32[128,1]{1,0:T(8,128)} copy(f32[128,1]{0,1:T(1,128)S(1)} %bitcast.21) | data formatting | bytes 1024 | tf_op jit(solution)/shard_map/reshape | solution.py:289
  27.9 1.0 %collective-permute-done.6.refs_1_ = bf16[1,3,256,128]{3,2,1,0:T(8,128)(2,1)} collective-permute-done((bf16[1,3,256,128]{3,2,1,0:T(8,128)(2,1)}, bf16[1,3,256,128]{3,2,1,0:T(8,128)(2,1)}, u32[]{:S(2)}, u32[]{:S(2)}) %collective-permute-start.6) | collective-permute-done | bytes 196640 | tf_op jit(solution)/shard_map/ppermute | solution.py:19
  28.9 0.0 copy-done.3
  28.9 0.0 copy-start.7
  28.9 0.9 %copy-done.7 = f32[1,128,256]{2,1,0:T(8,128)S(1)} copy-done((f32[1,128,256]{2,1,0:T(8,128)S(1)}, f32[1,128,256]{2,1,0:T(8,128)}, u32[]{:S(2)}) %copy-start.7) | copy-done | bytes 131096
  29.8 0.0 copy-start.8
  29.8 0.8 %copy-done.8 = f32[128,1]{1,0:T(8,128)S(1)} copy-done((f32[128,1]{1,0:T(8,128)S(1)}, f32[128,1]{1,0:T(8,128)}, u32[]{:S(2)}) %copy-start.8) | copy-done | bytes 536
  30.7 2.9 %shard_map.59 = bf16[1,128,256]{2,1,0:T(8,128)(2,1)} custom-call(s32[1]{0:T(128)} %bitcast.me_ref, bf16[1,3,256,128]{3,2,1,0:T(8,128)(2,1)} %collective-permute-done.4.refs_0_, bf16[1,3,256,128]{3,2,1,0:T(8,128)(2,1)} %collective-permute-done.6.refs_1_, f32[1,128,256]{2,1,0:T(8,128)S(1)} %copy-done.7, bf16[3,1152,512]{2,1,0:T(8,128)(2,1)S(1)} %bitcast.13, ...), custom_call_target="tpu_custom_call" | custom-call | flops 754974720 | bytes 4129284 | tf_op jit(solution)/shard_map/pallas_call | solution.py:209
Async XLA Ops:
  0.0 13.0 %collective-permute-start = (bf16[256,512]{1,0:T(8,128)(2,1)}, bf16[256,512]{1,0:T(8,128)(2,1)}, u32[]{:S(2)}, u32[]{:S(2)}) collective-permute-start(bf16[256,512]{1,0:T(8,128)(2,1)} %bitcast.16), channel_id=1, source_target_pairs={{28,0},{5,1},{30,2},{7,3},{0,4},{9,5},{2,6},{11,7},{4,8},{13,9},{6... | collective-permute-start | bytes 786440 | tf_op jit(solution)/shard_map/ppermute | solution.py:19
  2.9 11.4 %collective-permute-start.1 = (bf16[256,512]{1,0:T(8,128)(2,1)}, bf16[256,512]{1,0:T(8,128)(2,1)}, u32[]{:S(2)}, u32[]{:S(2)}) collective-permute-start(bf16[256,512]{1,0:T(8,128)(2,1)} %bitcast.17), channel_id=1, source_target_pairs={{24,0},{9,1},{26,2},{11,3},{28,4},{13,5},{30,6},{15,7},{0,8},{17,9... | collective-permute-start | bytes 786440 | tf_op jit(solution)/shard_map/ppermute | solution.py:19
  4.5 2.0 %copy-start = (bf16[3,3,3,128,512]{4,3,2,1,0:T(8,128)(2,1)S(1)}, bf16[3,3,3,128,512]{4,3,2,1,0:T(8,128)(2,1)}, u32[]{:S(2)}) copy-start(bf16[3,3,3,128,512]{4,3,2,1,0:T(8,128)(2,1)} %param.6) | copy-start | bytes 10616836
  6.5 0.9 %copy-start.9 = (bf16[1,4,64,512]{3,2,1,0:T(8,128)(2,1)S(1)}, bf16[1,4,64,512]{3,2,1,0:T(8,128)(2,1)}, u32[]{:S(2)}) copy-start(bf16[1,4,64,512]{3,2,1,0:T(8,128)(2,1)} %param.5) | copy-start | bytes 786436
  7.5 7.3 %copy-start.1 = (bf16[3,3,3,128,512]{4,3,2,1,0:T(8,128)(2,1)S(1)}, bf16[3,3,3,128,512]{4,3,2,1,0:T(8,128)(2,1)}, u32[]{:S(2)}) copy-start(bf16[3,3,3,128,512]{4,3,2,1,0:T(8,128)(2,1)} %param.6) | copy-start | bytes 10616836
  7.5 9.7 %copy-start.10 = (f32[128]{0:T(128)S(1)}, f32[128]{0:T(128)}, u32[]{:S(2)}) copy-start(f32[128]{0:T(128)} %param.7) | copy-start | bytes 1540
  8.7 0.8 %copy-start.4 = (f32[3,256,128]{2,1,0:T(8,128)}, f32[3,256,128]{2,1,0:T(8,128)S(1)}, u32[]{:S(2)}) copy-start(f32[3,256,128]{2,1,0:T(8,128)S(1)} %shard_map.55.part_ref) | copy-start | bytes 1179652
  14.3 2.8 %collective-permute-start.2 = (bf16[256,512]{1,0:T(8,128)(2,1)}, bf16[256,512]{1,0:T(8,128)(2,1)}, u32[]{:S(2)}, u32[]{:S(2)}) collective-permute-start(bf16[256,512]{1,0:T(8,128)(2,1)} %collective-permute-done.near_ref), channel_id=1, source_target_pairs={{1,0},{0,1},{3,2},{2,3},{5,4},{4,5},{7,6},{6,7},{9,8},{8,9},{11,10... | collective-permute-start | bytes 786440 | tf_op jit(solution)/shard_map/ppermute | solution.py:19
  14.5 2.7 %collective-permute-start.3 = (bf16[256,512]{1,0:T(8,128)(2,1)}, bf16[256,512]{1,0:T(8,128)(2,1)}, u32[]{:S(2)}, u32[]{:S(2)}) collective-permute-start(bf16[256,512]{1,0:T(8,128)(2,1)} %collective-permute-done.1.far_ref), channel_id=1, source_target_pairs={{1,0},{0,1},{3,2},{2,3},{5,4},{4,5},{7,6},{6,7},{9,8},{8,9},{11,10... | collective-permute-start | bytes 786440 | tf_op jit(solution)/shard_map/ppermute | solution.py:19
  14.8 2.4 %copy-start.5 = (f32[3,256,128]{2,1,0:T(8,128)S(1)}, f32[3,256,128]{2,1,0:T(8,128)}, u32[]{:S(2)}) copy-start(f32[3,256,128]{2,1,0:T(8,128)} %copy-done.4) | copy-start | bytes 1179652
  17.1 4.3 %copy-start.2 = (bf16[3,3,3,128,512]{4,3,2,1,0:T(8,128)(2,1)S(1)}, bf16[3,3,3,128,512]{4,3,2,1,0:T(8,128)(2,1)}, u32[]{:S(2)}) copy-start(bf16[3,3,3,128,512]{4,3,2,1,0:T(8,128)(2,1)} %param.8) | copy-start | bytes 10616836
  17.2 10.0 %copy-start.11 = (f32[128]{0:T(128)S(1)}, f32[128]{0:T(128)}, u32[]{:S(2)}) copy-start(f32[128]{0:T(128)} %param.9) | copy-start | bytes 1540
  19.6 9.3 %copy-start.3 = (bf16[3,3,3,128,512]{4,3,2,1,0:T(8,128)(2,1)S(1)}, bf16[3,3,3,128,512]{4,3,2,1,0:T(8,128)(2,1)}, u32[]{:S(2)}) copy-start(bf16[3,3,3,128,512]{4,3,2,1,0:T(8,128)(2,1)} %param.8) | copy-start | bytes 10616836
  19.6 1.8 %collective-permute-start.5 = (bf16[3,256,128]{2,1,0:T(8,128)(2,1)S(1)}, bf16[3,256,128]{2,1,0:T(8,128)(2,1)S(1)}, u32[]{:S(2)}, u32[]{:S(2)}) collective-permute-start(bf16[3,256,128]{2,1,0:T(8,128)(2,1)S(1)} %shard_map.57), channel_id=1, source_target_pairs={{1,0},{0,1},{3,2},{2,3},{5,4},{4,5},{7,6},{6,7},{9,8},{8,9},{11,10... | collective-permute-start | bytes 589832 | tf_op jit(solution)/shard_map/ppermute | solution.py:19
  19.9 7.2 %collective-permute-start.4 = (bf16[1,3,256,128]{3,2,1,0:T(8,128)(2,1)S(1)}, bf16[1,3,256,128]{3,2,1,0:T(8,128)(2,1)}, u32[]{:S(2)}, u32[]{:S(2)}) collective-permute-start(bf16[1,3,256,128]{3,2,1,0:T(8,128)(2,1)S(1)} %bitcast.14), channel_id=1, source_target_pairs={{2,0},{3,1},{0,2},{1,3},{6,4},{7,5},{4,6},{5,7},{10,8},{11,9},{8,1... | collective-permute-start | bytes 589832 | tf_op jit(solution)/shard_map/ppermute | solution.py:19
  22.7 0.6 %copy-start.6 = (f32[1,128,256]{2,1,0:T(8,128)}, f32[1,128,256]{2,1,0:T(8,128)S(1)}, u32[]{:S(2)}) copy-start(f32[1,128,256]{2,1,0:T(8,128)S(1)} %shard_map.58.refs_2_) | copy-start | bytes 393220
  27.1 1.8 %collective-permute-start.6 = (bf16[1,3,256,128]{3,2,1,0:T(8,128)(2,1)}, bf16[1,3,256,128]{3,2,1,0:T(8,128)(2,1)}, u32[]{:S(2)}, u32[]{:S(2)}) collective-permute-start(bf16[1,3,256,128]{3,2,1,0:T(8,128)(2,1)} %collective-permute-done.4.refs_0_), channel_id=1, source_target_pairs={{1,0},{0,1},{3,2},{2,3},{5,4},{4,5},{7,6},{6,7},{9,8},{8,9},{11,10... | collective-permute-start | bytes 589832 | tf_op jit(solution)/shard_map/ppermute | solution.py:19
  28.9 0.9 %copy-start.7 = (f32[1,128,256]{2,1,0:T(8,128)S(1)}, f32[1,128,256]{2,1,0:T(8,128)}, u32[]{:S(2)}) copy-start(f32[1,128,256]{2,1,0:T(8,128)} %copy-done.6) | copy-start | bytes 393220
  29.8 0.8 %copy-start.8 = (f32[128,1]{1,0:T(8,128)S(1)}, f32[128,1]{1,0:T(8,128)}, u32[]{:S(2)}) copy-start(f32[128,1]{1,0:T(8,128)} %copy.6.refs_4_) | copy-start | bytes 1540

commit v18 on v13

--- a/solution.py
+++ b/solution.py
@@ -169,7 +169,7 @@
     pair_products(acc_ref, full, me, pairs, w_ref, field_ref, outs, True)
     total = spatial_sum(acc_ref, 0, rows_n, cols_n, outs) + part_ref[0]
     result = jnp.maximum(total + b_ref[...], 0.0)
-    o_ref[0] = result.T.astype(o_ref.dtype)
+    o_ref[0] = result.astype(o_ref.dtype).T
 
 
 def vmem_call(kernel, out_shape, operands, scratch, flops, smem_first=False):

time: 30.2 us -> 30.1 us (level)
  no operation moved by 1% of the time
where the time goes in v18:
time: 30.1 us; the launch traced here: 29.9 us
  waiting for transfers between devices  11.1 us (37%)
  Pallas kernels  8.22 us (27%)
  starting transfers between devices  6.81 us (23%)
  local copies, waits for them, and re-layouts  3.71 us (12%)
    ppermute x7, waiting for transfers between devices, gathered_from(): return lax.ppermute(block, ('space', 'chan'), pairs)  11.1 us
    pallas_call x5, Pallas kernels, vmem_call(): pl.pallas_call(kernel, out_shape=out_shape, in_specs=specs, out_specs=pl....  8.22 us
    ppermute x7, starting transfers between devices, gathered_from(): return lax.ppermute(block, ('space', 'chan'), pairs)  6.81 us
    unnamed x16, local copies, waits for them, and re-layouts  3.71 us
  transfers between devices with their start and end apart: 7, of which 4 were waited for; matrix products, arithmetic and copies ran while one was open for 0% of the time, Pallas kernels for 14%

profile of v18, /device:TPU:0, one launch (start us, length us, event | category | flops | bytes accessed | tf_op | source)
XLA Modules:
  0.0 29.9 jit_solution(567796833545521127)
XLA Ops:
  0.0 2.9 %collective-permute-start = (bf16[256,512]{1,0:T(8,128)(2,1)}, bf16[256,512]{1,0:T(8,128)(2,1)}, u32[]{:S(2)}, u32[]{:S(2)}) collective-permute-start(bf16[256,512]{1,0:T(8,128)(2,1)} %bitcast.16), channel_id=1, source_target_pairs={{28,0},{5,1},{30,2},{7,3},{0,4},{9,5},{2,6},{11,7},{4,8},{13,9},{6... | collective-permute-start | bytes 786440 | tf_op jit(solution)/shard_map/ppermute | solution.py:19
  2.9 1.6 %collective-permute-start.1 = (bf16[256,512]{1,0:T(8,128)(2,1)}, bf16[256,512]{1,0:T(8,128)(2,1)}, u32[]{:S(2)}, u32[]{:S(2)}) collective-permute-start(bf16[256,512]{1,0:T(8,128)(2,1)} %bitcast.17), channel_id=1, source_target_pairs={{24,0},{9,1},{26,2},{11,3},{28,4},{13,5},{30,6},{15,7},{0,8},{17,9... | collective-permute-start | bytes 786440 | tf_op jit(solution)/shard_map/ppermute | solution.py:19
  4.5 0.0 copy-start
  4.5 2.0 %copy-done = bf16[3,3,3,128,512]{4,3,2,1,0:T(8,128)(2,1)S(1)} copy-done((bf16[3,3,3,128,512]{4,3,2,1,0:T(8,128)(2,1)S(1)}, bf16[3,3,3,128,512]{4,3,2,1,0:T(8,128)(2,1)}, u32[]{:S(2)}) %copy-start) | copy-done | bytes 3538968
  6.5 0.0 copy-start.5
  6.5 0.9 %copy-done.5 = bf16[1,4,64,512]{3,2,1,0:T(8,128)(2,1)S(1)} copy-done((bf16[1,4,64,512]{3,2,1,0:T(8,128)(2,1)S(1)}, bf16[1,4,64,512]{3,2,1,0:T(8,128)(2,1)}, u32[]{:S(2)}) %copy-start.5) | copy-done | bytes 262168
  7.5 0.0 copy-start.1
  7.5 0.0 copy-start.6
  7.5 1.2 %shard_map.55.part_ref = f32[3,256,128]{2,1,0:T(8,128)S(1)} custom-call(bf16[256,512]{1,0:T(8,128)(2,1)S(1)} %bitcast.18, bf16[3,1152,512]{2,1,0:T(8,128)(2,1)S(1)} %bitcast.9), custom_call_target="tpu_custom_call" | custom-call | flops 905969664 | bytes 4194304 | tf_op jit(solution)/shard_map/pallas_call | solution.py:180
  8.7 0.0 copy-start.3
  8.7 0.7 %copy-done.3 = f32[3,256,128]{2,1,0:T(8,128)} copy-done((f32[3,256,128]{2,1,0:T(8,128)}, f32[3,256,128]{2,1,0:T(8,128)S(1)}, u32[]{:S(2)}) %copy-start.3) | copy-done | bytes 393240
  9.4 3.6 %collective-permute-done.near_ref = bf16[256,512]{1,0:T(8,128)(2,1)} collective-permute-done((bf16[256,512]{1,0:T(8,128)(2,1)}, bf16[256,512]{1,0:T(8,128)(2,1)}, u32[]{:S(2)}, u32[]{:S(2)}) %collective-permute-start) | collective-permute-done | bytes 262176 | tf_op jit(solution)/shard_map/ppermute | solution.py:19
  13.0 1.3 %collective-permute-done.1.far_ref = bf16[256,512]{1,0:T(8,128)(2,1)} collective-permute-done((bf16[256,512]{1,0:T(8,128)(2,1)}, bf16[256,512]{1,0:T(8,128)(2,1)}, u32[]{:S(2)}, u32[]{:S(2)}) %collective-permute-start.1) | collective-permute-done | bytes 262176 | tf_op jit(solution)/shard_map/ppermute | solution.py:19
  14.3 0.2 collective-permute-start.2
  14.5 0.3 %collective-permute-start.3 = (bf16[256,512]{1,0:T(8,128)(2,1)}, bf16[256,512]{1,0:T(8,128)(2,1)}, u32[]{:S(2)}, u32[]{:S(2)}) collective-permute-start(bf16[256,512]{1,0:T(8,128)(2,1)} %collective-permute-done.1.far_ref), channel_id=1, source_target_pairs={{1,0},{0,1},{3,2},{2,3},{5,4},{4,5},{7,6},{6,7},{9,8},{8,9},{11,10... | collective-permute-start | bytes 786440 | tf_op jit(solution)/shard_map/ppermute | solution.py:19
  14.8 0.0 copy-start.4
  14.8 0.0 copy-done.1
  14.8 2.3 %shard_map.56.fetched_ref = f32[3,256,128]{2,1,0:T(8,128)S(1)} custom-call(s32[1]{0:T(128)} %bitcast.1.odd_ref, bf16[256,512]{1,0:T(8,128)(2,1)} %collective-permute-done.near_ref, bf16[256,512]{1,0:T(8,128)(2,1)} %collective-permute-done.1.far_ref, bf16[3,1152,512]{2,1,0:T(8,128)(2,1)S(1)} %bitcast.10), custom_call_target="tpu_custom_call" | custom-call | flops 905969664 | bytes 4456452 | tf_op jit(solution)/shard_map/pallas_call | solution.py:180
  17.1 0.0 copy-start.2
  17.1 0.0 collective-permute-done.2.their_near_ref
  17.2 0.0 collective-permute-done.3.their_far_ref
  17.2 0.0 copy-done.6
  17.2 0.0 copy-done.4
  17.2 0.0 copy-start.7
  17.2 2.4 %shard_map.57 = bf16[3,256,128]{2,1,0:T(8,128)(2,1)S(1)} custom-call(s32[1]{0:T(128)} %bitcast.1.odd_ref, bf16[256,512]{1,0:T(8,128)(2,1)} %collective-permute-done.2.their_near_ref, bf16[256,512]{1,0:T(8,128)(2,1)} %collective-permute-done.3.their_far_ref, f32[3,256,128]{2,1,0:T(8,128)S(1)} %shard_map.56.fetched_ref, f32[3,256,128]{2,1,0:T(8,128)S(1)} %copy-done.4, ...), custom_call_target="tpu_custom_call" | custom-call | flops 905969664 | bytes 5046788 | tf_op jit(solution)/shard_map/pallas_call | solution.py:180
  19.6 0.3 collective-permute-start.5
  19.9 1.5 %collective-permute-start.4 = (bf16[1,3,256,128]{3,2,1,0:T(8,128)(2,1)S(1)}, bf16[1,3,256,128]{3,2,1,0:T(8,128)(2,1)S(1)}, u32[]{:S(2)}, u32[]{:S(2)}) collective-permute-start(bf16[1,3,256,128]{3,2,1,0:T(8,128)(2,1)S(1)} %bitcast.14), channel_id=1, source_target_pairs={{2,0},{3,1},{0,2},{1,3},{6,4},{7,5},{4,6},{5,7},{10,8},{11,9},{8,1... | collective-permute-start | bytes 589832 | tf_op jit(solution)/shard_map/ppermute | solution.py:19
  21.4 0.0 collective-permute-done.5
  21.4 0.0 copy-done.2
  21.4 0.8 %shard_map.58.refs_2_ = f32[1,256,128]{2,1,0:T(8,128)S(1)} custom-call(s32[1]{0:T(128)} %bitcast.me_ref, bf16[1,3,256,128]{3,2,1,0:T(8,128)(2,1)S(1)} %bitcast.15, bf16[1,3,256,128]{3,2,1,0:T(8,128)(2,1)S(1)} %bitcast.19, bf16[3,1152,512]{2,1,0:T(8,128)(2,1)S(1)} %bitcast.12), custom_call_target="tpu_custom_call" | custom-call | flops 150994944 | bytes 4063236 | tf_op jit(solution)/shard_map/pallas_call | solution.py:180
  22.2 4.8 %collective-permute-done.4.refs_0_ = bf16[1,3,256,128]{3,2,1,0:T(8,128)(2,1)S(1)} collective-permute-done((bf16[1,3,256,128]{3,2,1,0:T(8,128)(2,1)S(1)}, bf16[1,3,256,128]{3,2,1,0:T(8,128)(2,1)S(1)}, u32[]{:S(2)}, u32[]{:S(2)}) %collective-permute-start.4) | collective-permute-done | bytes 196640 | tf_op jit(solution)/shard_map/ppermute | solution.py:19
  27.0 0.0 collective-permute-start.6
  27.0 1.4 %collective-permute-done.6.refs_1_ = bf16[1,3,256,128]{3,2,1,0:T(8,128)(2,1)S(1)} collective-permute-done((bf16[1,3,256,128]{3,2,1,0:T(8,128)(2,1)S(1)}, bf16[1,3,256,128]{3,2,1,0:T(8,128)(2,1)S(1)}, u32[]{:S(2)}, u32[]{:S(2)}) %collective-permute-start.6) | collective-permute-done | bytes 196640 | tf_op jit(solution)/shard_map/ppermute | solution.py:19
  28.5 0.0 copy-done.7
  28.5 1.5 %shard_map.59 = bf16[1,128,256]{2,1,0:T(8,128)(2,1)} custom-call(s32[1]{0:T(128)} %bitcast.me_ref, bf16[1,3,256,128]{3,2,1,0:T(8,128)(2,1)S(1)} %collective-permute-done.4.refs_0_, bf16[1,3,256,128]{3,2,1,0:T(8,128)(2,1)S(1)} %collective-permute-done.6.refs_1_, f32[1,256,128]{2,1,0:T(8,128)S(1)} %shard_map.58.refs_2_, bf16[3,1152,512]{2,1,0:T(8,128)(2,1)S(1)} %bitcast.13, ...), custom_call_target="tpu_custom_call" | custom-call | flops 754974720 | bytes 4129284 | tf_op jit(solution)/shard_map/pallas_call | solution.py:180
Async XLA Ops:
  0.0 13.0 %collective-permute-start = (bf16[256,512]{1,0:T(8,128)(2,1)}, bf16[256,512]{1,0:T(8,128)(2,1)}, u32[]{:S(2)}, u32[]{:S(2)}) collective-permute-start(bf16[256,512]{1,0:T(8,128)(2,1)} %bitcast.16), channel_id=1, source_target_pairs={{28,0},{5,1},{30,2},{7,3},{0,4},{9,5},{2,6},{11,7},{4,8},{13,9},{6... | collective-permute-start | bytes 786440 | tf_op jit(solution)/shard_map/ppermute | solution.py:19
  2.9 11.4 %collective-permute-start.1 = (bf16[256,512]{1,0:T(8,128)(2,1)}, bf16[256,512]{1,0:T(8,128)(2,1)}, u32[]{:S(2)}, u32[]{:S(2)}) collective-permute-start(bf16[256,512]{1,0:T(8,128)(2,1)} %bitcast.17), channel_id=1, source_target_pairs={{24,0},{9,1},{26,2},{11,3},{28,4},{13,5},{30,6},{15,7},{0,8},{17,9... | collective-permute-start | bytes 786440 | tf_op jit(solution)/shard_map/ppermute | solution.py:19
  4.5 2.0 %copy-start = (bf16[3,3,3,128,512]{4,3,2,1,0:T(8,128)(2,1)S(1)}, bf16[3,3,3,128,512]{4,3,2,1,0:T(8,128)(2,1)}, u32[]{:S(2)}) copy-start(bf16[3,3,3,128,512]{4,3,2,1,0:T(8,128)(2,1)} %param.6) | copy-start | bytes 10616836
  6.5 0.9 %copy-start.5 = (bf16[1,4,64,512]{3,2,1,0:T(8,128)(2,1)S(1)}, bf16[1,4,64,512]{3,2,1,0:T(8,128)(2,1)}, u32[]{:S(2)}) copy-start(bf16[1,4,64,512]{3,2,1,0:T(8,128)(2,1)} %param.5) | copy-start | bytes 786436
  7.5 7.3 %copy-start.1 = (bf16[3,3,3,128,512]{4,3,2,1,0:T(8,128)(2,1)S(1)}, bf16[3,3,3,128,512]{4,3,2,1,0:T(8,128)(2,1)}, u32[]{:S(2)}) copy-start(bf16[3,3,3,128,512]{4,3,2,1,0:T(8,128)(2,1)} %param.6) | copy-start | bytes 10616836
  7.5 9.7 %copy-start.6 = (f32[128]{0:T(128)S(1)}, f32[128]{0:T(128)}, u32[]{:S(2)}) copy-start(f32[128]{0:T(128)} %param.7) | copy-start | bytes 1540
  8.7 0.7 %copy-start.3 = (f32[3,256,128]{2,1,0:T(8,128)}, f32[3,256,128]{2,1,0:T(8,128)S(1)}, u32[]{:S(2)}) copy-start(f32[3,256,128]{2,1,0:T(8,128)S(1)} %shard_map.55.part_ref) | copy-start | bytes 1179652
  14.3 2.8 %collective-permute-start.2 = (bf16[256,512]{1,0:T(8,128)(2,1)}, bf16[256,512]{1,0:T(8,128)(2,1)}, u32[]{:S(2)}, u32[]{:S(2)}) collective-permute-start(bf16[256,512]{1,0:T(8,128)(2,1)} %collective-permute-done.near_ref), channel_id=1, source_target_pairs={{1,0},{0,1},{3,2},{2,3},{5,4},{4,5},{7,6},{6,7},{9,8},{8,9},{11,10... | collective-permute-start | bytes 786440 | tf_op jit(solution)/shard_map/ppermute | solution.py:19
  14.5 2.7 %collective-permute-start.3 = (bf16[256,512]{1,0:T(8,128)(2,1)}, bf16[256,512]{1,0:T(8,128)(2,1)}, u32[]{:S(2)}, u32[]{:S(2)}) collective-permute-start(bf16[256,512]{1,0:T(8,128)(2,1)} %collective-permute-done.1.far_ref), channel_id=1, source_target_pairs={{1,0},{0,1},{3,2},{2,3},{5,4},{4,5},{7,6},{6,7},{9,8},{8,9},{11,10... | collective-permute-start | bytes 786440 | tf_op jit(solution)/shard_map/ppermute | solution.py:19
  14.8 2.4 %copy-start.4 = (f32[3,256,128]{2,1,0:T(8,128)S(1)}, f32[3,256,128]{2,1,0:T(8,128)}, u32[]{:S(2)}) copy-start(f32[3,256,128]{2,1,0:T(8,128)} %copy-done.3) | copy-start | bytes 1179652
  17.1 4.3 %copy-start.2 = (bf16[3,3,3,128,512]{4,3,2,1,0:T(8,128)(2,1)S(1)}, bf16[3,3,3,128,512]{4,3,2,1,0:T(8,128)(2,1)}, u32[]{:S(2)}) copy-start(bf16[3,3,3,128,512]{4,3,2,1,0:T(8,128)(2,1)} %param.8) | copy-start | bytes 10616836
  17.2 11.3 %copy-start.7 = (f32[128]{0:T(128)S(1)}, f32[128]{0:T(128)}, u32[]{:S(2)}) copy-start(f32[128]{0:T(128)} %param.9) | copy-start | bytes 1540
  19.6 1.8 %collective-permute-start.5 = (bf16[3,256,128]{2,1,0:T(8,128)(2,1)S(1)}, bf16[3,256,128]{2,1,0:T(8,128)(2,1)S(1)}, u32[]{:S(2)}, u32[]{:S(2)}) collective-permute-start(bf16[3,256,128]{2,1,0:T(8,128)(2,1)S(1)} %shard_map.57), channel_id=1, source_target_pairs={{1,0},{0,1},{3,2},{2,3},{5,4},{4,5},{7,6},{6,7},{9,8},{8,9},{11,10... | collective-permute-start | bytes 589832 | tf_op jit(solution)/shard_map/ppermute | solution.py:19
  19.9 7.1 %collective-permute-start.4 = (bf16[1,3,256,128]{3,2,1,0:T(8,128)(2,1)S(1)}, bf16[1,3,256,128]{3,2,1,0:T(8,128)(2,1)S(1)}, u32[]{:S(2)}, u32[]{:S(2)}) collective-permute-start(bf16[1,3,256,128]{3,2,1,0:T(8,128)(2,1)S(1)} %bitcast.14), channel_id=1, source_target_pairs={{2,0},{3,1},{0,2},{1,3},{6,4},{7,5},{4,6},{5,7},{10,8},{11,9},{8,1... | collective-permute-start | bytes 589832 | tf_op jit(solution)/shard_map/ppermute | solution.py:19
  27.0 1.4 %collective-permute-start.6 = (bf16[1,3,256,128]{3,2,1,0:T(8,128)(2,1)S(1)}, bf16[1,3,256,128]{3,2,1,0:T(8,128)(2,1)S(1)}, u32[]{:S(2)}, u32[]{:S(2)}) collective-permute-start(bf16[1,3,256,128]{3,2,1,0:T(8,128)(2,1)S(1)} %collective-permute-done.4.refs_0_), channel_id=1, source_target_pairs={{1,0},{0,1},{3,2},{2,3},{5,4},{4,5},{7,6},{6,7},{9,8},{8,9},{11,10... | collective-permute-start | bytes 589832 | tf_op jit(solution)/shard_map/ppermute | solution.py:19

commit v19 on v13

--- a/solution.py
+++ b/solution.py
@@ -90,11 +90,8 @@
         @pl.when((odd_ref[0] == 0) == minus)
         def _():
             touched = side_products(acc_ref, near_ref, far_ref, w_ref, minus)
-            for plane in range(3):
-                if plane in touched:
-                    o_ref[plane] = spatial_sum(acc_ref, plane, rows_n, cols_n, outs)
-                else:
-                    o_ref[plane] = jnp.zeros(o_ref.shape[1:], o_ref.dtype)
+            for plane in touched:
+                o_ref[plane] = spatial_sum(acc_ref, plane, rows_n, cols_n, outs)
 
 
 def neighbour_kernel(rows_n, cols_n, odd_ref, their_near_ref, their_far_ref, fetched_ref, part_ref,
@@ -107,7 +104,9 @@
         def _():
             touched = side_products(acc_ref, their_near_ref, their_far_ref, w_ref, minus)
             for plane in range(3):
-                total = fetched_ref[plane] + part_ref[plane]
+                total = part_ref[plane]
+                if plane not in touched or plane == 1:
+                    total = total + fetched_ref[plane]
                 if plane in touched:
                     total = total + spatial_sum(acc_ref, plane, rows_n, cols_n, outs)
                 o_ref[plane] = jnp.maximum(total + bias, 0.0).astype(o_ref.dtype)

time: 30.2 us -> 30.2 us (level)
  no operation moved by 1% of the time
where the time goes in v19:
time: 30.2 us; the launch traced here: 30 us
  waiting for transfers between devices  11.1 us (37%)
  Pallas kernels  8.24 us (27%)
  starting transfers between devices  6.81 us (23%)
  local copies, waits for them, and re-layouts  3.71 us (12%)
    ppermute x7, waiting for transfers between devices, gathered_from(): return lax.ppermute(block, ('space', 'chan'), pairs)  11.1 us
    pallas_call x5, Pallas kernels, vmem_call(): pl.pallas_call(kernel, out_shape=out_shape, in_specs=specs, out_specs=pl....  8.24 us
    ppermute x7, starting transfers between devices, gathered_from(): return lax.ppermute(block, ('space', 'chan'), pairs)  6.81 us
    unnamed x16, local copies, waits for them, and re-layouts  3.71 us
  transfers between devices with their start and end apart: 7, of which 4 were waited for; matrix products, arithmetic and copies ran while one was open for 0% of the time, Pallas kernels for 14%

profile of v19, /device:TPU:0, one launch (start us, length us, event | category | flops | bytes accessed | tf_op | source)
XLA Modules:
  0.0 30.0 jit_solution(16814251905546215806)
XLA Ops:
  0.0 2.9 %collective-permute-start = (bf16[256,512]{1,0:T(8,128)(2,1)}, bf16[256,512]{1,0:T(8,128)(2,1)}, u32[]{:S(2)}, u32[]{:S(2)}) collective-permute-start(bf16[256,512]{1,0:T(8,128)(2,1)} %bitcast.16), channel_id=1, source_target_pairs={{28,0},{5,1},{30,2},{7,3},{0,4},{9,5},{2,6},{11,7},{4,8},{13,9},{6... | collective-permute-start | bytes 786440 | tf_op jit(solution)/shard_map/ppermute | solution.py:19
  2.9 1.6 %collective-permute-start.1 = (bf16[256,512]{1,0:T(8,128)(2,1)}, bf16[256,512]{1,0:T(8,128)(2,1)}, u32[]{:S(2)}, u32[]{:S(2)}) collective-permute-start(bf16[256,512]{1,0:T(8,128)(2,1)} %bitcast.17), channel_id=1, source_target_pairs={{24,0},{9,1},{26,2},{11,3},{28,4},{13,5},{30,6},{15,7},{0,8},{17,9... | collective-permute-start | bytes 786440 | tf_op jit(solution)/shard_map/ppermute | solution.py:19
  4.5 0.0 copy-start
  4.5 2.0 %copy-done = bf16[3,3,3,128,512]{4,3,2,1,0:T(8,128)(2,1)S(1)} copy-done((bf16[3,3,3,128,512]{4,3,2,1,0:T(8,128)(2,1)S(1)}, bf16[3,3,3,128,512]{4,3,2,1,0:T(8,128)(2,1)}, u32[]{:S(2)}) %copy-start) | copy-done | bytes 3538968
  6.5 0.0 copy-start.5
  6.5 0.9 %copy-done.5 = bf16[1,4,64,512]{3,2,1,0:T(8,128)(2,1)S(1)} copy-done((bf16[1,4,64,512]{3,2,1,0:T(8,128)(2,1)S(1)}, bf16[1,4,64,512]{3,2,1,0:T(8,128)(2,1)}, u32[]{:S(2)}) %copy-start.5) | copy-done | bytes 262168
  7.5 0.0 copy-start.1
  7.5 0.0 copy-start.6
  7.5 1.2 %shard_map.55.part_ref = f32[3,256,128]{2,1,0:T(8,128)S(1)} custom-call(bf16[256,512]{1,0:T(8,128)(2,1)S(1)} %bitcast.18, bf16[3,1152,512]{2,1,0:T(8,128)(2,1)S(1)} %bitcast.9), custom_call_target="tpu_custom_call" | custom-call | flops 905969664 | bytes 4194304 | tf_op jit(solution)/shard_map/pallas_call | solution.py:179
  8.7 0.0 copy-start.3
  8.7 0.7 %copy-done.3 = f32[3,256,128]{2,1,0:T(8,128)} copy-done((f32[3,256,128]{2,1,0:T(8,128)}, f32[3,256,128]{2,1,0:T(8,128)S(1)}, u32[]{:S(2)}) %copy-start.3) | copy-done | bytes 393240
  9.4 3.6 %collective-permute-done.near_ref = bf16[256,512]{1,0:T(8,128)(2,1)} collective-permute-done((bf16[256,512]{1,0:T(8,128)(2,1)}, bf16[256,512]{1,0:T(8,128)(2,1)}, u32[]{:S(2)}, u32[]{:S(2)}) %collective-permute-start) | collective-permute-done | bytes 262176 | tf_op jit(solution)/shard_map/ppermute | solution.py:19
  13.0 1.3 %collective-permute-done.1.far_ref = bf16[256,512]{1,0:T(8,128)(2,1)} collective-permute-done((bf16[256,512]{1,0:T(8,128)(2,1)}, bf16[256,512]{1,0:T(8,128)(2,1)}, u32[]{:S(2)}, u32[]{:S(2)}) %collective-permute-start.1) | collective-permute-done | bytes 262176 | tf_op jit(solution)/shard_map/ppermute | solution.py:19
  14.3 0.2 collective-permute-start.2
  14.5 0.3 %collective-permute-start.3 = (bf16[256,512]{1,0:T(8,128)(2,1)}, bf16[256,512]{1,0:T(8,128)(2,1)}, u32[]{:S(2)}, u32[]{:S(2)}) collective-permute-start(bf16[256,512]{1,0:T(8,128)(2,1)} %collective-permute-done.1.far_ref), channel_id=1, source_target_pairs={{1,0},{0,1},{3,2},{2,3},{5,4},{4,5},{7,6},{6,7},{9,8},{8,9},{11,10... | collective-permute-start | bytes 786440 | tf_op jit(solution)/shard_map/ppermute | solution.py:19
  14.8 0.0 copy-start.4
  14.8 0.0 copy-done.1
  14.8 2.3 %shard_map.56.fetched_ref = f32[3,256,128]{2,1,0:T(8,128)S(1)} custom-call(s32[1]{0:T(128)} %bitcast.1.odd_ref, bf16[256,512]{1,0:T(8,128)(2,1)} %collective-permute-done.near_ref, bf16[256,512]{1,0:T(8,128)(2,1)} %collective-permute-done.1.far_ref, bf16[3,1152,512]{2,1,0:T(8,128)(2,1)S(1)} %bitcast.10), custom_call_target="tpu_custom_call" | custom-call | flops 905969664 | bytes 4456452 | tf_op jit(solution)/shard_map/pallas_call | solution.py:179
  17.1 0.0 copy-start.2
  17.1 0.0 collective-permute-done.2.their_near_ref
  17.2 0.0 collective-permute-done.3.their_far_ref
  17.2 0.0 copy-done.6
  17.2 0.0 copy-done.4
  17.2 0.0 copy-start.7
  17.2 2.4 %shard_map.57 = bf16[3,256,128]{2,1,0:T(8,128)(2,1)S(1)} custom-call(s32[1]{0:T(128)} %bitcast.1.odd_ref, bf16[256,512]{1,0:T(8,128)(2,1)} %collective-permute-done.2.their_near_ref, bf16[256,512]{1,0:T(8,128)(2,1)} %collective-permute-done.3.their_far_ref, f32[3,256,128]{2,1,0:T(8,128)S(1)} %shard_map.56.fetched_ref, f32[3,256,128]{2,1,0:T(8,128)S(1)} %copy-done.4, ...), custom_call_target="tpu_custom_call" | custom-call | flops 905969664 | bytes 5046788 | tf_op jit(solution)/shard_map/pallas_call | solution.py:179
  19.6 0.3 collective-permute-start.5
  19.9 1.5 %collective-permute-start.4 = (bf16[1,3,256,128]{3,2,1,0:T(8,128)(2,1)S(1)}, bf16[1,3,256,128]{3,2,1,0:T(8,128)(2,1)S(1)}, u32[]{:S(2)}, u32[]{:S(2)}) collective-permute-start(bf16[1,3,256,128]{3,2,1,0:T(8,128)(2,1)S(1)} %bitcast.14), channel_id=1, source_target_pairs={{2,0},{3,1},{0,2},{1,3},{6,4},{7,5},{4,6},{5,7},{10,8},{11,9},{8,1... | collective-permute-start | bytes 589832 | tf_op jit(solution)/shard_map/ppermute | solution.py:19
  21.4 0.0 collective-permute-done.5
  21.4 0.0 copy-done.2
  21.4 0.8 %shard_map.58.refs_2_ = f32[1,256,128]{2,1,0:T(8,128)S(1)} custom-call(s32[1]{0:T(128)} %bitcast.me_ref, bf16[1,3,256,128]{3,2,1,0:T(8,128)(2,1)S(1)} %bitcast.15, bf16[1,3,256,128]{3,2,1,0:T(8,128)(2,1)S(1)} %bitcast.19, bf16[3,1152,512]{2,1,0:T(8,128)(2,1)S(1)} %bitcast.12), custom_call_target="tpu_custom_call" | custom-call | flops 150994944 | bytes 4063236 | tf_op jit(solution)/shard_map/pallas_call | solution.py:179
  22.2 4.8 %collective-permute-done.4.refs_0_ = bf16[1,3,256,128]{3,2,1,0:T(8,128)(2,1)S(1)} collective-permute-done((bf16[1,3,256,128]{3,2,1,0:T(8,128)(2,1)S(1)}, bf16[1,3,256,128]{3,2,1,0:T(8,128)(2,1)S(1)}, u32[]{:S(2)}, u32[]{:S(2)}) %collective-permute-start.4) | collective-permute-done | bytes 196640 | tf_op jit(solution)/shard_map/ppermute | solution.py:19
  27.0 0.0 collective-permute-start.6
  27.0 1.4 %collective-permute-done.6.refs_1_ = bf16[1,3,256,128]{3,2,1,0:T(8,128)(2,1)S(1)} collective-permute-done((bf16[1,3,256,128]{3,2,1,0:T(8,128)(2,1)S(1)}, bf16[1,3,256,128]{3,2,1,0:T(8,128)(2,1)S(1)}, u32[]{:S(2)}, u32[]{:S(2)}) %collective-permute-start.6) | collective-permute-done | bytes 196640 | tf_op jit(solution)/shard_map/ppermute | solution.py:19
  28.5 0.0 copy-done.7
  28.5 1.5 %shard_map.59 = bf16[1,128,256]{2,1,0:T(8,128)(2,1)} custom-call(s32[1]{0:T(128)} %bitcast.me_ref, bf16[1,3,256,128]{3,2,1,0:T(8,128)(2,1)S(1)} %collective-permute-done.4.refs_0_, bf16[1,3,256,128]{3,2,1,0:T(8,128)(2,1)S(1)} %collective-permute-done.6.refs_1_, f32[1,256,128]{2,1,0:T(8,128)S(1)} %shard_map.58.refs_2_, bf16[3,1152,512]{2,1,0:T(8,128)(2,1)S(1)} %bitcast.13, ...), custom_call_target="tpu_custom_call" | custom-call | flops 754974720 | bytes 4129284 | tf_op jit(solution)/shard_map/pallas_call | solution.py:179
Async XLA Ops:
  0.0 13.0 %collective-permute-start = (bf16[256,512]{1,0:T(8,128)(2,1)}, bf16[256,512]{1,0:T(8,128)(2,1)}, u32[]{:S(2)}, u32[]{:S(2)}) collective-permute-start(bf16[256,512]{1,0:T(8,128)(2,1)} %bitcast.16), channel_id=1, source_target_pairs={{28,0},{5,1},{30,2},{7,3},{0,4},{9,5},{2,6},{11,7},{4,8},{13,9},{6... | collective-permute-start | bytes 786440 | tf_op jit(solution)/shard_map/ppermute | solution.py:19
  2.9 11.4 %collective-permute-start.1 = (bf16[256,512]{1,0:T(8,128)(2,1)}, bf16[256,512]{1,0:T(8,128)(2,1)}, u32[]{:S(2)}, u32[]{:S(2)}) collective-permute-start(bf16[256,512]{1,0:T(8,128)(2,1)} %bitcast.17), channel_id=1, source_target_pairs={{24,0},{9,1},{26,2},{11,3},{28,4},{13,5},{30,6},{15,7},{0,8},{17,9... | collective-permute-start | bytes 786440 | tf_op jit(solution)/shard_map/ppermute | solution.py:19
  4.5 2.0 %copy-start = (bf16[3,3,3,128,512]{4,3,2,1,0:T(8,128)(2,1)S(1)}, bf16[3,3,3,128,512]{4,3,2,1,0:T(8,128)(2,1)}, u32[]{:S(2)}) copy-start(bf16[3,3,3,128,512]{4,3,2,1,0:T(8,128)(2,1)} %param.6) | copy-start | bytes 10616836
  6.5 0.9 %copy-start.5 = (bf16[1,4,64,512]{3,2,1,0:T(8,128)(2,1)S(1)}, bf16[1,4,64,512]{3,2,1,0:T(8,128)(2,1)}, u32[]{:S(2)}) copy-start(bf16[1,4,64,512]{3,2,1,0:T(8,128)(2,1)} %param.5) | copy-start | bytes 786436
  7.5 7.3 %copy-start.1 = (bf16[3,3,3,128,512]{4,3,2,1,0:T(8,128)(2,1)S(1)}, bf16[3,3,3,128,512]{4,3,2,1,0:T(8,128)(2,1)}, u32[]{:S(2)}) copy-start(bf16[3,3,3,128,512]{4,3,2,1,0:T(8,128)(2,1)} %param.6) | copy-start | bytes 10616836
  7.5 9.7 %copy-start.6 = (f32[128]{0:T(128)S(1)}, f32[128]{0:T(128)}, u32[]{:S(2)}) copy-start(f32[128]{0:T(128)} %param.7) | copy-start | bytes 1540
  8.7 0.7 %copy-start.3 = (f32[3,256,128]{2,1,0:T(8,128)}, f32[3,256,128]{2,1,0:T(8,128)S(1)}, u32[]{:S(2)}) copy-start(f32[3,256,128]{2,1,0:T(8,128)S(1)} %shard_map.55.part_ref) | copy-start | bytes 1179652
  14.3 2.8 %collective-permute-start.2 = (bf16[256,512]{1,0:T(8,128)(2,1)}, bf16[256,512]{1,0:T(8,128)(2,1)}, u32[]{:S(2)}, u32[]{:S(2)}) collective-permute-start(bf16[256,512]{1,0:T(8,128)(2,1)} %collective-permute-done.near_ref), channel_id=1, source_target_pairs={{1,0},{0,1},{3,2},{2,3},{5,4},{4,5},{7,6},{6,7},{9,8},{8,9},{11,10... | collective-permute-start | bytes 786440 | tf_op jit(solution)/shard_map/ppermute | solution.py:19
  14.5 2.7 %collective-permute-start.3 = (bf16[256,512]{1,0:T(8,128)(2,1)}, bf16[256,512]{1,0:T(8,128)(2,1)}, u32[]{:S(2)}, u32[]{:S(2)}) collective-permute-start(bf16[256,512]{1,0:T(8,128)(2,1)} %collective-permute-done.1.far_ref), channel_id=1, source_target_pairs={{1,0},{0,1},{3,2},{2,3},{5,4},{4,5},{7,6},{6,7},{9,8},{8,9},{11,10... | collective-permute-start | bytes 786440 | tf_op jit(solution)/shard_map/ppermute | solution.py:19
  14.8 2.4 %copy-start.4 = (f32[3,256,128]{2,1,0:T(8,128)S(1)}, f32[3,256,128]{2,1,0:T(8,128)}, u32[]{:S(2)}) copy-start(f32[3,256,128]{2,1,0:T(8,128)} %copy-done.3) | copy-start | bytes 1179652
  17.1 4.3 %copy-start.2 = (bf16[3,3,3,128,512]{4,3,2,1,0:T(8,128)(2,1)S(1)}, bf16[3,3,3,128,512]{4,3,2,1,0:T(8,128)(2,1)}, u32[]{:S(2)}) copy-start(bf16[3,3,3,128,512]{4,3,2,1,0:T(8,128)(2,1)} %param.8) | copy-start | bytes 10616836
  17.2 11.3 %copy-start.7 = (f32[128]{0:T(128)S(1)}, f32[128]{0:T(128)}, u32[]{:S(2)}) copy-start(f32[128]{0:T(128)} %param.9) | copy-start | bytes 1540
  19.6 1.8 %collective-permute-start.5 = (bf16[3,256,128]{2,1,0:T(8,128)(2,1)S(1)}, bf16[3,256,128]{2,1,0:T(8,128)(2,1)S(1)}, u32[]{:S(2)}, u32[]{:S(2)}) collective-permute-start(bf16[3,256,128]{2,1,0:T(8,128)(2,1)S(1)} %shard_map.57), channel_id=1, source_target_pairs={{1,0},{0,1},{3,2},{2,3},{5,4},{4,5},{7,6},{6,7},{9,8},{8,9},{11,10... | collective-permute-start | bytes 589832 | tf_op jit(solution)/shard_map/ppermute | solution.py:19
  19.9 7.1 %collective-permute-start.4 = (bf16[1,3,256,128]{3,2,1,0:T(8,128)(2,1)S(1)}, bf16[1,3,256,128]{3,2,1,0:T(8,128)(2,1)S(1)}, u32[]{:S(2)}, u32[]{:S(2)}) collective-permute-start(bf16[1,3,256,128]{3,2,1,0:T(8,128)(2,1)S(1)} %bitcast.14), channel_id=1, source_target_pairs={{2,0},{3,1},{0,2},{1,3},{6,4},{7,5},{4,6},{5,7},{10,8},{11,9},{8,1... | collective-permute-start | bytes 589832 | tf_op jit(solution)/shard_map/ppermute | solution.py:19
  27.0 1.4 %collective-permute-start.6 = (bf16[1,3,256,128]{3,2,1,0:T(8,128)(2,1)S(1)}, bf16[1,3,256,128]{3,2,1,0:T(8,128)(2,1)S(1)}, u32[]{:S(2)}, u32[]{:S(2)}) collective-permute-start(bf16[1,3,256,128]{3,2,1,0:T(8,128)(2,1)S(1)} %collective-permute-done.4.refs_0_), channel_id=1, source_target_pairs={{1,0},{0,1},{3,2},{2,3},{5,4},{4,5},{7,6},{6,7},{9,8},{8,9},{11,10... | collective-permute-start | bytes 589832 | tf_op jit(solution)/shard_map/ppermute | solution.py:19

commit v20 on v13

--- a/solution.py
+++ b/solution.py
@@ -147,14 +147,14 @@
 
 def own_pair_kernel(rows_n, cols_n, count, layout, me_ref, *refs):
     inputs = refs[:len(layout)]
-    w_ref, o_ref, field_ref, acc_ref = refs[len(layout):]
+    w_ref, b_ref, o_ref, field_ref, acc_ref = refs[len(layout):]
     outs = o_ref.shape[2]
     me = me_ref[0]
     blocks = held_blocks(inputs, layout)
     full = {j: None for j in range(count)}
     full.update(blocks)
     pair_products(acc_ref, full, me, lambda index: [index // 2], w_ref, field_ref, outs, True)
-    o_ref[0] = spatial_sum(acc_ref, 0, rows_n, cols_n, outs)
+    o_ref[0] = spatial_sum(acc_ref, 0, rows_n, cols_n, outs) + b_ref[...]
 
 
 def second_kernel(rows_n, cols_n, count, layout, me_ref, *refs):
@@ -168,7 +168,7 @@
     pairs = lambda index: [pair for pair in range(count // 2) if pair != index // 2]
     pair_products(acc_ref, full, me, pairs, w_ref, field_ref, outs, True)
     total = spatial_sum(acc_ref, 0, rows_n, cols_n, outs) + part_ref[0]
-    result = jnp.maximum(total + b_ref[...], 0.0)
+    result = jnp.maximum(total, 0.0)
     o_ref[0] = result.T.astype(o_ref.dtype)
 
 
@@ -242,7 +242,7 @@
     own_pair = vmem_call(
         functools.partial(own_pair_kernel, rows_n, cols_n, chans, ((0,), (1,))),
         jax.ShapeDtypeStruct((1, cells, outs), jnp.float32),
-        [me_flag, hidden[None], partner[None], two_stack],
+        [me_flag, hidden[None], partner[None], two_stack, bias_two.reshape(1, outs)],
         [pltpu.VMEM((3, cells, 2 * outs), jnp.bfloat16), pltpu.VMEM((1, cells, 9 * outs), jnp.float32)],
         2 * tap_flops // chans,
         smem_first=True,

time: 30.2 us -> 30.2 us (level)
  no operation moved by 1% of the time
where the time goes in v20:
time: 30.2 us; the launch traced here: 30 us
  waiting for transfers between devices  11.1 us (37%)
  Pallas kernels  8.25 us (27%)
  starting transfers between devices  6.81 us (23%)
  local copies, waits for them, and re-layouts  3.71 us (12%)
    ppermute x7, waiting for transfers between devices, gathered_from(): return lax.ppermute(block, ('space', 'chan'), pairs)  11.1 us
    pallas_call x5, Pallas kernels, vmem_call(): pl.pallas_call(kernel, out_shape=out_shape, in_specs=specs, out_specs=pl....  8.25 us
    ppermute x7, starting transfers between devices, gathered_from(): return lax.ppermute(block, ('space', 'chan'), pairs)  6.81 us
    unnamed x16, local copies, waits for them, and re-layouts  3.71 us
  transfers between devices with their start and end apart: 7, of which 4 were waited for; matrix products, arithmetic and copies ran while one was open for 0% of the time, Pallas kernels for 14%

profile of v20, /device:TPU:0, one launch (start us, length us, event | category | flops | bytes accessed | tf_op | source)
XLA Modules:
  0.0 30.0 jit_solution(11244685808422510811)
XLA Ops:
  0.0 2.9 %collective-permute-start = (bf16[256,512]{1,0:T(8,128)(2,1)}, bf16[256,512]{1,0:T(8,128)(2,1)}, u32[]{:S(2)}, u32[]{:S(2)}) collective-permute-start(bf16[256,512]{1,0:T(8,128)(2,1)} %bitcast.16), channel_id=1, source_target_pairs={{28,0},{5,1},{30,2},{7,3},{0,4},{9,5},{2,6},{11,7},{4,8},{13,9},{6... | collective-permute-start | bytes 786440 | tf_op jit(solution)/shard_map/ppermute | solution.py:19
  2.9 1.6 %collective-permute-start.1 = (bf16[256,512]{1,0:T(8,128)(2,1)}, bf16[256,512]{1,0:T(8,128)(2,1)}, u32[]{:S(2)}, u32[]{:S(2)}) collective-permute-start(bf16[256,512]{1,0:T(8,128)(2,1)} %bitcast.17), channel_id=1, source_target_pairs={{24,0},{9,1},{26,2},{11,3},{28,4},{13,5},{30,6},{15,7},{0,8},{17,9... | collective-permute-start | bytes 786440 | tf_op jit(solution)/shard_map/ppermute | solution.py:19
  4.5 0.0 copy-start
  4.5 2.0 %copy-done = bf16[3,3,3,128,512]{4,3,2,1,0:T(8,128)(2,1)S(1)} copy-done((bf16[3,3,3,128,512]{4,3,2,1,0:T(8,128)(2,1)S(1)}, bf16[3,3,3,128,512]{4,3,2,1,0:T(8,128)(2,1)}, u32[]{:S(2)}) %copy-start) | copy-done | bytes 3538968
  6.5 0.0 copy-start.5
  6.5 0.9 %copy-done.5 = bf16[1,4,64,512]{3,2,1,0:T(8,128)(2,1)S(1)} copy-done((bf16[1,4,64,512]{3,2,1,0:T(8,128)(2,1)S(1)}, bf16[1,4,64,512]{3,2,1,0:T(8,128)(2,1)}, u32[]{:S(2)}) %copy-start.5) | copy-done | bytes 262168
  7.5 0.0 copy-start.1
  7.5 0.0 copy-start.7
  7.5 1.2 %shard_map.55.part_ref = f32[3,256,128]{2,1,0:T(8,128)S(1)} custom-call(bf16[256,512]{1,0:T(8,128)(2,1)S(1)} %bitcast.18, bf16[3,1152,512]{2,1,0:T(8,128)(2,1)S(1)} %bitcast.9), custom_call_target="tpu_custom_call" | custom-call | flops 905969664 | bytes 4194304 | tf_op jit(solution)/shard_map/pallas_call | solution.py:180
  8.7 0.0 copy-start.3
  8.7 0.7 %copy-done.3 = f32[3,256,128]{2,1,0:T(8,128)} copy-done((f32[3,256,128]{2,1,0:T(8,128)}, f32[3,256,128]{2,1,0:T(8,128)S(1)}, u32[]{:S(2)}) %copy-start.3) | copy-done | bytes 393240
  9.4 3.6 %collective-permute-done.near_ref = bf16[256,512]{1,0:T(8,128)(2,1)} collective-permute-done((bf16[256,512]{1,0:T(8,128)(2,1)}, bf16[256,512]{1,0:T(8,128)(2,1)}, u32[]{:S(2)}, u32[]{:S(2)}) %collective-permute-start) | collective-permute-done | bytes 262176 | tf_op jit(solution)/shard_map/ppermute | solution.py:19
  13.0 1.3 %collective-permute-done.1.far_ref = bf16[256,512]{1,0:T(8,128)(2,1)} collective-permute-done((bf16[256,512]{1,0:T(8,128)(2,1)}, bf16[256,512]{1,0:T(8,128)(2,1)}, u32[]{:S(2)}, u32[]{:S(2)}) %collective-permute-start.1) | collective-permute-done | bytes 262176 | tf_op jit(solution)/shard_map/ppermute | solution.py:19
  14.3 0.2 collective-permute-start.2
  14.5 0.3 %collective-permute-start.3 = (bf16[256,512]{1,0:T(8,128)(2,1)}, bf16[256,512]{1,0:T(8,128)(2,1)}, u32[]{:S(2)}, u32[]{:S(2)}) collective-permute-start(bf16[256,512]{1,0:T(8,128)(2,1)} %collective-permute-done.1.far_ref), channel_id=1, source_target_pairs={{1,0},{0,1},{3,2},{2,3},{5,4},{4,5},{7,6},{6,7},{9,8},{8,9},{11,10... | collective-permute-start | bytes 786440 | tf_op jit(solution)/shard_map/ppermute | solution.py:19
  14.8 0.0 copy-start.4
  14.8 0.0 copy-done.1
  14.8 2.3 %shard_map.56.fetched_ref = f32[3,256,128]{2,1,0:T(8,128)S(1)} custom-call(s32[1]{0:T(128)} %bitcast.1.odd_ref, bf16[256,512]{1,0:T(8,128)(2,1)} %collective-permute-done.near_ref, bf16[256,512]{1,0:T(8,128)(2,1)} %collective-permute-done.1.far_ref, bf16[3,1152,512]{2,1,0:T(8,128)(2,1)S(1)} %bitcast.10), custom_call_target="tpu_custom_call" | custom-call | flops 905969664 | bytes 4456452 | tf_op jit(solution)/shard_map/pallas_call | solution.py:180
  17.1 0.0 copy-start.2
  17.1 0.0 copy-start.6
  17.2 0.0 collective-permute-done.2.their_near_ref
  17.2 0.0 collective-permute-done.3.their_far_ref
  17.2 0.0 copy-done.7
  17.2 0.0 copy-done.4
  17.2 2.4 %shard_map.57 = bf16[3,256,128]{2,1,0:T(8,128)(2,1)S(1)} custom-call(s32[1]{0:T(128)} %bitcast.1.odd_ref, bf16[256,512]{1,0:T(8,128)(2,1)} %collective-permute-done.2.their_near_ref, bf16[256,512]{1,0:T(8,128)(2,1)} %collective-permute-done.3.their_far_ref, f32[3,256,128]{2,1,0:T(8,128)S(1)} %shard_map.56.fetched_ref, f32[3,256,128]{2,1,0:T(8,128)S(1)} %copy-done.4, ...), custom_call_target="tpu_custom_call" | custom-call | flops 905969664 | bytes 5046788 | tf_op jit(solution)/shard_map/pallas_call | solution.py:180
  19.6 0.3 collective-permute-start.5
  19.9 1.5 %collective-permute-start.4 = (bf16[1,3,256,128]{3,2,1,0:T(8,128)(2,1)S(1)}, bf16[1,3,256,128]{3,2,1,0:T(8,128)(2,1)S(1)}, u32[]{:S(2)}, u32[]{:S(2)}) collective-permute-start(bf16[1,3,256,128]{3,2,1,0:T(8,128)(2,1)S(1)} %bitcast.14), channel_id=1, source_target_pairs={{2,0},{3,1},{0,2},{1,3},{6,4},{7,5},{4,6},{5,7},{10,8},{11,9},{8,1... | collective-permute-start | bytes 589832 | tf_op jit(solution)/shard_map/ppermute | solution.py:19
  21.4 0.0 collective-permute-done.5
  21.4 0.0 copy-done.2
  21.4 0.0 copy-done.6
  21.4 0.8 %shard_map.58.refs_2_ = f32[1,256,128]{2,1,0:T(8,128)S(1)} custom-call(s32[1]{0:T(128)} %bitcast.me_ref, bf16[1,3,256,128]{3,2,1,0:T(8,128)(2,1)S(1)} %bitcast.15, bf16[1,3,256,128]{3,2,1,0:T(8,128)(2,1)S(1)} %bitcast.19, bf16[3,1152,512]{2,1,0:T(8,128)(2,1)S(1)} %bitcast.12, f32[1,128]{1,0:T(1,128)S(1)} %bitcast.20), custom_call_target="tpu_custom_call" | custom-call | flops 150994944 | bytes 4063748 | tf_op jit(solution)/shard_map/pallas_call | solution.py:180
  22.2 4.8 %collective-permute-done.4.refs_0_ = bf16[1,3,256,128]{3,2,1,0:T(8,128)(2,1)S(1)} collective-permute-done((bf16[1,3,256,128]{3,2,1,0:T(8,128)(2,1)S(1)}, bf16[1,3,256,128]{3,2,1,0:T(8,128)(2,1)S(1)}, u32[]{:S(2)}, u32[]{:S(2)}) %collective-permute-start.4) | collective-permute-done | bytes 196640 | tf_op jit(solution)/shard_map/ppermute | solution.py:19
  27.0 0.0 collective-permute-start.6
  27.0 1.4 %collective-permute-done.6.refs_1_ = bf16[1,3,256,128]{3,2,1,0:T(8,128)(2,1)S(1)} collective-permute-done((bf16[1,3,256,128]{3,2,1,0:T(8,128)(2,1)S(1)}, bf16[1,3,256,128]{3,2,1,0:T(8,128)(2,1)S(1)}, u32[]{:S(2)}, u32[]{:S(2)}) %collective-permute-start.6) | collective-permute-done | bytes 196640 | tf_op jit(solution)/shard_map/ppermute | solution.py:19
  28.5 1.5 %shard_map.59 = bf16[1,128,256]{2,1,0:T(8,128)(2,1)} custom-call(s32[1]{0:T(128)} %bitcast.me_ref, bf16[1,3,256,128]{3,2,1,0:T(8,128)(2,1)S(1)} %collective-permute-done.4.refs_0_, bf16[1,3,256,128]{3,2,1,0:T(8,128)(2,1)S(1)} %collective-permute-done.6.refs_1_, f32[1,256,128]{2,1,0:T(8,128)S(1)} %shard_map.58.refs_2_, bf16[3,1152,512]{2,1,0:T(8,128)(2,1)S(1)} %bitcast.13, ...), custom_call_target="tpu_custom_call" | custom-call | flops 754974720 | bytes 4129284 | tf_op jit(solution)/shard_map/pallas_call | solution.py:180
Async XLA Ops:
  0.0 13.0 %collective-permute-start = (bf16[256,512]{1,0:T(8,128)(2,1)}, bf16[256,512]{1,0:T(8,128)(2,1)}, u32[]{:S(2)}, u32[]{:S(2)}) collective-permute-start(bf16[256,512]{1,0:T(8,128)(2,1)} %bitcast.16), channel_id=1, source_target_pairs={{28,0},{5,1},{30,2},{7,3},{0,4},{9,5},{2,6},{11,7},{4,8},{13,9},{6... | collective-permute-start | bytes 786440 | tf_op jit(solution)/shard_map/ppermute | solution.py:19
  2.9 11.4 %collective-permute-start.1 = (bf16[256,512]{1,0:T(8,128)(2,1)}, bf16[256,512]{1,0:T(8,128)(2,1)}, u32[]{:S(2)}, u32[]{:S(2)}) collective-permute-start(bf16[256,512]{1,0:T(8,128)(2,1)} %bitcast.17), channel_id=1, source_target_pairs={{24,0},{9,1},{26,2},{11,3},{28,4},{13,5},{30,6},{15,7},{0,8},{17,9... | collective-permute-start | bytes 786440 | tf_op jit(solution)/shard_map/ppermute | solution.py:19
  4.5 2.0 %copy-start = (bf16[3,3,3,128,512]{4,3,2,1,0:T(8,128)(2,1)S(1)}, bf16[3,3,3,128,512]{4,3,2,1,0:T(8,128)(2,1)}, u32[]{:S(2)}) copy-start(bf16[3,3,3,128,512]{4,3,2,1,0:T(8,128)(2,1)} %param.6) | copy-start | bytes 10616836
  6.5 0.9 %copy-start.5 = (bf16[1,4,64,512]{3,2,1,0:T(8,128)(2,1)S(1)}, bf16[1,4,64,512]{3,2,1,0:T(8,128)(2,1)}, u32[]{:S(2)}) copy-start(bf16[1,4,64,512]{3,2,1,0:T(8,128)(2,1)} %param.5) | copy-start | bytes 786436
  7.5 7.3 %copy-start.1 = (bf16[3,3,3,128,512]{4,3,2,1,0:T(8,128)(2,1)S(1)}, bf16[3,3,3,128,512]{4,3,2,1,0:T(8,128)(2,1)}, u32[]{:S(2)}) copy-start(bf16[3,3,3,128,512]{4,3,2,1,0:T(8,128)(2,1)} %param.6) | copy-start | bytes 10616836
  7.5 9.7 %copy-start.7 = (f32[128]{0:T(128)S(1)}, f32[128]{0:T(128)}, u32[]{:S(2)}) copy-start(f32[128]{0:T(128)} %param.7) | copy-start | bytes 1540
  8.7 0.7 %copy-start.3 = (f32[3,256,128]{2,1,0:T(8,128)}, f32[3,256,128]{2,1,0:T(8,128)S(1)}, u32[]{:S(2)}) copy-start(f32[3,256,128]{2,1,0:T(8,128)S(1)} %shard_map.55.part_ref) | copy-start | bytes 1179652
  14.3 2.9 %collective-permute-start.2 = (bf16[256,512]{1,0:T(8,128)(2,1)}, bf16[256,512]{1,0:T(8,128)(2,1)}, u32[]{:S(2)}, u32[]{:S(2)}) collective-permute-start(bf16[256,512]{1,0:T(8,128)(2,1)} %collective-permute-done.near_ref), channel_id=1, source_target_pairs={{1,0},{0,1},{3,2},{2,3},{5,4},{4,5},{7,6},{6,7},{9,8},{8,9},{11,10... | collective-permute-start | bytes 786440 | tf_op jit(solution)/shard_map/ppermute | solution.py:19
  14.5 2.7 %collective-permute-start.3 = (bf16[256,512]{1,0:T(8,128)(2,1)}, bf16[256,512]{1,0:T(8,128)(2,1)}, u32[]{:S(2)}, u32[]{:S(2)}) collective-permute-start(bf16[256,512]{1,0:T(8,128)(2,1)} %collective-permute-done.1.far_ref), channel_id=1, source_target_pairs={{1,0},{0,1},{3,2},{2,3},{5,4},{4,5},{7,6},{6,7},{9,8},{8,9},{11,10... | collective-permute-start | bytes 786440 | tf_op jit(solution)/shard_map/ppermute | solution.py:19
  14.8 2.4 %copy-start.4 = (f32[3,256,128]{2,1,0:T(8,128)S(1)}, f32[3,256,128]{2,1,0:T(8,128)}, u32[]{:S(2)}) copy-start(f32[3,256,128]{2,1,0:T(8,128)} %copy-done.3) | copy-start | bytes 1179652
  17.1 4.3 %copy-start.2 = (bf16[3,3,3,128,512]{4,3,2,1,0:T(8,128)(2,1)S(1)}, bf16[3,3,3,128,512]{4,3,2,1,0:T(8,128)(2,1)}, u32[]{:S(2)}) copy-start(bf16[3,3,3,128,512]{4,3,2,1,0:T(8,128)(2,1)} %param.8) | copy-start | bytes 10616836
  17.1 4.3 %copy-start.6 = (f32[128]{0:T(128)S(1)}, f32[128]{0:T(128)}, u32[]{:S(2)}) copy-start(f32[128]{0:T(128)} %param.9) | copy-start | bytes 1540
  19.6 1.8 %collective-permute-start.5 = (bf16[3,256,128]{2,1,0:T(8,128)(2,1)S(1)}, bf16[3,256,128]{2,1,0:T(8,128)(2,1)S(1)}, u32[]{:S(2)}, u32[]{:S(2)}) collective-permute-start(bf16[3,256,128]{2,1,0:T(8,128)(2,1)S(1)} %shard_map.57), channel_id=1, source_target_pairs={{1,0},{0,1},{3,2},{2,3},{5,4},{4,5},{7,6},{6,7},{9,8},{8,9},{11,10... | collective-permute-start | bytes 589832 | tf_op jit(solution)/shard_map/ppermute | solution.py:19
  19.9 7.1 %collective-permute-start.4 = (bf16[1,3,256,128]{3,2,1,0:T(8,128)(2,1)S(1)}, bf16[1,3,256,128]{3,2,1,0:T(8,128)(2,1)S(1)}, u32[]{:S(2)}, u32[]{:S(2)}) collective-permute-start(bf16[1,3,256,128]{3,2,1,0:T(8,128)(2,1)S(1)} %bitcast.14), channel_id=1, source_target_pairs={{2,0},{3,1},{0,2},{1,3},{6,4},{7,5},{4,6},{5,7},{10,8},{11,9},{8,1... | collective-permute-start | bytes 589832 | tf_op jit(solution)/shard_map/ppermute | solution.py:19
  27.0 1.4 %collective-permute-start.6 = (bf16[1,3,256,128]{3,2,1,0:T(8,128)(2,1)S(1)}, bf16[1,3,256,128]{3,2,1,0:T(8,128)(2,1)S(1)}, u32[]{:S(2)}, u32[]{:S(2)}) collective-permute-start(bf16[1,3,256,128]{3,2,1,0:T(8,128)(2,1)S(1)} %collective-permute-done.4.refs_0_), channel_id=1, source_target_pairs={{1,0},{0,1},{3,2},{2,3},{5,4},{4,5},{7,6},{6,7},{9,8},{8,9},{11,10... | collective-permute-start | bytes 589832 | tf_op jit(solution)/shard_map/ppermute | solution.py:19
